TPU v7x, 512 devices: a whole 4x4x16 slice. The times are simulated.
512 devices in a mesh: dp: 4 (over z_hi, core), tm: 8 (over z_lo), height: 16 (over x, y).
Axes of the slice: x: 4, y: 4, z: 16 (z_hi: 2, z_lo: 8; z = z_hi * 8 + z_lo), core: 2. Of those that a mesh axis runs over, the one named last changes fastest.
Arguments:
- clips: bfloat16 [4, 16, 64, 128, 128], P('dp', 'tm', 'height'), may hold values from -6 to 6
- frame_counts: int32 [4, 5], P('dp'), may hold values from 1 to 9, 16 in all within a row
- conv_first: bfloat16 [3, 3, 3, 128, 128], replicated, may hold values from -0.109375 to 0.109375
- conv_down: bfloat16 [3, 3, 3, 128, 128], replicated, may hold values from -0.109375 to 0.109375
- out_cotangent: bfloat16 [4, 8, 32, 64, 128], P('dp', 'tm', 'height'), may hold values from -6 to 6
Outputs:
- encoded: bfloat16 [4, 8, 32, 64, 128], P('dp', 'tm', 'height')
- grad_first: bfloat16 [3, 3, 3, 128, 128], P(None, None, None, 'dp')
- grad_down: bfloat16 [3, 3, 3, 128, 128], P(None, None, None, 'dp')
Inputs may be any that keep to these rules, and one draw needn't show every extreme that they name: `frame_counts`: each sequence's 5 clip lengths sum to 16; in every sequence one clip has exactly 9 frames.
All inputs are finite; a program needn't handle non-finite values.
Results may differ from a plain program's by a relative error of at most 0.0059.
Values may be sent and summed in bfloat16 or wider, within the bound.
No kernel may reach another device: no remote copies, remote signals or barrier semaphores. Data moves between devices by JAX's collectives and lax.ppermute only.
A program may use at most 64 MiB of HBM per device.

v0:
```python
import math

import jax
import jax.numpy as jnp
from jax import lax
from jax.sharding import PartitionSpec as P


def padded_2(cells, sides, width):
    for axis, dim in sides:
        count = lax.axis_size(axis)
        ends = count - 1
        head = lax.slice_in_dim(cells, 0, width, axis=dim)
        tail = lax.slice_in_dim(cells, cells.shape[dim] - width, cells.shape[dim], axis=dim)
        cells = jnp.concatenate(
            [
                lax.ppermute(tail, axis, [(i, (i + 1) % count) for i in range(ends)]),
                cells,
                lax.ppermute(head, axis, [((i + 1) % count, i) for i in range(ends)]),
            ],
            axis=dim,
        )
    return cells


def shifted(value, axis, steps):
    count = lax.axis_size(axis)
    leading, last = (max(0, -steps), min(count, count - steps))
    return lax.ppermute(value, axis, [(source, source + steps) for source in range(leading, last)])


def unfold(frame_slab, stride, pad_cols):
    padded = jnp.pad(frame_slab, ((0, 0), (0, 0), pad_cols, (0, 0)))
    out_rows = (padded.shape[1] - 3) // stride + 1
    out_cols = (padded.shape[2] - 3) // stride + 1
    pieces = []
    for tap_row in range(3):
        for tap_col in range(3):
            pieces.append(
                padded[
                    :,
                    tap_row : tap_row + stride * (out_rows - 1) + 1 : stride,
                    tap_col : tap_col + stride * (out_cols - 1) + 1 : stride,
                ]
            )
    joined = jnp.concatenate(pieces, axis=-1)
    return (joined.reshape(-1, joined.shape[-1]), (frame_slab.shape[0], out_rows, out_cols))


def conv_layer(extended, weight, tap_mask, out_frames, stride, pad_cols):
    channels_out = weight.shape[-1]
    summed = None
    for tap_time in range(3):
        frame_slab = extended[tap_time : tap_time + stride * (out_frames - 1) + 1 : stride]
        columns, shape_out = unfold(frame_slab, stride, pad_cols)
        kernel = weight[tap_time].reshape(-1, channels_out)
        tap_term = jnp.dot(columns, kernel, preferred_element_type=jnp.float32).reshape(
            shape_out + (channels_out,)
        )
        tap_term = tap_term * tap_mask[:, tap_time][:, None, None, None]
        summed = tap_term if summed is None else summed + tap_term
    return summed


def weight_grad(extended, grads, tap_mask, stride, pad_cols):
    out_frames = grads.shape[0]
    blocks = []
    for tap_time in range(3):
        frame_slab = extended[tap_time : tap_time + stride * (out_frames - 1) + 1 : stride]
        columns, shape_out = unfold(frame_slab, stride, pad_cols)
        masked = grads * tap_mask[:, tap_time].astype(jnp.bfloat16)[:, None, None, None]
        blocks.append(
            jnp.dot(
                columns.T, masked.reshape(-1, grads.shape[-1]), preferred_element_type=jnp.float32
            )
        )
    stacked = jnp.stack(blocks)
    return stacked.reshape(3, 3, 3, extended.shape[-1], grads.shape[-1])


def hidden_grad(grads_ext, weight, mask_ext):
    pieces = []
    for tap_time in range(3):
        masked = grads_ext * mask_ext[:, tap_time].astype(jnp.bfloat16)[:, None, None, None]
        kernel = jnp.transpose(weight[tap_time][::-1, ::-1], (0, 1, 3, 2))
        spread = lax.conv_general_dilated(
            masked,
            kernel,
            (1, 1),
            ((2, 0), (2, 2)),
            lhs_dilation=(2, 2),
            dimension_numbers=("NHWC", "HWIO", "NHWC"),
            preferred_element_type=jnp.float32,
        )
        pieces.append(spread[:, 1:, 1:])
    even_frames = pieces[2][:-1] + pieces[0][1:]
    odd_frames = pieces[1][1:]
    merged = jnp.stack([even_frames, odd_frames], axis=1)
    return merged.reshape((2 * even_frames.shape[0],) + even_frames.shape[1:])


def positions(counts_row, frame_index):
    starts = jnp.cumsum(counts_row) - counts_row
    latest = jnp.max(jnp.where(starts[None, :] <= frame_index[:, None], starts[None, :], 0), axis=1)
    return frame_index - latest


def tap_masks(place):
    return (place[:, None] >= (2 - jnp.arange(3, dtype=jnp.int32))[None, :]).astype(jnp.float32)


def body(clips, frame_counts, conv_first, conv_down, out_cotangent):
    frames_dev = clips.shape[1]
    rows_dev = clips.shape[2]
    columns_all = clips.shape[3]
    down_frames = frames_dev // 2
    counts_row = frame_counts[0]
    first_frame = lax.axis_index("tm") * frames_dev
    frame_index = first_frame + jnp.arange(frames_dev, dtype=jnp.int32)
    first_mask = tap_masks(positions(counts_row, frame_index))
    down_index = first_frame + 2 * jnp.arange(down_frames + 1, dtype=jnp.int32)
    mask_ext = tap_masks(positions(counts_row, down_index))
    down_mask = mask_ext[:down_frames]
    with_rows = padded_2(clips[0], (("height", 1),), 1)
    earlier = shifted(with_rows, "tm", 1)
    input_ext = jnp.concatenate([earlier, with_rows], axis=0)
    pre_act = conv_layer(input_ext, conv_first, first_mask, frames_dev, 1, (1, 1))
    hidden = jax.nn.silu(pre_act).astype(jnp.bfloat16)
    above = shifted(hidden[:, rows_dev - 1 :], "height", 1)
    hidden_rows = jnp.concatenate([above, hidden], axis=1)
    hidden_past = shifted(hidden_rows, "tm", 1)
    hidden_ext = jnp.concatenate([hidden_past, hidden_rows], axis=0)
    encoded = conv_layer(hidden_ext, conv_down, down_mask, down_frames, 2, (1, 0)).astype(
        jnp.bfloat16
    )
    cells_all = (
        lax.axis_size("dp")
        * clips.shape[0]
        * down_frames
        * lax.axis_size("tm")
        * (rows_dev // 2)
        * lax.axis_size("height")
        * (columns_all // 2)
    )
    scale = 1.0 / math.sqrt(cells_all)
    grads = (out_cotangent[0].astype(jnp.float32) * scale).astype(jnp.bfloat16)
    down_local = weight_grad(hidden_ext, grads, down_mask, 2, (1, 0))
    below = shifted(grads[:, 0:1], "height", -1)
    grads_rows = jnp.concatenate([grads, below], axis=1)
    grads_next = shifted(grads_rows, "tm", -1)
    grads_ext = jnp.concatenate([grads_rows, grads_next], axis=0)
    back_hidden = hidden_grad(grads_ext, conv_down, mask_ext).astype(jnp.bfloat16)
    sigma = jax.nn.sigmoid(pre_act)
    pre_grad = (back_hidden.astype(jnp.float32) * sigma * (1.0 + pre_act * (1.0 - sigma))).astype(
        jnp.bfloat16
    )
    first_local = weight_grad(input_ext, pre_grad, first_mask, 1, (1, 1))
    share = conv_first.shape[3] // lax.axis_size("dp")
    quarters = lax.axis_size("dp")

    def by_quarter(term):
        term = term.reshape(27, quarters, share, term.shape[-1])
        return jnp.transpose(term, (1, 0, 2, 3)).reshape(quarters, -1)

    stacked = jnp.concatenate([by_quarter(first_local), by_quarter(down_local)], axis=1)
    gathered = reduce_gradients(stacked).reshape(-1)
    half = gathered.shape[0] // 2
    kernel_shape = (3, 3, 3, share, conv_first.shape[-1])
    summed_first = gathered[:half].reshape(kernel_shape)
    summed_down = gathered[half:].reshape(kernel_shape)
    return (encoded[None], summed_first, summed_down)


def swap(value, axis, bit):
    return lax.ppermute(value, axis, [(i, i ^ bit) for i in range(lax.axis_size(axis))])


def swap_rows(value, bits):
    count = lax.axis_size("height")
    pairs = []
    for group in range(lax.axis_size("dp")):
        bit = bits[group % 2]
        pairs += [(group * count + i, group * count + (i ^ bit)) for i in range(count)]
    return lax.ppermute(value, ("dp", "height"), pairs)


def bits_of(count):
    return [1 << k for k in range(count.bit_length() - 1)]


def split_bit(blocks, names, name, high):
    place = names.index(name)
    mine = lax.dynamic_index_in_dim(blocks, high, place, keepdims=False)
    other = lax.dynamic_index_in_dim(blocks, 1 - high, place, keepdims=False)
    return mine, other, names[:place] + names[place + 1 :]


def reduce_gradients(stacked):
    dp_bits = bits_of(lax.axis_size("dp"))
    row_bits = bits_of(lax.axis_size("height"))
    frame_bits = bits_of(lax.axis_size("tm"))
    names = [("dp", bit) for bit in reversed(dp_bits)] + [("height", bit) for bit in reversed(row_bits)]
    blocks = stacked.reshape((2,) * len(names) + (-1, 128))
    for bit in dp_bits[:-1]:
        high = (lax.axis_index("dp") // bit) % 2
        mine, other, names = split_bit(blocks, names, ("dp", bit), high)
        blocks = mine + swap(other, "dp", bit)
    near = row_bits[0::2] + row_bits[1::2]
    crossed = [near[k ^ 1] if (k ^ 1) < len(near) else near[k] for k in range(len(near))]
    stages = list(zip(near, crossed))
    core = lax.axis_index("dp") % 2
    row = lax.axis_index("height")
    held = [names, names]
    for bits in stages:
        parts = []
        for variant in (0, 1):
            high = (row // bits[variant]) % 2
            mine, other, held[variant] = split_bit(blocks, held[variant], ("height", bits[variant]), high)
            parts.append((mine, other))
        mine = jnp.where(core == 0, parts[0][0], parts[1][0])
        other = jnp.where(core == 0, parts[0][1], parts[1][1])
        blocks = mine + swap_rows(other, bits)
    far = dp_bits[-1]
    high = (lax.axis_index("dp") // far) % 2
    mine, other, _ = split_bit(blocks, held[0], ("dp", far), high)
    blocks = mine + swap(other, "dp", far)
    for bit in frame_bits:
        blocks = blocks + swap(blocks, "tm", bit)
    piece = blocks.astype(jnp.bfloat16)
    present = [[], []]
    for bits in reversed(stages):
        other = swap_rows(piece, bits)
        options = []
        for variant in (0, 1):
            bit = bits[variant]
            high = (row // bit) % 2
            place = sum(1 for kept in present[variant] if kept > bit)
            low_first = jnp.stack([piece, other], axis=place)
            high_first = jnp.stack([other, piece], axis=place)
            options.append(jnp.where(high == 0, low_first, high_first))
            present[variant].append(bit)
        piece = jnp.where(core == 0, options[0], options[1])
    return piece


def solution(mesh):
    in_specs = (
        P("dp", "tm", "height", None, None),
        P("dp", None),
        P(),
        P(),
        P("dp", "tm", "height", None, None),
    )
    out_specs = (
        P("dp", "tm", "height", None, None),
        P(None, None, None, "dp", None),
        P(None, None, None, "dp", None),
    )
    return jax.shard_map(body, mesh=mesh, in_specs=in_specs, out_specs=out_specs, check_vma=False)
```

profile of v0, /device:TPU:6, one launch (start us, length us, event | category | flops | bytes accessed | tf_op | source)
XLA Modules:
  0.0 205.8 jit_solution(3145577231284005289)
XLA Ops:
  0.6 0.9 fusion.103
  1.6 3.5 %collective-permute-start = (bf16[2,1,128,128]{3,2,1,0:T(8,128)(2,1)S(1)}, bf16[2,1,128,128]{3,2,1,0:T(8,128)(2,1)S(1)}, u32[]{:S(2)}, u32[]{:S(2)}) collective-permute-start(bf16[2,1,128,128]{3,2,1,0:T(8,128)(2,1)S(1)} %get-tuple-element.23), channel_id=1, source_target_pairs={{0,1},{1,2},{2,3},{3,4},{4,5},{5,6},{6,7},{7,8},{8,9},{9,10},{10,1... | collective-permute-start | bytes 196616 | tf_op jit(solution)/shard_map/ppermute | solution.py:17
  5.1 4.5 %collective-permute-start.1 = (bf16[2,1,128,128]{3,2,1,0:T(8,128)(2,1)S(1)}, bf16[2,1,128,128]{3,2,1,0:T(8,128)(2,1)S(1)}, u32[]{:S(2)}, u32[]{:S(2)}) collective-permute-start(bf16[2,1,128,128]{3,2,1,0:T(8,128)(2,1)S(1)} %get-tuple-element.24), channel_id=1, source_target_pairs={{1,0},{2,1},{3,2},{4,3},{5,4},{6,5},{7,6},{8,7},{9,8},{10,9},{11,1... | collective-permute-start | bytes 196616 | tf_op jit(solution)/shard_map/ppermute | solution.py:19
  9.5 0.8 fusion.72
  10.3 3.1 %collective-permute-start.5 = (bf16[1,1,64,128]{3,2,1,0:T(8,128)(2,1)S(1)}, bf16[1,1,64,128]{3,2,1,0:T(8,128)(2,1)S(1)}, u32[]{:S(2)}, u32[]{:S(2)}) collective-permute-start(bf16[1,1,64,128]{3,2,1,0:T(8,128)(2,1)S(1)} %slice.452), channel_id=1, source_target_pairs={{1,0},{2,1},{3,2},{4,3},{5,4},{6,5},{7,6},{8,7},{9,8},{10,9},{11,1... | collective-permute-start | bytes 49160 | tf_op jit(solution)/shard_map/ppermute | solution.py:29
  13.4 0.8 reduce-window_clone.1
  14.3 0.7 subtract_bitcast_fusion
  15.3 1.3 fusion.100
  17.2 0.6 slice.457
  17.7 0.6 slice.461
  20.2 1.3 collective-permute-start.6
  21.6 4.6 %collective-permute-start.2 = (bf16[2,6,128,128]{3,2,1,0:T(8,128)(2,1)S(1)}, bf16[2,6,128,128]{3,2,1,0:T(8,128)(2,1)S(1)}, u32[]{:S(2)}, u32[]{:S(2)}) collective-permute-start(bf16[2,6,128,128]{3,2,1,0:T(8,128)(2,1)S(1)} %pad_maximum_fusion.4), channel_id=1, source_target_pairs={{0,16},{16,32},{32,48},{48,64},{64,80},{80,96},{96,112},{1,17},{17... | collective-permute-start | bytes 1179656 | tf_op jit(solution)/shard_map/ppermute | solution.py:29
  26.3 1.3 multiply_bitcast_fusion.1
  30.1 3.4 %collective-permute-done.2 = bf16[2,6,128,128]{3,2,1,0:T(8,128)(2,1)S(1)} collective-permute-done((bf16[2,6,128,128]{3,2,1,0:T(8,128)(2,1)S(1)}, bf16[2,6,128,128]{3,2,1,0:T(8,128)(2,1)S(1)}, u32[]{:S(2)}, u32[]{:S(2)}) %collective-permute-start.2) | collective-permute-done | bytes 393248 | tf_op jit(solution)/shard_map/ppermute | solution.py:29
  34.6 0.8 convolution_multiply_fusion.1
  36.3 0.8 fusion.1
  37.1 0.9 fusion.11
  38.0 0.9 convolution_bitcast_fusion.5
  38.9 0.9 convolution_bitcast_fusion.4
  39.7 0.9 convolution_bitcast_fusion.3
  40.6 2.8 %collective-permute-start.3 = (bf16[2,1,128,128]{3,2,1,0:T(8,128)(2,1)S(1)}, bf16[2,1,128,128]{3,2,1,0:T(8,128)(2,1)S(1)}, u32[]{:S(2)}, u32[]{:S(2)}) collective-permute-start(bf16[2,1,128,128]{3,2,1,0:T(8,128)(2,1)S(1)} %slice.447), channel_id=1, source_target_pairs={{0,1},{1,2},{2,3},{3,4},{4,5},{5,6},{6,7},{7,8},{8,9},{9,10},{10,1... | collective-permute-start | bytes 196616 | tf_op jit(solution)/shard_map/ppermute | solution.py:29
  43.7 2.4 %copy.350 = f32[1,4,864,128]{3,1,2,0:T(4,128)} copy(f32[1,4,864,128]{3,2,1,0:T(8,128)S(1)} %bitcast.303) | data formatting | bytes 3538944
  46.1 2.8 %collective-permute-done.3 = bf16[2,1,128,128]{3,2,1,0:T(8,128)(2,1)S(1)} collective-permute-done((bf16[2,1,128,128]{3,2,1,0:T(8,128)(2,1)S(1)}, bf16[2,1,128,128]{3,2,1,0:T(8,128)(2,1)S(1)}, u32[]{:S(2)}, u32[]{:S(2)}) %collective-permute-start.3) | collective-permute-done | bytes 65568 | tf_op jit(solution)/shard_map/ppermute | solution.py:29
  50.2 4.6 %collective-permute-start.4 = (bf16[2,5,128,128]{3,2,1,0:T(8,128)(2,1)S(1)}, bf16[2,5,128,128]{3,2,1,0:T(8,128)(2,1)S(1)}, u32[]{:S(2)}, u32[]{:S(2)}) collective-permute-start(bf16[2,5,128,128]{3,2,1,0:T(8,128)(2,1)S(1)} %pad_maximum_fusion.3), channel_id=1, source_target_pairs={{0,16},{16,32},{32,48},{48,64},{64,80},{80,96},{96,112},{1,17},{17... | collective-permute-start | bytes 983048 | tf_op jit(solution)/shard_map/ppermute | solution.py:29
  55.0 0.7 copy-done.4
  56.0 3.2 %collective-permute-done.4 = bf16[2,5,128,128]{3,2,1,0:T(8,128)(2,1)S(1)} collective-permute-done((bf16[2,5,128,128]{3,2,1,0:T(8,128)(2,1)S(1)}, bf16[2,5,128,128]{3,2,1,0:T(8,128)(2,1)S(1)}, u32[]{:S(2)}, u32[]{:S(2)}) %collective-permute-start.4) | collective-permute-done | bytes 327712 | tf_op jit(solution)/shard_map/ppermute | solution.py:29
  63.7 1.1 copy.349
  65.2 5.0 %pad_maximum_fusion = f32[4,221184]{1,0:T(4,128)S(1)} fusion(f32[4,110592]{1,0:T(4,128)S(1)} %bitcast.300, f32[4,110592]{1,0:T(4,128)S(1)} %bitcast.299), kind=kLoop, calls=%fused_computation | loop fusion | flops 884736 | bytes 7077888 | tf_op jit(solution)/shard_map/concatenate | solution.py:165
  70.2 4.2 %reshape.1921 = f32[2,2,2,2,2,2,108,128]{7,6,5,4,3,2,1,0:T(8,128)} reshape(f32[4,221184]{1,0:T(4,128)S(1)} %pad_maximum_fusion) | data formatting | bytes 7077888 | tf_op jit(solution)/shard_map/reshape | solution.py:203
  74.4 1.6 dynamic-slice_bitcast_fusion
  76.0 0.9 copy.275
  77.0 1.9 collective-permute-start.7
  78.9 3.7 %collective-permute-done.7 = f32[2,2,2,2,2,108,128]{6,4,5,3,2,1,0:T(2,128)} collective-permute-done((f32[2,2,2,2,2,108,128]{6,4,5,3,2,1,0:T(2,128)S(1)}, f32[2,2,2,2,2,108,128]{6,4,5,3,2,1,0:T(2,128)}, u32[]{:S(2)}, u32[]{:S(2)}) %collective-permute-start.7) | collective-permute-done | bytes 1769504 | tf_op jit(solution)/shard_map/ppermute | solution.py:175
  82.7 2.2 %bitcast_add_fusion = f32[2,2,2,2,2,108,128]{6,5,4,3,2,1,0:T(8,128)S(1)} fusion(f32[2,2,2,2,2,108,128]{6,4,5,3,2,1,0:T(2,128)} %collective-permute-done.7, f32[2,2,2,2,2,2,108,128]{7,6,5,4,3,2,1,0:T(8,128)} %reshape.1921, s32[]{:T(128)S(6)} %select_n.691), kind=kLoop, calls=%fused_computation.7 | loop fusion | flops 442368 | bytes 5308420 | tf_op jit(solution)/shard_map/add | solution.py:207
  85.1 1.4 copy.277
  86.4 1.9 collective-permute-start.8
  88.4 13.2 %collective-permute-done.8 = f32[2,2,2,2,108,128]{5,3,4,2,1,0:T(2,128)S(1)} collective-permute-done((f32[2,2,2,2,108,128]{5,3,4,2,1,0:T(2,128)}, f32[2,2,2,2,108,128]{5,3,4,2,1,0:T(2,128)S(1)}, u32[]{:S(2)}, u32[]{:S(2)}) %collective-permute-start.8) | collective-permute-done | bytes 884768 | tf_op jit(solution)/shard_map/ppermute | solution.py:184
  101.9 2.4 %collective-permute-start.9 = (f32[2,2,2,108,128]{4,3,2,0,1:T(8,128)S(1)}, f32[2,2,2,108,128]{4,3,2,0,1:T(8,128)S(1)}, u32[]{:S(2)}, u32[]{:S(2)}) collective-permute-start(f32[2,2,2,108,128]{4,3,2,0,1:T(8,128)S(1)} %copy_select_fusion), channel_id=1, source_target_pairs={{0,4},{1,5},{2,6},{3,7},{4,0},{5,1},{6,2},{7,3},{8,12},{9,13},{10,... | collective-permute-start | bytes 1327112 | tf_op jit(solution)/shard_map/ppermute | solution.py:184
  104.5 7.9 %collective-permute-done.9 = f32[2,2,2,108,128]{4,3,2,0,1:T(8,128)S(1)} collective-permute-done((f32[2,2,2,108,128]{4,3,2,0,1:T(8,128)S(1)}, f32[2,2,2,108,128]{4,3,2,0,1:T(8,128)S(1)}, u32[]{:S(2)}, u32[]{:S(2)}) %collective-permute-start.9) | collective-permute-done | bytes 442400 | tf_op jit(solution)/shard_map/ppermute | solution.py:184
  112.5 2.1 collective-permute-start.10
  114.5 7.5 %collective-permute-done.10 = f32[2,2,108,128]{3,2,0,1:T(8,128)S(1)} collective-permute-done((f32[2,2,108,128]{3,2,0,1:T(8,128)S(1)}, f32[2,2,108,128]{3,2,0,1:T(8,128)S(1)}, u32[]{:S(2)}, u32[]{:S(2)}) %collective-permute-start.10) | collective-permute-done | bytes 221216 | tf_op jit(solution)/shard_map/ppermute | solution.py:184
  122.1 3.2 %collective-permute-start.11 = (f32[2,108,128]{2,1,0:T(8,128)S(1)}, f32[2,108,128]{2,1,0:T(8,128)S(1)}, u32[]{:S(2)}, u32[]{:S(2)}) collective-permute-start(f32[2,108,128]{2,1,0:T(8,128)S(1)} %fusion.43), channel_id=1, source_target_pairs={{0,8},{1,9},{2,10},{3,11},{4,12},{5,13},{6,14},{7,15},{8,0},{9,1},... | collective-permute-start | bytes 331784 | tf_op jit(solution)/shard_map/ppermute | solution.py:184
  125.3 5.1 %collective-permute-done.11 = f32[2,108,128]{2,1,0:T(8,128)S(1)} collective-permute-done((f32[2,108,128]{2,1,0:T(8,128)S(1)}, f32[2,108,128]{2,1,0:T(8,128)S(1)}, u32[]{:S(2)}, u32[]{:S(2)}) %collective-permute-start.11) | collective-permute-done | bytes 110624 | tf_op jit(solution)/shard_map/ppermute | solution.py:184
  130.5 15.5 %collective-permute-start.12 = (f32[108,128]{1,0:T(8,128)S(1)}, f32[108,128]{1,0:T(8,128)S(1)}, u32[]{:S(2)}, u32[]{:S(2)}) collective-permute-start(f32[108,128]{1,0:T(8,128)S(1)} %dynamic-slice_bitcast_fusion.5), channel_id=1, source_target_pairs={{0,256},{128,384},{256,0},{384,128},{1,257},{129,385},{257,1},{385... | collective-permute-start | bytes 165896 | tf_op jit(solution)/shard_map/ppermute | solution.py:175
  146.0 3.8 %collective-permute-done.12 = f32[108,128]{1,0:T(8,128)S(1)} collective-permute-done((f32[108,128]{1,0:T(8,128)S(1)}, f32[108,128]{1,0:T(8,128)S(1)}, u32[]{:S(2)}, u32[]{:S(2)}) %collective-permute-start.12) | collective-permute-done | bytes 55328 | tf_op jit(solution)/shard_map/ppermute | solution.py:175
  149.8 2.7 %collective-permute-start.13 = (f32[108,128]{1,0:T(8,128)S(1)}, f32[108,128]{1,0:T(8,128)S(1)}, u32[]{:S(2)}, u32[]{:S(2)}) collective-permute-start(f32[108,128]{1,0:T(8,128)S(1)} %bitcast_add_fusion.2), channel_id=1, source_target_pairs={{0,16},{16,0},{32,48},{48,32},{64,80},{80,64},{96,112},{112,96},{1... | collective-permute-start | bytes 165896 | tf_op jit(solution)/shard_map/ppermute | solution.py:175
  152.7 3.8 %collective-permute-done.13 = f32[108,128]{1,0:T(8,128)S(1)} collective-permute-done((f32[108,128]{1,0:T(8,128)S(1)}, f32[108,128]{1,0:T(8,128)S(1)}, u32[]{:S(2)}, u32[]{:S(2)}) %collective-permute-start.13) | collective-permute-done | bytes 55328 | tf_op jit(solution)/shard_map/ppermute | solution.py:175
  156.5 4.2 %collective-permute-start.14 = (f32[108,128]{1,0:T(8,128)S(1)}, f32[108,128]{1,0:T(8,128)S(1)}, u32[]{:S(2)}, u32[]{:S(2)}) collective-permute-start(f32[108,128]{1,0:T(8,128)S(1)} %add.219), channel_id=1, source_target_pairs={{0,32},{16,48},{32,0},{48,16},{64,96},{80,112},{96,64},{112,80},{1... | collective-permute-start | bytes 165896 | tf_op jit(solution)/shard_map/ppermute | solution.py:175
  160.7 0.8 convolution_multiply_fusion.5
  161.5 2.3 %collective-permute-done.14 = f32[108,128]{1,0:T(8,128)S(1)} collective-permute-done((f32[108,128]{1,0:T(8,128)S(1)}, f32[108,128]{1,0:T(8,128)S(1)}, u32[]{:S(2)}, u32[]{:S(2)}) %collective-permute-start.14) | collective-permute-done | bytes 55328 | tf_op jit(solution)/shard_map/ppermute | solution.py:175
  163.8 8.2 %collective-permute-start.15 = (f32[108,128]{1,0:T(8,128)S(1)}, f32[108,128]{1,0:T(8,128)S(1)}, u32[]{:S(2)}, u32[]{:S(2)}) collective-permute-start(f32[108,128]{1,0:T(8,128)S(1)} %add.220), channel_id=1, source_target_pairs={{0,64},{16,80},{32,96},{48,112},{64,0},{80,16},{96,32},{112,48},{1... | collective-permute-start | bytes 165896 | tf_op jit(solution)/shard_map/ppermute | solution.py:175
  172.0 0.8 fusion.6
  172.9 1.3 collective-permute-done.15
  174.1 3.0 %collective-permute-start.16 = (bf16[108,128]{1,0:T(8,128)(2,1)S(1)}, bf16[108,128]{1,0:T(8,128)(2,1)S(1)}, u32[]{:S(2)}, u32[]{:S(2)}) collective-permute-start(bf16[108,128]{1,0:T(8,128)(2,1)S(1)} %add_convert_fusion), channel_id=1, source_target_pairs={{0,8},{1,9},{2,10},{3,11},{4,12},{5,13},{6,14},{7,15},{8,0},{9,1},... | collective-permute-start | bytes 82952 | tf_op jit(solution)/shard_map/ppermute | solution.py:184
  177.2 1.5 fusion.8
  178.7 2.7 %collective-permute-done.16 = bf16[108,128]{1,0:T(8,128)(2,1)S(1)} collective-permute-done((bf16[108,128]{1,0:T(8,128)(2,1)S(1)}, bf16[108,128]{1,0:T(8,128)(2,1)S(1)}, u32[]{:S(2)}, u32[]{:S(2)}) %collective-permute-start.16) | collective-permute-done | bytes 27680 | tf_op jit(solution)/shard_map/ppermute | solution.py:184
  181.5 1.9 collective-permute-start.17
  183.5 5.6 %collective-permute-done.17 = bf16[2,108,128]{2,1,0:T(8,128)(2,1)S(1)} collective-permute-done((bf16[2,108,128]{2,1,0:T(8,128)(2,1)S(1)}, bf16[2,108,128]{2,1,0:T(8,128)(2,1)S(1)}, u32[]{:S(2)}, u32[]{:S(2)}) %collective-permute-start.17) | collective-permute-done | bytes 55328 | tf_op jit(solution)/shard_map/ppermute | solution.py:184
  189.4 2.4 %collective-permute-start.18 = (bf16[2,2,108,128]{3,2,1,0:T(8,128)(2,1)S(1)}, bf16[2,2,108,128]{3,2,1,0:T(8,128)(2,1)S(1)}, u32[]{:S(2)}, u32[]{:S(2)}) collective-permute-start(bf16[2,2,108,128]{3,2,1,0:T(8,128)(2,1)S(1)} %fusion.40), channel_id=1, source_target_pairs={{0,4},{1,5},{2,6},{3,7},{4,0},{5,1},{6,2},{7,3},{8,12},{9,13},{10,... | collective-permute-start | bytes 331784 | tf_op jit(solution)/shard_map/ppermute | solution.py:184
  191.9 4.2 %collective-permute-done.18 = bf16[2,2,108,128]{3,2,1,0:T(8,128)(2,1)S(1)} collective-permute-done((bf16[2,2,108,128]{3,2,1,0:T(8,128)(2,1)S(1)}, bf16[2,2,108,128]{3,2,1,0:T(8,128)(2,1)S(1)}, u32[]{:S(2)}, u32[]{:S(2)}) %collective-permute-start.18) | collective-permute-done | bytes 110624 | tf_op jit(solution)/shard_map/ppermute | solution.py:184
  196.2 2.0 collective-permute-start.19
  198.4 5.8 %collective-permute-done.19 = bf16[2,2,2,108,128]{4,3,2,1,0:T(8,128)(2,1)S(1)} collective-permute-done((bf16[2,2,2,108,128]{4,3,2,1,0:T(8,128)(2,1)S(1)}, bf16[2,2,2,108,128]{4,3,2,1,0:T(8,128)(2,1)S(1)}, u32[]{:S(2)}, u32[]{:S(2)}) %collective-permute-start.19) | collective-permute-done | bytes 221216 | tf_op jit(solution)/shard_map/ppermute | solution.py:184
  204.4 0.7 reshape.1922
  205.1 0.7 reshape.1923
  (195 shorter events, 13.3 us)
Async XLA Ops:
  0.6 20.9 %copy-start = (bf16[1,2,4,128,128]{4,3,2,1,0:T(8,128)(2,1)S(1)}, bf16[1,2,4,128,128]{4,3,2,1,0:T(8,128)(2,1)}, u32[]{:S(2)}) copy-start(bf16[1,2,4,128,128]{4,3,2,1,0:T(8,128)(2,1)} %param.5) | copy-start | bytes 786436
  1.6 19.9 %collective-permute-start = (bf16[2,1,128,128]{3,2,1,0:T(8,128)(2,1)S(1)}, bf16[2,1,128,128]{3,2,1,0:T(8,128)(2,1)S(1)}, u32[]{:S(2)}, u32[]{:S(2)}) collective-permute-start(bf16[2,1,128,128]{3,2,1,0:T(8,128)(2,1)S(1)} %get-tuple-element.23), channel_id=1, source_target_pairs={{0,1},{1,2},{2,3},{3,4},{4,5},{5,6},{6,7},{7,8},{8,9},{9,10},{10,1... | collective-permute-start | bytes 196616 | tf_op jit(solution)/shard_map/ppermute | solution.py:17
  5.1 16.4 %collective-permute-start.1 = (bf16[2,1,128,128]{3,2,1,0:T(8,128)(2,1)S(1)}, bf16[2,1,128,128]{3,2,1,0:T(8,128)(2,1)S(1)}, u32[]{:S(2)}, u32[]{:S(2)}) collective-permute-start(bf16[2,1,128,128]{3,2,1,0:T(8,128)(2,1)S(1)} %get-tuple-element.24), channel_id=1, source_target_pairs={{1,0},{2,1},{3,2},{4,3},{5,4},{6,5},{7,6},{8,7},{9,8},{10,9},{11,1... | collective-permute-start | bytes 196616 | tf_op jit(solution)/shard_map/ppermute | solution.py:19
  10.3 9.8 %collective-permute-start.5 = (bf16[1,1,64,128]{3,2,1,0:T(8,128)(2,1)S(1)}, bf16[1,1,64,128]{3,2,1,0:T(8,128)(2,1)S(1)}, u32[]{:S(2)}, u32[]{:S(2)}) collective-permute-start(bf16[1,1,64,128]{3,2,1,0:T(8,128)(2,1)S(1)} %slice.452), channel_id=1, source_target_pairs={{1,0},{2,1},{3,2},{4,3},{5,4},{6,5},{7,6},{8,7},{9,8},{10,9},{11,1... | collective-permute-start | bytes 49160 | tf_op jit(solution)/shard_map/ppermute | solution.py:29
  15.3 12.7 %copy-start.8 = (bf16[3,3,3,128,128]{4,3,2,1,0:T(8,128)(2,1)S(1)}, bf16[3,3,3,128,128]{4,3,2,1,0:T(8,128)(2,1)}, u32[]{:S(2)}) copy-start(bf16[3,3,3,128,128]{4,3,2,1,0:T(8,128)(2,1)} %param.8) | copy-start | bytes 2654212
  15.3 12.7 %copy-start.11 = (pred[8,18]{0,1:T(8,128)(4,1)S(1)}, pred[8,18]{0,1:T(8,128)(4,1)}, u32[]{:S(2)}) copy-start(pred[8,18]{0,1:T(8,128)(4,1)} %constant.261) | copy-start | bytes 436
  20.2 6.1 %collective-permute-start.6 = (bf16[1,3,64,128]{3,2,1,0:T(8,128)(2,1)S(1)}, bf16[1,3,64,128]{3,2,1,0:T(8,128)(2,1)S(1)}, u32[]{:S(2)}, u32[]{:S(2)}) collective-permute-start(bf16[1,3,64,128]{3,2,1,0:T(8,128)(2,1)S(1)} %pad_maximum_fusion.14), channel_id=1, source_target_pairs={{16,0},{32,16},{48,32},{64,48},{80,64},{96,80},{112,96},{17,1},{33... | collective-permute-start | bytes 147464 | tf_op jit(solution)/shard_map/ppermute | solution.py:29
  21.6 12.0 %collective-permute-start.2 = (bf16[2,6,128,128]{3,2,1,0:T(8,128)(2,1)S(1)}, bf16[2,6,128,128]{3,2,1,0:T(8,128)(2,1)S(1)}, u32[]{:S(2)}, u32[]{:S(2)}) collective-permute-start(bf16[2,6,128,128]{3,2,1,0:T(8,128)(2,1)S(1)} %pad_maximum_fusion.4), channel_id=1, source_target_pairs={{0,16},{16,32},{32,48},{48,64},{64,80},{80,96},{96,112},{1,17},{17... | collective-permute-start | bytes 1179656 | tf_op jit(solution)/shard_map/ppermute | solution.py:29
  40.6 8.3 %collective-permute-start.3 = (bf16[2,1,128,128]{3,2,1,0:T(8,128)(2,1)S(1)}, bf16[2,1,128,128]{3,2,1,0:T(8,128)(2,1)S(1)}, u32[]{:S(2)}, u32[]{:S(2)}) collective-permute-start(bf16[2,1,128,128]{3,2,1,0:T(8,128)(2,1)S(1)} %slice.447), channel_id=1, source_target_pairs={{0,1},{1,2},{2,3},{3,4},{4,5},{5,6},{6,7},{7,8},{8,9},{9,10},{10,1... | collective-permute-start | bytes 196616 | tf_op jit(solution)/shard_map/ppermute | solution.py:29
  43.7 12.0 %copy-start.10 = (bf16[1,1,2,64,128]{4,3,2,1,0:T(8,128)(2,1)S(1)}, bf16[1,1,2,64,128]{4,3,2,1,0:T(8,128)(2,1)}, u32[]{:S(2)}) copy-start(bf16[1,1,2,64,128]{4,3,2,1,0:T(8,128)(2,1)} %param.9) | copy-start | bytes 98308
  50.2 9.0 %collective-permute-start.4 = (bf16[2,5,128,128]{3,2,1,0:T(8,128)(2,1)S(1)}, bf16[2,5,128,128]{3,2,1,0:T(8,128)(2,1)S(1)}, u32[]{:S(2)}, u32[]{:S(2)}) collective-permute-start(bf16[2,5,128,128]{3,2,1,0:T(8,128)(2,1)S(1)} %pad_maximum_fusion.3), channel_id=1, source_target_pairs={{0,16},{16,32},{32,48},{48,64},{64,80},{80,96},{96,112},{1,17},{17... | collective-permute-start | bytes 983048 | tf_op jit(solution)/shard_map/ppermute | solution.py:29
  55.0 0.7 copy-start.4
  61.9 0.7 copy-start.6
  62.3 0.7 copy-start.2
  63.7 1.5 copy-start.1
  77.0 5.7 %collective-permute-start.7 = (f32[2,2,2,2,2,108,128]{6,4,5,3,2,1,0:T(2,128)S(1)}, f32[2,2,2,2,2,108,128]{6,4,5,3,2,1,0:T(2,128)}, u32[]{:S(2)}, u32[]{:S(2)}) collective-permute-start(f32[2,2,2,2,2,108,128]{6,4,5,3,2,1,0:T(2,128)S(1)} %copy.275), channel_id=1, source_target_pairs={{0,128},{128,0},{256,384},{384,256},{1,129},{129,1},{257,385},{385... | collective-permute-start | bytes 5308424 | tf_op jit(solution)/shard_map/ppermute | solution.py:175
  86.4 15.1 %collective-permute-start.8 = (f32[2,2,2,2,108,128]{5,3,4,2,1,0:T(2,128)}, f32[2,2,2,2,108,128]{5,3,4,2,1,0:T(2,128)S(1)}, u32[]{:S(2)}, u32[]{:S(2)}) collective-permute-start(f32[2,2,2,2,108,128]{5,3,4,2,1,0:T(2,128)} %copy.277), channel_id=1, source_target_pairs={{0,1},{1,0},{2,3},{3,2},{4,5},{5,4},{6,7},{7,6},{8,9},{9,8},{10,11... | collective-permute-start | bytes 2654216 | tf_op jit(solution)/shard_map/ppermute | solution.py:184
  101.9 10.4 %collective-permute-start.9 = (f32[2,2,2,108,128]{4,3,2,0,1:T(8,128)S(1)}, f32[2,2,2,108,128]{4,3,2,0,1:T(8,128)S(1)}, u32[]{:S(2)}, u32[]{:S(2)}) collective-permute-start(f32[2,2,2,108,128]{4,3,2,0,1:T(8,128)S(1)} %copy_select_fusion), channel_id=1, source_target_pairs={{0,4},{1,5},{2,6},{3,7},{4,0},{5,1},{6,2},{7,3},{8,12},{9,13},{10,... | collective-permute-start | bytes 1327112 | tf_op jit(solution)/shard_map/ppermute | solution.py:184
  112.3 40.3 %copy-start.9 = (bf16[3,3,3,128,128]{4,3,2,1,0:T(8,128)(2,1)S(1)}, bf16[3,3,3,128,128]{4,3,2,1,0:T(8,128)(2,1)}, u32[]{:S(2)}) copy-start(bf16[3,3,3,128,128]{4,3,2,1,0:T(8,128)(2,1)} %param.8) | copy-start | bytes 2654212
  112.4 48.3 %copy-start.3 = (bf16[1,2,64,1152]{3,2,1,0:T(8,128)(2,1)S(1)}, bf16[1,2,64,1152]{3,2,1,0:T(8,128)(2,1)}, u32[]{:S(2)}) copy-start(bf16[1,2,64,1152]{3,2,1,0:T(8,128)(2,1)} %copy-done.2) | copy-start | bytes 884740
  112.5 9.6 %collective-permute-start.10 = (f32[2,2,108,128]{3,2,0,1:T(8,128)S(1)}, f32[2,2,108,128]{3,2,0,1:T(8,128)S(1)}, u32[]{:S(2)}, u32[]{:S(2)}) collective-permute-start(f32[2,2,108,128]{3,2,0,1:T(8,128)S(1)} %bitcast_select_fusion.2), channel_id=1, source_target_pairs={{0,2},{1,3},{2,0},{3,1},{4,6},{5,7},{6,4},{7,5},{8,10},{9,11},{10,... | collective-permute-start | bytes 663560 | tf_op jit(solution)/shard_map/ppermute | solution.py:184
  122.0 50.0 %copy-start.7 = (bf16[1,2,64,1152]{3,2,1,0:T(8,128)(2,1)S(1)}, bf16[1,2,64,1152]{3,2,1,0:T(8,128)(2,1)}, u32[]{:S(2)}) copy-start(bf16[1,2,64,1152]{3,2,1,0:T(8,128)(2,1)} %copy-done.6) | copy-start | bytes 884740
  122.1 55.1 %copy-start.5 = (bf16[1,2,64,1152]{3,2,1,0:T(8,128)(2,1)S(1)}, bf16[1,2,64,1152]{3,2,1,0:T(8,128)(2,1)}, u32[]{:S(2)}) copy-start(bf16[1,2,64,1152]{3,2,1,0:T(8,128)(2,1)} %copy-done.4) | copy-start | bytes 884740
  122.1 8.3 %collective-permute-start.11 = (f32[2,108,128]{2,1,0:T(8,128)S(1)}, f32[2,108,128]{2,1,0:T(8,128)S(1)}, u32[]{:S(2)}, u32[]{:S(2)}) collective-permute-start(f32[2,108,128]{2,1,0:T(8,128)S(1)} %fusion.43), channel_id=1, source_target_pairs={{0,8},{1,9},{2,10},{3,11},{4,12},{5,13},{6,14},{7,15},{8,0},{9,1},... | collective-permute-start | bytes 331784 | tf_op jit(solution)/shard_map/ppermute | solution.py:184
  130.5 19.4 %collective-permute-start.12 = (f32[108,128]{1,0:T(8,128)S(1)}, f32[108,128]{1,0:T(8,128)S(1)}, u32[]{:S(2)}, u32[]{:S(2)}) collective-permute-start(f32[108,128]{1,0:T(8,128)S(1)} %dynamic-slice_bitcast_fusion.5), channel_id=1, source_target_pairs={{0,256},{128,384},{256,0},{384,128},{1,257},{129,385},{257,1},{385... | collective-permute-start | bytes 165896 | tf_op jit(solution)/shard_map/ppermute | solution.py:175
  149.8 6.7 %collective-permute-start.13 = (f32[108,128]{1,0:T(8,128)S(1)}, f32[108,128]{1,0:T(8,128)S(1)}, u32[]{:S(2)}, u32[]{:S(2)}) collective-permute-start(f32[108,128]{1,0:T(8,128)S(1)} %bitcast_add_fusion.2), channel_id=1, source_target_pairs={{0,16},{16,0},{32,48},{48,32},{64,80},{80,64},{96,112},{112,96},{1... | collective-permute-start | bytes 165896 | tf_op jit(solution)/shard_map/ppermute | solution.py:175
  156.5 7.2 %collective-permute-start.14 = (f32[108,128]{1,0:T(8,128)S(1)}, f32[108,128]{1,0:T(8,128)S(1)}, u32[]{:S(2)}, u32[]{:S(2)}) collective-permute-start(f32[108,128]{1,0:T(8,128)S(1)} %add.219), channel_id=1, source_target_pairs={{0,32},{16,48},{32,0},{48,16},{64,96},{80,112},{96,64},{112,80},{1... | collective-permute-start | bytes 165896 | tf_op jit(solution)/shard_map/ppermute | solution.py:175
  163.8 10.4 %collective-permute-start.15 = (f32[108,128]{1,0:T(8,128)S(1)}, f32[108,128]{1,0:T(8,128)S(1)}, u32[]{:S(2)}, u32[]{:S(2)}) collective-permute-start(f32[108,128]{1,0:T(8,128)S(1)} %add.220), channel_id=1, source_target_pairs={{0,64},{16,80},{32,96},{48,112},{64,0},{80,16},{96,32},{112,48},{1... | collective-permute-start | bytes 165896 | tf_op jit(solution)/shard_map/ppermute | solution.py:175
  174.1 7.3 %collective-permute-start.16 = (bf16[108,128]{1,0:T(8,128)(2,1)S(1)}, bf16[108,128]{1,0:T(8,128)(2,1)S(1)}, u32[]{:S(2)}, u32[]{:S(2)}) collective-permute-start(bf16[108,128]{1,0:T(8,128)(2,1)S(1)} %add_convert_fusion), channel_id=1, source_target_pairs={{0,8},{1,9},{2,10},{3,11},{4,12},{5,13},{6,14},{7,15},{8,0},{9,1},... | collective-permute-start | bytes 82952 | tf_op jit(solution)/shard_map/ppermute | solution.py:184
  181.5 7.6 %collective-permute-start.17 = (bf16[2,108,128]{2,1,0:T(8,128)(2,1)S(1)}, bf16[2,108,128]{2,1,0:T(8,128)(2,1)S(1)}, u32[]{:S(2)}, u32[]{:S(2)}) collective-permute-start(bf16[2,108,128]{2,1,0:T(8,128)(2,1)S(1)} %select_select_fusion.1), channel_id=1, source_target_pairs={{0,2},{1,3},{2,0},{3,1},{4,6},{5,7},{6,4},{7,5},{8,10},{9,11},{10,... | collective-permute-start | bytes 165896 | tf_op jit(solution)/shard_map/ppermute | solution.py:184
  189.4 6.7 %collective-permute-start.18 = (bf16[2,2,108,128]{3,2,1,0:T(8,128)(2,1)S(1)}, bf16[2,2,108,128]{3,2,1,0:T(8,128)(2,1)S(1)}, u32[]{:S(2)}, u32[]{:S(2)}) collective-permute-start(bf16[2,2,108,128]{3,2,1,0:T(8,128)(2,1)S(1)} %fusion.40), channel_id=1, source_target_pairs={{0,4},{1,5},{2,6},{3,7},{4,0},{5,1},{6,2},{7,3},{8,12},{9,13},{10,... | collective-permute-start | bytes 331784 | tf_op jit(solution)/shard_map/ppermute | solution.py:184
  196.2 7.9 %collective-permute-start.19 = (bf16[2,2,2,108,128]{4,3,2,1,0:T(8,128)(2,1)S(1)}, bf16[2,2,2,108,128]{4,3,2,1,0:T(8,128)(2,1)S(1)}, u32[]{:S(2)}, u32[]{:S(2)}) collective-permute-start(bf16[2,2,2,108,128]{4,3,2,1,0:T(8,128)(2,1)S(1)} %copy.299), channel_id=1, source_target_pairs={{0,1},{1,0},{2,3},{3,2},{4,5},{5,4},{6,7},{7,6},{8,9},{9,8},{10,11... | collective-permute-start | bytes 663560 | tf_op jit(solution)/shard_map/ppermute | solution.py:184
where the time goes:
time: 207 us; the launch traced here: 206 us
  waiting for transfers between devices  76.4 us (37%)
  starting transfers between devices  75.7 us (37%)
  local copies, waits for them, and re-layouts  26.3 us (13%)
  other arithmetic  13.2 us (6%)
  matrix products  9.99 us (5%)
  between operations  4.23 us (2%)
    ppermute x8, waiting for transfers between devices, swap_rows(): return lax.ppermute(value, ('dp', 'height'), pairs)  52 us
    ppermute x5, starting transfers between devices, swap(): lax.ppermute(value, axis, [(i, i ^ bit) for i in range(lax.axis_size(axis...  32.6 us
    ppermute x8, starting transfers between devices, swap_rows(): return lax.ppermute(value, ('dp', 'height'), pairs)  18.9 us
    ppermute x5, starting transfers between devices, shifted(): lax.ppermute(value, axis, [(source, source + steps) for source in range(l...  16.3 us
    ppermute x5, waiting for transfers between devices, swap(): lax.ppermute(value, axis, [(i, i ^ bit) for i in range(lax.axis_size(axis...  14.9 us
    ppermute x5, waiting for transfers between devices, shifted(): lax.ppermute(value, axis, [(source, source + steps) for source in range(l...  9.51 us
    unnamed x77, local copies, waits for them, and re-layouts  7.82 us
    dot_general x6, matrix products, conv_layer(): jnp.dot(columns, kernel, preferred_element_type=jnp.float32)  5.61 us
  transfers between devices with their start and end apart: 20, of which 16 were waited for; matrix products, arithmetic and copies ran while one was open for 8% of the time, Pallas kernels for 0%

commit v1 on v0

--- a/solution.py
+++ b/solution.py
@@ -158,16 +158,22 @@
     share = conv_first.shape[3] // lax.axis_size("dp")
     quarters = lax.axis_size("dp")
 
+    lanes = conv_first.shape[-1]
+    rows_total = 27 * share
+    chunks = lax.axis_size("height") // 2
+    chunk_rows = -(-rows_total // (chunks * 16)) * 16
+    padded_rows = chunk_rows * chunks
+
     def by_quarter(term):
-        term = term.reshape(27, quarters, share, term.shape[-1])
-        return jnp.transpose(term, (1, 0, 2, 3)).reshape(quarters, -1)
-
-    stacked = jnp.concatenate([by_quarter(first_local), by_quarter(down_local)], axis=1)
-    gathered = reduce_gradients(stacked).reshape(-1)
-    half = gathered.shape[0] // 2
-    kernel_shape = (3, 3, 3, share, conv_first.shape[-1])
-    summed_first = gathered[:half].reshape(kernel_shape)
-    summed_down = gathered[half:].reshape(kernel_shape)
+        term = term.reshape(27, quarters, share, lanes)
+        term = jnp.transpose(term, (1, 0, 2, 3)).reshape(quarters, rows_total, lanes)
+        return jnp.pad(term, ((0, 0), (0, padded_rows - rows_total), (0, 0)))
+
+    stacked = jnp.stack([by_quarter(first_local), by_quarter(down_local)], axis=1)
+    gathered = reduce_gradients(stacked).reshape(2, padded_rows, lanes)[:, :rows_total]
+    kernel_shape = (3, 3, 3, share, lanes)
+    summed_first = gathered[0].reshape(kernel_shape)
+    summed_down = gathered[1].reshape(kernel_shape)
     return (encoded[None], summed_first, summed_down)
 
 

time: 207 us -> 207 us (level)
  other arithmetic: 13.2 us -> 10.4 us
    slice x27, local copies, waits for them, and re-layouts: 3.37 us -> 9.48 us  [unfold(): padded[:, tap_row:tap_row + stride * (out_rows - 1) + 1:stride, tap_col:t...]
    reshape x3 -> x0, local copies, waits for them, and re-layouts: 5.66 us -> none  [the longest x1 4.21 us: reduce_gradients(): blocks = stacked.reshape((2,) * len(names) + (-1, 128))]
    concatenate x1 -> x0, other arithmetic: 5.04 us -> none  [body(): jnp.concatenate([by_quarter(first_local), by_quarter(down_local)], axis=1)]
    unnamed x77 -> x65, local copies, waits for them, and re-layouts: 7.82 us -> 11.2 us
    squeeze x3 -> x1, local copies, waits for them, and re-layouts: 2.55 us -> 0.01 us  [split_bit(): other = lax.dynamic_index_in_dim(blocks, 1 - high, place, keepdims=False)]
where the time goes in v1:
time: 207 us; the launch traced here: 205 us
  waiting for transfers between devices  77.2 us (37%)
  starting transfers between devices  75.4 us (36%)
  local copies, waits for them, and re-layouts  28.2 us (14%)
  other arithmetic  10.4 us (5%)
  matrix products  9.99 us (5%)
  between operations  4.04 us (2%)
    ppermute x8, waiting for transfers between devices, swap_rows(): return lax.ppermute(value, ('dp', 'height'), pairs)  52.1 us
    ppermute x5, starting transfers between devices, swap(): lax.ppermute(value, axis, [(i, i ^ bit) for i in range(lax.axis_size(axis...  32.6 us
    ppermute x8, starting transfers between devices, swap_rows(): return lax.ppermute(value, ('dp', 'height'), pairs)  18.6 us
    ppermute x5, starting transfers between devices, shifted(): lax.ppermute(value, axis, [(source, source + steps) for source in range(l...  16.3 us
    ppermute x5, waiting for transfers between devices, swap(): lax.ppermute(value, axis, [(i, i ^ bit) for i in range(lax.axis_size(axis...  15.2 us
    unnamed x65, local copies, waits for them, and re-layouts  11.2 us
    ppermute x5, waiting for transfers between devices, shifted(): lax.ppermute(value, axis, [(source, source + steps) for source in range(l...  9.85 us
    slice x27, local copies, waits for them, and re-layouts, unfold(): padded[:, tap_row:tap_row + stride * (out_rows - 1) + 1:stride, tap_col:t...  9.48 us
  transfers between devices with their start and end apart: 20, of which 16 were waited for; matrix products, arithmetic and copies ran while one was open for 8% of the time, Pallas kernels for 0%

profile of v1, /device:TPU:6, one launch (start us, length us, event | category | flops | bytes accessed | tf_op | source)
XLA Modules:
  0.0 205.3 jit_solution(13871236355670802033)
XLA Ops:
  0.6 0.9 fusion.108
  1.6 3.5 %collective-permute-start = (bf16[2,1,128,128]{3,2,1,0:T(8,128)(2,1)S(1)}, bf16[2,1,128,128]{3,2,1,0:T(8,128)(2,1)S(1)}, u32[]{:S(2)}, u32[]{:S(2)}) collective-permute-start(bf16[2,1,128,128]{3,2,1,0:T(8,128)(2,1)S(1)} %get-tuple-element.27), channel_id=1, source_target_pairs={{0,1},{1,2},{2,3},{3,4},{4,5},{5,6},{6,7},{7,8},{8,9},{9,10},{10,1... | collective-permute-start | bytes 196616 | tf_op jit(solution)/shard_map/ppermute | solution.py:17
  5.1 4.5 %collective-permute-start.1 = (bf16[2,1,128,128]{3,2,1,0:T(8,128)(2,1)S(1)}, bf16[2,1,128,128]{3,2,1,0:T(8,128)(2,1)S(1)}, u32[]{:S(2)}, u32[]{:S(2)}) collective-permute-start(bf16[2,1,128,128]{3,2,1,0:T(8,128)(2,1)S(1)} %get-tuple-element.28), channel_id=1, source_target_pairs={{1,0},{2,1},{3,2},{4,3},{5,4},{6,5},{7,6},{8,7},{9,8},{10,9},{11,1... | collective-permute-start | bytes 196616 | tf_op jit(solution)/shard_map/ppermute | solution.py:19
  9.5 0.8 fusion.77
  10.3 3.1 %collective-permute-start.5 = (bf16[1,1,64,128]{3,2,1,0:T(8,128)(2,1)S(1)}, bf16[1,1,64,128]{3,2,1,0:T(8,128)(2,1)S(1)}, u32[]{:S(2)}, u32[]{:S(2)}) collective-permute-start(bf16[1,1,64,128]{3,2,1,0:T(8,128)(2,1)S(1)} %slice.453), channel_id=1, source_target_pairs={{1,0},{2,1},{3,2},{4,3},{5,4},{6,5},{7,6},{8,7},{9,8},{10,9},{11,1... | collective-permute-start | bytes 49160 | tf_op jit(solution)/shard_map/ppermute | solution.py:29
  13.4 0.8 reduce-window_clone.1
  15.3 1.3 fusion.105
  20.2 1.3 collective-permute-start.6
  21.6 4.6 %collective-permute-start.2 = (bf16[2,6,128,128]{3,2,1,0:T(8,128)(2,1)S(1)}, bf16[2,6,128,128]{3,2,1,0:T(8,128)(2,1)S(1)}, u32[]{:S(2)}, u32[]{:S(2)}) collective-permute-start(bf16[2,6,128,128]{3,2,1,0:T(8,128)(2,1)S(1)} %pad_maximum_fusion.4), channel_id=1, source_target_pairs={{0,16},{16,32},{32,48},{48,64},{64,80},{80,96},{96,112},{1,17},{17... | collective-permute-start | bytes 1179656 | tf_op jit(solution)/shard_map/ppermute | solution.py:29
  26.3 1.3 multiply_bitcast_fusion.1
  30.1 3.4 %collective-permute-done.2 = bf16[2,6,128,128]{3,2,1,0:T(8,128)(2,1)S(1)} collective-permute-done((bf16[2,6,128,128]{3,2,1,0:T(8,128)(2,1)S(1)}, bf16[2,6,128,128]{3,2,1,0:T(8,128)(2,1)S(1)}, u32[]{:S(2)}, u32[]{:S(2)}) %collective-permute-start.2) | collective-permute-done | bytes 393248 | tf_op jit(solution)/shard_map/ppermute | solution.py:29
  34.6 0.8 convolution_multiply_fusion.1
  36.3 0.8 fusion.6
  37.1 0.9 fusion.16
  38.1 2.8 %collective-permute-start.3 = (bf16[2,1,128,128]{3,2,1,0:T(8,128)(2,1)S(1)}, bf16[2,1,128,128]{3,2,1,0:T(8,128)(2,1)S(1)}, u32[]{:S(2)}, u32[]{:S(2)}) collective-permute-start(bf16[2,1,128,128]{3,2,1,0:T(8,128)(2,1)S(1)} %slice.448), channel_id=1, source_target_pairs={{0,1},{1,2},{2,3},{3,4},{4,5},{5,6},{6,7},{7,8},{8,9},{9,10},{10,1... | collective-permute-start | bytes 196616 | tf_op jit(solution)/shard_map/ppermute | solution.py:29
  40.8 0.9 convolution_bitcast_fusion.5
  41.7 0.9 convolution_bitcast_fusion.4
  42.6 0.9 convolution_bitcast_fusion.3
  43.9 2.5 %collective-permute-done.3 = bf16[2,1,128,128]{3,2,1,0:T(8,128)(2,1)S(1)} collective-permute-done((bf16[2,1,128,128]{3,2,1,0:T(8,128)(2,1)S(1)}, bf16[2,1,128,128]{3,2,1,0:T(8,128)(2,1)S(1)}, u32[]{:S(2)}, u32[]{:S(2)}) %collective-permute-start.3) | collective-permute-done | bytes 65568 | tf_op jit(solution)/shard_map/ppermute | solution.py:29
  47.6 4.6 %collective-permute-start.4 = (bf16[2,5,128,128]{3,2,1,0:T(8,128)(2,1)S(1)}, bf16[2,5,128,128]{3,2,1,0:T(8,128)(2,1)S(1)}, u32[]{:S(2)}, u32[]{:S(2)}) collective-permute-start(bf16[2,5,128,128]{3,2,1,0:T(8,128)(2,1)S(1)} %pad_maximum_fusion.3), channel_id=1, source_target_pairs={{0,16},{16,32},{32,48},{48,64},{64,80},{80,96},{96,112},{1,17},{17... | collective-permute-start | bytes 983048 | tf_op jit(solution)/shard_map/ppermute | solution.py:29
  52.7 3.9 %collective-permute-done.4 = bf16[2,5,128,128]{3,2,1,0:T(8,128)(2,1)S(1)} collective-permute-done((bf16[2,5,128,128]{3,2,1,0:T(8,128)(2,1)S(1)}, bf16[2,5,128,128]{3,2,1,0:T(8,128)(2,1)S(1)}, u32[]{:S(2)}, u32[]{:S(2)}) %collective-permute-start.4) | collective-permute-done | bytes 327712 | tf_op jit(solution)/shard_map/ppermute | solution.py:29
  61.5 0.8 slice.407
  66.0 0.8 constant_dynamic-update-slice_fusion.17
  66.7 0.8 constant_dynamic-update-slice_fusion.16
  67.5 0.8 constant_dynamic-update-slice_fusion.15
  68.3 0.8 constant_dynamic-update-slice_fusion.14
  69.0 0.8 constant_dynamic-update-slice_fusion.13
  69.8 0.8 constant_dynamic-update-slice_fusion.12
  70.6 0.8 constant_dynamic-update-slice_fusion.11
  71.3 0.8 constant_dynamic-update-slice_fusion.10
  72.4 0.8 constant_dynamic-update-slice_fusion.8
  74.8 1.5 fusion.1
  76.6 1.9 collective-permute-start.7
  78.6 4.0 %collective-permute-done.7 = f32[2,2,2,2,2,112,128]{6,5,4,3,2,0,1:T(8,128)} collective-permute-done((f32[2,2,2,2,2,112,128]{6,5,4,3,2,0,1:T(8,128)}, f32[2,2,2,2,2,112,128]{6,5,4,3,2,0,1:T(8,128)}, u32[]{:S(2)}, u32[]{:S(2)}) %collective-permute-start.7) | collective-permute-done | bytes 1835040 | tf_op jit(solution)/shard_map/ppermute | solution.py:181
  82.6 1.9 fusion.4
  84.9 1.9 collective-permute-start.8
  86.8 13.4 %collective-permute-done.8 = f32[2,2,2,2,112,128]{5,4,2,0,3,1:T(8,128)S(1)} collective-permute-done((f32[2,2,2,2,112,128]{5,4,2,0,3,1:T(8,128)S(1)}, f32[2,2,2,2,112,128]{5,4,2,0,3,1:T(8,128)S(1)}, u32[]{:S(2)}, u32[]{:S(2)}) %collective-permute-start.8) | collective-permute-done | bytes 917536 | tf_op jit(solution)/shard_map/ppermute | solution.py:190
  100.5 2.4 %collective-permute-start.9 = (f32[2,2,2,112,128]{4,3,1,0,2:T(8,128)S(1)}, f32[2,2,2,112,128]{4,3,1,0,2:T(8,128)S(1)}, u32[]{:S(2)}, u32[]{:S(2)}) collective-permute-start(f32[2,2,2,112,128]{4,3,1,0,2:T(8,128)S(1)} %bitcast_select_fusion.2), channel_id=1, source_target_pairs={{0,4},{1,5},{2,6},{3,7},{4,0},{5,1},{6,2},{7,3},{8,12},{9,13},{10,... | collective-permute-start | bytes 1376264 | tf_op jit(solution)/shard_map/ppermute | solution.py:190
  103.1 7.9 %collective-permute-done.9 = f32[2,2,2,112,128]{4,3,1,0,2:T(8,128)S(1)} collective-permute-done((f32[2,2,2,112,128]{4,3,1,0,2:T(8,128)S(1)}, f32[2,2,2,112,128]{4,3,1,0,2:T(8,128)S(1)}, u32[]{:S(2)}, u32[]{:S(2)}) %collective-permute-start.9) | collective-permute-done | bytes 458784 | tf_op jit(solution)/shard_map/ppermute | solution.py:190
  111.7 1.2 fusion.18
  112.9 1.9 collective-permute-start.10
  114.9 7.5 %collective-permute-done.10 = f32[2,2,112,128]{3,2,0,1:T(8,128)S(1)} collective-permute-done((f32[2,2,112,128]{3,2,0,1:T(8,128)S(1)}, f32[2,2,112,128]{3,2,0,1:T(8,128)S(1)}, u32[]{:S(2)}, u32[]{:S(2)}) %collective-permute-start.10) | collective-permute-done | bytes 229408 | tf_op jit(solution)/shard_map/ppermute | solution.py:190
  122.4 3.0 %collective-permute-start.11 = (f32[2,112,128]{2,1,0:T(8,128)S(1)}, f32[2,112,128]{2,1,0:T(8,128)S(1)}, u32[]{:S(2)}, u32[]{:S(2)}) collective-permute-start(f32[2,112,128]{2,1,0:T(8,128)S(1)} %fusion.48), channel_id=1, source_target_pairs={{0,8},{1,9},{2,10},{3,11},{4,12},{5,13},{6,14},{7,15},{8,0},{9,1},... | collective-permute-start | bytes 344072 | tf_op jit(solution)/shard_map/ppermute | solution.py:190
  125.5 5.1 %collective-permute-done.11 = f32[2,112,128]{2,1,0:T(8,128)S(1)} collective-permute-done((f32[2,112,128]{2,1,0:T(8,128)S(1)}, f32[2,112,128]{2,1,0:T(8,128)S(1)}, u32[]{:S(2)}, u32[]{:S(2)}) %collective-permute-start.11) | collective-permute-done | bytes 114720 | tf_op jit(solution)/shard_map/ppermute | solution.py:190
  130.7 15.5 %collective-permute-start.12 = (f32[112,128]{1,0:T(8,128)S(1)}, f32[112,128]{1,0:T(8,128)S(1)}, u32[]{:S(2)}, u32[]{:S(2)}) collective-permute-start(f32[112,128]{1,0:T(8,128)S(1)} %dynamic-slice_bitcast_fusion), channel_id=1, source_target_pairs={{0,256},{128,384},{256,0},{384,128},{1,257},{129,385},{257,1},{385... | collective-permute-start | bytes 172040 | tf_op jit(solution)/shard_map/ppermute | solution.py:181
  146.2 3.8 %collective-permute-done.12 = f32[112,128]{1,0:T(8,128)S(1)} collective-permute-done((f32[112,128]{1,0:T(8,128)S(1)}, f32[112,128]{1,0:T(8,128)S(1)}, u32[]{:S(2)}, u32[]{:S(2)}) %collective-permute-start.12) | collective-permute-done | bytes 57376 | tf_op jit(solution)/shard_map/ppermute | solution.py:181
  150.0 2.7 %collective-permute-start.13 = (f32[112,128]{1,0:T(8,128)S(1)}, f32[112,128]{1,0:T(8,128)S(1)}, u32[]{:S(2)}, u32[]{:S(2)}) collective-permute-start(f32[112,128]{1,0:T(8,128)S(1)} %bitcast_add_fusion.1), channel_id=1, source_target_pairs={{0,16},{16,0},{32,48},{48,32},{64,80},{80,64},{96,112},{112,96},{1... | collective-permute-start | bytes 172040 | tf_op jit(solution)/shard_map/ppermute | solution.py:181
  152.9 3.8 %collective-permute-done.13 = f32[112,128]{1,0:T(8,128)S(1)} collective-permute-done((f32[112,128]{1,0:T(8,128)S(1)}, f32[112,128]{1,0:T(8,128)S(1)}, u32[]{:S(2)}, u32[]{:S(2)}) %collective-permute-start.13) | collective-permute-done | bytes 57376 | tf_op jit(solution)/shard_map/ppermute | solution.py:181
  156.7 4.2 %collective-permute-start.14 = (f32[112,128]{1,0:T(8,128)S(1)}, f32[112,128]{1,0:T(8,128)S(1)}, u32[]{:S(2)}, u32[]{:S(2)}) collective-permute-start(f32[112,128]{1,0:T(8,128)S(1)} %add.223), channel_id=1, source_target_pairs={{0,32},{16,48},{32,0},{48,16},{64,96},{80,112},{96,64},{112,80},{1... | collective-permute-start | bytes 172040 | tf_op jit(solution)/shard_map/ppermute | solution.py:181
  160.9 0.8 convolution_multiply_fusion.5
  161.7 2.2 %collective-permute-done.14 = f32[112,128]{1,0:T(8,128)S(1)} collective-permute-done((f32[112,128]{1,0:T(8,128)S(1)}, f32[112,128]{1,0:T(8,128)S(1)}, u32[]{:S(2)}, u32[]{:S(2)}) %collective-permute-start.14) | collective-permute-done | bytes 57376 | tf_op jit(solution)/shard_map/ppermute | solution.py:181
  164.0 8.2 %collective-permute-start.15 = (f32[112,128]{1,0:T(8,128)S(1)}, f32[112,128]{1,0:T(8,128)S(1)}, u32[]{:S(2)}, u32[]{:S(2)}) collective-permute-start(f32[112,128]{1,0:T(8,128)S(1)} %add.224), channel_id=1, source_target_pairs={{0,64},{16,80},{32,96},{48,112},{64,0},{80,16},{96,32},{112,48},{1... | collective-permute-start | bytes 172040 | tf_op jit(solution)/shard_map/ppermute | solution.py:181
  172.2 0.8 fusion.11
  173.0 1.3 collective-permute-done.15
  174.3 3.0 %collective-permute-start.16 = (bf16[112,128]{1,0:T(8,128)(2,1)S(1)}, bf16[112,128]{1,0:T(8,128)(2,1)S(1)}, u32[]{:S(2)}, u32[]{:S(2)}) collective-permute-start(bf16[112,128]{1,0:T(8,128)(2,1)S(1)} %add_convert_fusion), channel_id=1, source_target_pairs={{0,8},{1,9},{2,10},{3,11},{4,12},{5,13},{6,14},{7,15},{8,0},{9,1},... | collective-permute-start | bytes 86024 | tf_op jit(solution)/shard_map/ppermute | solution.py:190
  177.4 1.5 fusion.13
  178.9 2.7 %collective-permute-done.16 = bf16[112,128]{1,0:T(8,128)(2,1)S(1)} collective-permute-done((bf16[112,128]{1,0:T(8,128)(2,1)S(1)}, bf16[112,128]{1,0:T(8,128)(2,1)S(1)}, u32[]{:S(2)}, u32[]{:S(2)}) %collective-permute-start.16) | collective-permute-done | bytes 28704 | tf_op jit(solution)/shard_map/ppermute | solution.py:190
  181.7 1.9 collective-permute-start.17
  183.7 5.6 %collective-permute-done.17 = bf16[2,112,128]{2,1,0:T(8,128)(2,1)S(1)} collective-permute-done((bf16[2,112,128]{2,1,0:T(8,128)(2,1)S(1)}, bf16[2,112,128]{2,1,0:T(8,128)(2,1)S(1)}, u32[]{:S(2)}, u32[]{:S(2)}) %collective-permute-start.17) | collective-permute-done | bytes 57376 | tf_op jit(solution)/shard_map/ppermute | solution.py:190
  189.6 2.4 %collective-permute-start.18 = (bf16[2,2,112,128]{3,2,1,0:T(8,128)(2,1)S(1)}, bf16[2,2,112,128]{3,2,1,0:T(8,128)(2,1)S(1)}, u32[]{:S(2)}, u32[]{:S(2)}) collective-permute-start(bf16[2,2,112,128]{3,2,1,0:T(8,128)(2,1)S(1)} %fusion.45), channel_id=1, source_target_pairs={{0,4},{1,5},{2,6},{3,7},{4,0},{5,1},{6,2},{7,3},{8,12},{9,13},{10,... | collective-permute-start | bytes 344072 | tf_op jit(solution)/shard_map/ppermute | solution.py:190
  192.1 4.2 %collective-permute-done.18 = bf16[2,2,112,128]{3,2,1,0:T(8,128)(2,1)S(1)} collective-permute-done((bf16[2,2,112,128]{3,2,1,0:T(8,128)(2,1)S(1)}, bf16[2,2,112,128]{3,2,1,0:T(8,128)(2,1)S(1)}, u32[]{:S(2)}, u32[]{:S(2)}) %collective-permute-start.18) | collective-permute-done | bytes 114720 | tf_op jit(solution)/shard_map/ppermute | solution.py:190
  196.4 1.9 collective-permute-start.19
  198.5 5.8 %collective-permute-done.19 = bf16[2,2,2,112,128]{4,3,1,0,2:T(8,128)(2,1)S(1)} collective-permute-done((bf16[2,2,2,112,128]{4,3,1,0,2:T(8,128)(2,1)S(1)}, bf16[2,2,2,112,128]{4,3,1,0,2:T(8,128)(2,1)S(1)}, u32[]{:S(2)}, u32[]{:S(2)}) %collective-permute-start.19) | collective-permute-done | bytes 229408 | tf_op jit(solution)/shard_map/ppermute | solution.py:190
  204.5 0.8 fusion.106
  (181 shorter events, 22.3 us)
Async XLA Ops:
  0.6 20.9 %copy-start.1 = (bf16[1,2,4,128,128]{4,3,2,1,0:T(8,128)(2,1)S(1)}, bf16[1,2,4,128,128]{4,3,2,1,0:T(8,128)(2,1)}, u32[]{:S(2)}) copy-start(bf16[1,2,4,128,128]{4,3,2,1,0:T(8,128)(2,1)} %param.5) | copy-start | bytes 786436
  1.6 19.9 %collective-permute-start = (bf16[2,1,128,128]{3,2,1,0:T(8,128)(2,1)S(1)}, bf16[2,1,128,128]{3,2,1,0:T(8,128)(2,1)S(1)}, u32[]{:S(2)}, u32[]{:S(2)}) collective-permute-start(bf16[2,1,128,128]{3,2,1,0:T(8,128)(2,1)S(1)} %get-tuple-element.27), channel_id=1, source_target_pairs={{0,1},{1,2},{2,3},{3,4},{4,5},{5,6},{6,7},{7,8},{8,9},{9,10},{10,1... | collective-permute-start | bytes 196616 | tf_op jit(solution)/shard_map/ppermute | solution.py:17
  5.1 16.5 %collective-permute-start.1 = (bf16[2,1,128,128]{3,2,1,0:T(8,128)(2,1)S(1)}, bf16[2,1,128,128]{3,2,1,0:T(8,128)(2,1)S(1)}, u32[]{:S(2)}, u32[]{:S(2)}) collective-permute-start(bf16[2,1,128,128]{3,2,1,0:T(8,128)(2,1)S(1)} %get-tuple-element.28), channel_id=1, source_target_pairs={{1,0},{2,1},{3,2},{4,3},{5,4},{6,5},{7,6},{8,7},{9,8},{10,9},{11,1... | collective-permute-start | bytes 196616 | tf_op jit(solution)/shard_map/ppermute | solution.py:19
  10.3 9.9 %collective-permute-start.5 = (bf16[1,1,64,128]{3,2,1,0:T(8,128)(2,1)S(1)}, bf16[1,1,64,128]{3,2,1,0:T(8,128)(2,1)S(1)}, u32[]{:S(2)}, u32[]{:S(2)}) collective-permute-start(bf16[1,1,64,128]{3,2,1,0:T(8,128)(2,1)S(1)} %slice.453), channel_id=1, source_target_pairs={{1,0},{2,1},{3,2},{4,3},{5,4},{6,5},{7,6},{8,7},{9,8},{10,9},{11,1... | collective-permute-start | bytes 49160 | tf_op jit(solution)/shard_map/ppermute | solution.py:29
  15.3 12.7 %copy-start.2 = (bf16[3,3,3,128,128]{4,3,2,1,0:T(8,128)(2,1)S(1)}, bf16[3,3,3,128,128]{4,3,2,1,0:T(8,128)(2,1)}, u32[]{:S(2)}) copy-start(bf16[3,3,3,128,128]{4,3,2,1,0:T(8,128)(2,1)} %param.8) | copy-start | bytes 2654212
  15.3 12.7 %copy-start.6 = (pred[8,18]{0,1:T(8,128)(4,1)S(1)}, pred[8,18]{0,1:T(8,128)(4,1)}, u32[]{:S(2)}) copy-start(pred[8,18]{0,1:T(8,128)(4,1)} %constant.267) | copy-start | bytes 436
  20.2 6.1 %collective-permute-start.6 = (bf16[1,3,64,128]{3,2,1,0:T(8,128)(2,1)S(1)}, bf16[1,3,64,128]{3,2,1,0:T(8,128)(2,1)S(1)}, u32[]{:S(2)}, u32[]{:S(2)}) collective-permute-start(bf16[1,3,64,128]{3,2,1,0:T(8,128)(2,1)S(1)} %pad_maximum_fusion.14), channel_id=1, source_target_pairs={{16,0},{32,16},{48,32},{64,48},{80,64},{96,80},{112,96},{17,1},{33... | collective-permute-start | bytes 147464 | tf_op jit(solution)/shard_map/ppermute | solution.py:29
  21.6 12.0 %collective-permute-start.2 = (bf16[2,6,128,128]{3,2,1,0:T(8,128)(2,1)S(1)}, bf16[2,6,128,128]{3,2,1,0:T(8,128)(2,1)S(1)}, u32[]{:S(2)}, u32[]{:S(2)}) collective-permute-start(bf16[2,6,128,128]{3,2,1,0:T(8,128)(2,1)S(1)} %pad_maximum_fusion.4), channel_id=1, source_target_pairs={{0,16},{16,32},{32,48},{48,64},{64,80},{80,96},{96,112},{1,17},{17... | collective-permute-start | bytes 1179656 | tf_op jit(solution)/shard_map/ppermute | solution.py:29
  38.1 8.3 %collective-permute-start.3 = (bf16[2,1,128,128]{3,2,1,0:T(8,128)(2,1)S(1)}, bf16[2,1,128,128]{3,2,1,0:T(8,128)(2,1)S(1)}, u32[]{:S(2)}, u32[]{:S(2)}) collective-permute-start(bf16[2,1,128,128]{3,2,1,0:T(8,128)(2,1)S(1)} %slice.448), channel_id=1, source_target_pairs={{0,1},{1,2},{2,3},{3,4},{4,5},{5,6},{6,7},{7,8},{8,9},{9,10},{10,1... | collective-permute-start | bytes 196616 | tf_op jit(solution)/shard_map/ppermute | solution.py:29
  43.7 8.7 %copy-start.4 = (bf16[1,1,2,64,128]{4,3,2,1,0:T(8,128)(2,1)S(1)}, bf16[1,1,2,64,128]{4,3,2,1,0:T(8,128)(2,1)}, u32[]{:S(2)}) copy-start(bf16[1,1,2,64,128]{4,3,2,1,0:T(8,128)(2,1)} %param.9) | copy-start | bytes 98308
  47.6 9.0 %collective-permute-start.4 = (bf16[2,5,128,128]{3,2,1,0:T(8,128)(2,1)S(1)}, bf16[2,5,128,128]{3,2,1,0:T(8,128)(2,1)S(1)}, u32[]{:S(2)}, u32[]{:S(2)}) collective-permute-start(bf16[2,5,128,128]{3,2,1,0:T(8,128)(2,1)S(1)} %pad_maximum_fusion.3), channel_id=1, source_target_pairs={{0,16},{16,32},{32,48},{48,64},{64,80},{80,96},{96,112},{1,17},{17... | collective-permute-start | bytes 983048 | tf_op jit(solution)/shard_map/ppermute | solution.py:29
  74.8 1.8 copy-start
  76.6 6.0 %collective-permute-start.7 = (f32[2,2,2,2,2,112,128]{6,5,4,3,2,0,1:T(8,128)}, f32[2,2,2,2,2,112,128]{6,5,4,3,2,0,1:T(8,128)}, u32[]{:S(2)}, u32[]{:S(2)}) collective-permute-start(f32[2,2,2,2,2,112,128]{6,5,4,3,2,0,1:T(8,128)} %fusion.1), channel_id=1, source_target_pairs={{0,128},{128,0},{256,384},{384,256},{1,129},{129,1},{257,385},{385... | collective-permute-start | bytes 5505032 | tf_op jit(solution)/shard_map/ppermute | solution.py:181
  84.9 15.3 %collective-permute-start.8 = (f32[2,2,2,2,112,128]{5,4,2,0,3,1:T(8,128)S(1)}, f32[2,2,2,2,112,128]{5,4,2,0,3,1:T(8,128)S(1)}, u32[]{:S(2)}, u32[]{:S(2)}) collective-permute-start(f32[2,2,2,2,112,128]{5,4,2,0,3,1:T(8,128)S(1)} %bitcast_select_fusion), channel_id=1, source_target_pairs={{0,1},{1,0},{2,3},{3,2},{4,5},{5,4},{6,7},{7,6},{8,9},{9,8},{10,11... | collective-permute-start | bytes 2752520 | tf_op jit(solution)/shard_map/ppermute | solution.py:190
  100.5 10.4 %collective-permute-start.9 = (f32[2,2,2,112,128]{4,3,1,0,2:T(8,128)S(1)}, f32[2,2,2,112,128]{4,3,1,0,2:T(8,128)S(1)}, u32[]{:S(2)}, u32[]{:S(2)}) collective-permute-start(f32[2,2,2,112,128]{4,3,1,0,2:T(8,128)S(1)} %bitcast_select_fusion.2), channel_id=1, source_target_pairs={{0,4},{1,5},{2,6},{3,7},{4,0},{5,1},{6,2},{7,3},{8,12},{9,13},{10,... | collective-permute-start | bytes 1376264 | tf_op jit(solution)/shard_map/ppermute | solution.py:190
  110.9 0.8 copy-start.5
  111.7 41.1 %copy-start.3 = (bf16[3,3,3,128,128]{4,3,2,1,0:T(8,128)(2,1)S(1)}, bf16[3,3,3,128,128]{4,3,2,1,0:T(8,128)(2,1)}, u32[]{:S(2)}) copy-start(bf16[3,3,3,128,128]{4,3,2,1,0:T(8,128)(2,1)} %param.8) | copy-start | bytes 2654212
  112.9 9.4 %collective-permute-start.10 = (f32[2,2,112,128]{3,2,0,1:T(8,128)S(1)}, f32[2,2,112,128]{3,2,0,1:T(8,128)S(1)}, u32[]{:S(2)}, u32[]{:S(2)}) collective-permute-start(f32[2,2,112,128]{3,2,0,1:T(8,128)S(1)} %bitcast_select_fusion.4), channel_id=1, source_target_pairs={{0,2},{1,3},{2,0},{3,1},{4,6},{5,7},{6,4},{7,5},{8,10},{9,11},{10,... | collective-permute-start | bytes 688136 | tf_op jit(solution)/shard_map/ppermute | solution.py:190
  122.4 8.2 %collective-permute-start.11 = (f32[2,112,128]{2,1,0:T(8,128)S(1)}, f32[2,112,128]{2,1,0:T(8,128)S(1)}, u32[]{:S(2)}, u32[]{:S(2)}) collective-permute-start(f32[2,112,128]{2,1,0:T(8,128)S(1)} %fusion.48), channel_id=1, source_target_pairs={{0,8},{1,9},{2,10},{3,11},{4,12},{5,13},{6,14},{7,15},{8,0},{9,1},... | collective-permute-start | bytes 344072 | tf_op jit(solution)/shard_map/ppermute | solution.py:190
  130.7 19.4 %collective-permute-start.12 = (f32[112,128]{1,0:T(8,128)S(1)}, f32[112,128]{1,0:T(8,128)S(1)}, u32[]{:S(2)}, u32[]{:S(2)}) collective-permute-start(f32[112,128]{1,0:T(8,128)S(1)} %dynamic-slice_bitcast_fusion), channel_id=1, source_target_pairs={{0,256},{128,384},{256,0},{384,128},{1,257},{129,385},{257,1},{385... | collective-permute-start | bytes 172040 | tf_op jit(solution)/shard_map/ppermute | solution.py:181
  150.0 6.7 %collective-permute-start.13 = (f32[112,128]{1,0:T(8,128)S(1)}, f32[112,128]{1,0:T(8,128)S(1)}, u32[]{:S(2)}, u32[]{:S(2)}) collective-permute-start(f32[112,128]{1,0:T(8,128)S(1)} %bitcast_add_fusion.1), channel_id=1, source_target_pairs={{0,16},{16,0},{32,48},{48,32},{64,80},{80,64},{96,112},{112,96},{1... | collective-permute-start | bytes 172040 | tf_op jit(solution)/shard_map/ppermute | solution.py:181
  156.7 7.2 %collective-permute-start.14 = (f32[112,128]{1,0:T(8,128)S(1)}, f32[112,128]{1,0:T(8,128)S(1)}, u32[]{:S(2)}, u32[]{:S(2)}) collective-permute-start(f32[112,128]{1,0:T(8,128)S(1)} %add.223), channel_id=1, source_target_pairs={{0,32},{16,48},{32,0},{48,16},{64,96},{80,112},{96,64},{112,80},{1... | collective-permute-start | bytes 172040 | tf_op jit(solution)/shard_map/ppermute | solution.py:181
  164.0 10.4 %collective-permute-start.15 = (f32[112,128]{1,0:T(8,128)S(1)}, f32[112,128]{1,0:T(8,128)S(1)}, u32[]{:S(2)}, u32[]{:S(2)}) collective-permute-start(f32[112,128]{1,0:T(8,128)S(1)} %add.224), channel_id=1, source_target_pairs={{0,64},{16,80},{32,96},{48,112},{64,0},{80,16},{96,32},{112,48},{1... | collective-permute-start | bytes 172040 | tf_op jit(solution)/shard_map/ppermute | solution.py:181
  174.3 7.3 %collective-permute-start.16 = (bf16[112,128]{1,0:T(8,128)(2,1)S(1)}, bf16[112,128]{1,0:T(8,128)(2,1)S(1)}, u32[]{:S(2)}, u32[]{:S(2)}) collective-permute-start(bf16[112,128]{1,0:T(8,128)(2,1)S(1)} %add_convert_fusion), channel_id=1, source_target_pairs={{0,8},{1,9},{2,10},{3,11},{4,12},{5,13},{6,14},{7,15},{8,0},{9,1},... | collective-permute-start | bytes 86024 | tf_op jit(solution)/shard_map/ppermute | solution.py:190
  181.7 7.6 %collective-permute-start.17 = (bf16[2,112,128]{2,1,0:T(8,128)(2,1)S(1)}, bf16[2,112,128]{2,1,0:T(8,128)(2,1)S(1)}, u32[]{:S(2)}, u32[]{:S(2)}) collective-permute-start(bf16[2,112,128]{2,1,0:T(8,128)(2,1)S(1)} %select_select_fusion.1), channel_id=1, source_target_pairs={{0,2},{1,3},{2,0},{3,1},{4,6},{5,7},{6,4},{7,5},{8,10},{9,11},{10,... | collective-permute-start | bytes 172040 | tf_op jit(solution)/shard_map/ppermute | solution.py:190
  189.6 6.7 %collective-permute-start.18 = (bf16[2,2,112,128]{3,2,1,0:T(8,128)(2,1)S(1)}, bf16[2,2,112,128]{3,2,1,0:T(8,128)(2,1)S(1)}, u32[]{:S(2)}, u32[]{:S(2)}) collective-permute-start(bf16[2,2,112,128]{3,2,1,0:T(8,128)(2,1)S(1)} %fusion.45), channel_id=1, source_target_pairs={{0,4},{1,5},{2,6},{3,7},{4,0},{5,1},{6,2},{7,3},{8,12},{9,13},{10,... | collective-permute-start | bytes 344072 | tf_op jit(solution)/shard_map/ppermute | solution.py:190
  196.4 7.9 %collective-permute-start.19 = (bf16[2,2,2,112,128]{4,3,1,0,2:T(8,128)(2,1)S(1)}, bf16[2,2,2,112,128]{4,3,1,0,2:T(8,128)(2,1)S(1)}, u32[]{:S(2)}, u32[]{:S(2)}) collective-permute-start(bf16[2,2,2,112,128]{4,3,1,0,2:T(8,128)(2,1)S(1)} %fusion.34), channel_id=1, source_target_pairs={{0,1},{1,0},{2,3},{3,2},{4,5},{5,4},{6,7},{7,6},{8,9},{9,8},{10,11... | collective-permute-start | bytes 688136 | tf_op jit(solution)/shard_map/ppermute | solution.py:190

commit v2 on v1

--- a/solution.py
+++ b/solution.py
@@ -29,33 +29,17 @@
     return lax.ppermute(value, axis, [(source, source + steps) for source in range(leading, last)])
 
 
-def unfold(frame_slab, stride, pad_cols):
-    padded = jnp.pad(frame_slab, ((0, 0), (0, 0), pad_cols, (0, 0)))
-    out_rows = (padded.shape[1] - 3) // stride + 1
-    out_cols = (padded.shape[2] - 3) // stride + 1
-    pieces = []
-    for tap_row in range(3):
-        for tap_col in range(3):
-            pieces.append(
-                padded[
-                    :,
-                    tap_row : tap_row + stride * (out_rows - 1) + 1 : stride,
-                    tap_col : tap_col + stride * (out_cols - 1) + 1 : stride,
-                ]
-            )
-    joined = jnp.concatenate(pieces, axis=-1)
-    return (joined.reshape(-1, joined.shape[-1]), (frame_slab.shape[0], out_rows, out_cols))
-
-
 def conv_layer(extended, weight, tap_mask, out_frames, stride, pad_cols):
-    channels_out = weight.shape[-1]
     summed = None
     for tap_time in range(3):
         frame_slab = extended[tap_time : tap_time + stride * (out_frames - 1) + 1 : stride]
-        columns, shape_out = unfold(frame_slab, stride, pad_cols)
-        kernel = weight[tap_time].reshape(-1, channels_out)
-        tap_term = jnp.dot(columns, kernel, preferred_element_type=jnp.float32).reshape(
-            shape_out + (channels_out,)
+        tap_term = lax.conv_general_dilated(
+            frame_slab,
+            weight[tap_time],
+            (stride, stride),
+            ((0, 0), pad_cols),
+            dimension_numbers=("NHWC", "HWIO", "NHWC"),
+            preferred_element_type=jnp.float32,
         )
         tap_term = tap_term * tap_mask[:, tap_time][:, None, None, None]
         summed = tap_term if summed is None else summed + tap_term
@@ -67,15 +51,19 @@
     blocks = []
     for tap_time in range(3):
         frame_slab = extended[tap_time : tap_time + stride * (out_frames - 1) + 1 : stride]
-        columns, shape_out = unfold(frame_slab, stride, pad_cols)
         masked = grads * tap_mask[:, tap_time].astype(jnp.bfloat16)[:, None, None, None]
         blocks.append(
-            jnp.dot(
-                columns.T, masked.reshape(-1, grads.shape[-1]), preferred_element_type=jnp.float32
+            lax.conv_general_dilated(
+                frame_slab,
+                masked,
+                (1, 1),
+                ((0, 0), pad_cols),
+                rhs_dilation=(stride, stride),
+                dimension_numbers=("CHWN", "IHWO", "HWNC"),
+                preferred_element_type=jnp.float32,
             )
         )
-    stacked = jnp.stack(blocks)
-    return stacked.reshape(3, 3, 3, extended.shape[-1], grads.shape[-1])
+    return jnp.stack(blocks)
 
 
 def hidden_grad(grads_ext, weight, mask_ext):

time: 207 us -> 195 us (0.942)
  local copies, waits for them, and re-layouts: 28.2 us -> 10.2 us
  waiting for transfers between devices: 77.2 us -> 69.9 us
  starting transfers between devices: 75.4 us -> 80.6 us
  matrix products: 9.99 us -> 14.7 us
  other arithmetic: 10.4 us -> 13.8 us
    conv_general_dilated x0 -> x12, matrix products: none -> 13.7 us  [the longest x6 8.47 us: weight_grad(): lax.conv_general_dilated(frame_slab, masked, (1, 1), ((0, 0), pad_cols),...]
    slice x30 -> x0, local copies, waits for them, and re-layouts: 10.9 us -> none  [the longest x27 9.48 us: unfold(): padded[:, tap_row:tap_row + stride * (out_rows - 1) + 1:stride, tap_col:t...]
    dot_general x12 -> x0, matrix products: 9 us -> none  [the longest x6 5.62 us: conv_layer(): jnp.dot(columns, kernel, preferred_element_type=jnp.float32)]
    unnamed x65 -> x26, local copies, waits for them, and re-layouts: 11.2 us -> 2.71 us
    ppermute x8, starting transfers between devices: 18.6 us -> 22.6 us  [swap_rows(): return lax.ppermute(value, ('dp', 'height'), pairs)]
    ppermute x8, waiting for transfers between devices: 52.1 us -> 49.2 us  [swap_rows(): return lax.ppermute(value, ('dp', 'height'), pairs)]
    ppermute x5, waiting for transfers between devices: 9.85 us -> 7.18 us  [shifted(): lax.ppermute(value, axis, [(source, source + steps) for source in range(l...]
    ppermute x5, starting transfers between devices: 16.3 us -> 18.5 us  [shifted(): lax.ppermute(value, axis, [(source, source + steps) for source in range(l...]
  transfers between devices with their start and end apart: 20 -> 20, of which waited for: 16 -> 15; matrix products, arithmetic and copies ran while one was open for 8% -> 12% of each run, Pallas kernels for 0% -> 0%
where the time goes in v2:
time: 195 us; the launch traced here: 193 us
  starting transfers between devices  80.6 us (41%)
  waiting for transfers between devices  69.9 us (36%)
  matrix products  14.7 us (8%)
  other arithmetic  13.8 us (7%)
  local copies, waits for them, and re-layouts  10.2 us (5%)
  between operations  3.95 us (2%)
    ppermute x8, waiting for transfers between devices, swap_rows(): return lax.ppermute(value, ('dp', 'height'), pairs)  49.2 us
    ppermute x5, starting transfers between devices, swap(): lax.ppermute(value, axis, [(i, i ^ bit) for i in range(lax.axis_size(axis...  32.4 us
    ppermute x8, starting transfers between devices, swap_rows(): return lax.ppermute(value, ('dp', 'height'), pairs)  22.6 us
    ppermute x5, starting transfers between devices, shifted(): lax.ppermute(value, axis, [(source, source + steps) for source in range(l...  18.5 us
    ppermute x5, waiting for transfers between devices, swap(): lax.ppermute(value, axis, [(i, i ^ bit) for i in range(lax.axis_size(axis...  13.6 us
    conv_general_dilated x6, matrix products, weight_grad(): lax.conv_general_dilated(frame_slab, masked, (1, 1), ((0, 0), pad_cols),...  8.47 us
    ppermute x5, waiting for transfers between devices, shifted(): lax.ppermute(value, axis, [(source, source + steps) for source in range(l...  7.18 us
    conv_general_dilated x6, matrix products, conv_layer(): lax.conv_general_dilated(frame_slab, weight[tap_time], (stride, stride),...  5.24 us
  transfers between devices with their start and end apart: 20, of which 15 were waited for; matrix products, arithmetic and copies ran while one was open for 12% of the time, Pallas kernels for 0%

profile of v2, /device:TPU:6, one launch (start us, length us, event | category | flops | bytes accessed | tf_op | source)
XLA Modules:
  0.0 193.2 jit_solution(13597313900908935918)
XLA Ops:
  0.6 1.2 copy.326
  2.0 5.2 %collective-permute-start.1 = (bf16[2,1,128,128]{3,0,2,1:T(2,128)(2,1)S(1)}, bf16[2,1,128,128]{3,0,2,1:T(2,128)(2,1)S(1)}, u32[]{:S(2)}, u32[]{:S(2)}) collective-permute-start(bf16[2,1,128,128]{3,0,2,1:T(2,128)(2,1)S(1)} %get-tuple-element.36), channel_id=1, source_target_pairs={{1,0},{2,1},{3,2},{4,3},{5,4},{6,5},{7,6},{8,7},{9,8},{10,9},{11,1... | collective-permute-start | bytes 196616 | tf_op jit(solution)/shard_map/ppermute | solution.py:19
  7.2 1.9 collective-permute-start
  9.1 0.8 fusion.128
  9.9 6.0 %collective-permute-start.5 = (bf16[1,1,64,128]{3,2,1,0:T(8,128)(2,1)S(1)}, bf16[1,1,64,128]{3,2,1,0:T(8,128)(2,1)S(1)}, u32[]{:S(2)}, u32[]{:S(2)}) collective-permute-start(bf16[1,1,64,128]{3,2,1,0:T(8,128)(2,1)S(1)} %slice.186), channel_id=1, source_target_pairs={{1,0},{2,1},{3,2},{4,3},{5,4},{6,5},{7,6},{8,7},{9,8},{10,9},{11,1... | collective-permute-start | bytes 49160 | tf_op jit(solution)/shard_map/ppermute | solution.py:29
  15.9 0.8 reduce-window_clone.1
  16.7 0.7 subtract_bitcast_fusion
  17.7 0.5 fusion.171
  20.1 1.4 broadcast_multiply_fusion.5
  21.5 0.6 slice.191
  22.1 0.6 slice.195
  22.8 1.3 collective-permute-start.6
  24.1 0.6 pad_maximum_fusion.6
  24.7 4.7 %collective-permute-start.2 = (bf16[2,6,128,128]{3,0,2,1:T(2,128)(2,1)S(1)}, bf16[2,6,128,128]{3,0,2,1:T(2,128)(2,1)S(1)}, u32[]{:S(2)}, u32[]{:S(2)}) collective-permute-start(bf16[2,6,128,128]{3,0,2,1:T(2,128)(2,1)S(1)} %pad_maximum_fusion.6), channel_id=1, source_target_pairs={{0,16},{16,32},{32,48},{48,64},{64,80},{80,96},{96,112},{1,17},{17... | collective-permute-start | bytes 1179656 | tf_op jit(solution)/shard_map/ppermute | solution.py:29
  29.4 0.6 fusion.185
  30.5 1.3 multiply_bitcast_fusion.1
  33.4 3.4 %collective-permute-done.2 = bf16[2,6,128,128]{3,0,2,1:T(2,128)(2,1)S(1)} collective-permute-done((bf16[2,6,128,128]{3,0,2,1:T(2,128)(2,1)S(1)}, bf16[2,6,128,128]{3,0,2,1:T(2,128)(2,1)S(1)}, u32[]{:S(2)}, u32[]{:S(2)}) %collective-permute-start.2) | collective-permute-done | bytes 393248 | tf_op jit(solution)/shard_map/ppermute | solution.py:29
  37.3 1.0 pad_maximum_fusion.3
  38.9 0.8 fusion.9
  39.8 0.8 fusion.8
  40.8 1.0 add_divide_fusion
  42.0 2.1 %collective-permute-start.3 = (bf16[2,1,128,128]{3,0,2,1:T(2,128)(2,1)S(1)}, bf16[2,1,128,128]{3,0,2,1:T(2,128)(2,1)S(1)}, u32[]{:S(2)}, u32[]{:S(2)}) collective-permute-start(bf16[2,1,128,128]{3,0,2,1:T(2,128)(2,1)S(1)} %bitcast.367), channel_id=1, source_target_pairs={{0,1},{1,2},{2,3},{3,4},{4,5},{5,6},{6,7},{7,8},{8,9},{9,10},{10,1... | collective-permute-start | bytes 196616 | tf_op jit(solution)/shard_map/ppermute | solution.py:29
  44.9 2.0 %convolution_bitcast_fusion.3 = f32[1,3,3,128,128]{4,3,2,1,0:T(8,128)S(1)} fusion(bf16[2,6,128,128]{3,0,2,1:T(2,128)(2,1)S(1)} %pad_maximum_fusion.6, bf16[2,4,128,128]{3,2,1,0:T(8,128)(2,1)S(1)} %get-tuple-element.34), kind=kOutput, calls=%fused_computation.14 | convolution fusion | flops 300417024 | bytes 1245184 | tf_op jit(solution)/shard_map/conv_general_dilated | solution.py:56
  46.9 2.0 %convolution_bitcast_fusion.4 = f32[1,3,3,128,128]{4,3,2,1,0:T(8,128)S(1)} fusion(bf16[2,6,128,128]{3,0,2,1:T(2,128)(2,1)S(1)} %pad_maximum_fusion.3, bf16[2,4,128,128]{3,2,1,0:T(8,128)(2,1)S(1)} %get-tuple-element.33), kind=kOutput, calls=%fused_computation.15 | convolution fusion | flops 300417024 | bytes 1245184 | tf_op jit(solution)/shard_map/conv_general_dilated | solution.py:56
  48.9 2.0 %convolution_bitcast_fusion.5 = f32[1,3,3,128,128]{4,3,2,1,0:T(8,128)S(1)} fusion(bf16[2,6,128,128]{3,0,2,1:T(2,128)(2,1)S(1)} %collective-permute-done.2, bf16[2,4,128,128]{3,2,1,0:T(8,128)(2,1)S(1)} %get-tuple-element.14), kind=kOutput, calls=%fused_computation.16 | convolution fusion | flops 300417024 | bytes 1245184 | tf_op jit(solution)/shard_map/conv_general_dilated | solution.py:56
  52.3 4.4 %collective-permute-start.4 = (bf16[2,5,128,128]{3,0,2,1:T(2,128)(2,1)S(1)}, bf16[2,5,128,128]{3,0,2,1:T(2,128)(2,1)S(1)}, u32[]{:S(2)}, u32[]{:S(2)}) collective-permute-start(bf16[2,5,128,128]{3,0,2,1:T(2,128)(2,1)S(1)} %pad_maximum_fusion.7), channel_id=1, source_target_pairs={{0,16},{16,32},{32,48},{48,64},{64,80},{80,96},{96,112},{1,17},{17... | collective-permute-start | bytes 983048 | tf_op jit(solution)/shard_map/ppermute | solution.py:29
  57.2 0.8 convolution_bitcast_fusion
  58.0 3.8 %collective-permute-done.4 = bf16[2,5,128,128]{3,0,2,1:T(2,128)(2,1)S(1)} collective-permute-done((bf16[2,5,128,128]{3,0,2,1:T(2,128)(2,1)S(1)}, bf16[2,5,128,128]{3,0,2,1:T(2,128)(2,1)S(1)}, u32[]{:S(2)}, u32[]{:S(2)}) %collective-permute-start.4) | collective-permute-done | bytes 327712 | tf_op jit(solution)/shard_map/ppermute | solution.py:29
  61.8 0.5 fusion.169
  62.3 0.8 convolution_bitcast_fusion.1
  63.2 0.8 convolution_bitcast_fusion.2
  64.5 1.5 fusion.1
  66.3 1.9 collective-permute-start.7
  68.2 4.0 %collective-permute-done.7 = f32[2,2,2,2,2,112,128]{6,5,4,3,2,0,1:T(8,128)} collective-permute-done((f32[2,2,2,2,2,112,128]{6,5,4,3,2,0,1:T(8,128)}, f32[2,2,2,2,2,112,128]{6,5,4,3,2,0,1:T(8,128)}, u32[]{:S(2)}, u32[]{:S(2)}) %collective-permute-start.7) | collective-permute-done | bytes 1835040 | tf_op jit(solution)/shard_map/ppermute | solution.py:169
  72.3 1.9 fusion.4
  74.6 2.1 %collective-permute-start.8 = (f32[2,2,2,2,112,128]{5,4,2,0,3,1:T(8,128)S(1)}, f32[2,2,2,2,112,128]{5,4,2,0,3,1:T(8,128)S(1)}, u32[]{:S(2)}, u32[]{:S(2)}) collective-permute-start(f32[2,2,2,2,112,128]{5,4,2,0,3,1:T(8,128)S(1)} %bitcast_select_fusion), channel_id=1, source_target_pairs={{0,1},{1,0},{2,3},{3,2},{4,5},{5,4},{6,7},{7,6},{8,9},{9,8},{10,11... | collective-permute-start | bytes 2752520 | tf_op jit(solution)/shard_map/ppermute | solution.py:178
  76.7 13.1 %collective-permute-done.8 = f32[2,2,2,2,112,128]{5,4,2,0,3,1:T(8,128)S(1)} collective-permute-done((f32[2,2,2,2,112,128]{5,4,2,0,3,1:T(8,128)S(1)}, f32[2,2,2,2,112,128]{5,4,2,0,3,1:T(8,128)S(1)}, u32[]{:S(2)}, u32[]{:S(2)}) %collective-permute-start.8) | collective-permute-done | bytes 917536 | tf_op jit(solution)/shard_map/ppermute | solution.py:178
  90.3 2.4 %collective-permute-start.9 = (f32[2,2,2,112,128]{4,3,1,0,2:T(8,128)S(1)}, f32[2,2,2,112,128]{4,3,1,0,2:T(8,128)S(1)}, u32[]{:S(2)}, u32[]{:S(2)}) collective-permute-start(f32[2,2,2,112,128]{4,3,1,0,2:T(8,128)S(1)} %bitcast_select_fusion.2), channel_id=1, source_target_pairs={{0,4},{1,5},{2,6},{3,7},{4,0},{5,1},{6,2},{7,3},{8,12},{9,13},{10,... | collective-permute-start | bytes 1376264 | tf_op jit(solution)/shard_map/ppermute | solution.py:178
  92.8 7.9 %collective-permute-done.9 = f32[2,2,2,112,128]{4,3,1,0,2:T(8,128)S(1)} collective-permute-done((f32[2,2,2,112,128]{4,3,1,0,2:T(8,128)S(1)}, f32[2,2,2,112,128]{4,3,1,0,2:T(8,128)S(1)}, u32[]{:S(2)}, u32[]{:S(2)}) %collective-permute-start.9) | collective-permute-done | bytes 458784 | tf_op jit(solution)/shard_map/ppermute | solution.py:178
  100.8 3.7 %collective-permute-start.10 = (f32[2,2,112,128]{3,2,0,1:T(8,128)S(1)}, f32[2,2,112,128]{3,2,0,1:T(8,128)S(1)}, u32[]{:S(2)}, u32[]{:S(2)}) collective-permute-start(f32[2,2,112,128]{3,2,0,1:T(8,128)S(1)} %bitcast_select_fusion.4), channel_id=1, source_target_pairs={{0,2},{1,3},{2,0},{3,1},{4,6},{5,7},{6,4},{7,5},{8,10},{9,11},{10,... | collective-permute-start | bytes 688136 | tf_op jit(solution)/shard_map/ppermute | solution.py:178
  104.6 5.7 %collective-permute-done.10 = f32[2,2,112,128]{3,2,0,1:T(8,128)S(1)} collective-permute-done((f32[2,2,112,128]{3,2,0,1:T(8,128)S(1)}, f32[2,2,112,128]{3,2,0,1:T(8,128)S(1)}, u32[]{:S(2)}, u32[]{:S(2)}) %collective-permute-start.10) | collective-permute-done | bytes 229408 | tf_op jit(solution)/shard_map/ppermute | solution.py:178
  110.3 3.1 %collective-permute-start.11 = (f32[2,112,128]{2,1,0:T(8,128)S(1)}, f32[2,112,128]{2,1,0:T(8,128)S(1)}, u32[]{:S(2)}, u32[]{:S(2)}) collective-permute-start(f32[2,112,128]{2,1,0:T(8,128)S(1)} %fusion.102), channel_id=1, source_target_pairs={{0,8},{1,9},{2,10},{3,11},{4,12},{5,13},{6,14},{7,15},{8,0},{9,1},... | collective-permute-start | bytes 344072 | tf_op jit(solution)/shard_map/ppermute | solution.py:178
  113.5 5.1 %collective-permute-done.11 = f32[2,112,128]{2,1,0:T(8,128)S(1)} collective-permute-done((f32[2,112,128]{2,1,0:T(8,128)S(1)}, f32[2,112,128]{2,1,0:T(8,128)S(1)}, u32[]{:S(2)}, u32[]{:S(2)}) %collective-permute-start.11) | collective-permute-done | bytes 114720 | tf_op jit(solution)/shard_map/ppermute | solution.py:178
  118.7 15.4 %collective-permute-start.12 = (f32[112,128]{1,0:T(8,128)S(1)}, f32[112,128]{1,0:T(8,128)S(1)}, u32[]{:S(2)}, u32[]{:S(2)}) collective-permute-start(f32[112,128]{1,0:T(8,128)S(1)} %dynamic-slice_bitcast_fusion), channel_id=1, source_target_pairs={{0,256},{128,384},{256,0},{384,128},{1,257},{129,385},{257,1},{385... | collective-permute-start | bytes 172040 | tf_op jit(solution)/shard_map/ppermute | solution.py:169
  134.3 3.6 %collective-permute-done.12 = f32[112,128]{1,0:T(8,128)S(1)} collective-permute-done((f32[112,128]{1,0:T(8,128)S(1)}, f32[112,128]{1,0:T(8,128)S(1)}, u32[]{:S(2)}, u32[]{:S(2)}) %collective-permute-start.12) | collective-permute-done | bytes 57376 | tf_op jit(solution)/shard_map/ppermute | solution.py:169
  137.9 2.7 %collective-permute-start.13 = (f32[112,128]{1,0:T(8,128)S(1)}, f32[112,128]{1,0:T(8,128)S(1)}, u32[]{:S(2)}, u32[]{:S(2)}) collective-permute-start(f32[112,128]{1,0:T(8,128)S(1)} %bitcast_add_fusion.1), channel_id=1, source_target_pairs={{0,16},{16,0},{32,48},{48,32},{64,80},{80,64},{96,112},{112,96},{1... | collective-permute-start | bytes 172040 | tf_op jit(solution)/shard_map/ppermute | solution.py:169
  140.6 0.9 fusion.13
  141.7 2.8 %collective-permute-done.13 = f32[112,128]{1,0:T(8,128)S(1)} collective-permute-done((f32[112,128]{1,0:T(8,128)S(1)}, f32[112,128]{1,0:T(8,128)S(1)}, u32[]{:S(2)}, u32[]{:S(2)}) %collective-permute-start.13) | collective-permute-done | bytes 57376 | tf_op jit(solution)/shard_map/ppermute | solution.py:169
  144.6 4.2 %collective-permute-start.14 = (f32[112,128]{1,0:T(8,128)S(1)}, f32[112,128]{1,0:T(8,128)S(1)}, u32[]{:S(2)}, u32[]{:S(2)}) collective-permute-start(f32[112,128]{1,0:T(8,128)S(1)} %add.209), channel_id=1, source_target_pairs={{0,32},{16,48},{32,0},{48,16},{64,96},{80,112},{96,64},{112,80},{1... | collective-permute-start | bytes 172040 | tf_op jit(solution)/shard_map/ppermute | solution.py:169
  148.8 0.8 fusion.14
  149.8 2.0 %collective-permute-done.14 = f32[112,128]{1,0:T(8,128)S(1)} collective-permute-done((f32[112,128]{1,0:T(8,128)S(1)}, f32[112,128]{1,0:T(8,128)S(1)}, u32[]{:S(2)}, u32[]{:S(2)}) %collective-permute-start.14) | collective-permute-done | bytes 57376 | tf_op jit(solution)/shard_map/ppermute | solution.py:169
  151.8 8.2 %collective-permute-start.15 = (f32[112,128]{1,0:T(8,128)S(1)}, f32[112,128]{1,0:T(8,128)S(1)}, u32[]{:S(2)}, u32[]{:S(2)}) collective-permute-start(f32[112,128]{1,0:T(8,128)S(1)} %add.210), channel_id=1, source_target_pairs={{0,64},{16,80},{32,96},{48,112},{64,0},{80,16},{96,32},{112,48},{1... | collective-permute-start | bytes 172040 | tf_op jit(solution)/shard_map/ppermute | solution.py:169
  160.0 0.9 fusion.18
  161.0 1.2 collective-permute-done.15
  162.2 3.1 %collective-permute-start.16 = (bf16[112,128]{1,0:T(8,128)(2,1)S(1)}, bf16[112,128]{1,0:T(8,128)(2,1)S(1)}, u32[]{:S(2)}, u32[]{:S(2)}) collective-permute-start(bf16[112,128]{1,0:T(8,128)(2,1)S(1)} %add_convert_fusion), channel_id=1, source_target_pairs={{0,8},{1,9},{2,10},{3,11},{4,12},{5,13},{6,14},{7,15},{8,0},{9,1},... | collective-permute-start | bytes 86024 | tf_op jit(solution)/shard_map/ppermute | solution.py:178
  165.3 0.6 copy.250
  165.9 3.6 %collective-permute-done.16 = bf16[112,128]{1,0:T(8,128)(2,1)S(1)} collective-permute-done((bf16[112,128]{1,0:T(8,128)(2,1)S(1)}, bf16[112,128]{1,0:T(8,128)(2,1)S(1)}, u32[]{:S(2)}, u32[]{:S(2)}) %collective-permute-start.16) | collective-permute-done | bytes 28704 | tf_op jit(solution)/shard_map/ppermute | solution.py:178
  169.6 3.6 %collective-permute-start.17 = (bf16[2,112,128]{2,1,0:T(8,128)(2,1)S(1)}, bf16[2,112,128]{2,1,0:T(8,128)(2,1)S(1)}, u32[]{:S(2)}, u32[]{:S(2)}) collective-permute-start(bf16[2,112,128]{2,1,0:T(8,128)(2,1)S(1)} %select_select_fusion.1), channel_id=1, source_target_pairs={{0,2},{1,3},{2,0},{3,1},{4,6},{5,7},{6,4},{7,5},{8,10},{9,11},{10,... | collective-permute-start | bytes 172040 | tf_op jit(solution)/shard_map/ppermute | solution.py:178
  173.2 3.9 %collective-permute-done.17 = bf16[2,112,128]{2,1,0:T(8,128)(2,1)S(1)} collective-permute-done((bf16[2,112,128]{2,1,0:T(8,128)(2,1)S(1)}, bf16[2,112,128]{2,1,0:T(8,128)(2,1)S(1)}, u32[]{:S(2)}, u32[]{:S(2)}) %collective-permute-start.17) | collective-permute-done | bytes 57376 | tf_op jit(solution)/shard_map/ppermute | solution.py:178
  177.4 2.5 %collective-permute-start.18 = (bf16[2,2,112,128]{3,2,1,0:T(8,128)(2,1)S(1)}, bf16[2,2,112,128]{3,2,1,0:T(8,128)(2,1)S(1)}, u32[]{:S(2)}, u32[]{:S(2)}) collective-permute-start(bf16[2,2,112,128]{3,2,1,0:T(8,128)(2,1)S(1)} %fusion.99), channel_id=1, source_target_pairs={{0,4},{1,5},{2,6},{3,7},{4,0},{5,1},{6,2},{7,3},{8,12},{9,13},{10,... | collective-permute-start | bytes 344072 | tf_op jit(solution)/shard_map/ppermute | solution.py:178
  180.0 4.1 %collective-permute-done.18 = bf16[2,2,112,128]{3,2,1,0:T(8,128)(2,1)S(1)} collective-permute-done((bf16[2,2,112,128]{3,2,1,0:T(8,128)(2,1)S(1)}, bf16[2,2,112,128]{3,2,1,0:T(8,128)(2,1)S(1)}, u32[]{:S(2)}, u32[]{:S(2)}) %collective-permute-start.18) | collective-permute-done | bytes 114720 | tf_op jit(solution)/shard_map/ppermute | solution.py:178
  184.2 1.9 collective-permute-start.19
  186.4 5.8 %collective-permute-done.19 = bf16[2,2,2,112,128]{4,3,1,0,2:T(8,128)(2,1)S(1)} collective-permute-done((bf16[2,2,2,112,128]{4,3,1,0,2:T(8,128)(2,1)S(1)}, bf16[2,2,2,112,128]{4,3,1,0,2:T(8,128)(2,1)S(1)}, u32[]{:S(2)}, u32[]{:S(2)}) %collective-permute-start.19) | collective-permute-done | bytes 229408 | tf_op jit(solution)/shard_map/ppermute | solution.py:178
  192.4 0.8 fusion.168
  (142 shorter events, 9.6 us)
Async XLA Ops:
  2.0 22.1 %collective-permute-start.1 = (bf16[2,1,128,128]{3,0,2,1:T(2,128)(2,1)S(1)}, bf16[2,1,128,128]{3,0,2,1:T(2,128)(2,1)S(1)}, u32[]{:S(2)}, u32[]{:S(2)}) collective-permute-start(bf16[2,1,128,128]{3,0,2,1:T(2,128)(2,1)S(1)} %get-tuple-element.36), channel_id=1, source_target_pairs={{1,0},{2,1},{3,2},{4,3},{5,4},{6,5},{7,6},{8,7},{9,8},{10,9},{11,1... | collective-permute-start | bytes 196616 | tf_op jit(solution)/shard_map/ppermute | solution.py:19
  7.2 16.9 %collective-permute-start = (bf16[2,1,128,128]{3,0,2,1:T(2,128)(2,1)S(1)}, bf16[2,1,128,128]{3,0,2,1:T(2,128)(2,1)S(1)}, u32[]{:S(2)}, u32[]{:S(2)}) collective-permute-start(bf16[2,1,128,128]{3,0,2,1:T(2,128)(2,1)S(1)} %get-tuple-element.35), channel_id=1, source_target_pairs={{0,1},{1,2},{2,3},{3,4},{4,5},{5,6},{6,7},{7,8},{8,9},{9,10},{10,1... | collective-permute-start | bytes 196616 | tf_op jit(solution)/shard_map/ppermute | solution.py:17
  9.9 12.9 %collective-permute-start.5 = (bf16[1,1,64,128]{3,2,1,0:T(8,128)(2,1)S(1)}, bf16[1,1,64,128]{3,2,1,0:T(8,128)(2,1)S(1)}, u32[]{:S(2)}, u32[]{:S(2)}) collective-permute-start(bf16[1,1,64,128]{3,2,1,0:T(8,128)(2,1)S(1)} %slice.186), channel_id=1, source_target_pairs={{1,0},{2,1},{3,2},{4,3},{5,4},{6,5},{7,6},{8,7},{9,8},{10,9},{11,1... | collective-permute-start | bytes 49160 | tf_op jit(solution)/shard_map/ppermute | solution.py:29
  22.8 7.7 %collective-permute-start.6 = (bf16[1,3,64,128]{3,2,1,0:T(8,128)(2,1)S(1)}, bf16[1,3,64,128]{3,2,1,0:T(8,128)(2,1)S(1)}, u32[]{:S(2)}, u32[]{:S(2)}) collective-permute-start(bf16[1,3,64,128]{3,2,1,0:T(8,128)(2,1)S(1)} %pad_maximum_fusion.15), channel_id=1, source_target_pairs={{16,0},{32,16},{48,32},{64,48},{80,64},{96,80},{112,96},{17,1},{33... | collective-permute-start | bytes 147464 | tf_op jit(solution)/shard_map/ppermute | solution.py:29
  24.7 7.2 %copy-start.3 = (bf16[3,3,3,128,128]{4,3,2,1,0:T(8,128)(2,1)S(1)}, bf16[3,3,3,128,128]{4,3,2,1,0:T(8,128)(2,1)}, u32[]{:S(2)}) copy-start(bf16[3,3,3,128,128]{4,3,2,1,0:T(8,128)(2,1)} %param.8) | copy-start | bytes 2654212
  24.7 7.2 %copy-start.6 = (pred[8,18]{0,1:T(8,128)(4,1)S(1)}, pred[8,18]{0,1:T(8,128)(4,1)}, u32[]{:S(2)}) copy-start(pred[8,18]{0,1:T(8,128)(4,1)} %constant.283) | copy-start | bytes 436
  24.7 12.1 %collective-permute-start.2 = (bf16[2,6,128,128]{3,0,2,1:T(2,128)(2,1)S(1)}, bf16[2,6,128,128]{3,0,2,1:T(2,128)(2,1)S(1)}, u32[]{:S(2)}, u32[]{:S(2)}) collective-permute-start(bf16[2,6,128,128]{3,0,2,1:T(2,128)(2,1)S(1)} %pad_maximum_fusion.6), channel_id=1, source_target_pairs={{0,16},{16,32},{32,48},{48,64},{64,80},{80,96},{96,112},{1,17},{17... | collective-permute-start | bytes 1179656 | tf_op jit(solution)/shard_map/ppermute | solution.py:29
  37.2 1.6 copy-start.2
  37.2 1.6 copy-start.5
  42.0 9.9 %collective-permute-start.3 = (bf16[2,1,128,128]{3,0,2,1:T(2,128)(2,1)S(1)}, bf16[2,1,128,128]{3,0,2,1:T(2,128)(2,1)S(1)}, u32[]{:S(2)}, u32[]{:S(2)}) collective-permute-start(bf16[2,1,128,128]{3,0,2,1:T(2,128)(2,1)S(1)} %bitcast.367), channel_id=1, source_target_pairs={{0,1},{1,2},{2,3},{3,4},{4,5},{5,6},{6,7},{7,8},{8,9},{9,10},{10,1... | collective-permute-start | bytes 196616 | tf_op jit(solution)/shard_map/ppermute | solution.py:29
  52.3 9.5 %collective-permute-start.4 = (bf16[2,5,128,128]{3,0,2,1:T(2,128)(2,1)S(1)}, bf16[2,5,128,128]{3,0,2,1:T(2,128)(2,1)S(1)}, u32[]{:S(2)}, u32[]{:S(2)}) collective-permute-start(bf16[2,5,128,128]{3,0,2,1:T(2,128)(2,1)S(1)} %pad_maximum_fusion.7), channel_id=1, source_target_pairs={{0,16},{16,32},{32,48},{48,64},{64,80},{80,96},{96,112},{1,17},{17... | collective-permute-start | bytes 983048 | tf_op jit(solution)/shard_map/ppermute | solution.py:29
  62.3 0.8 copy-start.1
  64.5 1.8 copy-start
  66.3 6.0 %collective-permute-start.7 = (f32[2,2,2,2,2,112,128]{6,5,4,3,2,0,1:T(8,128)}, f32[2,2,2,2,2,112,128]{6,5,4,3,2,0,1:T(8,128)}, u32[]{:S(2)}, u32[]{:S(2)}) collective-permute-start(f32[2,2,2,2,2,112,128]{6,5,4,3,2,0,1:T(8,128)} %fusion.1), channel_id=1, source_target_pairs={{0,128},{128,0},{256,384},{384,256},{1,129},{129,1},{257,385},{385... | collective-permute-start | bytes 5505032 | tf_op jit(solution)/shard_map/ppermute | solution.py:169
  74.6 15.3 %collective-permute-start.8 = (f32[2,2,2,2,112,128]{5,4,2,0,3,1:T(8,128)S(1)}, f32[2,2,2,2,112,128]{5,4,2,0,3,1:T(8,128)S(1)}, u32[]{:S(2)}, u32[]{:S(2)}) collective-permute-start(f32[2,2,2,2,112,128]{5,4,2,0,3,1:T(8,128)S(1)} %bitcast_select_fusion), channel_id=1, source_target_pairs={{0,1},{1,0},{2,3},{3,2},{4,5},{5,4},{6,7},{7,6},{8,9},{9,8},{10,11... | collective-permute-start | bytes 2752520 | tf_op jit(solution)/shard_map/ppermute | solution.py:178
  90.3 10.4 %collective-permute-start.9 = (f32[2,2,2,112,128]{4,3,1,0,2:T(8,128)S(1)}, f32[2,2,2,112,128]{4,3,1,0,2:T(8,128)S(1)}, u32[]{:S(2)}, u32[]{:S(2)}) collective-permute-start(f32[2,2,2,112,128]{4,3,1,0,2:T(8,128)S(1)} %bitcast_select_fusion.2), channel_id=1, source_target_pairs={{0,4},{1,5},{2,6},{3,7},{4,0},{5,1},{6,2},{7,3},{8,12},{9,13},{10,... | collective-permute-start | bytes 1376264 | tf_op jit(solution)/shard_map/ppermute | solution.py:178
  100.8 9.4 %collective-permute-start.10 = (f32[2,2,112,128]{3,2,0,1:T(8,128)S(1)}, f32[2,2,112,128]{3,2,0,1:T(8,128)S(1)}, u32[]{:S(2)}, u32[]{:S(2)}) collective-permute-start(f32[2,2,112,128]{3,2,0,1:T(8,128)S(1)} %bitcast_select_fusion.4), channel_id=1, source_target_pairs={{0,2},{1,3},{2,0},{3,1},{4,6},{5,7},{6,4},{7,5},{8,10},{9,11},{10,... | collective-permute-start | bytes 688136 | tf_op jit(solution)/shard_map/ppermute | solution.py:178
  110.2 30.4 %copy-start.7 = (pred[8,9]{0,1:T(8,128)(4,1)S(1)}, pred[8,9]{0,1:T(8,128)(4,1)}, u32[]{:S(2)}) copy-start(pred[8,9]{0,1:T(8,128)(4,1)} %constant.277) | copy-start | bytes 220
  110.3 30.3 %copy-start.4 = (bf16[3,3,3,128,128]{4,3,2,1,0:T(8,128)(2,1)S(1)}, bf16[3,3,3,128,128]{4,3,2,1,0:T(8,128)(2,1)}, u32[]{:S(2)}) copy-start(bf16[3,3,3,128,128]{4,3,2,1,0:T(8,128)(2,1)} %param.8) | copy-start | bytes 2654212
  110.3 8.3 %collective-permute-start.11 = (f32[2,112,128]{2,1,0:T(8,128)S(1)}, f32[2,112,128]{2,1,0:T(8,128)S(1)}, u32[]{:S(2)}, u32[]{:S(2)}) collective-permute-start(f32[2,112,128]{2,1,0:T(8,128)S(1)} %fusion.102), channel_id=1, source_target_pairs={{0,8},{1,9},{2,10},{3,11},{4,12},{5,13},{6,14},{7,15},{8,0},{9,1},... | collective-permute-start | bytes 344072 | tf_op jit(solution)/shard_map/ppermute | solution.py:178
  118.7 19.2 %collective-permute-start.12 = (f32[112,128]{1,0:T(8,128)S(1)}, f32[112,128]{1,0:T(8,128)S(1)}, u32[]{:S(2)}, u32[]{:S(2)}) collective-permute-start(f32[112,128]{1,0:T(8,128)S(1)} %dynamic-slice_bitcast_fusion), channel_id=1, source_target_pairs={{0,256},{128,384},{256,0},{384,128},{1,257},{129,385},{257,1},{385... | collective-permute-start | bytes 172040 | tf_op jit(solution)/shard_map/ppermute | solution.py:169
  137.9 6.7 %collective-permute-start.13 = (f32[112,128]{1,0:T(8,128)S(1)}, f32[112,128]{1,0:T(8,128)S(1)}, u32[]{:S(2)}, u32[]{:S(2)}) collective-permute-start(f32[112,128]{1,0:T(8,128)S(1)} %bitcast_add_fusion.1), channel_id=1, source_target_pairs={{0,16},{16,0},{32,48},{48,32},{64,80},{80,64},{96,112},{112,96},{1... | collective-permute-start | bytes 172040 | tf_op jit(solution)/shard_map/ppermute | solution.py:169
  144.6 7.2 %collective-permute-start.14 = (f32[112,128]{1,0:T(8,128)S(1)}, f32[112,128]{1,0:T(8,128)S(1)}, u32[]{:S(2)}, u32[]{:S(2)}) collective-permute-start(f32[112,128]{1,0:T(8,128)S(1)} %add.209), channel_id=1, source_target_pairs={{0,32},{16,48},{32,0},{48,16},{64,96},{80,112},{96,64},{112,80},{1... | collective-permute-start | bytes 172040 | tf_op jit(solution)/shard_map/ppermute | solution.py:169
  151.8 10.4 %collective-permute-start.15 = (f32[112,128]{1,0:T(8,128)S(1)}, f32[112,128]{1,0:T(8,128)S(1)}, u32[]{:S(2)}, u32[]{:S(2)}) collective-permute-start(f32[112,128]{1,0:T(8,128)S(1)} %add.210), channel_id=1, source_target_pairs={{0,64},{16,80},{32,96},{48,112},{64,0},{80,16},{96,32},{112,48},{1... | collective-permute-start | bytes 172040 | tf_op jit(solution)/shard_map/ppermute | solution.py:169
  162.2 7.3 %collective-permute-start.16 = (bf16[112,128]{1,0:T(8,128)(2,1)S(1)}, bf16[112,128]{1,0:T(8,128)(2,1)S(1)}, u32[]{:S(2)}, u32[]{:S(2)}) collective-permute-start(bf16[112,128]{1,0:T(8,128)(2,1)S(1)} %add_convert_fusion), channel_id=1, source_target_pairs={{0,8},{1,9},{2,10},{3,11},{4,12},{5,13},{6,14},{7,15},{8,0},{9,1},... | collective-permute-start | bytes 86024 | tf_op jit(solution)/shard_map/ppermute | solution.py:178
  169.6 7.6 %collective-permute-start.17 = (bf16[2,112,128]{2,1,0:T(8,128)(2,1)S(1)}, bf16[2,112,128]{2,1,0:T(8,128)(2,1)S(1)}, u32[]{:S(2)}, u32[]{:S(2)}) collective-permute-start(bf16[2,112,128]{2,1,0:T(8,128)(2,1)S(1)} %select_select_fusion.1), channel_id=1, source_target_pairs={{0,2},{1,3},{2,0},{3,1},{4,6},{5,7},{6,4},{7,5},{8,10},{9,11},{10,... | collective-permute-start | bytes 172040 | tf_op jit(solution)/shard_map/ppermute | solution.py:178
  177.4 6.7 %collective-permute-start.18 = (bf16[2,2,112,128]{3,2,1,0:T(8,128)(2,1)S(1)}, bf16[2,2,112,128]{3,2,1,0:T(8,128)(2,1)S(1)}, u32[]{:S(2)}, u32[]{:S(2)}) collective-permute-start(bf16[2,2,112,128]{3,2,1,0:T(8,128)(2,1)S(1)} %fusion.99), channel_id=1, source_target_pairs={{0,4},{1,5},{2,6},{3,7},{4,0},{5,1},{6,2},{7,3},{8,12},{9,13},{10,... | collective-permute-start | bytes 344072 | tf_op jit(solution)/shard_map/ppermute | solution.py:178
  184.2 7.9 %collective-permute-start.19 = (bf16[2,2,2,112,128]{4,3,1,0,2:T(8,128)(2,1)S(1)}, bf16[2,2,2,112,128]{4,3,1,0,2:T(8,128)(2,1)S(1)}, u32[]{:S(2)}, u32[]{:S(2)}) collective-permute-start(bf16[2,2,2,112,128]{4,3,1,0,2:T(8,128)(2,1)S(1)} %fusion.74), channel_id=1, source_target_pairs={{0,1},{1,0},{2,3},{3,2},{4,5},{5,4},{6,7},{7,6},{8,9},{9,8},{10,11... | collective-permute-start | bytes 688136 | tf_op jit(solution)/shard_map/ppermute | solution.py:178

commit v3 on v2

--- a/solution.py
+++ b/solution.py
@@ -221,20 +221,7 @@
     for bit in frame_bits:
         blocks = blocks + swap(blocks, "tm", bit)
     piece = blocks.astype(jnp.bfloat16)
-    present = [[], []]
-    for bits in reversed(stages):
-        other = swap_rows(piece, bits)
-        options = []
-        for variant in (0, 1):
-            bit = bits[variant]
-            high = (row // bit) % 2
-            place = sum(1 for kept in present[variant] if kept > bit)
-            low_first = jnp.stack([piece, other], axis=place)
-            high_first = jnp.stack([other, piece], axis=place)
-            options.append(jnp.where(high == 0, low_first, high_first))
-            present[variant].append(bit)
-        piece = jnp.where(core == 0, options[0], options[1])
-    return piece
+    return lax.all_gather(piece, "height", axis=0, tiled=False)
 
 
 def solution(mesh):

time: 195 us -> 190 us (0.974)
  blocking collectives: 0 us -> 23.4 us
  waiting for transfers between devices: 69.9 us -> 51.7 us
  starting transfers between devices: 80.6 us -> 69.5 us
    all_gather x0 -> x1, blocking collectives: none -> 23.4 us  [reduce_gradients(): return lax.all_gather(piece, 'height', axis=0, tiled=False)]
    ppermute x8 -> x4, waiting for transfers between devices: 49.2 us -> 31.7 us  [swap_rows(): return lax.ppermute(value, ('dp', 'height'), pairs)]
    ppermute x8 -> x4, starting transfers between devices: 22.6 us -> 11.5 us  [swap_rows(): return lax.ppermute(value, ('dp', 'height'), pairs)]
  transfers between devices with their start and end apart: 20 -> 16, of which waited for: 15 -> 11; matrix products, arithmetic and copies ran while one was open for 12% -> 12% of each run, Pallas kernels for 0% -> 0%
where the time goes in v3:
time: 190 us; the launch traced here: 187 us
  starting transfers between devices  69.5 us (37%)
  waiting for transfers between devices  51.7 us (27%)
  blocking collectives  23.4 us (12%)
  matrix products  14.7 us (8%)
  other arithmetic  14.4 us (8%)
  local copies, waits for them, and re-layouts  9.65 us (5%)
  between operations  3.83 us (2%)
    ppermute x5, starting transfers between devices, swap(): lax.ppermute(value, axis, [(i, i ^ bit) for i in range(lax.axis_size(axis...  32.4 us
    ppermute x4, waiting for transfers between devices, swap_rows(): return lax.ppermute(value, ('dp', 'height'), pairs)  31.7 us
    all_gather x1, blocking collectives, reduce_gradients(): return lax.all_gather(piece, 'height', axis=0, tiled=False)  23.4 us
    ppermute x5, starting transfers between devices, shifted(): lax.ppermute(value, axis, [(source, source + steps) for source in range(l...  18.5 us
    ppermute x5, waiting for transfers between devices, swap(): lax.ppermute(value, axis, [(i, i ^ bit) for i in range(lax.axis_size(axis...  12.9 us
    ppermute x4, starting transfers between devices, swap_rows(): return lax.ppermute(value, ('dp', 'height'), pairs)  11.5 us
    conv_general_dilated x6, matrix products, weight_grad(): lax.conv_general_dilated(frame_slab, masked, (1, 1), ((0, 0), pad_cols),...  8.4 us
    ppermute x5, waiting for transfers between devices, shifted(): lax.ppermute(value, axis, [(source, source + steps) for source in range(l...  7.16 us
  transfers between devices with their start and end apart: 16, of which 11 were waited for; matrix products, arithmetic and copies ran while one was open for 12% of the time, Pallas kernels for 0%

profile of v3, /device:TPU:6, one launch (start us, length us, event | category | flops | bytes accessed | tf_op | source)
XLA Modules:
  0.0 187.2 jit_solution(10044304578433401053)
XLA Ops:
  0.6 1.2 copy.332
  2.0 5.2 %collective-permute-start.1 = (bf16[2,1,128,128]{3,0,2,1:T(2,128)(2,1)S(1)}, bf16[2,1,128,128]{3,0,2,1:T(2,128)(2,1)S(1)}, u32[]{:S(2)}, u32[]{:S(2)}) collective-permute-start(bf16[2,1,128,128]{3,0,2,1:T(2,128)(2,1)S(1)} %get-tuple-element.34), channel_id=1, source_target_pairs={{1,0},{2,1},{3,2},{4,3},{5,4},{6,5},{7,6},{8,7},{9,8},{10,9},{11,1... | collective-permute-start | bytes 196616 | tf_op jit(solution)/shard_map/ppermute | solution.py:19
  7.2 1.9 %collective-permute-start = (bf16[2,1,128,128]{3,0,2,1:T(2,128)(2,1)S(1)}, bf16[2,1,128,128]{3,0,2,1:T(2,128)(2,1)S(1)}, u32[]{:S(2)}, u32[]{:S(2)}) collective-permute-start(bf16[2,1,128,128]{3,0,2,1:T(2,128)(2,1)S(1)} %get-tuple-element.33), channel_id=1, source_target_pairs={{0,1},{1,2},{2,3},{3,4},{4,5},{5,6},{6,7},{7,8},{8,9},{9,10},{10,1... | collective-permute-start | bytes 196616 | tf_op jit(solution)/shard_map/ppermute | solution.py:17
  9.1 0.8 fusion.118
  9.9 6.0 %collective-permute-start.5 = (bf16[1,1,64,128]{3,2,1,0:T(8,128)(2,1)S(1)}, bf16[1,1,64,128]{3,2,1,0:T(8,128)(2,1)S(1)}, u32[]{:S(2)}, u32[]{:S(2)}) collective-permute-start(bf16[1,1,64,128]{3,2,1,0:T(8,128)(2,1)S(1)} %slice.186), channel_id=1, source_target_pairs={{1,0},{2,1},{3,2},{4,3},{5,4},{6,5},{7,6},{8,7},{9,8},{10,9},{11,1... | collective-permute-start | bytes 49160 | tf_op jit(solution)/shard_map/ppermute | solution.py:29
  15.9 0.8 reduce-window_clone.1
  16.7 0.7 subtract_bitcast_fusion
  17.7 0.6 fusion.161
  20.3 1.4 broadcast_multiply_fusion.5
  21.7 0.6 slice.191
  22.2 0.7 slice.195
  22.9 1.3 collective-permute-start.6
  24.2 0.6 pad_maximum_fusion.5
  24.9 4.7 %collective-permute-start.2 = (bf16[2,6,128,128]{3,0,2,1:T(2,128)(2,1)S(1)}, bf16[2,6,128,128]{3,0,2,1:T(2,128)(2,1)S(1)}, u32[]{:S(2)}, u32[]{:S(2)}) collective-permute-start(bf16[2,6,128,128]{3,0,2,1:T(2,128)(2,1)S(1)} %pad_maximum_fusion.5), channel_id=1, source_target_pairs={{0,16},{16,32},{32,48},{48,64},{64,80},{80,96},{96,112},{1,17},{17... | collective-permute-start | bytes 1179656 | tf_op jit(solution)/shard_map/ppermute | solution.py:29
  29.6 0.6 fusion.168
  30.6 1.2 multiply_bitcast_fusion.1
  32.0 0.3 fusion.9
  32.7 0.3 convolution_select_fusion.5
  33.1 0.3 fusion.8
  33.5 3.4 %collective-permute-done.2 = bf16[2,6,128,128]{3,0,2,1:T(2,128)(2,1)S(1)} collective-permute-done((bf16[2,6,128,128]{3,0,2,1:T(2,128)(2,1)S(1)}, bf16[2,6,128,128]{3,0,2,1:T(2,128)(2,1)S(1)}, u32[]{:S(2)}, u32[]{:S(2)}) %collective-permute-start.2) | collective-permute-done | bytes 393248 | tf_op jit(solution)/shard_map/ppermute | solution.py:29
  37.4 1.0 pad_maximum_fusion.2
  38.4 0.3 pad.11
  39.0 0.8 fusion.6
  40.0 0.8 fusion.5
  41.0 1.0 add_divide_fusion
  42.1 2.1 %collective-permute-start.3 = (bf16[2,1,128,128]{3,0,2,1:T(2,128)(2,1)S(1)}, bf16[2,1,128,128]{3,0,2,1:T(2,128)(2,1)S(1)}, u32[]{:S(2)}, u32[]{:S(2)}) collective-permute-start(bf16[2,1,128,128]{3,0,2,1:T(2,128)(2,1)S(1)} %bitcast.297), channel_id=1, source_target_pairs={{0,1},{1,2},{2,3},{3,4},{4,5},{5,6},{6,7},{7,8},{8,9},{9,10},{10,1... | collective-permute-start | bytes 196616 | tf_op jit(solution)/shard_map/ppermute | solution.py:29
  45.0 2.0 %convolution_bitcast_fusion.3 = f32[1,3,3,128,128]{4,3,2,1,0:T(8,128)S(1)} fusion(bf16[2,6,128,128]{3,0,2,1:T(2,128)(2,1)S(1)} %pad_maximum_fusion.5, bf16[2,4,128,128]{3,2,1,0:T(8,128)(2,1)S(1)} %get-tuple-element.32), kind=kOutput, calls=%fused_computation.13 | convolution fusion | flops 300417024 | bytes 1245184 | tf_op jit(solution)/shard_map/conv_general_dilated | solution.py:56
  47.0 2.0 %convolution_bitcast_fusion.4 = f32[1,3,3,128,128]{4,3,2,1,0:T(8,128)S(1)} fusion(bf16[2,6,128,128]{3,0,2,1:T(2,128)(2,1)S(1)} %pad_maximum_fusion.2, bf16[2,4,128,128]{3,2,1,0:T(8,128)(2,1)S(1)} %get-tuple-element.31), kind=kOutput, calls=%fused_computation.14 | convolution fusion | flops 300417024 | bytes 1245184 | tf_op jit(solution)/shard_map/conv_general_dilated | solution.py:56
  48.9 2.0 %convolution_bitcast_fusion.5 = f32[1,3,3,128,128]{4,3,2,1,0:T(8,128)S(1)} fusion(bf16[2,6,128,128]{3,0,2,1:T(2,128)(2,1)S(1)} %collective-permute-done.2, bf16[2,4,128,128]{3,2,1,0:T(8,128)(2,1)S(1)} %get-tuple-element.20), kind=kOutput, calls=%fused_computation.15 | convolution fusion | flops 300417024 | bytes 1245184 | tf_op jit(solution)/shard_map/conv_general_dilated | solution.py:56
  51.9 0.4 pad_maximum_fusion.6
  52.3 4.4 %collective-permute-start.4 = (bf16[2,5,128,128]{3,0,2,1:T(2,128)(2,1)S(1)}, bf16[2,5,128,128]{3,0,2,1:T(2,128)(2,1)S(1)}, u32[]{:S(2)}, u32[]{:S(2)}) collective-permute-start(bf16[2,5,128,128]{3,0,2,1:T(2,128)(2,1)S(1)} %pad_maximum_fusion.6), channel_id=1, source_target_pairs={{0,16},{16,32},{32,48},{48,64},{64,80},{80,96},{96,112},{1,17},{17... | collective-permute-start | bytes 983048 | tf_op jit(solution)/shard_map/ppermute | solution.py:29
  56.7 0.4 slice_maximum_fusion
  57.2 0.9 convolution_bitcast_fusion
  58.1 3.7 %collective-permute-done.4 = bf16[2,5,128,128]{3,0,2,1:T(2,128)(2,1)S(1)} collective-permute-done((bf16[2,5,128,128]{3,0,2,1:T(2,128)(2,1)S(1)}, bf16[2,5,128,128]{3,0,2,1:T(2,128)(2,1)S(1)}, u32[]{:S(2)}, u32[]{:S(2)}) %collective-permute-start.4) | collective-permute-done | bytes 327712 | tf_op jit(solution)/shard_map/ppermute | solution.py:29
  61.8 0.5 fusion.159
  62.3 0.8 convolution_bitcast_fusion.1
  63.2 0.8 convolution_bitcast_fusion.2
  64.5 1.5 fusion.1
  66.2 1.9 %collective-permute-start.7 = (f32[2,2,2,2,2,112,128]{6,5,4,3,2,1,0:T(8,128)S(1)}, f32[2,2,2,2,2,112,128]{6,5,4,3,2,1,0:T(8,128)}, u32[]{:S(2)}, u32[]{:S(2)}) collective-permute-start(f32[2,2,2,2,2,112,128]{6,5,4,3,2,1,0:T(8,128)S(1)} %bitcast.273), channel_id=1, source_target_pairs={{0,128},{128,0},{256,384},{384,256},{1,129},{129,1},{257,385},{385... | collective-permute-start | bytes 5505032 | tf_op jit(solution)/shard_map/ppermute | solution.py:169
  68.1 3.8 %collective-permute-done.7 = f32[2,2,2,2,2,112,128]{6,5,4,3,2,1,0:T(8,128)} collective-permute-done((f32[2,2,2,2,2,112,128]{6,5,4,3,2,1,0:T(8,128)S(1)}, f32[2,2,2,2,2,112,128]{6,5,4,3,2,1,0:T(8,128)}, u32[]{:S(2)}, u32[]{:S(2)}) %collective-permute-start.7) | collective-permute-done | bytes 1835040 | tf_op jit(solution)/shard_map/ppermute | solution.py:169
  72.0 2.3 %bitcast_add_fusion = f32[2,2,2,2,2,112,128]{6,5,4,3,2,1,0:T(8,128)S(1)} fusion(f32[2,2,2,2,2,112,128]{6,5,4,3,2,1,0:T(8,128)} %collective-permute-done.7, f32[2,1,2,2,2,2,112,128]{7,6,5,4,3,1,0,2:T(8,128)} %get-tuple-element.22), kind=kLoop, calls=%fused_computation.6 | loop fusion | flops 458752 | bytes 5505024 | tf_op jit(solution)/shard_map/add | solution.py:201
  74.4 1.9 %collective-permute-start.8 = (f32[2,2,2,2,112,128]{5,4,3,2,1,0:T(8,128)S(1)}, f32[2,2,2,2,112,128]{5,4,3,2,1,0:T(8,128)}, u32[]{:S(2)}, u32[]{:S(2)}) collective-permute-start(f32[2,2,2,2,112,128]{5,4,3,2,1,0:T(8,128)S(1)} %bitcast_select_fusion), channel_id=1, source_target_pairs={{0,1},{1,0},{2,3},{3,2},{4,5},{5,4},{6,7},{7,6},{8,9},{9,8},{10,11... | collective-permute-start | bytes 2752520 | tf_op jit(solution)/shard_map/ppermute | solution.py:178
  76.3 13.4 %collective-permute-done.8 = f32[2,2,2,2,112,128]{5,4,3,2,1,0:T(8,128)} collective-permute-done((f32[2,2,2,2,112,128]{5,4,3,2,1,0:T(8,128)S(1)}, f32[2,2,2,2,112,128]{5,4,3,2,1,0:T(8,128)}, u32[]{:S(2)}, u32[]{:S(2)}) %collective-permute-start.8) | collective-permute-done | bytes 917536 | tf_op jit(solution)/shard_map/ppermute | solution.py:178
  89.8 1.3 fusion.19
  91.2 2.7 %collective-permute-start.9 = (f32[2,2,2,112,128]{4,3,2,1,0:T(8,128)S(1)}, f32[2,2,2,112,128]{4,3,2,1,0:T(8,128)S(1)}, u32[]{:S(2)}, u32[]{:S(2)}) collective-permute-start(f32[2,2,2,112,128]{4,3,2,1,0:T(8,128)S(1)} %bitcast_select_fusion.2), channel_id=1, source_target_pairs={{0,4},{1,5},{2,6},{3,7},{4,0},{5,1},{6,2},{7,3},{8,12},{9,13},{10,... | collective-permute-start | bytes 1376264 | tf_op jit(solution)/shard_map/ppermute | solution.py:178
  93.9 7.6 %collective-permute-done.9 = f32[2,2,2,112,128]{4,3,2,1,0:T(8,128)S(1)} collective-permute-done((f32[2,2,2,112,128]{4,3,2,1,0:T(8,128)S(1)}, f32[2,2,2,112,128]{4,3,2,1,0:T(8,128)S(1)}, u32[]{:S(2)}, u32[]{:S(2)}) %collective-permute-start.9) | collective-permute-done | bytes 458784 | tf_op jit(solution)/shard_map/ppermute | solution.py:178
  101.7 3.8 %collective-permute-start.10 = (f32[2,2,112,128]{3,2,1,0:T(8,128)S(1)}, f32[2,2,112,128]{3,2,1,0:T(8,128)S(1)}, u32[]{:S(2)}, u32[]{:S(2)}) collective-permute-start(f32[2,2,112,128]{3,2,1,0:T(8,128)S(1)} %bitcast_select_fusion.4), channel_id=1, source_target_pairs={{0,2},{1,3},{2,0},{3,1},{4,6},{5,7},{6,4},{7,5},{8,10},{9,11},{10,... | collective-permute-start | bytes 688136 | tf_op jit(solution)/shard_map/ppermute | solution.py:178
  105.6 5.7 %collective-permute-done.10 = f32[2,2,112,128]{3,2,1,0:T(8,128)S(1)} collective-permute-done((f32[2,2,112,128]{3,2,1,0:T(8,128)S(1)}, f32[2,2,112,128]{3,2,1,0:T(8,128)S(1)}, u32[]{:S(2)}, u32[]{:S(2)}) %collective-permute-start.10) | collective-permute-done | bytes 229408 | tf_op jit(solution)/shard_map/ppermute | solution.py:178
  111.3 3.0 %collective-permute-start.11 = (f32[2,112,128]{2,1,0:T(8,128)S(1)}, f32[2,112,128]{2,1,0:T(8,128)S(1)}, u32[]{:S(2)}, u32[]{:S(2)}) collective-permute-start(f32[2,112,128]{2,1,0:T(8,128)S(1)} %select_bitcast_fusion), channel_id=1, source_target_pairs={{0,8},{1,9},{2,10},{3,11},{4,12},{5,13},{6,14},{7,15},{8,0},{9,1},... | collective-permute-start | bytes 344072 | tf_op jit(solution)/shard_map/ppermute | solution.py:178
  114.6 4.9 %collective-permute-done.11 = f32[2,112,128]{2,1,0:T(8,128)S(1)} collective-permute-done((f32[2,112,128]{2,1,0:T(8,128)S(1)}, f32[2,112,128]{2,1,0:T(8,128)S(1)}, u32[]{:S(2)}, u32[]{:S(2)}) %collective-permute-start.11) | collective-permute-done | bytes 114720 | tf_op jit(solution)/shard_map/ppermute | solution.py:178
  119.5 15.4 %collective-permute-start.12 = (f32[112,128]{1,0:T(8,128)S(1)}, f32[112,128]{1,0:T(8,128)S(1)}, u32[]{:S(2)}, u32[]{:S(2)}) collective-permute-start(f32[112,128]{1,0:T(8,128)S(1)} %dynamic-slice_bitcast_fusion), channel_id=1, source_target_pairs={{0,256},{128,384},{256,0},{384,128},{1,257},{129,385},{257,1},{385... | collective-permute-start | bytes 172040 | tf_op jit(solution)/shard_map/ppermute | solution.py:169
  134.9 0.9 fusion.10
  136.0 2.7 %collective-permute-done.12 = f32[112,128]{1,0:T(8,128)S(1)} collective-permute-done((f32[112,128]{1,0:T(8,128)S(1)}, f32[112,128]{1,0:T(8,128)S(1)}, u32[]{:S(2)}, u32[]{:S(2)}) %collective-permute-start.12) | collective-permute-done | bytes 57376 | tf_op jit(solution)/shard_map/ppermute | solution.py:169
  138.7 2.7 %collective-permute-start.13 = (f32[112,128]{1,0:T(8,128)S(1)}, f32[112,128]{1,0:T(8,128)S(1)}, u32[]{:S(2)}, u32[]{:S(2)}) collective-permute-start(f32[112,128]{1,0:T(8,128)S(1)} %bitcast_add_fusion.1), channel_id=1, source_target_pairs={{0,16},{16,0},{32,48},{48,32},{64,80},{80,64},{96,112},{112,96},{1... | collective-permute-start | bytes 172040 | tf_op jit(solution)/shard_map/ppermute | solution.py:169
  141.4 0.9 fusion.11
  142.6 2.9 %collective-permute-done.13 = f32[112,128]{1,0:T(8,128)S(1)} collective-permute-done((f32[112,128]{1,0:T(8,128)S(1)}, f32[112,128]{1,0:T(8,128)S(1)}, u32[]{:S(2)}, u32[]{:S(2)}) %collective-permute-start.13) | collective-permute-done | bytes 57376 | tf_op jit(solution)/shard_map/ppermute | solution.py:169
  145.4 4.2 %collective-permute-start.14 = (f32[112,128]{1,0:T(8,128)S(1)}, f32[112,128]{1,0:T(8,128)S(1)}, u32[]{:S(2)}, u32[]{:S(2)}) collective-permute-start(f32[112,128]{1,0:T(8,128)S(1)} %add.201), channel_id=1, source_target_pairs={{0,32},{16,48},{32,0},{48,16},{64,96},{80,112},{96,64},{112,80},{1... | collective-permute-start | bytes 172040 | tf_op jit(solution)/shard_map/ppermute | solution.py:169
  149.7 0.9 fusion.15
  150.6 2.0 %collective-permute-done.14 = f32[112,128]{1,0:T(8,128)S(1)} collective-permute-done((f32[112,128]{1,0:T(8,128)S(1)}, f32[112,128]{1,0:T(8,128)S(1)}, u32[]{:S(2)}, u32[]{:S(2)}) %collective-permute-start.14) | collective-permute-done | bytes 57376 | tf_op jit(solution)/shard_map/ppermute | solution.py:169
  152.6 8.2 %collective-permute-start.15 = (f32[112,128]{1,0:T(8,128)S(1)}, f32[112,128]{1,0:T(8,128)S(1)}, u32[]{:S(2)}, u32[]{:S(2)}) collective-permute-start(f32[112,128]{1,0:T(8,128)S(1)} %add.202), channel_id=1, source_target_pairs={{0,64},{16,80},{32,96},{48,112},{64,0},{80,16},{96,32},{112,48},{1... | collective-permute-start | bytes 172040 | tf_op jit(solution)/shard_map/ppermute | solution.py:169
  160.9 0.6 copy.280
  161.5 1.5 collective-permute-done.15
  163.0 23.4 %all-gather = bf16[1792,128]{1,0:T(8,128)(2,1)S(1)} all-gather(bf16[112,128]{1,0:T(8,128)(2,1)S(1)} %add_convert_fusion), channel_id=2, replica_groups=mesh['dp'=4,'tm'=8,'height'=16] {'height'}, dimensions={0}, use_global_device_ids=true | all-gather | bytes 487424 | tf_op jit(solution)/shard_map/all_gather | solution.py:224
  186.4 0.8 fusion.158
  (115 shorter events, 5.8 us)
Async XLA Ops:
  2.0 22.3 %collective-permute-start.1 = (bf16[2,1,128,128]{3,0,2,1:T(2,128)(2,1)S(1)}, bf16[2,1,128,128]{3,0,2,1:T(2,128)(2,1)S(1)}, u32[]{:S(2)}, u32[]{:S(2)}) collective-permute-start(bf16[2,1,128,128]{3,0,2,1:T(2,128)(2,1)S(1)} %get-tuple-element.34), channel_id=1, source_target_pairs={{1,0},{2,1},{3,2},{4,3},{5,4},{6,5},{7,6},{8,7},{9,8},{10,9},{11,1... | collective-permute-start | bytes 196616 | tf_op jit(solution)/shard_map/ppermute | solution.py:19
  7.2 17.1 %collective-permute-start = (bf16[2,1,128,128]{3,0,2,1:T(2,128)(2,1)S(1)}, bf16[2,1,128,128]{3,0,2,1:T(2,128)(2,1)S(1)}, u32[]{:S(2)}, u32[]{:S(2)}) collective-permute-start(bf16[2,1,128,128]{3,0,2,1:T(2,128)(2,1)S(1)} %get-tuple-element.33), channel_id=1, source_target_pairs={{0,1},{1,2},{2,3},{3,4},{4,5},{5,6},{6,7},{7,8},{8,9},{9,10},{10,1... | collective-permute-start | bytes 196616 | tf_op jit(solution)/shard_map/ppermute | solution.py:17
  9.9 13.0 %collective-permute-start.5 = (bf16[1,1,64,128]{3,2,1,0:T(8,128)(2,1)S(1)}, bf16[1,1,64,128]{3,2,1,0:T(8,128)(2,1)S(1)}, u32[]{:S(2)}, u32[]{:S(2)}) collective-permute-start(bf16[1,1,64,128]{3,2,1,0:T(8,128)(2,1)S(1)} %slice.186), channel_id=1, source_target_pairs={{1,0},{2,1},{3,2},{4,3},{5,4},{6,5},{7,6},{8,7},{9,8},{10,9},{11,1... | collective-permute-start | bytes 49160 | tf_op jit(solution)/shard_map/ppermute | solution.py:29
  22.9 7.7 %collective-permute-start.6 = (bf16[1,3,64,128]{3,2,1,0:T(8,128)(2,1)S(1)}, bf16[1,3,64,128]{3,2,1,0:T(8,128)(2,1)S(1)}, u32[]{:S(2)}, u32[]{:S(2)}) collective-permute-start(bf16[1,3,64,128]{3,2,1,0:T(8,128)(2,1)S(1)} %pad_maximum_fusion.8), channel_id=1, source_target_pairs={{16,0},{32,16},{48,32},{64,48},{80,64},{96,80},{112,96},{17,1},{33... | collective-permute-start | bytes 147464 | tf_op jit(solution)/shard_map/ppermute | solution.py:29
  24.8 7.1 %copy-start.4 = (bf16[3,3,3,128,128]{4,3,2,1,0:T(8,128)(2,1)S(1)}, bf16[3,3,3,128,128]{4,3,2,1,0:T(8,128)(2,1)}, u32[]{:S(2)}) copy-start(bf16[3,3,3,128,128]{4,3,2,1,0:T(8,128)(2,1)} %param.8) | copy-start | bytes 2654212
  24.8 7.1 %copy-start.7 = (pred[8,18]{0,1:T(8,128)(4,1)S(1)}, pred[8,18]{0,1:T(8,128)(4,1)}, u32[]{:S(2)}) copy-start(pred[8,18]{0,1:T(8,128)(4,1)} %constant.251) | copy-start | bytes 436
  24.9 12.1 %collective-permute-start.2 = (bf16[2,6,128,128]{3,0,2,1:T(2,128)(2,1)S(1)}, bf16[2,6,128,128]{3,0,2,1:T(2,128)(2,1)S(1)}, u32[]{:S(2)}, u32[]{:S(2)}) collective-permute-start(bf16[2,6,128,128]{3,0,2,1:T(2,128)(2,1)S(1)} %pad_maximum_fusion.5), channel_id=1, source_target_pairs={{0,16},{16,32},{32,48},{48,64},{64,80},{80,96},{96,112},{1,17},{17... | collective-permute-start | bytes 1179656 | tf_op jit(solution)/shard_map/ppermute | solution.py:29
  37.4 1.6 copy-start.3
  37.4 1.6 copy-start.6
  42.1 9.8 %collective-permute-start.3 = (bf16[2,1,128,128]{3,0,2,1:T(2,128)(2,1)S(1)}, bf16[2,1,128,128]{3,0,2,1:T(2,128)(2,1)S(1)}, u32[]{:S(2)}, u32[]{:S(2)}) collective-permute-start(bf16[2,1,128,128]{3,0,2,1:T(2,128)(2,1)S(1)} %bitcast.297), channel_id=1, source_target_pairs={{0,1},{1,2},{2,3},{3,4},{4,5},{5,6},{6,7},{7,8},{8,9},{9,10},{10,1... | collective-permute-start | bytes 196616 | tf_op jit(solution)/shard_map/ppermute | solution.py:29
  52.3 9.5 %collective-permute-start.4 = (bf16[2,5,128,128]{3,0,2,1:T(2,128)(2,1)S(1)}, bf16[2,5,128,128]{3,0,2,1:T(2,128)(2,1)S(1)}, u32[]{:S(2)}, u32[]{:S(2)}) collective-permute-start(bf16[2,5,128,128]{3,0,2,1:T(2,128)(2,1)S(1)} %pad_maximum_fusion.6), channel_id=1, source_target_pairs={{0,16},{16,32},{32,48},{48,64},{64,80},{80,96},{96,112},{1,17},{17... | collective-permute-start | bytes 983048 | tf_op jit(solution)/shard_map/ppermute | solution.py:29
  57.2 0.9 copy-start
  62.3 0.8 copy-start.2
  66.2 5.8 %collective-permute-start.7 = (f32[2,2,2,2,2,112,128]{6,5,4,3,2,1,0:T(8,128)S(1)}, f32[2,2,2,2,2,112,128]{6,5,4,3,2,1,0:T(8,128)}, u32[]{:S(2)}, u32[]{:S(2)}) collective-permute-start(f32[2,2,2,2,2,112,128]{6,5,4,3,2,1,0:T(8,128)S(1)} %bitcast.273), channel_id=1, source_target_pairs={{0,128},{128,0},{256,384},{384,256},{1,129},{129,1},{257,385},{385... | collective-permute-start | bytes 5505032 | tf_op jit(solution)/shard_map/ppermute | solution.py:169
  74.4 15.4 %collective-permute-start.8 = (f32[2,2,2,2,112,128]{5,4,3,2,1,0:T(8,128)S(1)}, f32[2,2,2,2,112,128]{5,4,3,2,1,0:T(8,128)}, u32[]{:S(2)}, u32[]{:S(2)}) collective-permute-start(f32[2,2,2,2,112,128]{5,4,3,2,1,0:T(8,128)S(1)} %bitcast_select_fusion), channel_id=1, source_target_pairs={{0,1},{1,0},{2,3},{3,2},{4,5},{5,4},{6,7},{7,6},{8,9},{9,8},{10,11... | collective-permute-start | bytes 2752520 | tf_op jit(solution)/shard_map/ppermute | solution.py:178
  91.2 10.4 %collective-permute-start.9 = (f32[2,2,2,112,128]{4,3,2,1,0:T(8,128)S(1)}, f32[2,2,2,112,128]{4,3,2,1,0:T(8,128)S(1)}, u32[]{:S(2)}, u32[]{:S(2)}) collective-permute-start(f32[2,2,2,112,128]{4,3,2,1,0:T(8,128)S(1)} %bitcast_select_fusion.2), channel_id=1, source_target_pairs={{0,4},{1,5},{2,6},{3,7},{4,0},{5,1},{6,2},{7,3},{8,12},{9,13},{10,... | collective-permute-start | bytes 1376264 | tf_op jit(solution)/shard_map/ppermute | solution.py:178
  93.9 20.5 %copy-start.1 = (bf16[1,5,128,128]{3,0,2,1:T(2,128)(2,1)S(1)}, bf16[1,5,128,128]{3,0,2,1:T(2,128)(2,1)}, u32[]{:S(2)}) copy-start(bf16[1,5,128,128]{3,0,2,1:T(2,128)(2,1)} %copy-done) | copy-start | bytes 491524
  101.7 33.2 %copy-start.5 = (bf16[3,3,3,128,128]{4,3,2,1,0:T(8,128)(2,1)S(1)}, bf16[3,3,3,128,128]{4,3,2,1,0:T(8,128)(2,1)}, u32[]{:S(2)}) copy-start(bf16[3,3,3,128,128]{4,3,2,1,0:T(8,128)(2,1)} %param.8) | copy-start | bytes 2654212
  101.7 33.2 %copy-start.8 = (pred[8,9]{0,1:T(8,128)(4,1)S(1)}, pred[8,9]{0,1:T(8,128)(4,1)}, u32[]{:S(2)}) copy-start(pred[8,9]{0,1:T(8,128)(4,1)} %constant.245) | copy-start | bytes 220
  101.7 9.6 %collective-permute-start.10 = (f32[2,2,112,128]{3,2,1,0:T(8,128)S(1)}, f32[2,2,112,128]{3,2,1,0:T(8,128)S(1)}, u32[]{:S(2)}, u32[]{:S(2)}) collective-permute-start(f32[2,2,112,128]{3,2,1,0:T(8,128)S(1)} %bitcast_select_fusion.4), channel_id=1, source_target_pairs={{0,2},{1,3},{2,0},{3,1},{4,6},{5,7},{6,4},{7,5},{8,10},{9,11},{10,... | collective-permute-start | bytes 688136 | tf_op jit(solution)/shard_map/ppermute | solution.py:178
  111.3 8.2 %collective-permute-start.11 = (f32[2,112,128]{2,1,0:T(8,128)S(1)}, f32[2,112,128]{2,1,0:T(8,128)S(1)}, u32[]{:S(2)}, u32[]{:S(2)}) collective-permute-start(f32[2,112,128]{2,1,0:T(8,128)S(1)} %select_bitcast_fusion), channel_id=1, source_target_pairs={{0,8},{1,9},{2,10},{3,11},{4,12},{5,13},{6,14},{7,15},{8,0},{9,1},... | collective-permute-start | bytes 344072 | tf_op jit(solution)/shard_map/ppermute | solution.py:178
  119.5 19.2 %collective-permute-start.12 = (f32[112,128]{1,0:T(8,128)S(1)}, f32[112,128]{1,0:T(8,128)S(1)}, u32[]{:S(2)}, u32[]{:S(2)}) collective-permute-start(f32[112,128]{1,0:T(8,128)S(1)} %dynamic-slice_bitcast_fusion), channel_id=1, source_target_pairs={{0,256},{128,384},{256,0},{384,128},{1,257},{129,385},{257,1},{385... | collective-permute-start | bytes 172040 | tf_op jit(solution)/shard_map/ppermute | solution.py:169
  138.7 6.7 %collective-permute-start.13 = (f32[112,128]{1,0:T(8,128)S(1)}, f32[112,128]{1,0:T(8,128)S(1)}, u32[]{:S(2)}, u32[]{:S(2)}) collective-permute-start(f32[112,128]{1,0:T(8,128)S(1)} %bitcast_add_fusion.1), channel_id=1, source_target_pairs={{0,16},{16,0},{32,48},{48,32},{64,80},{80,64},{96,112},{112,96},{1... | collective-permute-start | bytes 172040 | tf_op jit(solution)/shard_map/ppermute | solution.py:169
  145.4 7.2 %collective-permute-start.14 = (f32[112,128]{1,0:T(8,128)S(1)}, f32[112,128]{1,0:T(8,128)S(1)}, u32[]{:S(2)}, u32[]{:S(2)}) collective-permute-start(f32[112,128]{1,0:T(8,128)S(1)} %add.201), channel_id=1, source_target_pairs={{0,32},{16,48},{32,0},{48,16},{64,96},{80,112},{96,64},{112,80},{1... | collective-permute-start | bytes 172040 | tf_op jit(solution)/shard_map/ppermute | solution.py:169
  152.6 10.4 %collective-permute-start.15 = (f32[112,128]{1,0:T(8,128)S(1)}, f32[112,128]{1,0:T(8,128)S(1)}, u32[]{:S(2)}, u32[]{:S(2)}) collective-permute-start(f32[112,128]{1,0:T(8,128)S(1)} %add.202), channel_id=1, source_target_pairs={{0,64},{16,80},{32,96},{48,112},{64,0},{80,16},{96,32},{112,48},{1... | collective-permute-start | bytes 172040 | tf_op jit(solution)/shard_map/ppermute | solution.py:169

commit v4 on v3

--- a/solution.py
+++ b/solution.py
@@ -214,13 +214,18 @@
         mine = jnp.where(core == 0, parts[0][0], parts[1][0])
         other = jnp.where(core == 0, parts[0][1], parts[1][1])
         blocks = mine + swap_rows(other, bits)
-    far = dp_bits[-1]
+    for bit in frame_bits:
+        blocks = blocks + swap(blocks, "tm", bit)
+    far, top = dp_bits[-1], frame_bits[-1]
+    frames = lax.axis_size("tm")
     high = (lax.axis_index("dp") // far) % 2
     mine, other, _ = split_bit(blocks, held[0], ("dp", far), high)
-    blocks = mine + swap(other, "dp", far)
-    for bit in frame_bits:
-        blocks = blocks + swap(blocks, "tm", bit)
-    piece = blocks.astype(jnp.bfloat16)
+    pairs = [
+        (group * frames + t, (group ^ far) * frames + (t ^ top))
+        for group in range(lax.axis_size("dp"))
+        for t in range(frames)
+    ]
+    piece = (mine + lax.ppermute(other, ("dp", "tm"), pairs)).astype(jnp.bfloat16)
     return lax.all_gather(piece, "height", axis=0, tiled=False)
 
 

time: 190 us -> 194 us (1.021)
  starting transfers between devices: 69.5 us -> 75.6 us
    ppermute x0 -> x1, starting transfers between devices: none -> 12.8 us  [reduce_gradients(): lax.ppermute(other, ('dp', 'tm'), pairs)]
    ppermute x5 -> x4, starting transfers between devices: 32.4 us -> 25.7 us  [swap(): lax.ppermute(value, axis, [(i, i ^ bit) for i in range(lax.axis_size(axis...]
    ppermute x5 -> x4, waiting for transfers between devices: 12.9 us -> 10.3 us  [swap(): lax.ppermute(value, axis, [(i, i ^ bit) for i in range(lax.axis_size(axis...]
where the time goes in v4:
time: 194 us; the launch traced here: 192 us
  starting transfers between devices  75.6 us (39%)
  waiting for transfers between devices  50.6 us (26%)
  blocking collectives  23.4 us (12%)
  matrix products  14.7 us (8%)
  other arithmetic  14.4 us (7%)
  local copies, waits for them, and re-layouts  9.65 us (5%)
  between operations  3.83 us (2%)
    ppermute x4, waiting for transfers between devices, swap_rows(): return lax.ppermute(value, ('dp', 'height'), pairs)  31.7 us
    ppermute x4, starting transfers between devices, swap(): lax.ppermute(value, axis, [(i, i ^ bit) for i in range(lax.axis_size(axis...  25.7 us
    all_gather x1, blocking collectives, reduce_gradients(): return lax.all_gather(piece, 'height', axis=0, tiled=False)  23.4 us
    ppermute x5, starting transfers between devices, shifted(): lax.ppermute(value, axis, [(source, source + steps) for source in range(l...  18.5 us
    ppermute x1, starting transfers between devices, reduce_gradients(): lax.ppermute(other, ('dp', 'tm'), pairs)  12.8 us
    ppermute x4, starting transfers between devices, swap_rows(): return lax.ppermute(value, ('dp', 'height'), pairs)  11.5 us
    ppermute x4, waiting for transfers between devices, swap(): lax.ppermute(value, axis, [(i, i ^ bit) for i in range(lax.axis_size(axis...  10.3 us
    conv_general_dilated x6, matrix products, weight_grad(): lax.conv_general_dilated(frame_slab, masked, (1, 1), ((0, 0), pad_cols),...  8.4 us
  transfers between devices with their start and end apart: 16, of which 11 were waited for; matrix products, arithmetic and copies ran while one was open for 12% of the time, Pallas kernels for 0%

profile of v4, /device:TPU:6, one launch (start us, length us, event | category | flops | bytes accessed | tf_op | source)
XLA Modules:
  0.0 192.3 jit_solution(15325504284282797682)
XLA Ops:
  0.6 1.2 copy.332
  2.0 5.2 %collective-permute-start.1 = (bf16[2,1,128,128]{3,0,2,1:T(2,128)(2,1)S(1)}, bf16[2,1,128,128]{3,0,2,1:T(2,128)(2,1)S(1)}, u32[]{:S(2)}, u32[]{:S(2)}) collective-permute-start(bf16[2,1,128,128]{3,0,2,1:T(2,128)(2,1)S(1)} %get-tuple-element.34), channel_id=1, source_target_pairs={{1,0},{2,1},{3,2},{4,3},{5,4},{6,5},{7,6},{8,7},{9,8},{10,9},{11,1... | collective-permute-start | bytes 196616 | tf_op jit(solution)/shard_map/ppermute | solution.py:19
  7.2 1.9 collective-permute-start
  9.1 0.8 fusion.119
  9.9 6.0 %collective-permute-start.5 = (bf16[1,1,64,128]{3,2,1,0:T(8,128)(2,1)S(1)}, bf16[1,1,64,128]{3,2,1,0:T(8,128)(2,1)S(1)}, u32[]{:S(2)}, u32[]{:S(2)}) collective-permute-start(bf16[1,1,64,128]{3,2,1,0:T(8,128)(2,1)S(1)} %slice.186), channel_id=1, source_target_pairs={{1,0},{2,1},{3,2},{4,3},{5,4},{6,5},{7,6},{8,7},{9,8},{10,9},{11,1... | collective-permute-start | bytes 49160 | tf_op jit(solution)/shard_map/ppermute | solution.py:29
  15.9 0.8 reduce-window_clone.1
  16.7 0.7 subtract_bitcast_fusion
  17.7 0.6 fusion.162
  20.3 1.4 broadcast_multiply_fusion.5
  21.7 0.6 slice.191
  22.2 0.7 slice.195
  22.9 1.3 collective-permute-start.6
  24.2 0.6 pad_maximum_fusion.5
  24.9 4.7 %collective-permute-start.2 = (bf16[2,6,128,128]{3,0,2,1:T(2,128)(2,1)S(1)}, bf16[2,6,128,128]{3,0,2,1:T(2,128)(2,1)S(1)}, u32[]{:S(2)}, u32[]{:S(2)}) collective-permute-start(bf16[2,6,128,128]{3,0,2,1:T(2,128)(2,1)S(1)} %pad_maximum_fusion.5), channel_id=1, source_target_pairs={{0,16},{16,32},{32,48},{48,64},{64,80},{80,96},{96,112},{1,17},{17... | collective-permute-start | bytes 1179656 | tf_op jit(solution)/shard_map/ppermute | solution.py:29
  29.6 0.6 fusion.169
  30.6 1.2 multiply_bitcast_fusion.1
  32.0 0.3 fusion.9
  32.7 0.3 convolution_select_fusion.5
  33.1 0.3 fusion.8
  33.5 3.4 %collective-permute-done.2 = bf16[2,6,128,128]{3,0,2,1:T(2,128)(2,1)S(1)} collective-permute-done((bf16[2,6,128,128]{3,0,2,1:T(2,128)(2,1)S(1)}, bf16[2,6,128,128]{3,0,2,1:T(2,128)(2,1)S(1)}, u32[]{:S(2)}, u32[]{:S(2)}) %collective-permute-start.2) | collective-permute-done | bytes 393248 | tf_op jit(solution)/shard_map/ppermute | solution.py:29
  37.4 1.0 pad_maximum_fusion.2
  38.4 0.3 pad.11
  39.0 0.8 fusion.6
  40.0 0.8 fusion.5
  41.0 1.0 add_divide_fusion
  42.1 2.1 %collective-permute-start.3 = (bf16[2,1,128,128]{3,0,2,1:T(2,128)(2,1)S(1)}, bf16[2,1,128,128]{3,0,2,1:T(2,128)(2,1)S(1)}, u32[]{:S(2)}, u32[]{:S(2)}) collective-permute-start(bf16[2,1,128,128]{3,0,2,1:T(2,128)(2,1)S(1)} %bitcast.299), channel_id=1, source_target_pairs={{0,1},{1,2},{2,3},{3,4},{4,5},{5,6},{6,7},{7,8},{8,9},{9,10},{10,1... | collective-permute-start | bytes 196616 | tf_op jit(solution)/shard_map/ppermute | solution.py:29
  45.0 2.0 %convolution_bitcast_fusion.3 = f32[1,3,3,128,128]{4,3,2,1,0:T(8,128)S(1)} fusion(bf16[2,6,128,128]{3,0,2,1:T(2,128)(2,1)S(1)} %pad_maximum_fusion.5, bf16[2,4,128,128]{3,2,1,0:T(8,128)(2,1)S(1)} %get-tuple-element.32), kind=kOutput, calls=%fused_computation.13 | convolution fusion | flops 300417024 | bytes 1245184 | tf_op jit(solution)/shard_map/conv_general_dilated | solution.py:56
  47.0 2.0 %convolution_bitcast_fusion.4 = f32[1,3,3,128,128]{4,3,2,1,0:T(8,128)S(1)} fusion(bf16[2,6,128,128]{3,0,2,1:T(2,128)(2,1)S(1)} %pad_maximum_fusion.2, bf16[2,4,128,128]{3,2,1,0:T(8,128)(2,1)S(1)} %get-tuple-element.31), kind=kOutput, calls=%fused_computation.14 | convolution fusion | flops 300417024 | bytes 1245184 | tf_op jit(solution)/shard_map/conv_general_dilated | solution.py:56
  48.9 2.0 %convolution_bitcast_fusion.5 = f32[1,3,3,128,128]{4,3,2,1,0:T(8,128)S(1)} fusion(bf16[2,6,128,128]{3,0,2,1:T(2,128)(2,1)S(1)} %collective-permute-done.2, bf16[2,4,128,128]{3,2,1,0:T(8,128)(2,1)S(1)} %get-tuple-element.20), kind=kOutput, calls=%fused_computation.15 | convolution fusion | flops 300417024 | bytes 1245184 | tf_op jit(solution)/shard_map/conv_general_dilated | solution.py:56
  51.9 0.4 pad_maximum_fusion.6
  52.3 4.4 %collective-permute-start.4 = (bf16[2,5,128,128]{3,0,2,1:T(2,128)(2,1)S(1)}, bf16[2,5,128,128]{3,0,2,1:T(2,128)(2,1)S(1)}, u32[]{:S(2)}, u32[]{:S(2)}) collective-permute-start(bf16[2,5,128,128]{3,0,2,1:T(2,128)(2,1)S(1)} %pad_maximum_fusion.6), channel_id=1, source_target_pairs={{0,16},{16,32},{32,48},{48,64},{64,80},{80,96},{96,112},{1,17},{17... | collective-permute-start | bytes 983048 | tf_op jit(solution)/shard_map/ppermute | solution.py:29
  56.7 0.4 slice_maximum_fusion
  57.2 0.9 convolution_bitcast_fusion
  58.1 3.7 %collective-permute-done.4 = bf16[2,5,128,128]{3,0,2,1:T(2,128)(2,1)S(1)} collective-permute-done((bf16[2,5,128,128]{3,0,2,1:T(2,128)(2,1)S(1)}, bf16[2,5,128,128]{3,0,2,1:T(2,128)(2,1)S(1)}, u32[]{:S(2)}, u32[]{:S(2)}) %collective-permute-start.4) | collective-permute-done | bytes 327712 | tf_op jit(solution)/shard_map/ppermute | solution.py:29
  61.8 0.5 fusion.160
  62.3 0.8 convolution_bitcast_fusion.1
  63.2 0.8 convolution_bitcast_fusion.2
  64.5 1.5 fusion.1
  66.2 1.9 collective-permute-start.7
  68.1 3.8 %collective-permute-done.7 = f32[2,2,2,2,2,112,128]{6,5,4,3,2,1,0:T(8,128)} collective-permute-done((f32[2,2,2,2,2,112,128]{6,5,4,3,2,1,0:T(8,128)S(1)}, f32[2,2,2,2,2,112,128]{6,5,4,3,2,1,0:T(8,128)}, u32[]{:S(2)}, u32[]{:S(2)}) %collective-permute-start.7) | collective-permute-done | bytes 1835040 | tf_op jit(solution)/shard_map/ppermute | solution.py:169
  72.0 2.3 %bitcast_add_fusion = f32[2,2,2,2,2,112,128]{6,5,4,3,2,1,0:T(8,128)S(1)} fusion(f32[2,2,2,2,2,112,128]{6,5,4,3,2,1,0:T(8,128)} %collective-permute-done.7, f32[2,1,2,2,2,2,112,128]{7,6,5,4,3,1,0,2:T(8,128)} %get-tuple-element.22), kind=kLoop, calls=%fused_computation.6 | loop fusion | flops 458752 | bytes 5505024 | tf_op jit(solution)/shard_map/add | solution.py:201
  74.4 1.9 collective-permute-start.8
  76.3 13.4 %collective-permute-done.8 = f32[2,2,2,2,112,128]{5,4,3,2,1,0:T(8,128)} collective-permute-done((f32[2,2,2,2,112,128]{5,4,3,2,1,0:T(8,128)S(1)}, f32[2,2,2,2,112,128]{5,4,3,2,1,0:T(8,128)}, u32[]{:S(2)}, u32[]{:S(2)}) %collective-permute-start.8) | collective-permute-done | bytes 917536 | tf_op jit(solution)/shard_map/ppermute | solution.py:178
  89.8 1.3 fusion.19
  91.2 2.7 %collective-permute-start.9 = (f32[2,2,2,112,128]{4,3,2,1,0:T(8,128)S(1)}, f32[2,2,2,112,128]{4,3,2,1,0:T(8,128)S(1)}, u32[]{:S(2)}, u32[]{:S(2)}) collective-permute-start(f32[2,2,2,112,128]{4,3,2,1,0:T(8,128)S(1)} %bitcast_select_fusion.2), channel_id=1, source_target_pairs={{0,4},{1,5},{2,6},{3,7},{4,0},{5,1},{6,2},{7,3},{8,12},{9,13},{10,... | collective-permute-start | bytes 1376264 | tf_op jit(solution)/shard_map/ppermute | solution.py:178
  93.9 7.6 %collective-permute-done.9 = f32[2,2,2,112,128]{4,3,2,1,0:T(8,128)S(1)} collective-permute-done((f32[2,2,2,112,128]{4,3,2,1,0:T(8,128)S(1)}, f32[2,2,2,112,128]{4,3,2,1,0:T(8,128)S(1)}, u32[]{:S(2)}, u32[]{:S(2)}) %collective-permute-start.9) | collective-permute-done | bytes 458784 | tf_op jit(solution)/shard_map/ppermute | solution.py:178
  101.7 3.8 %collective-permute-start.10 = (f32[2,2,112,128]{3,2,1,0:T(8,128)S(1)}, f32[2,2,112,128]{3,2,1,0:T(8,128)S(1)}, u32[]{:S(2)}, u32[]{:S(2)}) collective-permute-start(f32[2,2,112,128]{3,2,1,0:T(8,128)S(1)} %bitcast_select_fusion.4), channel_id=1, source_target_pairs={{0,2},{1,3},{2,0},{3,1},{4,6},{5,7},{6,4},{7,5},{8,10},{9,11},{10,... | collective-permute-start | bytes 688136 | tf_op jit(solution)/shard_map/ppermute | solution.py:178
  105.6 5.7 %collective-permute-done.10 = f32[2,2,112,128]{3,2,1,0:T(8,128)S(1)} collective-permute-done((f32[2,2,112,128]{3,2,1,0:T(8,128)S(1)}, f32[2,2,112,128]{3,2,1,0:T(8,128)S(1)}, u32[]{:S(2)}, u32[]{:S(2)}) %collective-permute-start.10) | collective-permute-done | bytes 229408 | tf_op jit(solution)/shard_map/ppermute | solution.py:178
  111.3 3.0 %collective-permute-start.11 = (f32[2,112,128]{2,1,0:T(8,128)S(1)}, f32[2,112,128]{2,1,0:T(8,128)S(1)}, u32[]{:S(2)}, u32[]{:S(2)}) collective-permute-start(f32[2,112,128]{2,1,0:T(8,128)S(1)} %select_bitcast_fusion), channel_id=1, source_target_pairs={{0,8},{1,9},{2,10},{3,11},{4,12},{5,13},{6,14},{7,15},{8,0},{9,1},... | collective-permute-start | bytes 344072 | tf_op jit(solution)/shard_map/ppermute | solution.py:178
  114.6 4.9 %collective-permute-done.11 = f32[2,112,128]{2,1,0:T(8,128)S(1)} collective-permute-done((f32[2,112,128]{2,1,0:T(8,128)S(1)}, f32[2,112,128]{2,1,0:T(8,128)S(1)}, u32[]{:S(2)}, u32[]{:S(2)}) %collective-permute-start.11) | collective-permute-done | bytes 114720 | tf_op jit(solution)/shard_map/ppermute | solution.py:178
  119.5 4.4 %collective-permute-start.12 = (f32[2,112,128]{2,1,0:T(8,128)S(1)}, f32[2,112,128]{2,1,0:T(8,128)S(1)}, u32[]{:S(2)}, u32[]{:S(2)}) collective-permute-start(f32[2,112,128]{2,1,0:T(8,128)S(1)} %fusion.92), channel_id=1, source_target_pairs={{0,16},{16,0},{32,48},{48,32},{64,80},{80,64},{96,112},{112,96},{1... | collective-permute-start | bytes 344072 | tf_op jit(solution)/shard_map/ppermute | solution.py:169
  123.9 0.9 fusion.10
  125.1 1.6 collective-permute-done.12
  126.7 7.3 %collective-permute-start.13 = (f32[2,112,128]{2,1,0:T(8,128)S(1)}, f32[2,112,128]{2,1,0:T(8,128)S(1)}, u32[]{:S(2)}, u32[]{:S(2)}) collective-permute-start(f32[2,112,128]{2,1,0:T(8,128)S(1)} %add.197), channel_id=1, source_target_pairs={{0,32},{16,48},{32,0},{48,16},{64,96},{80,112},{96,64},{112,80},{1... | collective-permute-start | bytes 344072 | tf_op jit(solution)/shard_map/ppermute | solution.py:169
  134.0 0.9 fusion.11
  135.1 1.7 collective-permute-done.13
  136.8 12.1 %collective-permute-start.14 = (f32[2,112,128]{2,1,0:T(8,128)S(1)}, f32[2,112,128]{2,1,0:T(8,128)S(1)}, u32[]{:S(2)}, u32[]{:S(2)}) collective-permute-start(f32[2,112,128]{2,1,0:T(8,128)S(1)} %add.198), channel_id=1, source_target_pairs={{0,64},{16,80},{32,96},{48,112},{64,0},{80,16},{96,32},{112,48},{1... | collective-permute-start | bytes 344072 | tf_op jit(solution)/shard_map/ppermute | solution.py:169
  148.9 0.9 fusion.15
  149.8 3.2 %collective-permute-done.14 = f32[2,112,128]{2,1,0:T(8,128)S(1)} collective-permute-done((f32[2,112,128]{2,1,0:T(8,128)S(1)}, f32[2,112,128]{2,1,0:T(8,128)S(1)}, u32[]{:S(2)}, u32[]{:S(2)}) %collective-permute-start.14) | collective-permute-done | bytes 114720 | tf_op jit(solution)/shard_map/ppermute | solution.py:169
  153.1 12.8 %collective-permute-start.15 = (f32[112,128]{1,0:T(8,128)S(1)}, f32[112,128]{1,0:T(8,128)S(1)}, u32[]{:S(2)}, u32[]{:S(2)}) collective-permute-start(f32[112,128]{1,0:T(8,128)S(1)} %dynamic-slice_bitcast_fusion), channel_id=1, source_target_pairs={{0,320},{16,336},{32,352},{48,368},{64,256},{80,272},{96,288},{112... | collective-permute-start | bytes 172040 | tf_op jit(solution)/shard_map/ppermute | solution.py:228
  166.0 0.6 copy.280
  166.6 1.5 collective-permute-done.15
  168.1 23.4 %all-gather = bf16[1792,128]{1,0:T(8,128)(2,1)S(1)} all-gather(bf16[112,128]{1,0:T(8,128)(2,1)S(1)} %fusion.117), channel_id=2, replica_groups=mesh['dp'=4,'tm'=8,'height'=16] {'height'}, dimensions={0}, use_global_device_ids=true | all-gather | bytes 487424 | tf_op jit(solution)/shard_map/all_gather | solution.py:229
  191.5 0.8 fusion.159
  (115 shorter events, 5.8 us)
Async XLA Ops:
  2.0 22.3 %collective-permute-start.1 = (bf16[2,1,128,128]{3,0,2,1:T(2,128)(2,1)S(1)}, bf16[2,1,128,128]{3,0,2,1:T(2,128)(2,1)S(1)}, u32[]{:S(2)}, u32[]{:S(2)}) collective-permute-start(bf16[2,1,128,128]{3,0,2,1:T(2,128)(2,1)S(1)} %get-tuple-element.34), channel_id=1, source_target_pairs={{1,0},{2,1},{3,2},{4,3},{5,4},{6,5},{7,6},{8,7},{9,8},{10,9},{11,1... | collective-permute-start | bytes 196616 | tf_op jit(solution)/shard_map/ppermute | solution.py:19
  7.2 17.1 %collective-permute-start = (bf16[2,1,128,128]{3,0,2,1:T(2,128)(2,1)S(1)}, bf16[2,1,128,128]{3,0,2,1:T(2,128)(2,1)S(1)}, u32[]{:S(2)}, u32[]{:S(2)}) collective-permute-start(bf16[2,1,128,128]{3,0,2,1:T(2,128)(2,1)S(1)} %get-tuple-element.33), channel_id=1, source_target_pairs={{0,1},{1,2},{2,3},{3,4},{4,5},{5,6},{6,7},{7,8},{8,9},{9,10},{10,1... | collective-permute-start | bytes 196616 | tf_op jit(solution)/shard_map/ppermute | solution.py:17
  9.9 13.0 %collective-permute-start.5 = (bf16[1,1,64,128]{3,2,1,0:T(8,128)(2,1)S(1)}, bf16[1,1,64,128]{3,2,1,0:T(8,128)(2,1)S(1)}, u32[]{:S(2)}, u32[]{:S(2)}) collective-permute-start(bf16[1,1,64,128]{3,2,1,0:T(8,128)(2,1)S(1)} %slice.186), channel_id=1, source_target_pairs={{1,0},{2,1},{3,2},{4,3},{5,4},{6,5},{7,6},{8,7},{9,8},{10,9},{11,1... | collective-permute-start | bytes 49160 | tf_op jit(solution)/shard_map/ppermute | solution.py:29
  22.9 7.7 %collective-permute-start.6 = (bf16[1,3,64,128]{3,2,1,0:T(8,128)(2,1)S(1)}, bf16[1,3,64,128]{3,2,1,0:T(8,128)(2,1)S(1)}, u32[]{:S(2)}, u32[]{:S(2)}) collective-permute-start(bf16[1,3,64,128]{3,2,1,0:T(8,128)(2,1)S(1)} %pad_maximum_fusion.8), channel_id=1, source_target_pairs={{16,0},{32,16},{48,32},{64,48},{80,64},{96,80},{112,96},{17,1},{33... | collective-permute-start | bytes 147464 | tf_op jit(solution)/shard_map/ppermute | solution.py:29
  24.8 7.1 %copy-start.4 = (bf16[3,3,3,128,128]{4,3,2,1,0:T(8,128)(2,1)S(1)}, bf16[3,3,3,128,128]{4,3,2,1,0:T(8,128)(2,1)}, u32[]{:S(2)}) copy-start(bf16[3,3,3,128,128]{4,3,2,1,0:T(8,128)(2,1)} %param.8) | copy-start | bytes 2654212
  24.8 7.1 %copy-start.7 = (pred[8,18]{0,1:T(8,128)(4,1)S(1)}, pred[8,18]{0,1:T(8,128)(4,1)}, u32[]{:S(2)}) copy-start(pred[8,18]{0,1:T(8,128)(4,1)} %constant.251) | copy-start | bytes 436
  24.9 12.1 %collective-permute-start.2 = (bf16[2,6,128,128]{3,0,2,1:T(2,128)(2,1)S(1)}, bf16[2,6,128,128]{3,0,2,1:T(2,128)(2,1)S(1)}, u32[]{:S(2)}, u32[]{:S(2)}) collective-permute-start(bf16[2,6,128,128]{3,0,2,1:T(2,128)(2,1)S(1)} %pad_maximum_fusion.5), channel_id=1, source_target_pairs={{0,16},{16,32},{32,48},{48,64},{64,80},{80,96},{96,112},{1,17},{17... | collective-permute-start | bytes 1179656 | tf_op jit(solution)/shard_map/ppermute | solution.py:29
  37.4 1.6 copy-start.3
  37.4 1.6 copy-start.6
  42.1 9.8 %collective-permute-start.3 = (bf16[2,1,128,128]{3,0,2,1:T(2,128)(2,1)S(1)}, bf16[2,1,128,128]{3,0,2,1:T(2,128)(2,1)S(1)}, u32[]{:S(2)}, u32[]{:S(2)}) collective-permute-start(bf16[2,1,128,128]{3,0,2,1:T(2,128)(2,1)S(1)} %bitcast.299), channel_id=1, source_target_pairs={{0,1},{1,2},{2,3},{3,4},{4,5},{5,6},{6,7},{7,8},{8,9},{9,10},{10,1... | collective-permute-start | bytes 196616 | tf_op jit(solution)/shard_map/ppermute | solution.py:29
  52.3 9.5 %collective-permute-start.4 = (bf16[2,5,128,128]{3,0,2,1:T(2,128)(2,1)S(1)}, bf16[2,5,128,128]{3,0,2,1:T(2,128)(2,1)S(1)}, u32[]{:S(2)}, u32[]{:S(2)}) collective-permute-start(bf16[2,5,128,128]{3,0,2,1:T(2,128)(2,1)S(1)} %pad_maximum_fusion.6), channel_id=1, source_target_pairs={{0,16},{16,32},{32,48},{48,64},{64,80},{80,96},{96,112},{1,17},{17... | collective-permute-start | bytes 983048 | tf_op jit(solution)/shard_map/ppermute | solution.py:29
  57.2 0.9 copy-start
  62.3 0.8 copy-start.2
  66.2 5.8 %collective-permute-start.7 = (f32[2,2,2,2,2,112,128]{6,5,4,3,2,1,0:T(8,128)S(1)}, f32[2,2,2,2,2,112,128]{6,5,4,3,2,1,0:T(8,128)}, u32[]{:S(2)}, u32[]{:S(2)}) collective-permute-start(f32[2,2,2,2,2,112,128]{6,5,4,3,2,1,0:T(8,128)S(1)} %bitcast.275), channel_id=1, source_target_pairs={{0,128},{128,0},{256,384},{384,256},{1,129},{129,1},{257,385},{385... | collective-permute-start | bytes 5505032 | tf_op jit(solution)/shard_map/ppermute | solution.py:169
  74.4 15.4 %collective-permute-start.8 = (f32[2,2,2,2,112,128]{5,4,3,2,1,0:T(8,128)S(1)}, f32[2,2,2,2,112,128]{5,4,3,2,1,0:T(8,128)}, u32[]{:S(2)}, u32[]{:S(2)}) collective-permute-start(f32[2,2,2,2,112,128]{5,4,3,2,1,0:T(8,128)S(1)} %bitcast_select_fusion), channel_id=1, source_target_pairs={{0,1},{1,0},{2,3},{3,2},{4,5},{5,4},{6,7},{7,6},{8,9},{9,8},{10,11... | collective-permute-start | bytes 2752520 | tf_op jit(solution)/shard_map/ppermute | solution.py:178
  91.2 10.4 %collective-permute-start.9 = (f32[2,2,2,112,128]{4,3,2,1,0:T(8,128)S(1)}, f32[2,2,2,112,128]{4,3,2,1,0:T(8,128)S(1)}, u32[]{:S(2)}, u32[]{:S(2)}) collective-permute-start(f32[2,2,2,112,128]{4,3,2,1,0:T(8,128)S(1)} %bitcast_select_fusion.2), channel_id=1, source_target_pairs={{0,4},{1,5},{2,6},{3,7},{4,0},{5,1},{6,2},{7,3},{8,12},{9,13},{10,... | collective-permute-start | bytes 1376264 | tf_op jit(solution)/shard_map/ppermute | solution.py:178
  93.9 20.5 %copy-start.1 = (bf16[1,5,128,128]{3,0,2,1:T(2,128)(2,1)S(1)}, bf16[1,5,128,128]{3,0,2,1:T(2,128)(2,1)}, u32[]{:S(2)}) copy-start(bf16[1,5,128,128]{3,0,2,1:T(2,128)(2,1)} %copy-done) | copy-start | bytes 491524
  101.7 22.3 %copy-start.5 = (bf16[3,3,3,128,128]{4,3,2,1,0:T(8,128)(2,1)S(1)}, bf16[3,3,3,128,128]{4,3,2,1,0:T(8,128)(2,1)}, u32[]{:S(2)}) copy-start(bf16[3,3,3,128,128]{4,3,2,1,0:T(8,128)(2,1)} %param.8) | copy-start | bytes 2654212
  101.7 22.3 %copy-start.8 = (pred[8,9]{0,1:T(8,128)(4,1)S(1)}, pred[8,9]{0,1:T(8,128)(4,1)}, u32[]{:S(2)}) copy-start(pred[8,9]{0,1:T(8,128)(4,1)} %constant.245) | copy-start | bytes 220
  101.7 9.6 %collective-permute-start.10 = (f32[2,2,112,128]{3,2,1,0:T(8,128)S(1)}, f32[2,2,112,128]{3,2,1,0:T(8,128)S(1)}, u32[]{:S(2)}, u32[]{:S(2)}) collective-permute-start(f32[2,2,112,128]{3,2,1,0:T(8,128)S(1)} %bitcast_select_fusion.4), channel_id=1, source_target_pairs={{0,2},{1,3},{2,0},{3,1},{4,6},{5,7},{6,4},{7,5},{8,10},{9,11},{10,... | collective-permute-start | bytes 688136 | tf_op jit(solution)/shard_map/ppermute | solution.py:178
  111.3 8.2 %collective-permute-start.11 = (f32[2,112,128]{2,1,0:T(8,128)S(1)}, f32[2,112,128]{2,1,0:T(8,128)S(1)}, u32[]{:S(2)}, u32[]{:S(2)}) collective-permute-start(f32[2,112,128]{2,1,0:T(8,128)S(1)} %select_bitcast_fusion), channel_id=1, source_target_pairs={{0,8},{1,9},{2,10},{3,11},{4,12},{5,13},{6,14},{7,15},{8,0},{9,1},... | collective-permute-start | bytes 344072 | tf_op jit(solution)/shard_map/ppermute | solution.py:178
  119.5 7.2 %collective-permute-start.12 = (f32[2,112,128]{2,1,0:T(8,128)S(1)}, f32[2,112,128]{2,1,0:T(8,128)S(1)}, u32[]{:S(2)}, u32[]{:S(2)}) collective-permute-start(f32[2,112,128]{2,1,0:T(8,128)S(1)} %fusion.92), channel_id=1, source_target_pairs={{0,16},{16,0},{32,48},{48,32},{64,80},{80,64},{96,112},{112,96},{1... | collective-permute-start | bytes 344072 | tf_op jit(solution)/shard_map/ppermute | solution.py:169
  126.7 10.1 %collective-permute-start.13 = (f32[2,112,128]{2,1,0:T(8,128)S(1)}, f32[2,112,128]{2,1,0:T(8,128)S(1)}, u32[]{:S(2)}, u32[]{:S(2)}) collective-permute-start(f32[2,112,128]{2,1,0:T(8,128)S(1)} %add.197), channel_id=1, source_target_pairs={{0,32},{16,48},{32,0},{48,16},{64,96},{80,112},{96,64},{112,80},{1... | collective-permute-start | bytes 344072 | tf_op jit(solution)/shard_map/ppermute | solution.py:169
  136.8 16.3 %collective-permute-start.14 = (f32[2,112,128]{2,1,0:T(8,128)S(1)}, f32[2,112,128]{2,1,0:T(8,128)S(1)}, u32[]{:S(2)}, u32[]{:S(2)}) collective-permute-start(f32[2,112,128]{2,1,0:T(8,128)S(1)} %add.198), channel_id=1, source_target_pairs={{0,64},{16,80},{32,96},{48,112},{64,0},{80,16},{96,32},{112,48},{1... | collective-permute-start | bytes 344072 | tf_op jit(solution)/shard_map/ppermute | solution.py:169
  153.1 15.0 %collective-permute-start.15 = (f32[112,128]{1,0:T(8,128)S(1)}, f32[112,128]{1,0:T(8,128)S(1)}, u32[]{:S(2)}, u32[]{:S(2)}) collective-permute-start(f32[112,128]{1,0:T(8,128)S(1)} %dynamic-slice_bitcast_fusion), channel_id=1, source_target_pairs={{0,320},{16,336},{32,352},{48,368},{64,256},{80,272},{96,288},{112... | collective-permute-start | bytes 172040 | tf_op jit(solution)/shard_map/ppermute | solution.py:228

commit v5 on v3

--- a/solution.py
+++ b/solution.py
@@ -104,20 +104,28 @@
     down_frames = frames_dev // 2
     counts_row = frame_counts[0]
     first_frame = lax.axis_index("tm") * frames_dev
-    frame_index = first_frame + jnp.arange(frames_dev, dtype=jnp.int32)
-    first_mask = tap_masks(positions(counts_row, frame_index))
+    wide_index = first_frame - 2 + jnp.arange(frames_dev + 2, dtype=jnp.int32)
+    wide_mask = tap_masks(positions(counts_row, wide_index))
+    first_mask = wide_mask[2:]
     down_index = first_frame + 2 * jnp.arange(down_frames + 1, dtype=jnp.int32)
     mask_ext = tap_masks(positions(counts_row, down_index))
     down_mask = mask_ext[:down_frames]
-    with_rows = padded_2(clips[0], (("height", 1),), 1)
-    earlier = shifted(with_rows, "tm", 1)
-    input_ext = jnp.concatenate([earlier, with_rows], axis=0)
-    pre_act = conv_layer(input_ext, conv_first, first_mask, frames_dev, 1, (1, 1))
-    hidden = jax.nn.silu(pre_act).astype(jnp.bfloat16)
-    above = shifted(hidden[:, rows_dev - 1 :], "height", 1)
-    hidden_rows = jnp.concatenate([above, hidden], axis=1)
-    hidden_past = shifted(hidden_rows, "tm", 1)
-    hidden_ext = jnp.concatenate([hidden_past, hidden_rows], axis=0)
+    cells = clips[0]
+    above = shifted(cells[:, rows_dev - 2 :], "height", 1)
+    below = shifted(cells[:, :1], "height", -1)
+    with_rows = jnp.concatenate([above, cells, below], axis=1)
+    if frames_dev >= 4:
+        earlier = shifted(with_rows[frames_dev - 4 :], "tm", 1)
+    else:
+        earlier = jnp.concatenate([shifted(with_rows, "tm", 2), shifted(with_rows, "tm", 1)], axis=0)
+    wide_input = jnp.concatenate([earlier, with_rows], axis=0)
+    wide_pre = conv_layer(wide_input, conv_first, wide_mask, frames_dev + 2, 1, (1, 1))
+    row_valid = jnp.arange(rows_dev + 1) >= jnp.where(lax.axis_index("height") == 0, 1, 0)
+    hidden_ext = jnp.where(
+        row_valid[None, :, None, None], jax.nn.silu(wide_pre).astype(jnp.bfloat16), 0
+    ).astype(jnp.bfloat16)
+    pre_act = wide_pre[2:, 1:]
+    input_ext = wide_input[2:, 1:]
     encoded = conv_layer(hidden_ext, conv_down, down_mask, down_frames, 2, (1, 0)).astype(
         jnp.bfloat16
     )

time: 190 us -> 219 us (1.15)
  local copies, waits for them, and re-layouts: 9.65 us -> 20.8 us
  starting transfers between devices: 69.5 us -> 76.7 us
  matrix products: 14.7 us -> 20.2 us
  waiting for transfers between devices: 51.7 us -> 55.3 us
    ppermute x5, starting transfers between devices: 32.4 us -> 43 us  [swap(): lax.ppermute(value, axis, [(i, i ^ bit) for i in range(lax.axis_size(axis...]
    ppermute x2 -> x0, starting transfers between devices: 7.11 us -> none  [the longest x1 5.19 us: padded_2(): lax.ppermute(head, axis, [((i + 1) % count, i) for i in range(ends)])]
    ppermute x5 -> x6, starting transfers between devices: 18.5 us -> 24.2 us  [shifted(): lax.ppermute(value, axis, [(source, source + steps) for source in range(l...]
    ppermute x5 -> x6, waiting for transfers between devices: 7.16 us -> 12.3 us  [shifted(): lax.ppermute(value, axis, [(source, source + steps) for source in range(l...]
    mul x4 -> x7, local copies, waits for them, and re-layouts: 0.42 us -> 4.75 us  [conv_layer(): tap_term = tap_term * tap_mask[:, tap_time][:, None, None, None]]
    conv_general_dilated x6, matrix products: 5.32 us -> 9.21 us  [conv_layer(): lax.conv_general_dilated(frame_slab, weight[tap_time], (stride, stride),...]
    unnamed x28 -> x52, local copies, waits for them, and re-layouts: 2.45 us -> 5.99 us
    ppermute x5, waiting for transfers between devices: 12.9 us -> 9.34 us  [swap(): lax.ppermute(value, axis, [(i, i ^ bit) for i in range(lax.axis_size(axis...]
  transfers between devices with their start and end apart: 16 -> 15, of which waited for: 11 -> 11; matrix products, arithmetic and copies ran while one was open for 12% -> 9% of each run, Pallas kernels for 0% -> 0%
where the time goes in v5:
time: 219 us; the launch traced here: 216 us
  starting transfers between devices  76.7 us (35%)
  waiting for transfers between devices  55.3 us (25%)
  blocking collectives  23.8 us (11%)
  local copies, waits for them, and re-layouts  20.8 us (9%)
  matrix products  20.2 us (9%)
  other arithmetic  15.8 us (7%)
  between operations  3.81 us (2%)
    ppermute x5, starting transfers between devices, swap(): lax.ppermute(value, axis, [(i, i ^ bit) for i in range(lax.axis_size(axis...  43 us
    ppermute x4, waiting for transfers between devices, swap_rows(): return lax.ppermute(value, ('dp', 'height'), pairs)  33.7 us
    ppermute x6, starting transfers between devices, shifted(): lax.ppermute(value, axis, [(source, source + steps) for source in range(l...  24.2 us
    all_gather x1, blocking collectives, reduce_gradients(): return lax.all_gather(piece, 'height', axis=0, tiled=False)  23.8 us
    ppermute x6, waiting for transfers between devices, shifted(): lax.ppermute(value, axis, [(source, source + steps) for source in range(l...  12.3 us
    ppermute x4, starting transfers between devices, swap_rows(): return lax.ppermute(value, ('dp', 'height'), pairs)  9.44 us
    ppermute x5, waiting for transfers between devices, swap(): lax.ppermute(value, axis, [(i, i ^ bit) for i in range(lax.axis_size(axis...  9.34 us
    conv_general_dilated x6, matrix products, conv_layer(): lax.conv_general_dilated(frame_slab, weight[tap_time], (stride, stride),...  9.21 us
  transfers between devices with their start and end apart: 15, of which 11 were waited for; matrix products, arithmetic and copies ran while one was open for 9% of the time, Pallas kernels for 0%

profile of v5, /device:TPU:6, one launch (start us, length us, event | category | flops | bytes accessed | tf_op | source)
XLA Modules:
  0.0 216.5 jit_solution(16308253590546861382)
XLA Ops:
  0.6 1.2 copy.300
  1.9 5.2 %collective-permute-start.1 = (bf16[2,1,128,128]{3,0,2,1:T(2,128)(2,1)S(1)}, bf16[2,1,128,128]{3,0,2,1:T(2,128)(2,1)S(1)}, u32[]{:S(2)}, u32[]{:S(2)}) collective-permute-start(bf16[2,1,128,128]{3,0,2,1:T(2,128)(2,1)S(1)} %slice.198), channel_id=1, source_target_pairs={{1,0},{2,1},{3,2},{4,3},{5,4},{6,5},{7,6},{8,7},{9,8},{10,9},{11,1... | collective-permute-start | bytes 196616 | tf_op jit(solution)/shard_map/ppermute | solution.py:29
  7.2 1.9 collective-permute-start
  9.1 0.8 fusion.119
  9.9 6.0 %collective-permute-start.4 = (bf16[1,1,64,128]{3,2,1,0:T(8,128)(2,1)S(1)}, bf16[1,1,64,128]{3,2,1,0:T(8,128)(2,1)S(1)}, u32[]{:S(2)}, u32[]{:S(2)}) collective-permute-start(bf16[1,1,64,128]{3,2,1,0:T(8,128)(2,1)S(1)} %slice.210), channel_id=1, source_target_pairs={{1,0},{2,1},{3,2},{4,3},{5,4},{6,5},{7,6},{8,7},{9,8},{10,9},{11,1... | collective-permute-start | bytes 49160 | tf_op jit(solution)/shard_map/ppermute | solution.py:29
  16.0 0.8 reduce-window_clone.1
  16.8 0.7 subtract_bitcast_fusion
  18.0 0.6 fusion.158
  20.6 1.4 broadcast_multiply_fusion.5
  22.0 1.3 collective-permute-start.5
  23.5 1.4 reshape.200
  25.1 1.4 reshape.194
  26.7 1.4 reshape.188
  28.2 0.6 slice.215
  29.3 1.2 multiply_bitcast_fusion.1
  30.8 1.3 convolution_select_fusion.5
  32.7 0.7 pad_maximum_fusion.5
  33.4 4.6 %collective-permute-start.3 = (bf16[2,7,128,128]{3,0,2,1:T(2,128)(2,1)S(1)}, bf16[2,7,128,128]{3,0,2,1:T(2,128)(2,1)S(1)}, u32[]{:S(2)}, u32[]{:S(2)}) collective-permute-start(bf16[2,7,128,128]{3,0,2,1:T(2,128)(2,1)S(1)} %pad_maximum_fusion.5), channel_id=1, source_target_pairs={{0,16},{16,32},{32,48},{48,64},{64,80},{80,96},{96,112},{1,17},{17... | collective-permute-start | bytes 1376264 | tf_op jit(solution)/shard_map/ppermute | solution.py:29
  38.0 5.2 %collective-permute-start.2 = (bf16[2,7,128,128]{3,0,2,1:T(2,128)(2,1)S(1)}, bf16[2,7,128,128]{3,0,2,1:T(2,128)(2,1)S(1)}, u32[]{:S(2)}, u32[]{:S(2)}) collective-permute-start(bf16[2,7,128,128]{3,0,2,1:T(2,128)(2,1)S(1)} %pad_maximum_fusion.5), channel_id=1, source_target_pairs={{0,32},{16,48},{32,64},{48,80},{64,96},{80,112},{1,33},{17,49},{33... | collective-permute-start | bytes 1376264 | tf_op jit(solution)/shard_map/ppermute | solution.py:29
  43.7 0.7 copy_bitcast_fusion.7
  44.4 4.6 %collective-permute-done.3 = bf16[2,7,128,128]{3,0,2,1:T(2,128)(2,1)S(1)} collective-permute-done((bf16[2,7,128,128]{3,0,2,1:T(2,128)(2,1)S(1)}, bf16[2,7,128,128]{3,0,2,1:T(2,128)(2,1)S(1)}, u32[]{:S(2)}, u32[]{:S(2)}) %collective-permute-start.3) | collective-permute-done | bytes 458784 | tf_op jit(solution)/shard_map/ppermute | solution.py:29
  49.0 7.7 %collective-permute-done.2 = bf16[2,7,128,128]{3,0,2,1:T(2,128)(2,1)S(1)} collective-permute-done((bf16[2,7,128,128]{3,0,2,1:T(2,128)(2,1)S(1)}, bf16[2,7,128,128]{3,0,2,1:T(2,128)(2,1)S(1)}, u32[]{:S(2)}, u32[]{:S(2)}) %collective-permute-start.2) | collective-permute-done | bytes 458784 | tf_op jit(solution)/shard_map/ppermute | solution.py:29
  56.7 3.4 %maximum_bitcast_fusion = (bf16[7,4,128,128]{3,1,2,0:T(4,128)(2,1)S(1)}, bf16[7,4,128,128]{3,1,2,0:T(4,128)(2,1)S(1)}, bf16[4,7,128,128]{3,0,2,1:T(4,128)(2,1)S(1)}) fusion(bf16[2,7,128,128]{3,0,2,1:T(2,128)(2,1)S(1)} %collective-permute-done.3, bf16[2,7,128,128]{3,0,2,1:T(2,128)(2,1)S(1)} %collective-permute-done.2, ...), kind=kLoop, calls=%fused_computation.64 | loop fusion | flops 10092544 | bytes 4128768 | tf_op jit(solution)/shard_map/concatenate | solution.py:120
  62.3 0.9 copy-done.3
  63.5 2.0 fusion.5
  65.5 2.0 fusion.6
  67.5 2.5 %fusion.38 = (bf16[5,32,17,128]{3,1,2,0:T(8,128)(2,1)S(1)}, f32[5,32,17,128]{3,1,2,0:T(8,128)S(1)}) fusion(pred[5]{0:T(512)(128)(4,1)S(1)} %iota_compare_fusion.3, f32[5,32,17,128]{3,1,2,0:T(8,128)S(1)} %fusion.5, f32[5,32,17,128]{3,1,2,0:T(8,128)S(1)} %fusion.6, f32[5,32,17,128]{3,2,1,0:T(8,128)S(1)} %copy-done.2, ...), kind=kOutput, calls=%fused_computation.69 | convolution fusion | flops 808910848 | bytes 8228352 | tf_op jit(solution)/shard_map/conv_general_dilated | solution.py:36
  71.2 1.7 fusion.156
  72.9 0.8 copy.245
  74.0 0.7 copy-done.9
  75.1 2.3 %convolution_bitcast_fusion.3 = f32[1,3,3,128,128]{4,3,2,1,0:T(8,128)S(1)} fusion(bf16[2,7,128,128]{3,0,2,1:T(2,128)(2,1)S(1)} %copy-done.11, bf16[2,4,128,128]{3,2,1,0:T(8,128)(2,1)S(1)} %get-tuple-element.31), kind=kOutput, calls=%fused_computation.26 | convolution fusion | flops 300417024 | bytes 1310720 | tf_op jit(solution)/shard_map/conv_general_dilated | solution.py:56
  77.4 2.3 %convolution_bitcast_fusion.4 = f32[1,3,3,128,128]{4,3,2,1,0:T(8,128)S(1)} fusion(bf16[4,7,128,128]{3,0,2,1:T(4,128)(2,1)S(1)} %copy-done.1, bf16[2,4,128,128]{3,2,1,0:T(8,128)(2,1)S(1)} %get-tuple-element.30), kind=kOutput, calls=%fused_computation.27 | convolution fusion | flops 300417024 | bytes 1245184 | tf_op jit(solution)/shard_map/conv_general_dilated | solution.py:56
  79.7 2.1 convolution_bitcast_fusion.5
  82.1 0.8 copy-done.6
  82.9 0.8 convolution_bitcast_fusion
  83.9 0.8 convolution_bitcast_fusion.1
  84.9 0.8 convolution_bitcast_fusion.2
  86.3 1.5 fusion.4
  88.0 1.9 collective-permute-start.6
  90.0 3.8 %collective-permute-done.6 = f32[2,2,2,2,2,112,128]{6,5,4,3,2,1,0:T(8,128)} collective-permute-done((f32[2,2,2,2,2,112,128]{6,5,4,3,2,1,0:T(8,128)S(1)}, f32[2,2,2,2,2,112,128]{6,5,4,3,2,1,0:T(8,128)}, u32[]{:S(2)}, u32[]{:S(2)}) %collective-permute-start.6) | collective-permute-done | bytes 1835040 | tf_op jit(solution)/shard_map/ppermute | solution.py:177
  93.8 2.3 %bitcast_add_fusion = f32[2,2,2,2,2,112,128]{6,5,4,3,2,1,0:T(8,128)S(1)} fusion(f32[2,2,2,2,2,112,128]{6,5,4,3,2,1,0:T(8,128)} %collective-permute-done.6, f32[2,1,2,2,2,2,112,128]{7,6,5,4,3,1,0,2:T(8,128)} %get-tuple-element.20), kind=kLoop, calls=%fused_computation.10 | loop fusion | flops 458752 | bytes 5505024 | tf_op jit(solution)/shard_map/add | solution.py:209
  96.2 1.9 collective-permute-start.7
  98.2 13.4 %collective-permute-done.7 = f32[2,2,2,2,112,128]{5,4,3,2,1,0:T(8,128)} collective-permute-done((f32[2,2,2,2,112,128]{5,4,3,2,1,0:T(8,128)S(1)}, f32[2,2,2,2,112,128]{5,4,3,2,1,0:T(8,128)}, u32[]{:S(2)}, u32[]{:S(2)}) %collective-permute-start.7) | collective-permute-done | bytes 917536 | tf_op jit(solution)/shard_map/ppermute | solution.py:186
  111.6 1.3 fusion.37
  113.0 2.4 %collective-permute-start.8 = (f32[2,2,2,112,128]{4,3,2,1,0:T(8,128)S(1)}, f32[2,2,2,112,128]{4,3,2,1,0:T(8,128)S(1)}, u32[]{:S(2)}, u32[]{:S(2)}) collective-permute-start(f32[2,2,2,112,128]{4,3,2,1,0:T(8,128)S(1)} %bitcast_select_fusion.2), channel_id=1, source_target_pairs={{0,4},{1,5},{2,6},{3,7},{4,0},{5,1},{6,2},{7,3},{8,12},{9,13},{10,... | collective-permute-start | bytes 1376264 | tf_op jit(solution)/shard_map/ppermute | solution.py:186
  115.5 7.8 %collective-permute-done.8 = f32[2,2,2,112,128]{4,3,2,1,0:T(8,128)S(1)} collective-permute-done((f32[2,2,2,112,128]{4,3,2,1,0:T(8,128)S(1)}, f32[2,2,2,112,128]{4,3,2,1,0:T(8,128)S(1)}, u32[]{:S(2)}, u32[]{:S(2)}) %collective-permute-start.8) | collective-permute-done | bytes 458784 | tf_op jit(solution)/shard_map/ppermute | solution.py:186
  123.5 1.9 collective-permute-start.9
  125.5 7.4 %collective-permute-done.9 = f32[2,2,112,128]{3,2,1,0:T(8,128)S(1)} collective-permute-done((f32[2,2,112,128]{3,2,1,0:T(8,128)S(1)}, f32[2,2,112,128]{3,2,1,0:T(8,128)S(1)}, u32[]{:S(2)}, u32[]{:S(2)}) %collective-permute-start.9) | collective-permute-done | bytes 229408 | tf_op jit(solution)/shard_map/ppermute | solution.py:186
  133.0 3.2 %collective-permute-start.10 = (f32[2,112,128]{2,1,0:T(8,128)S(1)}, f32[2,112,128]{2,1,0:T(8,128)S(1)}, u32[]{:S(2)}, u32[]{:S(2)}) collective-permute-start(f32[2,112,128]{2,1,0:T(8,128)S(1)} %select_bitcast_fusion), channel_id=1, source_target_pairs={{0,8},{1,9},{2,10},{3,11},{4,12},{5,13},{6,14},{7,15},{8,0},{9,1},... | collective-permute-start | bytes 344072 | tf_op jit(solution)/shard_map/ppermute | solution.py:186
  136.4 4.9 %collective-permute-done.10 = f32[2,112,128]{2,1,0:T(8,128)S(1)} collective-permute-done((f32[2,112,128]{2,1,0:T(8,128)S(1)}, f32[2,112,128]{2,1,0:T(8,128)S(1)}, u32[]{:S(2)}, u32[]{:S(2)}) %collective-permute-start.10) | collective-permute-done | bytes 114720 | tf_op jit(solution)/shard_map/ppermute | solution.py:186
  141.4 15.5 %collective-permute-start.11 = (f32[112,128]{1,0:T(8,128)S(1)}, f32[112,128]{1,0:T(8,128)S(1)}, u32[]{:S(2)}, u32[]{:S(2)}) collective-permute-start(f32[112,128]{1,0:T(8,128)S(1)} %dynamic-slice_bitcast_fusion), channel_id=1, source_target_pairs={{0,256},{128,384},{256,0},{384,128},{1,257},{129,385},{257,1},{385... | collective-permute-start | bytes 172040 | tf_op jit(solution)/shard_map/ppermute | solution.py:177
  156.9 0.9 fusion.11
  158.0 1.0 collective-permute-done.11
  159.1 12.9 %collective-permute-start.12 = (f32[112,128]{1,0:T(8,128)S(1)}, f32[112,128]{1,0:T(8,128)S(1)}, u32[]{:S(2)}, u32[]{:S(2)}) collective-permute-start(f32[112,128]{1,0:T(8,128)S(1)} %bitcast_add_fusion.1), channel_id=1, source_target_pairs={{0,16},{16,0},{32,48},{48,32},{64,80},{80,64},{96,112},{112,96},{1... | collective-permute-start | bytes 172040 | tf_op jit(solution)/shard_map/ppermute | solution.py:177
  172.0 0.9 fusion.12
  173.1 1.6 collective-permute-done.12
  174.7 5.0 %collective-permute-start.13 = (f32[112,128]{1,0:T(8,128)S(1)}, f32[112,128]{1,0:T(8,128)S(1)}, u32[]{:S(2)}, u32[]{:S(2)}) collective-permute-start(f32[112,128]{1,0:T(8,128)S(1)} %add.208), channel_id=1, source_target_pairs={{0,32},{16,48},{32,0},{48,16},{64,96},{80,112},{96,64},{112,80},{1... | collective-permute-start | bytes 172040 | tf_op jit(solution)/shard_map/ppermute | solution.py:177
  179.8 0.9 fusion.16
  180.7 1.2 collective-permute-done.13
  181.9 7.7 %collective-permute-start.14 = (f32[112,128]{1,0:T(8,128)S(1)}, f32[112,128]{1,0:T(8,128)S(1)}, u32[]{:S(2)}, u32[]{:S(2)}) collective-permute-start(f32[112,128]{1,0:T(8,128)S(1)} %add.209), channel_id=1, source_target_pairs={{0,64},{16,80},{32,96},{48,112},{64,0},{80,16},{96,32},{112,48},{1... | collective-permute-start | bytes 172040 | tf_op jit(solution)/shard_map/ppermute | solution.py:177
  189.6 0.6 copy.260
  190.2 1.6 collective-permute-done.14
  191.9 23.8 %all-gather = bf16[1792,128]{1,0:T(8,128)(2,1)S(1)} all-gather(bf16[112,128]{1,0:T(8,128)(2,1)S(1)} %add_convert_fusion), channel_id=2, replica_groups=mesh['dp'=4,'tm'=8,'height'=16] {'height'}, dimensions={0}, use_global_device_ids=true | all-gather | bytes 487424 | tf_op jit(solution)/shard_map/all_gather | solution.py:232
  215.7 0.8 fusion.157
  (137 shorter events, 9.5 us)
Async XLA Ops:
  1.9 30.8 %collective-permute-start.1 = (bf16[2,1,128,128]{3,0,2,1:T(2,128)(2,1)S(1)}, bf16[2,1,128,128]{3,0,2,1:T(2,128)(2,1)S(1)}, u32[]{:S(2)}, u32[]{:S(2)}) collective-permute-start(bf16[2,1,128,128]{3,0,2,1:T(2,128)(2,1)S(1)} %slice.198), channel_id=1, source_target_pairs={{1,0},{2,1},{3,2},{4,3},{5,4},{6,5},{7,6},{8,7},{9,8},{10,9},{11,1... | collective-permute-start | bytes 196616 | tf_op jit(solution)/shard_map/ppermute | solution.py:29
  7.2 25.5 %collective-permute-start = (bf16[2,2,128,128]{3,0,2,1:T(2,128)(2,1)S(1)}, bf16[2,2,128,128]{3,0,2,1:T(2,128)(2,1)S(1)}, u32[]{:S(2)}, u32[]{:S(2)}) collective-permute-start(bf16[2,2,128,128]{3,0,2,1:T(2,128)(2,1)S(1)} %slice.197), channel_id=1, source_target_pairs={{0,1},{1,2},{2,3},{3,4},{4,5},{5,6},{6,7},{7,8},{8,9},{9,10},{10,1... | collective-permute-start | bytes 393224 | tf_op jit(solution)/shard_map/ppermute | solution.py:29
  9.9 12.1 %collective-permute-start.4 = (bf16[1,1,64,128]{3,2,1,0:T(8,128)(2,1)S(1)}, bf16[1,1,64,128]{3,2,1,0:T(8,128)(2,1)S(1)}, u32[]{:S(2)}, u32[]{:S(2)}) collective-permute-start(bf16[1,1,64,128]{3,2,1,0:T(8,128)(2,1)S(1)} %slice.210), channel_id=1, source_target_pairs={{1,0},{2,1},{3,2},{4,3},{5,4},{6,5},{7,6},{8,7},{9,8},{10,9},{11,1... | collective-permute-start | bytes 49160 | tf_op jit(solution)/shard_map/ppermute | solution.py:29
  22.0 7.3 %collective-permute-start.5 = (bf16[1,3,64,128]{3,2,1,0:T(8,128)(2,1)S(1)}, bf16[1,3,64,128]{3,2,1,0:T(8,128)(2,1)S(1)}, u32[]{:S(2)}, u32[]{:S(2)}) collective-permute-start(bf16[1,3,64,128]{3,2,1,0:T(8,128)(2,1)S(1)} %pad_maximum_fusion.7), channel_id=1, source_target_pairs={{16,0},{32,16},{48,32},{64,48},{80,64},{96,80},{112,96},{17,1},{33... | collective-permute-start | bytes 147464 | tf_op jit(solution)/shard_map/ppermute | solution.py:29
  26.7 4.1 %copy-start.20 = (pred[8,18]{0,1:T(8,128)(4,1)S(1)}, pred[8,18]{0,1:T(8,128)(4,1)}, u32[]{:S(2)}) copy-start(pred[8,18]{0,1:T(8,128)(4,1)} %constant.255) | copy-start | bytes 436
  28.1 4.0 %copy-start.17 = (bf16[3,3,3,128,128]{4,3,2,1,0:T(8,128)(2,1)S(1)}, bf16[3,3,3,128,128]{4,3,2,1,0:T(8,128)(2,1)}, u32[]{:S(2)}) copy-start(bf16[3,3,3,128,128]{4,3,2,1,0:T(8,128)(2,1)} %param.8) | copy-start | bytes 2654212
  33.4 26.7 %copy-start.10 = (bf16[2,7,128,128]{3,0,2,1:T(2,128)(2,1)}, bf16[2,7,128,128]{3,0,2,1:T(2,128)(2,1)S(1)}, u32[]{:S(2)}) copy-start(bf16[2,7,128,128]{3,0,2,1:T(2,128)(2,1)S(1)} %pad_maximum_fusion.5) | copy-start | bytes 1376260
  33.4 15.5 %collective-permute-start.3 = (bf16[2,7,128,128]{3,0,2,1:T(2,128)(2,1)S(1)}, bf16[2,7,128,128]{3,0,2,1:T(2,128)(2,1)S(1)}, u32[]{:S(2)}, u32[]{:S(2)}) collective-permute-start(bf16[2,7,128,128]{3,0,2,1:T(2,128)(2,1)S(1)} %pad_maximum_fusion.5), channel_id=1, source_target_pairs={{0,16},{16,32},{32,48},{48,64},{64,80},{80,96},{96,112},{1,17},{17... | collective-permute-start | bytes 1376264 | tf_op jit(solution)/shard_map/ppermute | solution.py:29
  38.0 18.7 %collective-permute-start.2 = (bf16[2,7,128,128]{3,0,2,1:T(2,128)(2,1)S(1)}, bf16[2,7,128,128]{3,0,2,1:T(2,128)(2,1)S(1)}, u32[]{:S(2)}, u32[]{:S(2)}) collective-permute-start(bf16[2,7,128,128]{3,0,2,1:T(2,128)(2,1)S(1)} %pad_maximum_fusion.5), channel_id=1, source_target_pairs={{0,32},{16,48},{32,64},{48,80},{64,96},{80,112},{1,33},{17,49},{33... | collective-permute-start | bytes 1376264 | tf_op jit(solution)/shard_map/ppermute | solution.py:29
  49.0 11.2 %copy-start.12 = (bf16[2,7,128,128]{3,0,2,1:T(2,128)(2,1)}, bf16[2,7,128,128]{3,0,2,1:T(2,128)(2,1)S(1)}, u32[]{:S(2)}) copy-start(bf16[2,7,128,128]{3,0,2,1:T(2,128)(2,1)S(1)} %collective-permute-done.3) | copy-start | bytes 1376260
  60.1 0.9 copy-start
  61.7 1.5 copy-start.3
  61.7 1.7 copy-start.16
  61.7 1.7 copy-start.19
  63.5 2.0 copy-start.4
  65.5 2.1 copy-start.2
  73.8 0.9 copy-start.9
  73.8 1.3 copy-start.11
  75.1 2.3 %copy-start.1 = (bf16[4,7,128,128]{3,0,2,1:T(4,128)(2,1)S(1)}, bf16[4,7,128,128]{3,0,2,1:T(4,128)(2,1)}, u32[]{:S(2)}) copy-start(bf16[4,7,128,128]{3,0,2,1:T(4,128)(2,1)} %copy-done) | copy-start | bytes 2752516
  77.4 2.3 %copy-start.13 = (bf16[2,7,128,128]{3,0,2,1:T(2,128)(2,1)S(1)}, bf16[2,7,128,128]{3,0,2,1:T(2,128)(2,1)}, u32[]{:S(2)}) copy-start(bf16[2,7,128,128]{3,0,2,1:T(2,128)(2,1)} %copy-done.12) | copy-start | bytes 1376260
  81.9 1.0 copy-start.6
  82.9 1.0 copy-start.7
  82.9 1.0 copy-start.15
  83.9 1.0 copy-start.5
  83.9 1.0 copy-start.14
  88.0 5.8 %collective-permute-start.6 = (f32[2,2,2,2,2,112,128]{6,5,4,3,2,1,0:T(8,128)S(1)}, f32[2,2,2,2,2,112,128]{6,5,4,3,2,1,0:T(8,128)}, u32[]{:S(2)}, u32[]{:S(2)}) collective-permute-start(f32[2,2,2,2,2,112,128]{6,5,4,3,2,1,0:T(8,128)S(1)} %bitcast.255), channel_id=1, source_target_pairs={{0,128},{128,0},{256,384},{384,256},{1,129},{129,1},{257,385},{385... | collective-permute-start | bytes 5505032 | tf_op jit(solution)/shard_map/ppermute | solution.py:177
  96.2 15.4 %collective-permute-start.7 = (f32[2,2,2,2,112,128]{5,4,3,2,1,0:T(8,128)S(1)}, f32[2,2,2,2,112,128]{5,4,3,2,1,0:T(8,128)}, u32[]{:S(2)}, u32[]{:S(2)}) collective-permute-start(f32[2,2,2,2,112,128]{5,4,3,2,1,0:T(8,128)S(1)} %bitcast_select_fusion), channel_id=1, source_target_pairs={{0,1},{1,0},{2,3},{3,2},{4,5},{5,4},{6,7},{7,6},{8,9},{9,8},{10,11... | collective-permute-start | bytes 2752520 | tf_op jit(solution)/shard_map/ppermute | solution.py:186
  113.0 10.4 %collective-permute-start.8 = (f32[2,2,2,112,128]{4,3,2,1,0:T(8,128)S(1)}, f32[2,2,2,112,128]{4,3,2,1,0:T(8,128)S(1)}, u32[]{:S(2)}, u32[]{:S(2)}) collective-permute-start(f32[2,2,2,112,128]{4,3,2,1,0:T(8,128)S(1)} %bitcast_select_fusion.2), channel_id=1, source_target_pairs={{0,4},{1,5},{2,6},{3,7},{4,0},{5,1},{6,2},{7,3},{8,12},{9,13},{10,... | collective-permute-start | bytes 1376264 | tf_op jit(solution)/shard_map/ppermute | solution.py:186
  115.5 20.6 %copy-start.8 = (bf16[1,5,128,128]{3,0,2,1:T(2,128)(2,1)S(1)}, bf16[1,5,128,128]{3,0,2,1:T(2,128)(2,1)}, u32[]{:S(2)}) copy-start(bf16[1,5,128,128]{3,0,2,1:T(2,128)(2,1)} %get-tuple-element.27) | copy-start | bytes 491524
  123.5 9.4 %collective-permute-start.9 = (f32[2,2,112,128]{3,2,1,0:T(8,128)S(1)}, f32[2,2,112,128]{3,2,1,0:T(8,128)S(1)}, u32[]{:S(2)}, u32[]{:S(2)}) collective-permute-start(f32[2,2,112,128]{3,2,1,0:T(8,128)S(1)} %bitcast_select_fusion.4), channel_id=1, source_target_pairs={{0,2},{1,3},{2,0},{3,1},{4,6},{5,7},{6,4},{7,5},{8,10},{9,11},{10,... | collective-permute-start | bytes 688136 | tf_op jit(solution)/shard_map/ppermute | solution.py:186
  132.9 24.0 %copy-start.18 = (bf16[3,3,3,128,128]{4,3,2,1,0:T(8,128)(2,1)S(1)}, bf16[3,3,3,128,128]{4,3,2,1,0:T(8,128)(2,1)}, u32[]{:S(2)}) copy-start(bf16[3,3,3,128,128]{4,3,2,1,0:T(8,128)(2,1)} %param.8) | copy-start | bytes 2654212
  133.0 24.0 %copy-start.21 = (pred[8,9]{0,1:T(8,128)(4,1)S(1)}, pred[8,9]{0,1:T(8,128)(4,1)}, u32[]{:S(2)}) copy-start(pred[8,9]{0,1:T(8,128)(4,1)} %constant.249) | copy-start | bytes 220
  133.0 8.3 %collective-permute-start.10 = (f32[2,112,128]{2,1,0:T(8,128)S(1)}, f32[2,112,128]{2,1,0:T(8,128)S(1)}, u32[]{:S(2)}, u32[]{:S(2)}) collective-permute-start(f32[2,112,128]{2,1,0:T(8,128)S(1)} %select_bitcast_fusion), channel_id=1, source_target_pairs={{0,8},{1,9},{2,10},{3,11},{4,12},{5,13},{6,14},{7,15},{8,0},{9,1},... | collective-permute-start | bytes 344072 | tf_op jit(solution)/shard_map/ppermute | solution.py:186
  141.4 17.7 %collective-permute-start.11 = (f32[112,128]{1,0:T(8,128)S(1)}, f32[112,128]{1,0:T(8,128)S(1)}, u32[]{:S(2)}, u32[]{:S(2)}) collective-permute-start(f32[112,128]{1,0:T(8,128)S(1)} %dynamic-slice_bitcast_fusion), channel_id=1, source_target_pairs={{0,256},{128,384},{256,0},{384,128},{1,257},{129,385},{257,1},{385... | collective-permute-start | bytes 172040 | tf_op jit(solution)/shard_map/ppermute | solution.py:177
  159.1 15.6 %collective-permute-start.12 = (f32[112,128]{1,0:T(8,128)S(1)}, f32[112,128]{1,0:T(8,128)S(1)}, u32[]{:S(2)}, u32[]{:S(2)}) collective-permute-start(f32[112,128]{1,0:T(8,128)S(1)} %bitcast_add_fusion.1), channel_id=1, source_target_pairs={{0,16},{16,0},{32,48},{48,32},{64,80},{80,64},{96,112},{112,96},{1... | collective-permute-start | bytes 172040 | tf_op jit(solution)/shard_map/ppermute | solution.py:177
  174.7 7.2 %collective-permute-start.13 = (f32[112,128]{1,0:T(8,128)S(1)}, f32[112,128]{1,0:T(8,128)S(1)}, u32[]{:S(2)}, u32[]{:S(2)}) collective-permute-start(f32[112,128]{1,0:T(8,128)S(1)} %add.208), channel_id=1, source_target_pairs={{0,32},{16,48},{32,0},{48,16},{64,96},{80,112},{96,64},{112,80},{1... | collective-permute-start | bytes 172040 | tf_op jit(solution)/shard_map/ppermute | solution.py:177
  181.9 10.0 %collective-permute-start.14 = (f32[112,128]{1,0:T(8,128)S(1)}, f32[112,128]{1,0:T(8,128)S(1)}, u32[]{:S(2)}, u32[]{:S(2)}) collective-permute-start(f32[112,128]{1,0:T(8,128)S(1)} %add.209), channel_id=1, source_target_pairs={{0,64},{16,80},{32,96},{48,112},{64,0},{80,16},{96,32},{112,48},{1... | collective-permute-start | bytes 172040 | tf_op jit(solution)/shard_map/ppermute | solution.py:177

commit v6 on v3

--- a/solution.py
+++ b/solution.py
@@ -1,6 +1,7 @@
 import math
 
 import jax
+import numpy as np
 import jax.numpy as jnp
 from jax import lax
 from jax.sharding import PartitionSpec as P
@@ -169,13 +170,23 @@
     return lax.ppermute(value, axis, [(i, i ^ bit) for i in range(lax.axis_size(axis))])
 
 
-def swap_rows(value, bits):
+def ring_mask(bit, low_bits):
+    return bit if bit in low_bits else bit | bit // 2
+
+
+def swap_rows(value, bits, low_bits):
     count = lax.axis_size("height")
     pairs = []
     for group in range(lax.axis_size("dp")):
-        bit = bits[group % 2]
-        pairs += [(group * count + i, group * count + (i ^ bit)) for i in range(count)]
+        mask = ring_mask(bits[group % 2], low_bits)
+        pairs += [(group * count + i, group * count + (i ^ mask)) for i in range(count)]
     return lax.ppermute(value, ("dp", "height"), pairs)
+
+
+def kept_bit(row, bit, low_bits):
+    if bit in low_bits:
+        return ((row // bit) ^ (row // (2 * bit))) % 2
+    return (row // bit) % 2
 
 
 def bits_of(count):
@@ -205,15 +216,16 @@
     core = lax.axis_index("dp") % 2
     row = lax.axis_index("height")
     held = [names, names]
+    low_bits = row_bits[0::2]
     for bits in stages:
         parts = []
         for variant in (0, 1):
-            high = (row // bits[variant]) % 2
+            high = kept_bit(row, bits[variant], low_bits)
             mine, other, held[variant] = split_bit(blocks, held[variant], ("height", bits[variant]), high)
             parts.append((mine, other))
         mine = jnp.where(core == 0, parts[0][0], parts[1][0])
         other = jnp.where(core == 0, parts[0][1], parts[1][1])
-        blocks = mine + swap_rows(other, bits)
+        blocks = mine + swap_rows(other, bits, low_bits)
     far = dp_bits[-1]
     high = (lax.axis_index("dp") // far) % 2
     mine, other, _ = split_bit(blocks, held[0], ("dp", far), high)
@@ -221,7 +233,9 @@
     for bit in frame_bits:
         blocks = blocks + swap(blocks, "tm", bit)
     piece = blocks.astype(jnp.bfloat16)
-    return lax.all_gather(piece, "height", axis=0, tiled=False)
+    gathered = lax.all_gather(piece, "height", axis=0, tiled=False)
+    owner = [h ^ sum((h >> 1) & bit for bit in low_bits) for h in range(gathered.shape[0])]
+    return gathered[np.array(owner)]
 
 
 def solution(mesh):

time: 190 us -> 189 us (level)
  waiting for transfers between devices: 51.7 us -> 49.8 us
  transfers between devices with their start and end apart: 16 -> 16, of which waited for: 11 -> 11; matrix products, arithmetic and copies ran while one was open for 12% -> 13% of each run, Pallas kernels for 0% -> 0%
where the time goes in v6:
time: 189 us; the launch traced here: 187 us
  starting transfers between devices  69.6 us (37%)
  waiting for transfers between devices  49.8 us (26%)
  blocking collectives  23.3 us (12%)
  matrix products  15.7 us (8%)
  other arithmetic  14.5 us (8%)
  local copies, waits for them, and re-layouts  10.3 us (5%)
  between operations  3.9 us (2%)
    ppermute x5, starting transfers between devices, swap(): lax.ppermute(value, axis, [(i, i ^ bit) for i in range(lax.axis_size(axis...  32.3 us
    ppermute x4, waiting for transfers between devices, swap_rows(): return lax.ppermute(value, ('dp', 'height'), pairs)  30.7 us
    all_gather x1, blocking collectives, reduce_gradients(): gathered = lax.all_gather(piece, 'height', axis=0, tiled=False)  23.3 us
    ppermute x5, starting transfers between devices, shifted(): lax.ppermute(value, axis, [(source, source + steps) for source in range(l...  18.5 us
    ppermute x5, waiting for transfers between devices, swap(): lax.ppermute(value, axis, [(i, i ^ bit) for i in range(lax.axis_size(axis...  12 us
    ppermute x4, starting transfers between devices, swap_rows(): return lax.ppermute(value, ('dp', 'height'), pairs)  11.6 us
    conv_general_dilated x6, matrix products, weight_grad(): lax.conv_general_dilated(frame_slab, masked, (1, 1), ((0, 0), pad_cols),...  8.4 us
    ppermute x5, waiting for transfers between devices, shifted(): lax.ppermute(value, axis, [(source, source + steps) for source in range(l...  7.12 us
  transfers between devices with their start and end apart: 16, of which 11 were waited for; matrix products, arithmetic and copies ran while one was open for 13% of the time, Pallas kernels for 0%

profile of v6, /device:TPU:6, one launch (start us, length us, event | category | flops | bytes accessed | tf_op | source)
XLA Modules:
  0.0 187.2 jit_solution(7030841595048276955)
XLA Ops:
  0.6 1.2 copy.340
  2.0 5.2 %collective-permute-start.1 = (bf16[2,1,128,128]{3,0,2,1:T(2,128)(2,1)S(1)}, bf16[2,1,128,128]{3,0,2,1:T(2,128)(2,1)S(1)}, u32[]{:S(2)}, u32[]{:S(2)}) collective-permute-start(bf16[2,1,128,128]{3,0,2,1:T(2,128)(2,1)S(1)} %get-tuple-element.34), channel_id=1, source_target_pairs={{1,0},{2,1},{3,2},{4,3},{5,4},{6,5},{7,6},{8,7},{9,8},{10,9},{11,1... | collective-permute-start | bytes 196616 | tf_op jit(solution)/shard_map/ppermute | solution.py:20
  7.2 1.9 %collective-permute-start = (bf16[2,1,128,128]{3,0,2,1:T(2,128)(2,1)S(1)}, bf16[2,1,128,128]{3,0,2,1:T(2,128)(2,1)S(1)}, u32[]{:S(2)}, u32[]{:S(2)}) collective-permute-start(bf16[2,1,128,128]{3,0,2,1:T(2,128)(2,1)S(1)} %get-tuple-element.33), channel_id=1, source_target_pairs={{0,1},{1,2},{2,3},{3,4},{4,5},{5,6},{6,7},{7,8},{8,9},{9,10},{10,1... | collective-permute-start | bytes 196616 | tf_op jit(solution)/shard_map/ppermute | solution.py:18
  9.1 0.8 fusion.118
  9.9 6.0 %collective-permute-start.5 = (bf16[1,1,64,128]{3,2,1,0:T(8,128)(2,1)S(1)}, bf16[1,1,64,128]{3,2,1,0:T(8,128)(2,1)S(1)}, u32[]{:S(2)}, u32[]{:S(2)}) collective-permute-start(bf16[1,1,64,128]{3,2,1,0:T(8,128)(2,1)S(1)} %slice.188), channel_id=1, source_target_pairs={{1,0},{2,1},{3,2},{4,3},{5,4},{6,5},{7,6},{8,7},{9,8},{10,9},{11,1... | collective-permute-start | bytes 49160 | tf_op jit(solution)/shard_map/ppermute | solution.py:30
  15.9 0.8 reduce-window_clone.1
  16.7 0.7 subtract_bitcast_fusion
  17.7 0.6 fusion.161
  20.3 1.4 broadcast_multiply_fusion.5
  21.7 0.7 slice.193
  22.4 0.6 slice.197
  23.0 1.3 collective-permute-start.6
  24.3 0.6 pad_maximum_fusion.5
  24.9 4.7 %collective-permute-start.2 = (bf16[2,6,128,128]{3,0,2,1:T(2,128)(2,1)S(1)}, bf16[2,6,128,128]{3,0,2,1:T(2,128)(2,1)S(1)}, u32[]{:S(2)}, u32[]{:S(2)}) collective-permute-start(bf16[2,6,128,128]{3,0,2,1:T(2,128)(2,1)S(1)} %pad_maximum_fusion.5), channel_id=1, source_target_pairs={{0,16},{16,32},{32,48},{48,64},{64,80},{80,96},{96,112},{1,17},{17... | collective-permute-start | bytes 1179656 | tf_op jit(solution)/shard_map/ppermute | solution.py:30
  29.6 0.6 fusion.168
  30.7 1.3 multiply_bitcast_fusion.1
  32.1 0.3 fusion.9
  32.8 0.3 convolution_select_fusion.5
  33.2 0.3 fusion.8
  33.7 3.4 %collective-permute-done.2 = bf16[2,6,128,128]{3,0,2,1:T(2,128)(2,1)S(1)} collective-permute-done((bf16[2,6,128,128]{3,0,2,1:T(2,128)(2,1)S(1)}, bf16[2,6,128,128]{3,0,2,1:T(2,128)(2,1)S(1)}, u32[]{:S(2)}, u32[]{:S(2)}) %collective-permute-start.2) | collective-permute-done | bytes 393248 | tf_op jit(solution)/shard_map/ppermute | solution.py:30
  37.5 1.0 pad_maximum_fusion.2
  39.1 0.8 fusion.6
  40.1 0.8 fusion.5
  41.0 1.0 add_divide_fusion
  42.2 2.1 %collective-permute-start.3 = (bf16[2,1,128,128]{3,0,2,1:T(2,128)(2,1)S(1)}, bf16[2,1,128,128]{3,0,2,1:T(2,128)(2,1)S(1)}, u32[]{:S(2)}, u32[]{:S(2)}) collective-permute-start(bf16[2,1,128,128]{3,0,2,1:T(2,128)(2,1)S(1)} %bitcast.299), channel_id=1, source_target_pairs={{0,1},{1,2},{2,3},{3,4},{4,5},{5,6},{6,7},{7,8},{8,9},{9,10},{10,1... | collective-permute-start | bytes 196616 | tf_op jit(solution)/shard_map/ppermute | solution.py:30
  45.1 2.0 %convolution_bitcast_fusion.3 = f32[1,3,3,128,128]{4,3,2,1,0:T(8,128)S(1)} fusion(bf16[2,6,128,128]{3,0,2,1:T(2,128)(2,1)S(1)} %pad_maximum_fusion.5, bf16[2,4,128,128]{3,2,1,0:T(8,128)(2,1)S(1)} %get-tuple-element.32), kind=kOutput, calls=%fused_computation.14 | convolution fusion | flops 300417024 | bytes 1245184 | tf_op jit(solution)/shard_map/conv_general_dilated | solution.py:57
  47.1 2.0 %convolution_bitcast_fusion.4 = f32[1,3,3,128,128]{4,3,2,1,0:T(8,128)S(1)} fusion(bf16[2,6,128,128]{3,0,2,1:T(2,128)(2,1)S(1)} %pad_maximum_fusion.2, bf16[2,4,128,128]{3,2,1,0:T(8,128)(2,1)S(1)} %get-tuple-element.31), kind=kOutput, calls=%fused_computation.15 | convolution fusion | flops 300417024 | bytes 1245184 | tf_op jit(solution)/shard_map/conv_general_dilated | solution.py:57
  49.0 2.0 %convolution_bitcast_fusion.5 = f32[1,3,3,128,128]{4,3,2,1,0:T(8,128)S(1)} fusion(bf16[2,6,128,128]{3,0,2,1:T(2,128)(2,1)S(1)} %collective-permute-done.2, bf16[2,4,128,128]{3,2,1,0:T(8,128)(2,1)S(1)} %get-tuple-element.20), kind=kOutput, calls=%fused_computation.16 | convolution fusion | flops 300417024 | bytes 1245184 | tf_op jit(solution)/shard_map/conv_general_dilated | solution.py:57
  52.0 0.4 pad_maximum_fusion.6
  52.4 4.4 %collective-permute-start.4 = (bf16[2,5,128,128]{3,0,2,1:T(2,128)(2,1)S(1)}, bf16[2,5,128,128]{3,0,2,1:T(2,128)(2,1)S(1)}, u32[]{:S(2)}, u32[]{:S(2)}) collective-permute-start(bf16[2,5,128,128]{3,0,2,1:T(2,128)(2,1)S(1)} %pad_maximum_fusion.6), channel_id=1, source_target_pairs={{0,16},{16,32},{32,48},{48,64},{64,80},{80,96},{96,112},{1,17},{17... | collective-permute-start | bytes 983048 | tf_op jit(solution)/shard_map/ppermute | solution.py:30
  56.8 0.4 slice_maximum_fusion
  57.3 0.9 convolution_bitcast_fusion
  58.1 3.7 %collective-permute-done.4 = bf16[2,5,128,128]{3,0,2,1:T(2,128)(2,1)S(1)} collective-permute-done((bf16[2,5,128,128]{3,0,2,1:T(2,128)(2,1)S(1)}, bf16[2,5,128,128]{3,0,2,1:T(2,128)(2,1)S(1)}, u32[]{:S(2)}, u32[]{:S(2)}) %collective-permute-start.4) | collective-permute-done | bytes 327712 | tf_op jit(solution)/shard_map/ppermute | solution.py:30
  61.9 0.5 fusion.159
  62.4 0.8 convolution_bitcast_fusion.1
  63.3 0.8 convolution_bitcast_fusion.2
  64.6 1.5 fusion.1
  66.2 1.9 %collective-permute-start.7 = (f32[2,2,2,2,2,112,128]{6,5,4,3,2,1,0:T(8,128)S(1)}, f32[2,2,2,2,2,112,128]{6,5,4,3,2,1,0:T(8,128)}, u32[]{:S(2)}, u32[]{:S(2)}) collective-permute-start(f32[2,2,2,2,2,112,128]{6,5,4,3,2,1,0:T(8,128)S(1)} %bitcast.274), channel_id=1, source_target_pairs={{0,128},{128,0},{256,384},{384,256},{1,129},{129,1},{257,385},{385... | collective-permute-start | bytes 5505032 | tf_op jit(solution)/shard_map/ppermute | solution.py:170
  68.2 3.8 %collective-permute-done.7 = f32[2,2,2,2,2,112,128]{6,5,4,3,2,1,0:T(8,128)} collective-permute-done((f32[2,2,2,2,2,112,128]{6,5,4,3,2,1,0:T(8,128)S(1)}, f32[2,2,2,2,2,112,128]{6,5,4,3,2,1,0:T(8,128)}, u32[]{:S(2)}, u32[]{:S(2)}) %collective-permute-start.7) | collective-permute-done | bytes 1835040 | tf_op jit(solution)/shard_map/ppermute | solution.py:170
  72.1 2.3 %bitcast_add_fusion = f32[2,2,2,2,2,112,128]{6,5,4,3,2,1,0:T(8,128)S(1)} fusion(f32[2,2,2,2,2,112,128]{6,5,4,3,2,1,0:T(8,128)} %collective-permute-done.7, f32[2,1,2,2,2,2,112,128]{7,6,5,4,3,1,0,2:T(8,128)} %get-tuple-element.22), kind=kLoop, calls=%fused_computation.7 | loop fusion | flops 458752 | bytes 5505024 | tf_op jit(solution)/shard_map/add | solution.py:212
  74.5 1.9 %collective-permute-start.8 = (f32[2,2,2,2,112,128]{5,4,3,2,1,0:T(8,128)S(1)}, f32[2,2,2,2,112,128]{5,4,3,2,1,0:T(8,128)}, u32[]{:S(2)}, u32[]{:S(2)}) collective-permute-start(f32[2,2,2,2,112,128]{5,4,3,2,1,0:T(8,128)S(1)} %bitcast_select_fusion), channel_id=1, source_target_pairs={{0,1},{1,0},{2,3},{3,2},{4,5},{5,4},{6,7},{7,6},{8,9},{9,8},{10,11... | collective-permute-start | bytes 2752520 | tf_op jit(solution)/shard_map/ppermute | solution.py:183
  76.4 13.4 %collective-permute-done.8 = f32[2,2,2,2,112,128]{5,4,3,2,1,0:T(8,128)} collective-permute-done((f32[2,2,2,2,112,128]{5,4,3,2,1,0:T(8,128)S(1)}, f32[2,2,2,2,112,128]{5,4,3,2,1,0:T(8,128)}, u32[]{:S(2)}, u32[]{:S(2)}) %collective-permute-start.8) | collective-permute-done | bytes 917536 | tf_op jit(solution)/shard_map/ppermute | solution.py:183
  89.9 1.3 fusion.19
  91.3 2.7 %collective-permute-start.9 = (f32[2,2,2,112,128]{4,3,2,1,0:T(8,128)S(1)}, f32[2,2,2,112,128]{4,3,2,1,0:T(8,128)S(1)}, u32[]{:S(2)}, u32[]{:S(2)}) collective-permute-start(f32[2,2,2,112,128]{4,3,2,1,0:T(8,128)S(1)} %bitcast_select_fusion.2), channel_id=1, source_target_pairs={{0,4},{1,5},{2,6},{3,7},{4,0},{5,1},{6,2},{7,3},{8,12},{9,13},{10,... | collective-permute-start | bytes 1376264 | tf_op jit(solution)/shard_map/ppermute | solution.py:183
  94.0 7.6 %collective-permute-done.9 = f32[2,2,2,112,128]{4,3,2,1,0:T(8,128)S(1)} collective-permute-done((f32[2,2,2,112,128]{4,3,2,1,0:T(8,128)S(1)}, f32[2,2,2,112,128]{4,3,2,1,0:T(8,128)S(1)}, u32[]{:S(2)}, u32[]{:S(2)}) %collective-permute-start.9) | collective-permute-done | bytes 458784 | tf_op jit(solution)/shard_map/ppermute | solution.py:183
  101.8 4.3 %collective-permute-start.10 = (f32[2,2,112,128]{3,2,1,0:T(8,128)S(1)}, f32[2,2,112,128]{3,2,1,0:T(8,128)S(1)}, u32[]{:S(2)}, u32[]{:S(2)}) collective-permute-start(f32[2,2,112,128]{3,2,1,0:T(8,128)S(1)} %bitcast_select_fusion.4), channel_id=1, source_target_pairs={{0,3},{1,2},{2,1},{3,0},{4,7},{5,6},{6,5},{7,4},{8,11},{9,10},{10,... | collective-permute-start | bytes 688136 | tf_op jit(solution)/shard_map/ppermute | solution.py:183
  106.1 4.8 %collective-permute-done.10 = f32[2,2,112,128]{3,2,1,0:T(8,128)S(1)} collective-permute-done((f32[2,2,112,128]{3,2,1,0:T(8,128)S(1)}, f32[2,2,112,128]{3,2,1,0:T(8,128)S(1)}, u32[]{:S(2)}, u32[]{:S(2)}) %collective-permute-start.10) | collective-permute-done | bytes 229408 | tf_op jit(solution)/shard_map/ppermute | solution.py:183
  111.0 2.7 %collective-permute-start.11 = (f32[2,112,128]{2,1,0:T(8,128)S(1)}, f32[2,112,128]{2,1,0:T(8,128)S(1)}, u32[]{:S(2)}, u32[]{:S(2)}) collective-permute-start(f32[2,112,128]{2,1,0:T(8,128)S(1)} %select_bitcast_fusion), channel_id=1, source_target_pairs={{0,12},{1,13},{2,14},{3,15},{4,8},{5,9},{6,10},{7,11},{8,4},{9,5},... | collective-permute-start | bytes 344072 | tf_op jit(solution)/shard_map/ppermute | solution.py:183
  114.0 4.9 %collective-permute-done.11 = f32[2,112,128]{2,1,0:T(8,128)S(1)} collective-permute-done((f32[2,112,128]{2,1,0:T(8,128)S(1)}, f32[2,112,128]{2,1,0:T(8,128)S(1)}, u32[]{:S(2)}, u32[]{:S(2)}) %collective-permute-start.11) | collective-permute-done | bytes 114720 | tf_op jit(solution)/shard_map/ppermute | solution.py:183
  118.9 15.4 %collective-permute-start.12 = (f32[112,128]{1,0:T(8,128)S(1)}, f32[112,128]{1,0:T(8,128)S(1)}, u32[]{:S(2)}, u32[]{:S(2)}) collective-permute-start(f32[112,128]{1,0:T(8,128)S(1)} %dynamic-slice_bitcast_fusion), channel_id=1, source_target_pairs={{0,256},{128,384},{256,0},{384,128},{1,257},{129,385},{257,1},{385... | collective-permute-start | bytes 172040 | tf_op jit(solution)/shard_map/ppermute | solution.py:170
  134.3 1.9 fusion.10
  136.4 1.7 collective-permute-done.12
  138.1 2.7 %collective-permute-start.13 = (f32[112,128]{1,0:T(8,128)S(1)}, f32[112,128]{1,0:T(8,128)S(1)}, u32[]{:S(2)}, u32[]{:S(2)}) collective-permute-start(f32[112,128]{1,0:T(8,128)S(1)} %bitcast_add_fusion.1), channel_id=1, source_target_pairs={{0,16},{16,0},{32,48},{48,32},{64,80},{80,64},{96,112},{112,96},{1... | collective-permute-start | bytes 172040 | tf_op jit(solution)/shard_map/ppermute | solution.py:170
  140.8 0.9 fusion.11
  142.0 2.8 %collective-permute-done.13 = f32[112,128]{1,0:T(8,128)S(1)} collective-permute-done((f32[112,128]{1,0:T(8,128)S(1)}, f32[112,128]{1,0:T(8,128)S(1)}, u32[]{:S(2)}, u32[]{:S(2)}) %collective-permute-start.13) | collective-permute-done | bytes 57376 | tf_op jit(solution)/shard_map/ppermute | solution.py:170
  144.8 4.1 %collective-permute-start.14 = (f32[112,128]{1,0:T(8,128)S(1)}, f32[112,128]{1,0:T(8,128)S(1)}, u32[]{:S(2)}, u32[]{:S(2)}) collective-permute-start(f32[112,128]{1,0:T(8,128)S(1)} %add.204), channel_id=1, source_target_pairs={{0,32},{16,48},{32,0},{48,16},{64,96},{80,112},{96,64},{112,80},{1... | collective-permute-start | bytes 172040 | tf_op jit(solution)/shard_map/ppermute | solution.py:170
  148.9 0.9 fusion.15
  149.8 2.2 %collective-permute-done.14 = f32[112,128]{1,0:T(8,128)S(1)} collective-permute-done((f32[112,128]{1,0:T(8,128)S(1)}, f32[112,128]{1,0:T(8,128)S(1)}, u32[]{:S(2)}, u32[]{:S(2)}) %collective-permute-start.14) | collective-permute-done | bytes 57376 | tf_op jit(solution)/shard_map/ppermute | solution.py:170
  152.0 8.2 %collective-permute-start.15 = (f32[112,128]{1,0:T(8,128)S(1)}, f32[112,128]{1,0:T(8,128)S(1)}, u32[]{:S(2)}, u32[]{:S(2)}) collective-permute-start(f32[112,128]{1,0:T(8,128)S(1)} %add.205), channel_id=1, source_target_pairs={{0,64},{16,80},{32,96},{48,112},{64,0},{80,16},{96,32},{112,48},{1... | collective-permute-start | bytes 172040 | tf_op jit(solution)/shard_map/ppermute | solution.py:170
  160.3 0.6 copy.288
  160.9 1.5 collective-permute-done.15
  162.4 23.3 %all-gather = bf16[1792,128]{1,0:T(8,128)(2,1)S(1)} all-gather(bf16[112,128]{1,0:T(8,128)(2,1)S(1)} %add_convert_fusion), channel_id=2, replica_groups=mesh['dp'=4,'tm'=8,'height'=16] {'height'}, dimensions={0}, use_global_device_ids=true | all-gather | bytes 487424 | tf_op jit(solution)/shard_map/all_gather | solution.py:236
  185.7 0.6 gather_fusion
  186.4 0.8 fusion.158
  (119 shorter events, 6.1 us)
Async XLA Ops:
  2.0 22.3 %collective-permute-start.1 = (bf16[2,1,128,128]{3,0,2,1:T(2,128)(2,1)S(1)}, bf16[2,1,128,128]{3,0,2,1:T(2,128)(2,1)S(1)}, u32[]{:S(2)}, u32[]{:S(2)}) collective-permute-start(bf16[2,1,128,128]{3,0,2,1:T(2,128)(2,1)S(1)} %get-tuple-element.34), channel_id=1, source_target_pairs={{1,0},{2,1},{3,2},{4,3},{5,4},{6,5},{7,6},{8,7},{9,8},{10,9},{11,1... | collective-permute-start | bytes 196616 | tf_op jit(solution)/shard_map/ppermute | solution.py:20
  7.2 17.1 %collective-permute-start = (bf16[2,1,128,128]{3,0,2,1:T(2,128)(2,1)S(1)}, bf16[2,1,128,128]{3,0,2,1:T(2,128)(2,1)S(1)}, u32[]{:S(2)}, u32[]{:S(2)}) collective-permute-start(bf16[2,1,128,128]{3,0,2,1:T(2,128)(2,1)S(1)} %get-tuple-element.33), channel_id=1, source_target_pairs={{0,1},{1,2},{2,3},{3,4},{4,5},{5,6},{6,7},{7,8},{8,9},{9,10},{10,1... | collective-permute-start | bytes 196616 | tf_op jit(solution)/shard_map/ppermute | solution.py:18
  9.9 13.1 %collective-permute-start.5 = (bf16[1,1,64,128]{3,2,1,0:T(8,128)(2,1)S(1)}, bf16[1,1,64,128]{3,2,1,0:T(8,128)(2,1)S(1)}, u32[]{:S(2)}, u32[]{:S(2)}) collective-permute-start(bf16[1,1,64,128]{3,2,1,0:T(8,128)(2,1)S(1)} %slice.188), channel_id=1, source_target_pairs={{1,0},{2,1},{3,2},{4,3},{5,4},{6,5},{7,6},{8,7},{9,8},{10,9},{11,1... | collective-permute-start | bytes 49160 | tf_op jit(solution)/shard_map/ppermute | solution.py:30
  23.0 7.7 %collective-permute-start.6 = (bf16[1,3,64,128]{3,2,1,0:T(8,128)(2,1)S(1)}, bf16[1,3,64,128]{3,2,1,0:T(8,128)(2,1)S(1)}, u32[]{:S(2)}, u32[]{:S(2)}) collective-permute-start(bf16[1,3,64,128]{3,2,1,0:T(8,128)(2,1)S(1)} %pad_maximum_fusion.8), channel_id=1, source_target_pairs={{16,0},{32,16},{48,32},{64,48},{80,64},{96,80},{112,96},{17,1},{33... | collective-permute-start | bytes 147464 | tf_op jit(solution)/shard_map/ppermute | solution.py:30
  24.9 7.2 %copy-start.5 = (bf16[3,3,3,128,128]{4,3,2,1,0:T(8,128)(2,1)S(1)}, bf16[3,3,3,128,128]{4,3,2,1,0:T(8,128)(2,1)}, u32[]{:S(2)}) copy-start(bf16[3,3,3,128,128]{4,3,2,1,0:T(8,128)(2,1)} %param.10) | copy-start | bytes 2654212
  24.9 7.2 %copy-start.8 = (pred[8,18]{0,1:T(8,128)(4,1)S(1)}, pred[8,18]{0,1:T(8,128)(4,1)}, u32[]{:S(2)}) copy-start(pred[8,18]{0,1:T(8,128)(4,1)} %constant.267) | copy-start | bytes 436
  24.9 12.1 %collective-permute-start.2 = (bf16[2,6,128,128]{3,0,2,1:T(2,128)(2,1)S(1)}, bf16[2,6,128,128]{3,0,2,1:T(2,128)(2,1)S(1)}, u32[]{:S(2)}, u32[]{:S(2)}) collective-permute-start(bf16[2,6,128,128]{3,0,2,1:T(2,128)(2,1)S(1)} %pad_maximum_fusion.5), channel_id=1, source_target_pairs={{0,16},{16,32},{32,48},{48,64},{64,80},{80,96},{96,112},{1,17},{17... | collective-permute-start | bytes 1179656 | tf_op jit(solution)/shard_map/ppermute | solution.py:30
  37.4 1.6 copy-start.4
  37.4 1.6 copy-start.7
  42.2 9.8 %collective-permute-start.3 = (bf16[2,1,128,128]{3,0,2,1:T(2,128)(2,1)S(1)}, bf16[2,1,128,128]{3,0,2,1:T(2,128)(2,1)S(1)}, u32[]{:S(2)}, u32[]{:S(2)}) collective-permute-start(bf16[2,1,128,128]{3,0,2,1:T(2,128)(2,1)S(1)} %bitcast.299), channel_id=1, source_target_pairs={{0,1},{1,2},{2,3},{3,4},{4,5},{5,6},{6,7},{7,8},{8,9},{9,10},{10,1... | collective-permute-start | bytes 196616 | tf_op jit(solution)/shard_map/ppermute | solution.py:30
  52.4 9.5 %collective-permute-start.4 = (bf16[2,5,128,128]{3,0,2,1:T(2,128)(2,1)S(1)}, bf16[2,5,128,128]{3,0,2,1:T(2,128)(2,1)S(1)}, u32[]{:S(2)}, u32[]{:S(2)}) collective-permute-start(bf16[2,5,128,128]{3,0,2,1:T(2,128)(2,1)S(1)} %pad_maximum_fusion.6), channel_id=1, source_target_pairs={{0,16},{16,32},{32,48},{48,64},{64,80},{80,96},{96,112},{1,17},{17... | collective-permute-start | bytes 983048 | tf_op jit(solution)/shard_map/ppermute | solution.py:30
  57.3 0.9 copy-start
  62.4 0.8 copy-start.2
  66.2 5.8 %collective-permute-start.7 = (f32[2,2,2,2,2,112,128]{6,5,4,3,2,1,0:T(8,128)S(1)}, f32[2,2,2,2,2,112,128]{6,5,4,3,2,1,0:T(8,128)}, u32[]{:S(2)}, u32[]{:S(2)}) collective-permute-start(f32[2,2,2,2,2,112,128]{6,5,4,3,2,1,0:T(8,128)S(1)} %bitcast.274), channel_id=1, source_target_pairs={{0,128},{128,0},{256,384},{384,256},{1,129},{129,1},{257,385},{385... | collective-permute-start | bytes 5505032 | tf_op jit(solution)/shard_map/ppermute | solution.py:170
  74.5 15.4 %collective-permute-start.8 = (f32[2,2,2,2,112,128]{5,4,3,2,1,0:T(8,128)S(1)}, f32[2,2,2,2,112,128]{5,4,3,2,1,0:T(8,128)}, u32[]{:S(2)}, u32[]{:S(2)}) collective-permute-start(f32[2,2,2,2,112,128]{5,4,3,2,1,0:T(8,128)S(1)} %bitcast_select_fusion), channel_id=1, source_target_pairs={{0,1},{1,0},{2,3},{3,2},{4,5},{5,4},{6,7},{7,6},{8,9},{9,8},{10,11... | collective-permute-start | bytes 2752520 | tf_op jit(solution)/shard_map/ppermute | solution.py:183
  91.3 10.4 %collective-permute-start.9 = (f32[2,2,2,112,128]{4,3,2,1,0:T(8,128)S(1)}, f32[2,2,2,112,128]{4,3,2,1,0:T(8,128)S(1)}, u32[]{:S(2)}, u32[]{:S(2)}) collective-permute-start(f32[2,2,2,112,128]{4,3,2,1,0:T(8,128)S(1)} %bitcast_select_fusion.2), channel_id=1, source_target_pairs={{0,4},{1,5},{2,6},{3,7},{4,0},{5,1},{6,2},{7,3},{8,12},{9,13},{10,... | collective-permute-start | bytes 1376264 | tf_op jit(solution)/shard_map/ppermute | solution.py:183
  94.0 19.8 %copy-start.3 = (s32[16]{0:T(128)S(1)}, s32[16]{0:T(128)}, u32[]{:S(2)}) copy-start(s32[16]{0:T(128)} %constant.271) | copy-start | bytes 196
  94.0 19.8 %copy-start.1 = (bf16[1,5,128,128]{3,0,2,1:T(2,128)(2,1)S(1)}, bf16[1,5,128,128]{3,0,2,1:T(2,128)(2,1)}, u32[]{:S(2)}) copy-start(bf16[1,5,128,128]{3,0,2,1:T(2,128)(2,1)} %copy-done) | copy-start | bytes 491524
  101.7 32.5 %copy-start.9 = (pred[8,9]{0,1:T(8,128)(4,1)S(1)}, pred[8,9]{0,1:T(8,128)(4,1)}, u32[]{:S(2)}) copy-start(pred[8,9]{0,1:T(8,128)(4,1)} %constant.261) | copy-start | bytes 220
  101.8 9.1 %collective-permute-start.10 = (f32[2,2,112,128]{3,2,1,0:T(8,128)S(1)}, f32[2,2,112,128]{3,2,1,0:T(8,128)S(1)}, u32[]{:S(2)}, u32[]{:S(2)}) collective-permute-start(f32[2,2,112,128]{3,2,1,0:T(8,128)S(1)} %bitcast_select_fusion.4), channel_id=1, source_target_pairs={{0,3},{1,2},{2,1},{3,0},{4,7},{5,6},{6,5},{7,4},{8,11},{9,10},{10,... | collective-permute-start | bytes 688136 | tf_op jit(solution)/shard_map/ppermute | solution.py:183
  111.0 7.9 %collective-permute-start.11 = (f32[2,112,128]{2,1,0:T(8,128)S(1)}, f32[2,112,128]{2,1,0:T(8,128)S(1)}, u32[]{:S(2)}, u32[]{:S(2)}) collective-permute-start(f32[2,112,128]{2,1,0:T(8,128)S(1)} %select_bitcast_fusion), channel_id=1, source_target_pairs={{0,12},{1,13},{2,14},{3,15},{4,8},{5,9},{6,10},{7,11},{8,4},{9,5},... | collective-permute-start | bytes 344072 | tf_op jit(solution)/shard_map/ppermute | solution.py:183
  113.9 26.9 %copy-start.6 = (bf16[3,3,3,128,128]{4,3,2,1,0:T(8,128)(2,1)S(1)}, bf16[3,3,3,128,128]{4,3,2,1,0:T(8,128)(2,1)}, u32[]{:S(2)}) copy-start(bf16[3,3,3,128,128]{4,3,2,1,0:T(8,128)(2,1)} %param.10) | copy-start | bytes 2654212
  118.9 19.2 %collective-permute-start.12 = (f32[112,128]{1,0:T(8,128)S(1)}, f32[112,128]{1,0:T(8,128)S(1)}, u32[]{:S(2)}, u32[]{:S(2)}) collective-permute-start(f32[112,128]{1,0:T(8,128)S(1)} %dynamic-slice_bitcast_fusion), channel_id=1, source_target_pairs={{0,256},{128,384},{256,0},{384,128},{1,257},{129,385},{257,1},{385... | collective-permute-start | bytes 172040 | tf_op jit(solution)/shard_map/ppermute | solution.py:170
  138.1 6.7 %collective-permute-start.13 = (f32[112,128]{1,0:T(8,128)S(1)}, f32[112,128]{1,0:T(8,128)S(1)}, u32[]{:S(2)}, u32[]{:S(2)}) collective-permute-start(f32[112,128]{1,0:T(8,128)S(1)} %bitcast_add_fusion.1), channel_id=1, source_target_pairs={{0,16},{16,0},{32,48},{48,32},{64,80},{80,64},{96,112},{112,96},{1... | collective-permute-start | bytes 172040 | tf_op jit(solution)/shard_map/ppermute | solution.py:170
  144.8 7.2 %collective-permute-start.14 = (f32[112,128]{1,0:T(8,128)S(1)}, f32[112,128]{1,0:T(8,128)S(1)}, u32[]{:S(2)}, u32[]{:S(2)}) collective-permute-start(f32[112,128]{1,0:T(8,128)S(1)} %add.204), channel_id=1, source_target_pairs={{0,32},{16,48},{32,0},{48,16},{64,96},{80,112},{96,64},{112,80},{1... | collective-permute-start | bytes 172040 | tf_op jit(solution)/shard_map/ppermute | solution.py:170
  152.0 10.4 %collective-permute-start.15 = (f32[112,128]{1,0:T(8,128)S(1)}, f32[112,128]{1,0:T(8,128)S(1)}, u32[]{:S(2)}, u32[]{:S(2)}) collective-permute-start(f32[112,128]{1,0:T(8,128)S(1)} %add.205), channel_id=1, source_target_pairs={{0,64},{16,80},{32,96},{48,112},{64,0},{80,16},{96,32},{112,48},{1... | collective-permute-start | bytes 172040 | tf_op jit(solution)/shard_map/ppermute | solution.py:170

commit v7 on v6

--- a/solution.py
+++ b/solution.py
@@ -110,7 +110,23 @@
     down_index = first_frame + 2 * jnp.arange(down_frames + 1, dtype=jnp.int32)
     mask_ext = tap_masks(positions(counts_row, down_index))
     down_mask = mask_ext[:down_frames]
-    with_rows = padded_2(clips[0], (("height", 1),), 1)
+    cells = clips[0]
+    scale = 1.0 / math.sqrt(
+        lax.axis_size("dp")
+        * clips.shape[0]
+        * down_frames
+        * lax.axis_size("tm")
+        * (rows_dev // 2)
+        * lax.axis_size("height")
+        * (columns_all // 2)
+    )
+    grads = (out_cotangent[0].astype(jnp.float32) * scale).astype(jnp.bfloat16)
+    head, grads_head = cells[:, :1], grads[:, 0:1]
+    joined = shifted(jnp.concatenate([head.reshape(-1), grads_head.reshape(-1)]), "height", -1)
+    below_cells = joined[: head.size].reshape(head.shape)
+    below = joined[head.size :].reshape(grads_head.shape)
+    above_cells = shifted(cells[:, rows_dev - 1 :], "height", 1)
+    with_rows = jnp.concatenate([above_cells, cells, below_cells], axis=1)
     earlier = shifted(with_rows, "tm", 1)
     input_ext = jnp.concatenate([earlier, with_rows], axis=0)
     pre_act = conv_layer(input_ext, conv_first, first_mask, frames_dev, 1, (1, 1))
@@ -122,19 +138,7 @@
     encoded = conv_layer(hidden_ext, conv_down, down_mask, down_frames, 2, (1, 0)).astype(
         jnp.bfloat16
     )
-    cells_all = (
-        lax.axis_size("dp")
-        * clips.shape[0]
-        * down_frames
-        * lax.axis_size("tm")
-        * (rows_dev // 2)
-        * lax.axis_size("height")
-        * (columns_all // 2)
-    )
-    scale = 1.0 / math.sqrt(cells_all)
-    grads = (out_cotangent[0].astype(jnp.float32) * scale).astype(jnp.bfloat16)
     down_local = weight_grad(hidden_ext, grads, down_mask, 2, (1, 0))
-    below = shifted(grads[:, 0:1], "height", -1)
     grads_rows = jnp.concatenate([grads, below], axis=1)
     grads_next = shifted(grads_rows, "tm", -1)
     grads_ext = jnp.concatenate([grads_rows, grads_next], axis=0)

time: 189 us -> 182 us (0.963)
  waiting for transfers between devices: 49.8 us -> 45.9 us
    ppermute x2 -> x0, starting transfers between devices: 7.11 us -> none  [the longest x1 5.19 us: padded_2(): lax.ppermute(head, axis, [((i + 1) % count, i) for i in range(ends)])]
    ppermute x5, starting transfers between devices: 32.3 us -> 36.3 us  [swap(): lax.ppermute(value, axis, [(i, i ^ bit) for i in range(lax.axis_size(axis...]
    ppermute x5, waiting for transfers between devices: 12 us -> 8.71 us  [swap(): lax.ppermute(value, axis, [(i, i ^ bit) for i in range(lax.axis_size(axis...]
    ppermute x5 -> x6, waiting for transfers between devices: 7.12 us -> 7.74 us  [shifted(): lax.ppermute(value, axis, [(source, source + steps) for source in range(l...]
    ppermute x5 -> x6, starting transfers between devices: 18.5 us -> 18.6 us  [shifted(): lax.ppermute(value, axis, [(source, source + steps) for source in range(l...]
  transfers between devices with their start and end apart: 16 -> 15, of which waited for: 11 -> 10; matrix products, arithmetic and copies ran while one was open for 13% -> 13% of each run, Pallas kernels for 0% -> 0%
where the time goes in v7:
time: 182 us; the launch traced here: 180 us
  starting transfers between devices  67.8 us (37%)
  waiting for transfers between devices  45.9 us (25%)
  blocking collectives  22.3 us (12%)
  matrix products  15.7 us (9%)
  other arithmetic  14.4 us (8%)
  local copies, waits for them, and re-layouts  10.4 us (6%)
  between operations  3.89 us (2%)
    ppermute x5, starting transfers between devices, swap(): lax.ppermute(value, axis, [(i, i ^ bit) for i in range(lax.axis_size(axis...  36.3 us
    ppermute x4, waiting for transfers between devices, swap_rows(): return lax.ppermute(value, ('dp', 'height'), pairs)  29.4 us
    all_gather x1, blocking collectives, reduce_gradients(): gathered = lax.all_gather(piece, 'height', axis=0, tiled=False)  22.3 us
    ppermute x6, starting transfers between devices, shifted(): lax.ppermute(value, axis, [(source, source + steps) for source in range(l...  18.6 us
    ppermute x4, starting transfers between devices, swap_rows(): return lax.ppermute(value, ('dp', 'height'), pairs)  12.9 us
    ppermute x5, waiting for transfers between devices, swap(): lax.ppermute(value, axis, [(i, i ^ bit) for i in range(lax.axis_size(axis...  8.71 us
    conv_general_dilated x6, matrix products, weight_grad(): lax.conv_general_dilated(frame_slab, masked, (1, 1), ((0, 0), pad_cols),...  8.4 us
    ppermute x6, waiting for transfers between devices, shifted(): lax.ppermute(value, axis, [(source, source + steps) for source in range(l...  7.74 us
  transfers between devices with their start and end apart: 15, of which 10 were waited for; matrix products, arithmetic and copies ran while one was open for 13% of the time, Pallas kernels for 0%

profile of v7, /device:TPU:6, one launch (start us, length us, event | category | flops | bytes accessed | tf_op | source)
XLA Modules:
  0.0 180.4 jit_solution(5248347835950629391)
XLA Ops:
  0.6 0.8 fusion.118
  1.4 1.2 copy.350
  2.8 5.2 %collective-permute-start.1 = (bf16[40960]{0:T(1024)(128)(2,1)S(1)}, bf16[40960]{0:T(1024)(128)(2,1)S(1)}, u32[]{:S(2)}, u32[]{:S(2)}) collective-permute-start(bf16[40960]{0:T(1024)(128)(2,1)S(1)} %pad_maximum_fusion.8), channel_id=1, source_target_pairs={{1,0},{2,1},{3,2},{4,3},{5,4},{6,5},{7,6},{8,7},{9,8},{10,9},{11,1... | collective-permute-start | bytes 245768 | tf_op jit(solution)/shard_map/ppermute | solution.py:30
  8.0 1.9 %collective-permute-start = (bf16[2,1,128,128]{3,0,2,1:T(2,128)(2,1)S(1)}, bf16[2,1,128,128]{3,0,2,1:T(2,128)(2,1)S(1)}, u32[]{:S(2)}, u32[]{:S(2)}) collective-permute-start(bf16[2,1,128,128]{3,0,2,1:T(2,128)(2,1)S(1)} %get-tuple-element.33), channel_id=1, source_target_pairs={{0,1},{1,2},{2,3},{3,4},{4,5},{5,6},{6,7},{7,8},{8,9},{9,10},{10,1... | collective-permute-start | bytes 196616 | tf_op jit(solution)/shard_map/ppermute | solution.py:30
  9.9 0.8 reduce-window_clone.1
  10.7 0.7 subtract_bitcast_fusion
  11.7 0.6 fusion.161
  14.3 1.4 broadcast_multiply_fusion.5
  15.7 0.6 slice.214
  16.2 0.7 slice.218
  17.0 0.6 pad_maximum_fusion.5
  17.6 4.0 %collective-permute-start.2 = (bf16[2,6,128,128]{3,0,2,1:T(2,128)(2,1)S(1)}, bf16[2,6,128,128]{3,0,2,1:T(2,128)(2,1)S(1)}, u32[]{:S(2)}, u32[]{:S(2)}) collective-permute-start(bf16[2,6,128,128]{3,0,2,1:T(2,128)(2,1)S(1)} %pad_maximum_fusion.5), channel_id=1, source_target_pairs={{0,16},{16,32},{32,48},{48,64},{64,80},{80,96},{96,112},{1,17},{17... | collective-permute-start | bytes 1179656 | tf_op jit(solution)/shard_map/ppermute | solution.py:30
  21.6 1.3 collective-permute-start.5
  22.9 0.6 fusion.168
  24.0 3.7 %collective-permute-done.5 = bf16[1,3,64,128]{3,2,1,0:T(8,128)(2,1)S(1)} collective-permute-done((bf16[1,3,64,128]{3,2,1,0:T(8,128)(2,1)S(1)}, bf16[1,3,64,128]{3,2,1,0:T(8,128)(2,1)S(1)}, u32[]{:S(2)}, u32[]{:S(2)}) %collective-permute-start.5) | collective-permute-done | bytes 49184 | tf_op jit(solution)/shard_map/ppermute | solution.py:30
  27.6 1.2 multiply_bitcast_fusion.1
  29.0 0.3 fusion.9
  29.7 0.3 convolution_select_fusion.5
  30.1 0.3 fusion.8
  30.6 0.3 pad.9
  31.0 1.0 pad_maximum_fusion.2
  32.0 0.3 pad.11
  32.6 0.8 fusion.6
  33.6 0.8 fusion.5
  34.6 1.0 add_divide_fusion
  35.7 2.4 %collective-permute-start.3 = (bf16[2,1,128,128]{3,0,2,1:T(2,128)(2,1)S(1)}, bf16[2,1,128,128]{3,0,2,1:T(2,128)(2,1)S(1)}, u32[]{:S(2)}, u32[]{:S(2)}) collective-permute-start(bf16[2,1,128,128]{3,0,2,1:T(2,128)(2,1)S(1)} %bitcast.307), channel_id=1, source_target_pairs={{0,1},{1,2},{2,3},{3,4},{4,5},{5,6},{6,7},{7,8},{8,9},{9,10},{10,1... | collective-permute-start | bytes 196616 | tf_op jit(solution)/shard_map/ppermute | solution.py:30
  38.9 2.0 %convolution_bitcast_fusion.3 = f32[1,3,3,128,128]{4,3,2,1,0:T(8,128)S(1)} fusion(bf16[2,6,128,128]{3,0,2,1:T(2,128)(2,1)S(1)} %pad_maximum_fusion.5, bf16[2,4,128,128]{3,2,1,0:T(8,128)(2,1)S(1)} %get-tuple-element.32), kind=kOutput, calls=%fused_computation.14 | convolution fusion | flops 300417024 | bytes 1245184 | tf_op jit(solution)/shard_map/conv_general_dilated | solution.py:57
  40.9 2.0 %convolution_bitcast_fusion.4 = f32[1,3,3,128,128]{4,3,2,1,0:T(8,128)S(1)} fusion(bf16[2,6,128,128]{3,0,2,1:T(2,128)(2,1)S(1)} %pad_maximum_fusion.2, bf16[2,4,128,128]{3,2,1,0:T(8,128)(2,1)S(1)} %get-tuple-element.31), kind=kOutput, calls=%fused_computation.15 | convolution fusion | flops 300417024 | bytes 1245184 | tf_op jit(solution)/shard_map/conv_general_dilated | solution.py:57
  42.9 2.0 %convolution_bitcast_fusion.5 = f32[1,3,3,128,128]{4,3,2,1,0:T(8,128)S(1)} fusion(bf16[2,6,128,128]{3,0,2,1:T(2,128)(2,1)S(1)} %collective-permute-done.2, bf16[2,4,128,128]{3,2,1,0:T(8,128)(2,1)S(1)} %get-tuple-element.20), kind=kOutput, calls=%fused_computation.16 | convolution fusion | flops 300417024 | bytes 1245184 | tf_op jit(solution)/shard_map/conv_general_dilated | solution.py:57
  45.8 0.4 pad_maximum_fusion.6
  46.3 3.8 %collective-permute-start.4 = (bf16[2,5,128,128]{3,0,2,1:T(2,128)(2,1)S(1)}, bf16[2,5,128,128]{3,0,2,1:T(2,128)(2,1)S(1)}, u32[]{:S(2)}, u32[]{:S(2)}) collective-permute-start(bf16[2,5,128,128]{3,0,2,1:T(2,128)(2,1)S(1)} %pad_maximum_fusion.6), channel_id=1, source_target_pairs={{0,16},{16,32},{32,48},{48,64},{64,80},{80,96},{96,112},{1,17},{17... | collective-permute-start | bytes 983048 | tf_op jit(solution)/shard_map/ppermute | solution.py:30
  50.1 0.4 slice_maximum_fusion
  50.5 0.9 convolution_bitcast_fusion
  51.4 4.1 %collective-permute-done.4 = bf16[2,5,128,128]{3,0,2,1:T(2,128)(2,1)S(1)} collective-permute-done((bf16[2,5,128,128]{3,0,2,1:T(2,128)(2,1)S(1)}, bf16[2,5,128,128]{3,0,2,1:T(2,128)(2,1)S(1)}, u32[]{:S(2)}, u32[]{:S(2)}) %collective-permute-start.4) | collective-permute-done | bytes 327712 | tf_op jit(solution)/shard_map/ppermute | solution.py:30
  55.5 0.5 fusion.159
  56.0 0.8 convolution_bitcast_fusion.1
  56.8 0.8 convolution_bitcast_fusion.2
  58.2 1.5 fusion.1
  59.8 1.9 %collective-permute-start.6 = (f32[2,2,2,2,2,112,128]{6,5,4,3,2,1,0:T(8,128)S(1)}, f32[2,2,2,2,2,112,128]{6,5,4,3,2,1,0:T(8,128)}, u32[]{:S(2)}, u32[]{:S(2)}) collective-permute-start(f32[2,2,2,2,2,112,128]{6,5,4,3,2,1,0:T(8,128)S(1)} %bitcast.280), channel_id=1, source_target_pairs={{0,128},{128,0},{256,384},{384,256},{1,129},{129,1},{257,385},{385... | collective-permute-start | bytes 5505032 | tf_op jit(solution)/shard_map/ppermute | solution.py:174
  61.8 3.8 %collective-permute-done.6 = f32[2,2,2,2,2,112,128]{6,5,4,3,2,1,0:T(8,128)} collective-permute-done((f32[2,2,2,2,2,112,128]{6,5,4,3,2,1,0:T(8,128)S(1)}, f32[2,2,2,2,2,112,128]{6,5,4,3,2,1,0:T(8,128)}, u32[]{:S(2)}, u32[]{:S(2)}) %collective-permute-start.6) | collective-permute-done | bytes 1835040 | tf_op jit(solution)/shard_map/ppermute | solution.py:174
  65.6 2.3 %bitcast_add_fusion = f32[2,2,2,2,2,112,128]{6,5,4,3,2,1,0:T(8,128)S(1)} fusion(f32[2,2,2,2,2,112,128]{6,5,4,3,2,1,0:T(8,128)} %collective-permute-done.6, f32[2,1,2,2,2,2,112,128]{7,6,5,4,3,1,0,2:T(8,128)} %get-tuple-element.22), kind=kLoop, calls=%fused_computation.7 | loop fusion | flops 458752 | bytes 5505024 | tf_op jit(solution)/shard_map/add | solution.py:216
  68.1 3.2 %collective-permute-start.7 = (f32[2,2,2,2,112,128]{5,4,3,2,1,0:T(8,128)S(1)}, f32[2,2,2,2,112,128]{5,4,3,2,1,0:T(8,128)}, u32[]{:S(2)}, u32[]{:S(2)}) collective-permute-start(f32[2,2,2,2,112,128]{5,4,3,2,1,0:T(8,128)S(1)} %bitcast_select_fusion), channel_id=1, source_target_pairs={{0,1},{1,0},{2,3},{3,2},{4,5},{5,4},{6,7},{7,6},{8,9},{9,8},{10,11... | collective-permute-start | bytes 2752520 | tf_op jit(solution)/shard_map/ppermute | solution.py:187
  71.3 12.2 %collective-permute-done.7 = f32[2,2,2,2,112,128]{5,4,3,2,1,0:T(8,128)} collective-permute-done((f32[2,2,2,2,112,128]{5,4,3,2,1,0:T(8,128)S(1)}, f32[2,2,2,2,112,128]{5,4,3,2,1,0:T(8,128)}, u32[]{:S(2)}, u32[]{:S(2)}) %collective-permute-start.7) | collective-permute-done | bytes 917536 | tf_op jit(solution)/shard_map/ppermute | solution.py:187
  83.5 1.3 fusion.19
  84.8 2.7 %collective-permute-start.8 = (f32[2,2,2,112,128]{4,3,2,1,0:T(8,128)S(1)}, f32[2,2,2,112,128]{4,3,2,1,0:T(8,128)S(1)}, u32[]{:S(2)}, u32[]{:S(2)}) collective-permute-start(f32[2,2,2,112,128]{4,3,2,1,0:T(8,128)S(1)} %bitcast_select_fusion.2), channel_id=1, source_target_pairs={{0,4},{1,5},{2,6},{3,7},{4,0},{5,1},{6,2},{7,3},{8,12},{9,13},{10,... | collective-permute-start | bytes 1376264 | tf_op jit(solution)/shard_map/ppermute | solution.py:187
  87.6 7.6 %collective-permute-done.8 = f32[2,2,2,112,128]{4,3,2,1,0:T(8,128)S(1)} collective-permute-done((f32[2,2,2,112,128]{4,3,2,1,0:T(8,128)S(1)}, f32[2,2,2,112,128]{4,3,2,1,0:T(8,128)S(1)}, u32[]{:S(2)}, u32[]{:S(2)}) %collective-permute-start.8) | collective-permute-done | bytes 458784 | tf_op jit(solution)/shard_map/ppermute | solution.py:187
  95.3 4.3 %collective-permute-start.9 = (f32[2,2,112,128]{3,2,1,0:T(8,128)S(1)}, f32[2,2,112,128]{3,2,1,0:T(8,128)S(1)}, u32[]{:S(2)}, u32[]{:S(2)}) collective-permute-start(f32[2,2,112,128]{3,2,1,0:T(8,128)S(1)} %bitcast_select_fusion.4), channel_id=1, source_target_pairs={{0,3},{1,2},{2,1},{3,0},{4,7},{5,6},{6,5},{7,4},{8,11},{9,10},{10,... | collective-permute-start | bytes 688136 | tf_op jit(solution)/shard_map/ppermute | solution.py:187
  99.7 4.8 %collective-permute-done.9 = f32[2,2,112,128]{3,2,1,0:T(8,128)S(1)} collective-permute-done((f32[2,2,112,128]{3,2,1,0:T(8,128)S(1)}, f32[2,2,112,128]{3,2,1,0:T(8,128)S(1)}, u32[]{:S(2)}, u32[]{:S(2)}) %collective-permute-start.9) | collective-permute-done | bytes 229408 | tf_op jit(solution)/shard_map/ppermute | solution.py:187
  104.5 2.7 %collective-permute-start.10 = (f32[2,112,128]{2,1,0:T(8,128)S(1)}, f32[2,112,128]{2,1,0:T(8,128)S(1)}, u32[]{:S(2)}, u32[]{:S(2)}) collective-permute-start(f32[2,112,128]{2,1,0:T(8,128)S(1)} %select_bitcast_fusion), channel_id=1, source_target_pairs={{0,12},{1,13},{2,14},{3,15},{4,8},{5,9},{6,10},{7,11},{8,4},{9,5},... | collective-permute-start | bytes 344072 | tf_op jit(solution)/shard_map/ppermute | solution.py:187
  107.6 4.9 %collective-permute-done.10 = f32[2,112,128]{2,1,0:T(8,128)S(1)} collective-permute-done((f32[2,112,128]{2,1,0:T(8,128)S(1)}, f32[2,112,128]{2,1,0:T(8,128)S(1)}, u32[]{:S(2)}, u32[]{:S(2)}) %collective-permute-start.10) | collective-permute-done | bytes 114720 | tf_op jit(solution)/shard_map/ppermute | solution.py:187
  112.5 14.5 %collective-permute-start.11 = (f32[112,128]{1,0:T(8,128)S(1)}, f32[112,128]{1,0:T(8,128)S(1)}, u32[]{:S(2)}, u32[]{:S(2)}) collective-permute-start(f32[112,128]{1,0:T(8,128)S(1)} %dynamic-slice_bitcast_fusion), channel_id=1, source_target_pairs={{0,256},{128,384},{256,0},{384,128},{1,257},{129,385},{257,1},{385... | collective-permute-start | bytes 172040 | tf_op jit(solution)/shard_map/ppermute | solution.py:174
  127.0 1.9 %fusion.10 = f32[2,8,9,128]{3,1,2,0:T(8,128)S(1)} fusion(bf16[3,3,3,128,128]{4,3,2,1,0:T(8,128)(2,1)} %param.10, bf16[5,1,7,2,128]{4,2,3,0,1:T(8,128)(2,1)S(1)} %slice.207, bf16[5,1,8,18,128]{4,2,3,0,1:T(8,128)(2,1)S(1)} %copy.266, f32[]{:T(128)} %bitcast.35, pred[8,9]{0,1:T(8,128)(4,1)S(1)} %copy-done.9), kind=kOutput, calls=%fused_computation.32 | convolution fusion | flops 43118592 | bytes 571464 | tf_op jit(solution)/shard_map/conv_general_dilated | solution.py:37
  129.2 4.9 %collective-permute-start.12 = (f32[112,128]{1,0:T(8,128)S(1)}, f32[112,128]{1,0:T(8,128)S(1)}, u32[]{:S(2)}, u32[]{:S(2)}) collective-permute-start(f32[112,128]{1,0:T(8,128)S(1)} %bitcast_add_fusion.1), channel_id=1, source_target_pairs={{0,16},{16,0},{32,48},{48,32},{64,80},{80,64},{96,112},{112,96},{1... | collective-permute-start | bytes 172040 | tf_op jit(solution)/shard_map/ppermute | solution.py:174
  134.1 0.9 fusion.11
  135.2 1.0 collective-permute-done.12
  136.2 5.6 %collective-permute-start.13 = (f32[112,128]{1,0:T(8,128)S(1)}, f32[112,128]{1,0:T(8,128)S(1)}, u32[]{:S(2)}, u32[]{:S(2)}) collective-permute-start(f32[112,128]{1,0:T(8,128)S(1)} %add.204), channel_id=1, source_target_pairs={{0,32},{16,48},{32,0},{48,16},{64,96},{80,112},{96,64},{112,80},{1... | collective-permute-start | bytes 172040 | tf_op jit(solution)/shard_map/ppermute | solution.py:174
  141.8 0.9 fusion.15
  142.7 1.2 collective-permute-done.13
  143.9 9.4 %collective-permute-start.14 = (f32[112,128]{1,0:T(8,128)S(1)}, f32[112,128]{1,0:T(8,128)S(1)}, u32[]{:S(2)}, u32[]{:S(2)}) collective-permute-start(f32[112,128]{1,0:T(8,128)S(1)} %add.205), channel_id=1, source_target_pairs={{0,64},{16,80},{32,96},{48,112},{64,0},{80,16},{96,32},{112,48},{1... | collective-permute-start | bytes 172040 | tf_op jit(solution)/shard_map/ppermute | solution.py:174
  153.4 0.6 copy.298
  154.0 2.7 %collective-permute-done.14 = f32[112,128]{1,0:T(8,128)S(1)} collective-permute-done((f32[112,128]{1,0:T(8,128)S(1)}, f32[112,128]{1,0:T(8,128)S(1)}, u32[]{:S(2)}, u32[]{:S(2)}) %collective-permute-start.14) | collective-permute-done | bytes 57376 | tf_op jit(solution)/shard_map/ppermute | solution.py:174
  156.7 22.3 %all-gather = bf16[1792,128]{1,0:T(8,128)(2,1)S(1)} all-gather(bf16[112,128]{1,0:T(8,128)(2,1)S(1)} %add_convert_fusion), channel_id=2, replica_groups=mesh['dp'=4,'tm'=8,'height'=16] {'height'}, dimensions={0}, use_global_device_ids=true | all-gather | bytes 487424 | tf_op jit(solution)/shard_map/all_gather | solution.py:240
  178.9 0.6 gather_fusion
  179.6 0.8 fusion.158
  (122 shorter events, 5.6 us)
Async XLA Ops:
  2.8 14.1 %collective-permute-start.1 = (bf16[40960]{0:T(1024)(128)(2,1)S(1)}, bf16[40960]{0:T(1024)(128)(2,1)S(1)}, u32[]{:S(2)}, u32[]{:S(2)}) collective-permute-start(bf16[40960]{0:T(1024)(128)(2,1)S(1)} %pad_maximum_fusion.8), channel_id=1, source_target_pairs={{1,0},{2,1},{3,2},{4,3},{5,4},{6,5},{7,6},{8,7},{9,8},{10,9},{11,1... | collective-permute-start | bytes 245768 | tf_op jit(solution)/shard_map/ppermute | solution.py:30
  8.0 9.0 %collective-permute-start = (bf16[2,1,128,128]{3,0,2,1:T(2,128)(2,1)S(1)}, bf16[2,1,128,128]{3,0,2,1:T(2,128)(2,1)S(1)}, u32[]{:S(2)}, u32[]{:S(2)}) collective-permute-start(bf16[2,1,128,128]{3,0,2,1:T(2,128)(2,1)S(1)} %get-tuple-element.33), channel_id=1, source_target_pairs={{0,1},{1,2},{2,3},{3,4},{4,5},{5,6},{6,7},{7,8},{8,9},{9,10},{10,1... | collective-permute-start | bytes 196616 | tf_op jit(solution)/shard_map/ppermute | solution.py:30
  17.6 11.4 %copy-start.5 = (bf16[3,3,3,128,128]{4,3,2,1,0:T(8,128)(2,1)S(1)}, bf16[3,3,3,128,128]{4,3,2,1,0:T(8,128)(2,1)}, u32[]{:S(2)}) copy-start(bf16[3,3,3,128,128]{4,3,2,1,0:T(8,128)(2,1)} %param.10) | copy-start | bytes 2654212
  17.6 11.4 %copy-start.8 = (pred[8,18]{0,1:T(8,128)(4,1)S(1)}, pred[8,18]{0,1:T(8,128)(4,1)}, u32[]{:S(2)}) copy-start(pred[8,18]{0,1:T(8,128)(4,1)} %constant.267) | copy-start | bytes 436
  17.6 12.9 %collective-permute-start.2 = (bf16[2,6,128,128]{3,0,2,1:T(2,128)(2,1)S(1)}, bf16[2,6,128,128]{3,0,2,1:T(2,128)(2,1)S(1)}, u32[]{:S(2)}, u32[]{:S(2)}) collective-permute-start(bf16[2,6,128,128]{3,0,2,1:T(2,128)(2,1)S(1)} %pad_maximum_fusion.5), channel_id=1, source_target_pairs={{0,16},{16,32},{32,48},{48,64},{64,80},{80,96},{96,112},{1,17},{17... | collective-permute-start | bytes 1179656 | tf_op jit(solution)/shard_map/ppermute | solution.py:30
  21.6 6.0 %collective-permute-start.5 = (bf16[1,3,64,128]{3,2,1,0:T(8,128)(2,1)S(1)}, bf16[1,3,64,128]{3,2,1,0:T(8,128)(2,1)S(1)}, u32[]{:S(2)}, u32[]{:S(2)}) collective-permute-start(bf16[1,3,64,128]{3,2,1,0:T(8,128)(2,1)S(1)} %pad_maximum_fusion.9), channel_id=1, source_target_pairs={{16,0},{32,16},{48,32},{64,48},{80,64},{96,80},{112,96},{17,1},{33... | collective-permute-start | bytes 147464 | tf_op jit(solution)/shard_map/ppermute | solution.py:30
  31.0 1.6 copy-start.4
  31.0 1.6 copy-start.7
  35.7 10.1 %collective-permute-start.3 = (bf16[2,1,128,128]{3,0,2,1:T(2,128)(2,1)S(1)}, bf16[2,1,128,128]{3,0,2,1:T(2,128)(2,1)S(1)}, u32[]{:S(2)}, u32[]{:S(2)}) collective-permute-start(bf16[2,1,128,128]{3,0,2,1:T(2,128)(2,1)S(1)} %bitcast.307), channel_id=1, source_target_pairs={{0,1},{1,2},{2,3},{3,4},{4,5},{5,6},{6,7},{7,8},{8,9},{9,10},{10,1... | collective-permute-start | bytes 196616 | tf_op jit(solution)/shard_map/ppermute | solution.py:30
  46.3 9.2 %collective-permute-start.4 = (bf16[2,5,128,128]{3,0,2,1:T(2,128)(2,1)S(1)}, bf16[2,5,128,128]{3,0,2,1:T(2,128)(2,1)S(1)}, u32[]{:S(2)}, u32[]{:S(2)}) collective-permute-start(bf16[2,5,128,128]{3,0,2,1:T(2,128)(2,1)S(1)} %pad_maximum_fusion.6), channel_id=1, source_target_pairs={{0,16},{16,32},{32,48},{48,64},{64,80},{80,96},{96,112},{1,17},{17... | collective-permute-start | bytes 983048 | tf_op jit(solution)/shard_map/ppermute | solution.py:30
  50.5 0.9 copy-start
  56.0 0.8 copy-start.2
  59.8 5.8 %collective-permute-start.6 = (f32[2,2,2,2,2,112,128]{6,5,4,3,2,1,0:T(8,128)S(1)}, f32[2,2,2,2,2,112,128]{6,5,4,3,2,1,0:T(8,128)}, u32[]{:S(2)}, u32[]{:S(2)}) collective-permute-start(f32[2,2,2,2,2,112,128]{6,5,4,3,2,1,0:T(8,128)S(1)} %bitcast.280), channel_id=1, source_target_pairs={{0,128},{128,0},{256,384},{384,256},{1,129},{129,1},{257,385},{385... | collective-permute-start | bytes 5505032 | tf_op jit(solution)/shard_map/ppermute | solution.py:174
  68.1 15.4 %collective-permute-start.7 = (f32[2,2,2,2,112,128]{5,4,3,2,1,0:T(8,128)S(1)}, f32[2,2,2,2,112,128]{5,4,3,2,1,0:T(8,128)}, u32[]{:S(2)}, u32[]{:S(2)}) collective-permute-start(f32[2,2,2,2,112,128]{5,4,3,2,1,0:T(8,128)S(1)} %bitcast_select_fusion), channel_id=1, source_target_pairs={{0,1},{1,0},{2,3},{3,2},{4,5},{5,4},{6,7},{7,6},{8,9},{9,8},{10,11... | collective-permute-start | bytes 2752520 | tf_op jit(solution)/shard_map/ppermute | solution.py:187
  84.8 10.4 %collective-permute-start.8 = (f32[2,2,2,112,128]{4,3,2,1,0:T(8,128)S(1)}, f32[2,2,2,112,128]{4,3,2,1,0:T(8,128)S(1)}, u32[]{:S(2)}, u32[]{:S(2)}) collective-permute-start(f32[2,2,2,112,128]{4,3,2,1,0:T(8,128)S(1)} %bitcast_select_fusion.2), channel_id=1, source_target_pairs={{0,4},{1,5},{2,6},{3,7},{4,0},{5,1},{6,2},{7,3},{8,12},{9,13},{10,... | collective-permute-start | bytes 1376264 | tf_op jit(solution)/shard_map/ppermute | solution.py:187
  87.6 19.7 %copy-start.3 = (s32[16]{0:T(128)S(1)}, s32[16]{0:T(128)}, u32[]{:S(2)}) copy-start(s32[16]{0:T(128)} %constant.271) | copy-start | bytes 196
  87.6 19.7 %copy-start.1 = (bf16[1,5,128,128]{3,0,2,1:T(2,128)(2,1)S(1)}, bf16[1,5,128,128]{3,0,2,1:T(2,128)(2,1)}, u32[]{:S(2)}) copy-start(bf16[1,5,128,128]{3,0,2,1:T(2,128)(2,1)} %copy-done) | copy-start | bytes 491524
  95.3 31.7 %copy-start.9 = (pred[8,9]{0,1:T(8,128)(4,1)S(1)}, pred[8,9]{0,1:T(8,128)(4,1)}, u32[]{:S(2)}) copy-start(pred[8,9]{0,1:T(8,128)(4,1)} %constant.261) | copy-start | bytes 220
  95.3 9.1 %collective-permute-start.9 = (f32[2,2,112,128]{3,2,1,0:T(8,128)S(1)}, f32[2,2,112,128]{3,2,1,0:T(8,128)S(1)}, u32[]{:S(2)}, u32[]{:S(2)}) collective-permute-start(f32[2,2,112,128]{3,2,1,0:T(8,128)S(1)} %bitcast_select_fusion.4), channel_id=1, source_target_pairs={{0,3},{1,2},{2,1},{3,0},{4,7},{5,6},{6,5},{7,4},{8,11},{9,10},{10,... | collective-permute-start | bytes 688136 | tf_op jit(solution)/shard_map/ppermute | solution.py:187
  104.5 7.9 %collective-permute-start.10 = (f32[2,112,128]{2,1,0:T(8,128)S(1)}, f32[2,112,128]{2,1,0:T(8,128)S(1)}, u32[]{:S(2)}, u32[]{:S(2)}) collective-permute-start(f32[2,112,128]{2,1,0:T(8,128)S(1)} %select_bitcast_fusion), channel_id=1, source_target_pairs={{0,12},{1,13},{2,14},{3,15},{4,8},{5,9},{6,10},{7,11},{8,4},{9,5},... | collective-permute-start | bytes 344072 | tf_op jit(solution)/shard_map/ppermute | solution.py:187
  107.5 26.6 %copy-start.6 = (bf16[3,3,3,128,128]{4,3,2,1,0:T(8,128)(2,1)S(1)}, bf16[3,3,3,128,128]{4,3,2,1,0:T(8,128)(2,1)}, u32[]{:S(2)}) copy-start(bf16[3,3,3,128,128]{4,3,2,1,0:T(8,128)(2,1)} %param.10) | copy-start | bytes 2654212
  112.5 16.7 %collective-permute-start.11 = (f32[112,128]{1,0:T(8,128)S(1)}, f32[112,128]{1,0:T(8,128)S(1)}, u32[]{:S(2)}, u32[]{:S(2)}) collective-permute-start(f32[112,128]{1,0:T(8,128)S(1)} %dynamic-slice_bitcast_fusion), channel_id=1, source_target_pairs={{0,256},{128,384},{256,0},{384,128},{1,257},{129,385},{257,1},{385... | collective-permute-start | bytes 172040 | tf_op jit(solution)/shard_map/ppermute | solution.py:174
  129.2 7.0 %collective-permute-start.12 = (f32[112,128]{1,0:T(8,128)S(1)}, f32[112,128]{1,0:T(8,128)S(1)}, u32[]{:S(2)}, u32[]{:S(2)}) collective-permute-start(f32[112,128]{1,0:T(8,128)S(1)} %bitcast_add_fusion.1), channel_id=1, source_target_pairs={{0,16},{16,0},{32,48},{48,32},{64,80},{80,64},{96,112},{112,96},{1... | collective-permute-start | bytes 172040 | tf_op jit(solution)/shard_map/ppermute | solution.py:174
  136.2 7.7 %collective-permute-start.13 = (f32[112,128]{1,0:T(8,128)S(1)}, f32[112,128]{1,0:T(8,128)S(1)}, u32[]{:S(2)}, u32[]{:S(2)}) collective-permute-start(f32[112,128]{1,0:T(8,128)S(1)} %add.204), channel_id=1, source_target_pairs={{0,32},{16,48},{32,0},{48,16},{64,96},{80,112},{96,64},{112,80},{1... | collective-permute-start | bytes 172040 | tf_op jit(solution)/shard_map/ppermute | solution.py:174
  143.9 12.7 %collective-permute-start.14 = (f32[112,128]{1,0:T(8,128)S(1)}, f32[112,128]{1,0:T(8,128)S(1)}, u32[]{:S(2)}, u32[]{:S(2)}) collective-permute-start(f32[112,128]{1,0:T(8,128)S(1)} %add.205), channel_id=1, source_target_pairs={{0,64},{16,80},{32,96},{48,112},{64,0},{80,16},{96,32},{112,48},{1... | collective-permute-start | bytes 172040 | tf_op jit(solution)/shard_map/ppermute | solution.py:174

commit v8 on v7

--- a/solution.py
+++ b/solution.py
@@ -125,14 +125,17 @@
     joined = shifted(jnp.concatenate([head.reshape(-1), grads_head.reshape(-1)]), "height", -1)
     below_cells = joined[: head.size].reshape(head.shape)
     below = joined[head.size :].reshape(grads_head.shape)
-    above_cells = shifted(cells[:, rows_dev - 1 :], "height", 1)
+    above_cells = shifted(cells[:, rows_dev - 2 :], "height", 1)
     with_rows = jnp.concatenate([above_cells, cells, below_cells], axis=1)
     earlier = shifted(with_rows, "tm", 1)
-    input_ext = jnp.concatenate([earlier, with_rows], axis=0)
-    pre_act = conv_layer(input_ext, conv_first, first_mask, frames_dev, 1, (1, 1))
-    hidden = jax.nn.silu(pre_act).astype(jnp.bfloat16)
-    above = shifted(hidden[:, rows_dev - 1 :], "height", 1)
-    hidden_rows = jnp.concatenate([above, hidden], axis=1)
+    wide_ext = jnp.concatenate([earlier, with_rows], axis=0)
+    wide_pre = conv_layer(wide_ext, conv_first, first_mask, frames_dev, 1, (1, 1))
+    row_valid = jnp.arange(rows_dev + 1) >= jnp.where(lax.axis_index("height") == 0, 1, 0)
+    hidden_rows = jnp.where(
+        row_valid[None, :, None, None], jax.nn.silu(wide_pre).astype(jnp.bfloat16), 0
+    ).astype(jnp.bfloat16)
+    pre_act = wide_pre[:, 1:]
+    input_ext = wide_ext[:, 1:]
     hidden_past = shifted(hidden_rows, "tm", 1)
     hidden_ext = jnp.concatenate([hidden_past, hidden_rows], axis=0)
     encoded = conv_layer(hidden_ext, conv_down, down_mask, down_frames, 2, (1, 0)).astype(

time: 182 us -> 182 us (level)
  starting transfers between devices: 67.8 us -> 63.3 us
  local copies, waits for them, and re-layouts: 10.4 us -> 14.4 us
    ppermute x6 -> x5, waiting for transfers between devices: 7.74 us -> 4.87 us  [shifted(): lax.ppermute(value, axis, [(source, source + steps) for source in range(l...]
    ppermute x5, starting transfers between devices: 36.3 us -> 33.7 us  [swap(): lax.ppermute(value, axis, [(i, i ^ bit) for i in range(lax.axis_size(axis...]
    mul x4 -> x7, local copies, waits for them, and re-layouts: 0.42 us -> 2.42 us  [conv_layer(): tap_term = tap_term * tap_mask[:, tap_time][:, None, None, None]]
    unnamed x30 -> x41, local copies, waits for them, and re-layouts: 2.46 us -> 3.74 us
    ppermute x6 -> x5, starting transfers between devices: 18.6 us -> 17.6 us  [shifted(): lax.ppermute(value, axis, [(source, source + steps) for source in range(l...]
  transfers between devices with their start and end apart: 15 -> 14, of which waited for: 10 -> 10; matrix products, arithmetic and copies ran while one was open for 13% -> 14% of each run, Pallas kernels for 0% -> 0%
where the time goes in v8:
time: 182 us; the launch traced here: 180 us
  starting transfers between devices  63.3 us (35%)
  waiting for transfers between devices  44.9 us (25%)
  blocking collectives  23.3 us (13%)
  matrix products  17.4 us (10%)
  local copies, waits for them, and re-layouts  14.4 us (8%)
  other arithmetic  13.1 us (7%)
  between operations  3.93 us (2%)
    ppermute x5, starting transfers between devices, swap(): lax.ppermute(value, axis, [(i, i ^ bit) for i in range(lax.axis_size(axis...  33.7 us
    ppermute x4, waiting for transfers between devices, swap_rows(): return lax.ppermute(value, ('dp', 'height'), pairs)  30.6 us
    all_gather x1, blocking collectives, reduce_gradients(): gathered = lax.all_gather(piece, 'height', axis=0, tiled=False)  23.3 us
    ppermute x5, starting transfers between devices, shifted(): lax.ppermute(value, axis, [(source, source + steps) for source in range(l...  17.6 us
    ppermute x4, starting transfers between devices, swap_rows(): return lax.ppermute(value, ('dp', 'height'), pairs)  12 us
    conv_general_dilated x6, matrix products, weight_grad(): lax.conv_general_dilated(frame_slab, masked, (1, 1), ((0, 0), pad_cols),...  9.51 us
    ppermute x5, waiting for transfers between devices, swap(): lax.ppermute(value, axis, [(i, i ^ bit) for i in range(lax.axis_size(axis...  9.38 us
    conv_general_dilated x6, matrix products, conv_layer(): lax.conv_general_dilated(frame_slab, weight[tap_time], (stride, stride),...  6.87 us
  transfers between devices with their start and end apart: 14, of which 10 were waited for; matrix products, arithmetic and copies ran while one was open for 14% of the time, Pallas kernels for 0%

profile of v8, /device:TPU:6, one launch (start us, length us, event | category | flops | bytes accessed | tf_op | source)
XLA Modules:
  0.0 180.3 jit_solution(10429861230778668223)
XLA Ops:
  0.6 0.8 fusion.124
  1.4 1.2 copy.338
  2.7 5.2 %collective-permute-start.1 = (bf16[40960]{0:T(1024)(128)(2,1)S(1)}, bf16[40960]{0:T(1024)(128)(2,1)S(1)}, u32[]{:S(2)}, u32[]{:S(2)}) collective-permute-start(bf16[40960]{0:T(1024)(128)(2,1)S(1)} %pad_maximum_fusion.6), channel_id=1, source_target_pairs={{1,0},{2,1},{3,2},{4,3},{5,4},{6,5},{7,6},{8,7},{9,8},{10,9},{11,1... | collective-permute-start | bytes 245768 | tf_op jit(solution)/shard_map/ppermute | solution.py:30
  8.0 1.9 %collective-permute-start = (bf16[2,2,128,128]{3,0,2,1:T(2,128)(2,1)S(1)}, bf16[2,2,128,128]{3,0,2,1:T(2,128)(2,1)S(1)}, u32[]{:S(2)}, u32[]{:S(2)}) collective-permute-start(bf16[2,2,128,128]{3,0,2,1:T(2,128)(2,1)S(1)} %slice.201), channel_id=1, source_target_pairs={{0,1},{1,2},{2,3},{3,4},{4,5},{5,6},{6,7},{7,8},{8,9},{9,10},{10,1... | collective-permute-start | bytes 393224 | tf_op jit(solution)/shard_map/ppermute | solution.py:30
  10.0 0.8 reduce-window_clone.1
  10.8 0.7 subtract_bitcast_fusion
  11.9 1.0 reshape.218
  13.1 1.0 reshape.212
  14.3 0.5 fusion.167
  14.8 0.6 slice.222
  15.4 0.7 slice.226
  18.0 0.6 broadcast_multiply_fusion.5
  18.8 1.3 collective-permute-start.4
  20.1 0.7 fusion.173
  20.8 0.7 pad_maximum_fusion.2
  21.5 0.4 pad.13
  22.0 4.6 %collective-permute-start.2 = (bf16[2,7,128,128]{3,0,2,1:T(2,128)(2,1)S(1)}, bf16[2,7,128,128]{3,0,2,1:T(2,128)(2,1)S(1)}, u32[]{:S(2)}, u32[]{:S(2)}) collective-permute-start(bf16[2,7,128,128]{3,0,2,1:T(2,128)(2,1)S(1)} %pad_maximum_fusion.2), channel_id=1, source_target_pairs={{0,16},{16,32},{32,48},{48,64},{64,80},{80,96},{96,112},{1,17},{17... | collective-permute-start | bytes 1376264 | tf_op jit(solution)/shard_map/ppermute | solution.py:30
  26.6 1.3 multiply_bitcast_fusion.1
  30.0 1.1 fusion.2
  31.1 4.9 %collective-permute-done.2 = bf16[2,7,128,128]{3,0,2,1:T(2,128)(2,1)S(1)} collective-permute-done((bf16[2,7,128,128]{3,0,2,1:T(2,128)(2,1)S(1)}, bf16[2,7,128,128]{3,0,2,1:T(2,128)(2,1)S(1)}, u32[]{:S(2)}, u32[]{:S(2)}) %collective-permute-start.2) | collective-permute-done | bytes 458784 | tf_op jit(solution)/shard_map/ppermute | solution.py:30
  35.9 0.9 maximum_maximum_fusion
  36.9 0.5 slice_bitcast_fusion
  37.4 0.4 pad.11
  37.9 0.4 pad.9
  38.6 1.1 fusion.3
  39.7 2.0 %fusion.50 = (bf16[5,16,17,128]{3,1,2,0:T(8,128)(2,1)S(1)}, f32[5,16,17,128]{3,1,2,0:T(8,128)}) fusion(pred[5]{0:T(512)(128)(4,1)S(1)} %iota_compare_fusion.3, f32[5,16,17,128]{3,1,2,0:T(8,128)S(1)} %fusion.2, f32[5,16,17,128]{3,1,2,0:T(8,128)S(1)} %fusion.3, f32[5,16,17,128]{3,2,1,0:T(8,128)S(1)} %reshape.206, ...), kind=kOutput, calls=%fused_computation.86 | convolution fusion | flops 404455424 | bytes 4263424 | tf_op jit(solution)/shard_map/conv_general_dilated | solution.py:37
  42.0 0.3 copy.337
  42.3 4.6 %collective-permute-start.3 = (bf16[2,5,128,128]{3,0,2,1:T(2,128)(2,1)S(1)}, bf16[2,5,128,128]{3,0,2,1:T(2,128)(2,1)S(1)}, u32[]{:S(2)}, u32[]{:S(2)}) collective-permute-start(bf16[2,5,128,128]{3,0,2,1:T(2,128)(2,1)S(1)} %bitcast.287), channel_id=1, source_target_pairs={{0,16},{16,32},{32,48},{48,64},{64,80},{80,96},{96,112},{1,17},{17... | collective-permute-start | bytes 983048 | tf_op jit(solution)/shard_map/ppermute | solution.py:30
  47.9 0.7 copy-done.5
  48.6 2.1 %convolution_bitcast_fusion.3 = f32[1,3,3,128,128]{4,3,2,1,0:T(8,128)S(1)} fusion(bf16[2,7,128,128]{3,0,2,1:T(2,128)(2,1)S(1)} %copy-done.5, bf16[2,4,128,128]{3,2,1,0:T(8,128)(2,1)S(1)} %get-tuple-element.31), kind=kOutput, calls=%fused_computation.22 | convolution fusion | flops 300417024 | bytes 1310720 | tf_op jit(solution)/shard_map/conv_general_dilated | solution.py:57
  50.7 3.0 %convolution_bitcast_fusion.4 = f32[1,3,3,128,128]{4,3,2,1,0:T(8,128)S(1)} fusion(bf16[2,7,128,128]{3,0,2,1:T(2,128)(2,1)S(1)} %collective-permute-done.2, bf16[2,1,128,128]{3,0,2,1:T(2,128)(2,1)S(1)} %copy.239, bf16[2,4,128,128]{3,0,2,1:T(2,128)(2,1)S(1)} %bitcast.277, bf16[2,2,128,128]{3,0,2,1:T(2,128)(2,1)S(1)} %collective-permute-done, ...), kind=kOutput, calls=%fused_computation.23 | convolution fusion | flops 301989888 | bytes 1769472 | tf_op jit(solution)/shard_map/conv_general_dilated | solution.py:57
  53.7 2.0 %convolution_bitcast_fusion.5 = f32[1,3,3,128,128]{4,3,2,1,0:T(8,128)S(1)} fusion(bf16[2,7,128,128]{3,0,2,1:T(2,128)(2,1)S(1)} %collective-permute-done.2, bf16[2,4,128,128]{3,2,1,0:T(8,128)(2,1)S(1)} %get-tuple-element.20), kind=kOutput, calls=%fused_computation.24 | convolution fusion | flops 300417024 | bytes 1310720 | tf_op jit(solution)/shard_map/conv_general_dilated | solution.py:57
  55.7 0.8 convolution_bitcast_fusion
  57.0 0.5 fusion.166
  57.5 0.8 convolution_bitcast_fusion.1
  58.3 0.8 convolution_bitcast_fusion.2
  59.6 1.5 fusion.1
  61.2 1.9 %collective-permute-start.5 = (f32[2,2,2,2,2,112,128]{6,5,4,3,2,1,0:T(8,128)S(1)}, f32[2,2,2,2,2,112,128]{6,5,4,3,2,1,0:T(8,128)}, u32[]{:S(2)}, u32[]{:S(2)}) collective-permute-start(f32[2,2,2,2,2,112,128]{6,5,4,3,2,1,0:T(8,128)S(1)} %bitcast.284), channel_id=1, source_target_pairs={{0,128},{128,0},{256,384},{384,256},{1,129},{129,1},{257,385},{385... | collective-permute-start | bytes 5505032 | tf_op jit(solution)/shard_map/ppermute | solution.py:177
  63.2 3.8 %collective-permute-done.5 = f32[2,2,2,2,2,112,128]{6,5,4,3,2,1,0:T(8,128)} collective-permute-done((f32[2,2,2,2,2,112,128]{6,5,4,3,2,1,0:T(8,128)S(1)}, f32[2,2,2,2,2,112,128]{6,5,4,3,2,1,0:T(8,128)}, u32[]{:S(2)}, u32[]{:S(2)}) %collective-permute-start.5) | collective-permute-done | bytes 1835040 | tf_op jit(solution)/shard_map/ppermute | solution.py:177
  67.1 2.3 %bitcast_add_fusion = f32[2,2,2,2,2,112,128]{6,5,4,3,2,1,0:T(8,128)S(1)} fusion(f32[2,2,2,2,2,112,128]{6,5,4,3,2,1,0:T(8,128)} %collective-permute-done.5, f32[2,1,2,2,2,2,112,128]{7,6,5,4,3,1,0,2:T(8,128)} %get-tuple-element.22), kind=kLoop, calls=%fused_computation.7 | loop fusion | flops 458752 | bytes 5505024 | tf_op jit(solution)/shard_map/add | solution.py:219
  69.5 1.9 %collective-permute-start.6 = (f32[2,2,2,2,112,128]{5,4,3,2,1,0:T(8,128)S(1)}, f32[2,2,2,2,112,128]{5,4,3,2,1,0:T(8,128)}, u32[]{:S(2)}, u32[]{:S(2)}) collective-permute-start(f32[2,2,2,2,112,128]{5,4,3,2,1,0:T(8,128)S(1)} %bitcast_select_fusion), channel_id=1, source_target_pairs={{0,1},{1,0},{2,3},{3,2},{4,5},{5,4},{6,7},{7,6},{8,9},{9,8},{10,11... | collective-permute-start | bytes 2752520 | tf_op jit(solution)/shard_map/ppermute | solution.py:190
  71.4 13.4 %collective-permute-done.6 = f32[2,2,2,2,112,128]{5,4,3,2,1,0:T(8,128)} collective-permute-done((f32[2,2,2,2,112,128]{5,4,3,2,1,0:T(8,128)S(1)}, f32[2,2,2,2,112,128]{5,4,3,2,1,0:T(8,128)}, u32[]{:S(2)}, u32[]{:S(2)}) %collective-permute-start.6) | collective-permute-done | bytes 917536 | tf_op jit(solution)/shard_map/ppermute | solution.py:190
  84.9 1.3 fusion.19
  86.3 2.4 %collective-permute-start.7 = (f32[2,2,2,112,128]{4,3,2,1,0:T(8,128)S(1)}, f32[2,2,2,112,128]{4,3,2,1,0:T(8,128)S(1)}, u32[]{:S(2)}, u32[]{:S(2)}) collective-permute-start(f32[2,2,2,112,128]{4,3,2,1,0:T(8,128)S(1)} %bitcast_select_fusion.2), channel_id=1, source_target_pairs={{0,4},{1,5},{2,6},{3,7},{4,0},{5,1},{6,2},{7,3},{8,12},{9,13},{10,... | collective-permute-start | bytes 1376264 | tf_op jit(solution)/shard_map/ppermute | solution.py:190
  88.8 7.9 %collective-permute-done.7 = f32[2,2,2,112,128]{4,3,2,1,0:T(8,128)S(1)} collective-permute-done((f32[2,2,2,112,128]{4,3,2,1,0:T(8,128)S(1)}, f32[2,2,2,112,128]{4,3,2,1,0:T(8,128)S(1)}, u32[]{:S(2)}, u32[]{:S(2)}) %collective-permute-start.7) | collective-permute-done | bytes 458784 | tf_op jit(solution)/shard_map/ppermute | solution.py:190
  96.8 4.4 %collective-permute-start.8 = (f32[2,2,112,128]{3,2,1,0:T(8,128)S(1)}, f32[2,2,112,128]{3,2,1,0:T(8,128)S(1)}, u32[]{:S(2)}, u32[]{:S(2)}) collective-permute-start(f32[2,2,112,128]{3,2,1,0:T(8,128)S(1)} %bitcast_select_fusion.4), channel_id=1, source_target_pairs={{0,3},{1,2},{2,1},{3,0},{4,7},{5,6},{6,5},{7,4},{8,11},{9,10},{10,... | collective-permute-start | bytes 688136 | tf_op jit(solution)/shard_map/ppermute | solution.py:190
  101.2 4.8 %collective-permute-done.8 = f32[2,2,112,128]{3,2,1,0:T(8,128)S(1)} collective-permute-done((f32[2,2,112,128]{3,2,1,0:T(8,128)S(1)}, f32[2,2,112,128]{3,2,1,0:T(8,128)S(1)}, u32[]{:S(2)}, u32[]{:S(2)}) %collective-permute-start.8) | collective-permute-done | bytes 229408 | tf_op jit(solution)/shard_map/ppermute | solution.py:190
  106.1 3.2 %collective-permute-start.9 = (f32[2,112,128]{2,1,0:T(8,128)S(1)}, f32[2,112,128]{2,1,0:T(8,128)S(1)}, u32[]{:S(2)}, u32[]{:S(2)}) collective-permute-start(f32[2,112,128]{2,1,0:T(8,128)S(1)} %select_bitcast_fusion), channel_id=1, source_target_pairs={{0,12},{1,13},{2,14},{3,15},{4,8},{5,9},{6,10},{7,11},{8,4},{9,5},... | collective-permute-start | bytes 344072 | tf_op jit(solution)/shard_map/ppermute | solution.py:190
  109.6 4.5 %collective-permute-done.9 = f32[2,112,128]{2,1,0:T(8,128)S(1)} collective-permute-done((f32[2,112,128]{2,1,0:T(8,128)S(1)}, f32[2,112,128]{2,1,0:T(8,128)S(1)}, u32[]{:S(2)}, u32[]{:S(2)}) %collective-permute-start.9) | collective-permute-done | bytes 114720 | tf_op jit(solution)/shard_map/ppermute | solution.py:190
  114.2 15.5 %collective-permute-start.10 = (f32[112,128]{1,0:T(8,128)S(1)}, f32[112,128]{1,0:T(8,128)S(1)}, u32[]{:S(2)}, u32[]{:S(2)}) collective-permute-start(f32[112,128]{1,0:T(8,128)S(1)} %dynamic-slice_bitcast_fusion), channel_id=1, source_target_pairs={{0,256},{128,384},{256,0},{384,128},{1,257},{129,385},{257,1},{385... | collective-permute-start | bytes 172040 | tf_op jit(solution)/shard_map/ppermute | solution.py:177
  129.7 0.9 fusion.10
  130.9 1.4 collective-permute-done.10
  132.2 3.5 %collective-permute-start.11 = (f32[112,128]{1,0:T(8,128)S(1)}, f32[112,128]{1,0:T(8,128)S(1)}, u32[]{:S(2)}, u32[]{:S(2)}) collective-permute-start(f32[112,128]{1,0:T(8,128)S(1)} %bitcast_add_fusion.1), channel_id=1, source_target_pairs={{0,16},{16,0},{32,48},{48,32},{64,80},{80,64},{96,112},{112,96},{1... | collective-permute-start | bytes 172040 | tf_op jit(solution)/shard_map/ppermute | solution.py:177
  135.8 0.9 fusion.11
  136.9 1.4 collective-permute-done.11
  138.3 5.0 %collective-permute-start.12 = (f32[112,128]{1,0:T(8,128)S(1)}, f32[112,128]{1,0:T(8,128)S(1)}, u32[]{:S(2)}, u32[]{:S(2)}) collective-permute-start(f32[112,128]{1,0:T(8,128)S(1)} %add.207), channel_id=1, source_target_pairs={{0,32},{16,48},{32,0},{48,16},{64,96},{80,112},{96,64},{112,80},{1... | collective-permute-start | bytes 172040 | tf_op jit(solution)/shard_map/ppermute | solution.py:177
  143.3 0.9 fusion.15
  144.3 1.2 collective-permute-done.12
  145.5 7.7 %collective-permute-start.13 = (f32[112,128]{1,0:T(8,128)S(1)}, f32[112,128]{1,0:T(8,128)S(1)}, u32[]{:S(2)}, u32[]{:S(2)}) collective-permute-start(f32[112,128]{1,0:T(8,128)S(1)} %add.208), channel_id=1, source_target_pairs={{0,64},{16,80},{32,96},{48,112},{64,0},{80,16},{96,32},{112,48},{1... | collective-permute-start | bytes 172040 | tf_op jit(solution)/shard_map/ppermute | solution.py:177
  153.2 0.6 copy.288
  153.9 1.6 collective-permute-done.13
  155.5 23.3 %all-gather = bf16[1792,128]{1,0:T(8,128)(2,1)S(1)} all-gather(bf16[112,128]{1,0:T(8,128)(2,1)S(1)} %add_convert_fusion), channel_id=2, replica_groups=mesh['dp'=4,'tm'=8,'height'=16] {'height'}, dimensions={0}, use_global_device_ids=true | all-gather | bytes 487424 | tf_op jit(solution)/shard_map/all_gather | solution.py:243
  178.8 0.6 gather_fusion
  179.5 0.8 fusion.165
  (133 shorter events, 6.7 us)
Async XLA Ops:
  2.7 15.9 %collective-permute-start.1 = (bf16[40960]{0:T(1024)(128)(2,1)S(1)}, bf16[40960]{0:T(1024)(128)(2,1)S(1)}, u32[]{:S(2)}, u32[]{:S(2)}) collective-permute-start(bf16[40960]{0:T(1024)(128)(2,1)S(1)} %pad_maximum_fusion.6), channel_id=1, source_target_pairs={{1,0},{2,1},{3,2},{4,3},{5,4},{6,5},{7,6},{8,7},{9,8},{10,9},{11,1... | collective-permute-start | bytes 245768 | tf_op jit(solution)/shard_map/ppermute | solution.py:30
  8.0 12.0 %collective-permute-start = (bf16[2,2,128,128]{3,0,2,1:T(2,128)(2,1)S(1)}, bf16[2,2,128,128]{3,0,2,1:T(2,128)(2,1)S(1)}, u32[]{:S(2)}, u32[]{:S(2)}) collective-permute-start(bf16[2,2,128,128]{3,0,2,1:T(2,128)(2,1)S(1)} %slice.201), channel_id=1, source_target_pairs={{0,1},{1,2},{2,3},{3,4},{4,5},{5,6},{6,7},{7,8},{8,9},{9,10},{10,1... | collective-permute-start | bytes 393224 | tf_op jit(solution)/shard_map/ppermute | solution.py:30
  13.1 4.9 %copy-start.7 = (bf16[1,1,2,64,128]{4,3,2,1,0:T(8,128)(2,1)S(1)}, bf16[1,1,2,64,128]{4,3,2,1,0:T(8,128)(2,1)}, u32[]{:S(2)}) copy-start(bf16[1,1,2,64,128]{4,3,2,1,0:T(8,128)(2,1)} %param.11) | copy-start | bytes 98308
  18.8 7.8 %collective-permute-start.4 = (bf16[1,3,64,128]{3,2,1,0:T(8,128)(2,1)S(1)}, bf16[1,3,64,128]{3,2,1,0:T(8,128)(2,1)S(1)}, u32[]{:S(2)}, u32[]{:S(2)}) collective-permute-start(bf16[1,3,64,128]{3,2,1,0:T(8,128)(2,1)S(1)} %pad_maximum_fusion.7), channel_id=1, source_target_pairs={{16,0},{32,16},{48,32},{64,48},{80,64},{96,80},{112,96},{17,1},{33... | collective-permute-start | bytes 147464 | tf_op jit(solution)/shard_map/ppermute | solution.py:30
  20.8 7.2 %copy-start.11 = (bf16[3,3,3,128,128]{4,3,2,1,0:T(8,128)(2,1)S(1)}, bf16[3,3,3,128,128]{4,3,2,1,0:T(8,128)(2,1)}, u32[]{:S(2)}) copy-start(bf16[3,3,3,128,128]{4,3,2,1,0:T(8,128)(2,1)} %param.10) | copy-start | bytes 2654212
  20.8 7.2 %copy-start.14 = (pred[8,18]{0,1:T(8,128)(4,1)S(1)}, pred[8,18]{0,1:T(8,128)(4,1)}, u32[]{:S(2)}) copy-start(pred[8,18]{0,1:T(8,128)(4,1)} %constant.269) | copy-start | bytes 436
  21.5 6.9 %copy-start.4 = (bf16[2,7,128,128]{3,0,2,1:T(2,128)(2,1)}, bf16[2,7,128,128]{3,0,2,1:T(2,128)(2,1)S(1)}, u32[]{:S(2)}) copy-start(bf16[2,7,128,128]{3,0,2,1:T(2,128)(2,1)S(1)} %pad_maximum_fusion.2) | copy-start | bytes 1376260
  22.0 13.9 %collective-permute-start.2 = (bf16[2,7,128,128]{3,0,2,1:T(2,128)(2,1)S(1)}, bf16[2,7,128,128]{3,0,2,1:T(2,128)(2,1)S(1)}, u32[]{:S(2)}, u32[]{:S(2)}) collective-permute-start(bf16[2,7,128,128]{3,0,2,1:T(2,128)(2,1)S(1)} %pad_maximum_fusion.2), channel_id=1, source_target_pairs={{0,16},{16,32},{32,48},{48,64},{64,80},{80,96},{96,112},{1,17},{17... | collective-permute-start | bytes 1376264 | tf_op jit(solution)/shard_map/ppermute | solution.py:30
  28.5 1.2 copy-start.3
  28.5 1.5 copy-start.10
  28.5 1.4 copy-start.13
  37.4 1.2 copy-start.2
  41.7 5.2 %copy-start.6 = (f32[5,16,17,128]{3,1,2,0:T(8,128)S(1)}, f32[5,16,17,128]{3,1,2,0:T(8,128)}, u32[]{:S(2)}) copy-start(f32[5,16,17,128]{3,1,2,0:T(8,128)} %get-tuple-element.54) | copy-start | bytes 2088964
  42.3 14.6 %collective-permute-start.3 = (bf16[2,5,128,128]{3,0,2,1:T(2,128)(2,1)S(1)}, bf16[2,5,128,128]{3,0,2,1:T(2,128)(2,1)S(1)}, u32[]{:S(2)}, u32[]{:S(2)}) collective-permute-start(bf16[2,5,128,128]{3,0,2,1:T(2,128)(2,1)S(1)} %bitcast.287), channel_id=1, source_target_pairs={{0,16},{16,32},{32,48},{48,64},{64,80},{80,96},{96,112},{1,17},{17... | collective-permute-start | bytes 983048 | tf_op jit(solution)/shard_map/ppermute | solution.py:30
  47.6 1.0 copy-start.5
  57.5 0.9 copy-start
  57.5 0.9 copy-start.8
  61.2 5.8 %collective-permute-start.5 = (f32[2,2,2,2,2,112,128]{6,5,4,3,2,1,0:T(8,128)S(1)}, f32[2,2,2,2,2,112,128]{6,5,4,3,2,1,0:T(8,128)}, u32[]{:S(2)}, u32[]{:S(2)}) collective-permute-start(f32[2,2,2,2,2,112,128]{6,5,4,3,2,1,0:T(8,128)S(1)} %bitcast.284), channel_id=1, source_target_pairs={{0,128},{128,0},{256,384},{384,256},{1,129},{129,1},{257,385},{385... | collective-permute-start | bytes 5505032 | tf_op jit(solution)/shard_map/ppermute | solution.py:177
  69.5 15.4 %collective-permute-start.6 = (f32[2,2,2,2,112,128]{5,4,3,2,1,0:T(8,128)S(1)}, f32[2,2,2,2,112,128]{5,4,3,2,1,0:T(8,128)}, u32[]{:S(2)}, u32[]{:S(2)}) collective-permute-start(f32[2,2,2,2,112,128]{5,4,3,2,1,0:T(8,128)S(1)} %bitcast_select_fusion), channel_id=1, source_target_pairs={{0,1},{1,0},{2,3},{3,2},{4,5},{5,4},{6,7},{7,6},{8,9},{9,8},{10,11... | collective-permute-start | bytes 2752520 | tf_op jit(solution)/shard_map/ppermute | solution.py:190
  86.3 10.4 %collective-permute-start.7 = (f32[2,2,2,112,128]{4,3,2,1,0:T(8,128)S(1)}, f32[2,2,2,112,128]{4,3,2,1,0:T(8,128)S(1)}, u32[]{:S(2)}, u32[]{:S(2)}) collective-permute-start(f32[2,2,2,112,128]{4,3,2,1,0:T(8,128)S(1)} %bitcast_select_fusion.2), channel_id=1, source_target_pairs={{0,4},{1,5},{2,6},{3,7},{4,0},{5,1},{6,2},{7,3},{8,12},{9,13},{10,... | collective-permute-start | bytes 1376264 | tf_op jit(solution)/shard_map/ppermute | solution.py:190
  88.8 20.6 %copy-start.9 = (s32[16]{0:T(128)S(1)}, s32[16]{0:T(128)}, u32[]{:S(2)}) copy-start(s32[16]{0:T(128)} %constant.273) | copy-start | bytes 196
  96.7 33.0 %copy-start.12 = (bf16[3,3,3,128,128]{4,3,2,1,0:T(8,128)(2,1)S(1)}, bf16[3,3,3,128,128]{4,3,2,1,0:T(8,128)(2,1)}, u32[]{:S(2)}) copy-start(bf16[3,3,3,128,128]{4,3,2,1,0:T(8,128)(2,1)} %param.10) | copy-start | bytes 2654212
  96.8 33.0 %copy-start.15 = (pred[8,9]{0,1:T(8,128)(4,1)S(1)}, pred[8,9]{0,1:T(8,128)(4,1)}, u32[]{:S(2)}) copy-start(pred[8,9]{0,1:T(8,128)(4,1)} %constant.263) | copy-start | bytes 220
  96.8 9.3 %collective-permute-start.8 = (f32[2,2,112,128]{3,2,1,0:T(8,128)S(1)}, f32[2,2,112,128]{3,2,1,0:T(8,128)S(1)}, u32[]{:S(2)}, u32[]{:S(2)}) collective-permute-start(f32[2,2,112,128]{3,2,1,0:T(8,128)S(1)} %bitcast_select_fusion.4), channel_id=1, source_target_pairs={{0,3},{1,2},{2,1},{3,0},{4,7},{5,6},{6,5},{7,4},{8,11},{9,10},{10,... | collective-permute-start | bytes 688136 | tf_op jit(solution)/shard_map/ppermute | solution.py:190
  106.1 24.6 %copy-start.1 = (bf16[1,5,128,128]{3,0,2,1:T(2,128)(2,1)S(1)}, bf16[1,5,128,128]{3,0,2,1:T(2,128)(2,1)}, u32[]{:S(2)}) copy-start(bf16[1,5,128,128]{3,0,2,1:T(2,128)(2,1)} %copy-done) | copy-start | bytes 491524
  106.1 8.0 %collective-permute-start.9 = (f32[2,112,128]{2,1,0:T(8,128)S(1)}, f32[2,112,128]{2,1,0:T(8,128)S(1)}, u32[]{:S(2)}, u32[]{:S(2)}) collective-permute-start(f32[2,112,128]{2,1,0:T(8,128)S(1)} %select_bitcast_fusion), channel_id=1, source_target_pairs={{0,12},{1,13},{2,14},{3,15},{4,8},{5,9},{6,10},{7,11},{8,4},{9,5},... | collective-permute-start | bytes 344072 | tf_op jit(solution)/shard_map/ppermute | solution.py:190
  114.2 18.1 %collective-permute-start.10 = (f32[112,128]{1,0:T(8,128)S(1)}, f32[112,128]{1,0:T(8,128)S(1)}, u32[]{:S(2)}, u32[]{:S(2)}) collective-permute-start(f32[112,128]{1,0:T(8,128)S(1)} %dynamic-slice_bitcast_fusion), channel_id=1, source_target_pairs={{0,256},{128,384},{256,0},{384,128},{1,257},{129,385},{257,1},{385... | collective-permute-start | bytes 172040 | tf_op jit(solution)/shard_map/ppermute | solution.py:177
  132.2 6.1 %collective-permute-start.11 = (f32[112,128]{1,0:T(8,128)S(1)}, f32[112,128]{1,0:T(8,128)S(1)}, u32[]{:S(2)}, u32[]{:S(2)}) collective-permute-start(f32[112,128]{1,0:T(8,128)S(1)} %bitcast_add_fusion.1), channel_id=1, source_target_pairs={{0,16},{16,0},{32,48},{48,32},{64,80},{80,64},{96,112},{112,96},{1... | collective-permute-start | bytes 172040 | tf_op jit(solution)/shard_map/ppermute | solution.py:177
  138.3 7.2 %collective-permute-start.12 = (f32[112,128]{1,0:T(8,128)S(1)}, f32[112,128]{1,0:T(8,128)S(1)}, u32[]{:S(2)}, u32[]{:S(2)}) collective-permute-start(f32[112,128]{1,0:T(8,128)S(1)} %add.207), channel_id=1, source_target_pairs={{0,32},{16,48},{32,0},{48,16},{64,96},{80,112},{96,64},{112,80},{1... | collective-permute-start | bytes 172040 | tf_op jit(solution)/shard_map/ppermute | solution.py:177
  145.5 10.0 %collective-permute-start.13 = (f32[112,128]{1,0:T(8,128)S(1)}, f32[112,128]{1,0:T(8,128)S(1)}, u32[]{:S(2)}, u32[]{:S(2)}) collective-permute-start(f32[112,128]{1,0:T(8,128)S(1)} %add.208), channel_id=1, source_target_pairs={{0,64},{16,80},{32,96},{48,112},{64,0},{80,16},{96,32},{112,48},{1... | collective-permute-start | bytes 172040 | tf_op jit(solution)/shard_map/ppermute | solution.py:177

commit v9 on v7

--- a/solution.py
+++ b/solution.py
@@ -134,11 +134,6 @@
     above = shifted(hidden[:, rows_dev - 1 :], "height", 1)
     hidden_rows = jnp.concatenate([above, hidden], axis=1)
     hidden_past = shifted(hidden_rows, "tm", 1)
-    hidden_ext = jnp.concatenate([hidden_past, hidden_rows], axis=0)
-    encoded = conv_layer(hidden_ext, conv_down, down_mask, down_frames, 2, (1, 0)).astype(
-        jnp.bfloat16
-    )
-    down_local = weight_grad(hidden_ext, grads, down_mask, 2, (1, 0))
     grads_rows = jnp.concatenate([grads, below], axis=1)
     grads_next = shifted(grads_rows, "tm", -1)
     grads_ext = jnp.concatenate([grads_rows, grads_next], axis=0)
@@ -148,6 +143,12 @@
         jnp.bfloat16
     )
     first_local = weight_grad(input_ext, pre_grad, first_mask, 1, (1, 1))
+    hidden_past, first_local = lax.optimization_barrier((hidden_past, first_local))
+    hidden_ext = jnp.concatenate([hidden_past, hidden_rows], axis=0)
+    encoded = conv_layer(hidden_ext, conv_down, down_mask, down_frames, 2, (1, 0)).astype(
+        jnp.bfloat16
+    )
+    down_local = weight_grad(hidden_ext, grads, down_mask, 2, (1, 0))
     share = conv_first.shape[3] // lax.axis_size("dp")
     quarters = lax.axis_size("dp")
 

time: 182 us -> 182 us (level)
  transfers between devices with their start and end apart: 15 -> 15, of which waited for: 10 -> 11; matrix products, arithmetic and copies ran while one was open for 13% -> 12% of each run, Pallas kernels for 0% -> 0%
where the time goes in v9:
time: 182 us; the launch traced here: 180 us
  starting transfers between devices  67.8 us (37%)
  waiting for transfers between devices  45.9 us (25%)
  blocking collectives  22.3 us (12%)
  matrix products  15.7 us (9%)
  other arithmetic  14.4 us (8%)
  local copies, waits for them, and re-layouts  10.4 us (6%)
  between operations  3.89 us (2%)
    ppermute x5, starting transfers between devices, swap(): lax.ppermute(value, axis, [(i, i ^ bit) for i in range(lax.axis_size(axis...  36.3 us
    ppermute x4, waiting for transfers between devices, swap_rows(): return lax.ppermute(value, ('dp', 'height'), pairs)  29.4 us
    all_gather x1, blocking collectives, reduce_gradients(): gathered = lax.all_gather(piece, 'height', axis=0, tiled=False)  22.3 us
    ppermute x6, starting transfers between devices, shifted(): lax.ppermute(value, axis, [(source, source + steps) for source in range(l...  18.6 us
    ppermute x4, starting transfers between devices, swap_rows(): return lax.ppermute(value, ('dp', 'height'), pairs)  12.9 us
    ppermute x5, waiting for transfers between devices, swap(): lax.ppermute(value, axis, [(i, i ^ bit) for i in range(lax.axis_size(axis...  8.71 us
    conv_general_dilated x6, matrix products, weight_grad(): lax.conv_general_dilated(frame_slab, masked, (1, 1), ((0, 0), pad_cols),...  8.43 us
    ppermute x6, waiting for transfers between devices, shifted(): lax.ppermute(value, axis, [(source, source + steps) for source in range(l...  7.78 us
  transfers between devices with their start and end apart: 15, of which 11 were waited for; matrix products, arithmetic and copies ran while one was open for 12% of the time, Pallas kernels for 0%

profile of v9, /device:TPU:6, one launch (start us, length us, event | category | flops | bytes accessed | tf_op | source)
XLA Modules:
  0.0 180.4 jit_solution(1616394049070187285)
XLA Ops:
  0.6 0.8 fusion.118
  1.4 1.2 copy.350
  2.8 5.2 %collective-permute-start.1 = (bf16[40960]{0:T(1024)(128)(2,1)S(1)}, bf16[40960]{0:T(1024)(128)(2,1)S(1)}, u32[]{:S(2)}, u32[]{:S(2)}) collective-permute-start(bf16[40960]{0:T(1024)(128)(2,1)S(1)} %pad_maximum_fusion.8), channel_id=1, source_target_pairs={{1,0},{2,1},{3,2},{4,3},{5,4},{6,5},{7,6},{8,7},{9,8},{10,9},{11,1... | collective-permute-start | bytes 245768 | tf_op jit(solution)/shard_map/ppermute | solution.py:30
  8.0 1.9 %collective-permute-start = (bf16[2,1,128,128]{3,0,2,1:T(2,128)(2,1)S(1)}, bf16[2,1,128,128]{3,0,2,1:T(2,128)(2,1)S(1)}, u32[]{:S(2)}, u32[]{:S(2)}) collective-permute-start(bf16[2,1,128,128]{3,0,2,1:T(2,128)(2,1)S(1)} %get-tuple-element.37), channel_id=1, source_target_pairs={{0,1},{1,2},{2,3},{3,4},{4,5},{5,6},{6,7},{7,8},{8,9},{9,10},{10,1... | collective-permute-start | bytes 196616 | tf_op jit(solution)/shard_map/ppermute | solution.py:30
  9.9 0.8 reduce-window_clone.1
  10.7 0.7 subtract_bitcast_fusion
  11.7 0.6 fusion.161
  14.3 1.4 broadcast_multiply_fusion.5
  15.7 0.6 slice.206
  16.2 0.7 slice.210
  17.0 0.6 pad_maximum_fusion.5
  17.6 4.0 %collective-permute-start.2 = (bf16[2,6,128,128]{3,0,2,1:T(2,128)(2,1)S(1)}, bf16[2,6,128,128]{3,0,2,1:T(2,128)(2,1)S(1)}, u32[]{:S(2)}, u32[]{:S(2)}) collective-permute-start(bf16[2,6,128,128]{3,0,2,1:T(2,128)(2,1)S(1)} %pad_maximum_fusion.5), channel_id=1, source_target_pairs={{0,16},{16,32},{32,48},{48,64},{64,80},{80,96},{96,112},{1,17},{17... | collective-permute-start | bytes 1179656 | tf_op jit(solution)/shard_map/ppermute | solution.py:30
  21.6 1.3 collective-permute-start.5
  22.9 0.6 fusion.168
  23.5 0.3 pad.13
  24.0 3.7 %collective-permute-done.5 = bf16[1,3,64,128]{3,2,1,0:T(8,128)(2,1)S(1)} collective-permute-done((bf16[1,3,64,128]{3,2,1,0:T(8,128)(2,1)S(1)}, bf16[1,3,64,128]{3,2,1,0:T(8,128)(2,1)S(1)}, u32[]{:S(2)}, u32[]{:S(2)}) %collective-permute-start.5) | collective-permute-done | bytes 49184 | tf_op jit(solution)/shard_map/ppermute | solution.py:30
  27.6 1.2 multiply_bitcast_fusion.1
  29.0 0.3 fusion.9
  29.7 0.3 convolution_select_fusion.5
  30.1 0.3 fusion.8
  30.6 0.3 pad.9
  31.0 1.0 pad_maximum_fusion.2
  32.6 0.8 fusion.6
  33.6 0.8 fusion.5
  34.6 1.0 add_divide_fusion
  35.7 2.4 %collective-permute-start.3 = (bf16[2,1,128,128]{3,0,2,1:T(2,128)(2,1)S(1)}, bf16[2,1,128,128]{3,0,2,1:T(2,128)(2,1)S(1)}, u32[]{:S(2)}, u32[]{:S(2)}) collective-permute-start(bf16[2,1,128,128]{3,0,2,1:T(2,128)(2,1)S(1)} %bitcast.307), channel_id=1, source_target_pairs={{0,1},{1,2},{2,3},{3,4},{4,5},{5,6},{6,7},{7,8},{8,9},{9,10},{10,1... | collective-permute-start | bytes 196616 | tf_op jit(solution)/shard_map/ppermute | solution.py:30
  38.9 2.0 %convolution_bitcast_fusion.3 = f32[1,3,3,128,128]{4,3,2,1,0:T(8,128)S(1)} fusion(bf16[2,6,128,128]{3,0,2,1:T(2,128)(2,1)S(1)} %pad_maximum_fusion.5, bf16[2,4,128,128]{3,2,1,0:T(8,128)(2,1)S(1)} %get-tuple-element.36), kind=kOutput, calls=%fused_computation.14 | convolution fusion | flops 300417024 | bytes 1245184 | tf_op jit(solution)/shard_map/conv_general_dilated | solution.py:57
  40.9 2.0 %convolution_bitcast_fusion.4 = f32[1,3,3,128,128]{4,3,2,1,0:T(8,128)S(1)} fusion(bf16[2,6,128,128]{3,0,2,1:T(2,128)(2,1)S(1)} %pad_maximum_fusion.2, bf16[2,4,128,128]{3,2,1,0:T(8,128)(2,1)S(1)} %get-tuple-element.35), kind=kOutput, calls=%fused_computation.15 | convolution fusion | flops 300417024 | bytes 1245184 | tf_op jit(solution)/shard_map/conv_general_dilated | solution.py:57
  42.9 2.0 %convolution_bitcast_fusion.5 = f32[1,3,3,128,128]{4,3,2,1,0:T(8,128)S(1)} fusion(bf16[2,6,128,128]{3,0,2,1:T(2,128)(2,1)S(1)} %collective-permute-done.2, bf16[2,4,128,128]{3,2,1,0:T(8,128)(2,1)S(1)} %get-tuple-element.24), kind=kOutput, calls=%fused_computation.16 | convolution fusion | flops 300417024 | bytes 1245184 | tf_op jit(solution)/shard_map/conv_general_dilated | solution.py:57
  45.6 0.4 pad_maximum_fusion.6
  46.0 3.8 %collective-permute-start.4 = (bf16[2,5,128,128]{3,0,2,1:T(2,128)(2,1)S(1)}, bf16[2,5,128,128]{3,0,2,1:T(2,128)(2,1)S(1)}, u32[]{:S(2)}, u32[]{:S(2)}) collective-permute-start(bf16[2,5,128,128]{3,0,2,1:T(2,128)(2,1)S(1)} %pad_maximum_fusion.6), channel_id=1, source_target_pairs={{0,16},{16,32},{32,48},{48,64},{64,80},{80,96},{96,112},{1,17},{17... | collective-permute-start | bytes 983048 | tf_op jit(solution)/shard_map/ppermute | solution.py:30
  49.9 0.4 slice_maximum_fusion
  50.3 0.8 convolution_bitcast_fusion
  51.2 4.1 %collective-permute-done.4 = bf16[2,5,128,128]{3,0,2,1:T(2,128)(2,1)S(1)} collective-permute-done((bf16[2,5,128,128]{3,0,2,1:T(2,128)(2,1)S(1)}, bf16[2,5,128,128]{3,0,2,1:T(2,128)(2,1)S(1)}, u32[]{:S(2)}, u32[]{:S(2)}) %collective-permute-start.4) | collective-permute-done | bytes 327712 | tf_op jit(solution)/shard_map/ppermute | solution.py:30
  55.3 0.5 fusion.159
  56.0 0.8 convolution_bitcast_fusion.1
  56.8 0.8 convolution_bitcast_fusion.2
  58.2 1.5 fusion.1
  59.9 1.9 %collective-permute-start.6 = (f32[2,2,2,2,2,112,128]{6,5,4,3,2,1,0:T(8,128)S(1)}, f32[2,2,2,2,2,112,128]{6,5,4,3,2,1,0:T(8,128)}, u32[]{:S(2)}, u32[]{:S(2)}) collective-permute-start(f32[2,2,2,2,2,112,128]{6,5,4,3,2,1,0:T(8,128)S(1)} %bitcast.280), channel_id=1, source_target_pairs={{0,128},{128,0},{256,384},{384,256},{1,129},{129,1},{257,385},{385... | collective-permute-start | bytes 5505032 | tf_op jit(solution)/shard_map/ppermute | solution.py:175
  61.9 3.8 %collective-permute-done.6 = f32[2,2,2,2,2,112,128]{6,5,4,3,2,1,0:T(8,128)} collective-permute-done((f32[2,2,2,2,2,112,128]{6,5,4,3,2,1,0:T(8,128)S(1)}, f32[2,2,2,2,2,112,128]{6,5,4,3,2,1,0:T(8,128)}, u32[]{:S(2)}, u32[]{:S(2)}) %collective-permute-start.6) | collective-permute-done | bytes 1835040 | tf_op jit(solution)/shard_map/ppermute | solution.py:175
  65.7 2.3 %bitcast_add_fusion = f32[2,2,2,2,2,112,128]{6,5,4,3,2,1,0:T(8,128)S(1)} fusion(f32[2,2,2,2,2,112,128]{6,5,4,3,2,1,0:T(8,128)} %collective-permute-done.6, f32[2,1,2,2,2,2,112,128]{7,6,5,4,3,1,0,2:T(8,128)} %get-tuple-element.26), kind=kLoop, calls=%fused_computation.7 | loop fusion | flops 458752 | bytes 5505024 | tf_op jit(solution)/shard_map/add | solution.py:217
  68.1 3.2 %collective-permute-start.7 = (f32[2,2,2,2,112,128]{5,4,3,2,1,0:T(8,128)S(1)}, f32[2,2,2,2,112,128]{5,4,3,2,1,0:T(8,128)}, u32[]{:S(2)}, u32[]{:S(2)}) collective-permute-start(f32[2,2,2,2,112,128]{5,4,3,2,1,0:T(8,128)S(1)} %bitcast_select_fusion), channel_id=1, source_target_pairs={{0,1},{1,0},{2,3},{3,2},{4,5},{5,4},{6,7},{7,6},{8,9},{9,8},{10,11... | collective-permute-start | bytes 2752520 | tf_op jit(solution)/shard_map/ppermute | solution.py:188
  71.3 12.2 %collective-permute-done.7 = f32[2,2,2,2,112,128]{5,4,3,2,1,0:T(8,128)} collective-permute-done((f32[2,2,2,2,112,128]{5,4,3,2,1,0:T(8,128)S(1)}, f32[2,2,2,2,112,128]{5,4,3,2,1,0:T(8,128)}, u32[]{:S(2)}, u32[]{:S(2)}) %collective-permute-start.7) | collective-permute-done | bytes 917536 | tf_op jit(solution)/shard_map/ppermute | solution.py:188
  83.5 1.3 fusion.19
  84.9 2.7 %collective-permute-start.8 = (f32[2,2,2,112,128]{4,3,2,1,0:T(8,128)S(1)}, f32[2,2,2,112,128]{4,3,2,1,0:T(8,128)S(1)}, u32[]{:S(2)}, u32[]{:S(2)}) collective-permute-start(f32[2,2,2,112,128]{4,3,2,1,0:T(8,128)S(1)} %bitcast_select_fusion.2), channel_id=1, source_target_pairs={{0,4},{1,5},{2,6},{3,7},{4,0},{5,1},{6,2},{7,3},{8,12},{9,13},{10,... | collective-permute-start | bytes 1376264 | tf_op jit(solution)/shard_map/ppermute | solution.py:188
  87.7 7.6 %collective-permute-done.8 = f32[2,2,2,112,128]{4,3,2,1,0:T(8,128)S(1)} collective-permute-done((f32[2,2,2,112,128]{4,3,2,1,0:T(8,128)S(1)}, f32[2,2,2,112,128]{4,3,2,1,0:T(8,128)S(1)}, u32[]{:S(2)}, u32[]{:S(2)}) %collective-permute-start.8) | collective-permute-done | bytes 458784 | tf_op jit(solution)/shard_map/ppermute | solution.py:188
  95.4 4.3 %collective-permute-start.9 = (f32[2,2,112,128]{3,2,1,0:T(8,128)S(1)}, f32[2,2,112,128]{3,2,1,0:T(8,128)S(1)}, u32[]{:S(2)}, u32[]{:S(2)}) collective-permute-start(f32[2,2,112,128]{3,2,1,0:T(8,128)S(1)} %bitcast_select_fusion.4), channel_id=1, source_target_pairs={{0,3},{1,2},{2,1},{3,0},{4,7},{5,6},{6,5},{7,4},{8,11},{9,10},{10,... | collective-permute-start | bytes 688136 | tf_op jit(solution)/shard_map/ppermute | solution.py:188
  99.7 4.8 %collective-permute-done.9 = f32[2,2,112,128]{3,2,1,0:T(8,128)S(1)} collective-permute-done((f32[2,2,112,128]{3,2,1,0:T(8,128)S(1)}, f32[2,2,112,128]{3,2,1,0:T(8,128)S(1)}, u32[]{:S(2)}, u32[]{:S(2)}) %collective-permute-start.9) | collective-permute-done | bytes 229408 | tf_op jit(solution)/shard_map/ppermute | solution.py:188
  104.6 2.7 %collective-permute-start.10 = (f32[2,112,128]{2,1,0:T(8,128)S(1)}, f32[2,112,128]{2,1,0:T(8,128)S(1)}, u32[]{:S(2)}, u32[]{:S(2)}) collective-permute-start(f32[2,112,128]{2,1,0:T(8,128)S(1)} %select_bitcast_fusion), channel_id=1, source_target_pairs={{0,12},{1,13},{2,14},{3,15},{4,8},{5,9},{6,10},{7,11},{8,4},{9,5},... | collective-permute-start | bytes 344072 | tf_op jit(solution)/shard_map/ppermute | solution.py:188
  107.7 4.9 %collective-permute-done.10 = f32[2,112,128]{2,1,0:T(8,128)S(1)} collective-permute-done((f32[2,112,128]{2,1,0:T(8,128)S(1)}, f32[2,112,128]{2,1,0:T(8,128)S(1)}, u32[]{:S(2)}, u32[]{:S(2)}) %collective-permute-start.10) | collective-permute-done | bytes 114720 | tf_op jit(solution)/shard_map/ppermute | solution.py:188
  112.6 14.5 %collective-permute-start.11 = (f32[112,128]{1,0:T(8,128)S(1)}, f32[112,128]{1,0:T(8,128)S(1)}, u32[]{:S(2)}, u32[]{:S(2)}) collective-permute-start(f32[112,128]{1,0:T(8,128)S(1)} %dynamic-slice_bitcast_fusion), channel_id=1, source_target_pairs={{0,256},{128,384},{256,0},{384,128},{1,257},{129,385},{257,1},{385... | collective-permute-start | bytes 172040 | tf_op jit(solution)/shard_map/ppermute | solution.py:175
  127.1 1.9 %fusion.10 = f32[2,8,9,128]{3,1,2,0:T(8,128)S(1)} fusion(bf16[3,3,3,128,128]{4,3,2,1,0:T(8,128)(2,1)} %param.10, bf16[5,1,7,2,128]{4,2,3,0,1:T(8,128)(2,1)S(1)} %slice.219, bf16[5,1,8,18,128]{4,2,3,0,1:T(8,128)(2,1)S(1)} %copy.286, f32[]{:T(128)} %bitcast.60, pred[8,9]{0,1:T(8,128)(4,1)S(1)} %copy-done.9), kind=kOutput, calls=%fused_computation.32 | convolution fusion | flops 43118592 | bytes 571464 | tf_op jit(solution)/shard_map/conv_general_dilated | solution.py:37
  129.2 4.9 %collective-permute-start.12 = (f32[112,128]{1,0:T(8,128)S(1)}, f32[112,128]{1,0:T(8,128)S(1)}, u32[]{:S(2)}, u32[]{:S(2)}) collective-permute-start(f32[112,128]{1,0:T(8,128)S(1)} %bitcast_add_fusion.1), channel_id=1, source_target_pairs={{0,16},{16,0},{32,48},{48,32},{64,80},{80,64},{96,112},{112,96},{1... | collective-permute-start | bytes 172040 | tf_op jit(solution)/shard_map/ppermute | solution.py:175
  134.2 0.9 fusion.11
  135.3 1.0 collective-permute-done.12
  136.3 5.6 %collective-permute-start.13 = (f32[112,128]{1,0:T(8,128)S(1)}, f32[112,128]{1,0:T(8,128)S(1)}, u32[]{:S(2)}, u32[]{:S(2)}) collective-permute-start(f32[112,128]{1,0:T(8,128)S(1)} %add.204), channel_id=1, source_target_pairs={{0,32},{16,48},{32,0},{48,16},{64,96},{80,112},{96,64},{112,80},{1... | collective-permute-start | bytes 172040 | tf_op jit(solution)/shard_map/ppermute | solution.py:175
  141.9 0.9 fusion.15
  142.8 1.2 collective-permute-done.13
  144.0 9.4 %collective-permute-start.14 = (f32[112,128]{1,0:T(8,128)S(1)}, f32[112,128]{1,0:T(8,128)S(1)}, u32[]{:S(2)}, u32[]{:S(2)}) collective-permute-start(f32[112,128]{1,0:T(8,128)S(1)} %add.205), channel_id=1, source_target_pairs={{0,64},{16,80},{32,96},{48,112},{64,0},{80,16},{96,32},{112,48},{1... | collective-permute-start | bytes 172040 | tf_op jit(solution)/shard_map/ppermute | solution.py:175
  153.5 0.6 copy.298
  154.1 2.7 %collective-permute-done.14 = f32[112,128]{1,0:T(8,128)S(1)} collective-permute-done((f32[112,128]{1,0:T(8,128)S(1)}, f32[112,128]{1,0:T(8,128)S(1)}, u32[]{:S(2)}, u32[]{:S(2)}) %collective-permute-start.14) | collective-permute-done | bytes 57376 | tf_op jit(solution)/shard_map/ppermute | solution.py:175
  156.8 22.3 %all-gather = bf16[1792,128]{1,0:T(8,128)(2,1)S(1)} all-gather(bf16[112,128]{1,0:T(8,128)(2,1)S(1)} %add_convert_fusion), channel_id=2, replica_groups=mesh['dp'=4,'tm'=8,'height'=16] {'height'}, dimensions={0}, use_global_device_ids=true | all-gather | bytes 487424 | tf_op jit(solution)/shard_map/all_gather | solution.py:241
  179.0 0.6 gather_fusion
  179.7 0.8 fusion.158
  (122 shorter events, 5.7 us)
Async XLA Ops:
  2.8 14.1 %collective-permute-start.1 = (bf16[40960]{0:T(1024)(128)(2,1)S(1)}, bf16[40960]{0:T(1024)(128)(2,1)S(1)}, u32[]{:S(2)}, u32[]{:S(2)}) collective-permute-start(bf16[40960]{0:T(1024)(128)(2,1)S(1)} %pad_maximum_fusion.8), channel_id=1, source_target_pairs={{1,0},{2,1},{3,2},{4,3},{5,4},{6,5},{7,6},{8,7},{9,8},{10,9},{11,1... | collective-permute-start | bytes 245768 | tf_op jit(solution)/shard_map/ppermute | solution.py:30
  8.0 9.0 %collective-permute-start = (bf16[2,1,128,128]{3,0,2,1:T(2,128)(2,1)S(1)}, bf16[2,1,128,128]{3,0,2,1:T(2,128)(2,1)S(1)}, u32[]{:S(2)}, u32[]{:S(2)}) collective-permute-start(bf16[2,1,128,128]{3,0,2,1:T(2,128)(2,1)S(1)} %get-tuple-element.37), channel_id=1, source_target_pairs={{0,1},{1,2},{2,3},{3,4},{4,5},{5,6},{6,7},{7,8},{8,9},{9,10},{10,1... | collective-permute-start | bytes 196616 | tf_op jit(solution)/shard_map/ppermute | solution.py:30
  17.6 11.4 %copy-start.5 = (bf16[3,3,3,128,128]{4,3,2,1,0:T(8,128)(2,1)S(1)}, bf16[3,3,3,128,128]{4,3,2,1,0:T(8,128)(2,1)}, u32[]{:S(2)}) copy-start(bf16[3,3,3,128,128]{4,3,2,1,0:T(8,128)(2,1)} %param.10) | copy-start | bytes 2654212
  17.6 11.4 %copy-start.8 = (pred[8,18]{0,1:T(8,128)(4,1)S(1)}, pred[8,18]{0,1:T(8,128)(4,1)}, u32[]{:S(2)}) copy-start(pred[8,18]{0,1:T(8,128)(4,1)} %constant.265) | copy-start | bytes 436
  17.6 12.9 %collective-permute-start.2 = (bf16[2,6,128,128]{3,0,2,1:T(2,128)(2,1)S(1)}, bf16[2,6,128,128]{3,0,2,1:T(2,128)(2,1)S(1)}, u32[]{:S(2)}, u32[]{:S(2)}) collective-permute-start(bf16[2,6,128,128]{3,0,2,1:T(2,128)(2,1)S(1)} %pad_maximum_fusion.5), channel_id=1, source_target_pairs={{0,16},{16,32},{32,48},{48,64},{64,80},{80,96},{96,112},{1,17},{17... | collective-permute-start | bytes 1179656 | tf_op jit(solution)/shard_map/ppermute | solution.py:30
  21.6 6.0 %collective-permute-start.5 = (bf16[1,3,64,128]{3,2,1,0:T(8,128)(2,1)S(1)}, bf16[1,3,64,128]{3,2,1,0:T(8,128)(2,1)S(1)}, u32[]{:S(2)}, u32[]{:S(2)}) collective-permute-start(bf16[1,3,64,128]{3,2,1,0:T(8,128)(2,1)S(1)} %pad_maximum_fusion.9), channel_id=1, source_target_pairs={{16,0},{32,16},{48,32},{64,48},{80,64},{96,80},{112,96},{17,1},{33... | collective-permute-start | bytes 147464 | tf_op jit(solution)/shard_map/ppermute | solution.py:30
  31.0 1.6 copy-start.4
  31.0 1.6 copy-start.7
  35.7 9.9 %collective-permute-start.3 = (bf16[2,1,128,128]{3,0,2,1:T(2,128)(2,1)S(1)}, bf16[2,1,128,128]{3,0,2,1:T(2,128)(2,1)S(1)}, u32[]{:S(2)}, u32[]{:S(2)}) collective-permute-start(bf16[2,1,128,128]{3,0,2,1:T(2,128)(2,1)S(1)} %bitcast.307), channel_id=1, source_target_pairs={{0,1},{1,2},{2,3},{3,4},{4,5},{5,6},{6,7},{7,8},{8,9},{9,10},{10,1... | collective-permute-start | bytes 196616 | tf_op jit(solution)/shard_map/ppermute | solution.py:30
  46.0 9.2 %collective-permute-start.4 = (bf16[2,5,128,128]{3,0,2,1:T(2,128)(2,1)S(1)}, bf16[2,5,128,128]{3,0,2,1:T(2,128)(2,1)S(1)}, u32[]{:S(2)}, u32[]{:S(2)}) collective-permute-start(bf16[2,5,128,128]{3,0,2,1:T(2,128)(2,1)S(1)} %pad_maximum_fusion.6), channel_id=1, source_target_pairs={{0,16},{16,32},{32,48},{48,64},{64,80},{80,96},{96,112},{1,17},{17... | collective-permute-start | bytes 983048 | tf_op jit(solution)/shard_map/ppermute | solution.py:30
  50.3 0.8 copy-start
  55.9 0.8 copy-start.2
  59.9 5.8 %collective-permute-start.6 = (f32[2,2,2,2,2,112,128]{6,5,4,3,2,1,0:T(8,128)S(1)}, f32[2,2,2,2,2,112,128]{6,5,4,3,2,1,0:T(8,128)}, u32[]{:S(2)}, u32[]{:S(2)}) collective-permute-start(f32[2,2,2,2,2,112,128]{6,5,4,3,2,1,0:T(8,128)S(1)} %bitcast.280), channel_id=1, source_target_pairs={{0,128},{128,0},{256,384},{384,256},{1,129},{129,1},{257,385},{385... | collective-permute-start | bytes 5505032 | tf_op jit(solution)/shard_map/ppermute | solution.py:175
  68.1 15.4 %collective-permute-start.7 = (f32[2,2,2,2,112,128]{5,4,3,2,1,0:T(8,128)S(1)}, f32[2,2,2,2,112,128]{5,4,3,2,1,0:T(8,128)}, u32[]{:S(2)}, u32[]{:S(2)}) collective-permute-start(f32[2,2,2,2,112,128]{5,4,3,2,1,0:T(8,128)S(1)} %bitcast_select_fusion), channel_id=1, source_target_pairs={{0,1},{1,0},{2,3},{3,2},{4,5},{5,4},{6,7},{7,6},{8,9},{9,8},{10,11... | collective-permute-start | bytes 2752520 | tf_op jit(solution)/shard_map/ppermute | solution.py:188
  84.9 10.4 %collective-permute-start.8 = (f32[2,2,2,112,128]{4,3,2,1,0:T(8,128)S(1)}, f32[2,2,2,112,128]{4,3,2,1,0:T(8,128)S(1)}, u32[]{:S(2)}, u32[]{:S(2)}) collective-permute-start(f32[2,2,2,112,128]{4,3,2,1,0:T(8,128)S(1)} %bitcast_select_fusion.2), channel_id=1, source_target_pairs={{0,4},{1,5},{2,6},{3,7},{4,0},{5,1},{6,2},{7,3},{8,12},{9,13},{10,... | collective-permute-start | bytes 1376264 | tf_op jit(solution)/shard_map/ppermute | solution.py:188
  87.7 19.7 %copy-start.3 = (s32[16]{0:T(128)S(1)}, s32[16]{0:T(128)}, u32[]{:S(2)}) copy-start(s32[16]{0:T(128)} %constant.271) | copy-start | bytes 196
  87.7 19.7 %copy-start.1 = (bf16[1,5,128,128]{3,0,2,1:T(2,128)(2,1)S(1)}, bf16[1,5,128,128]{3,0,2,1:T(2,128)(2,1)}, u32[]{:S(2)}) copy-start(bf16[1,5,128,128]{3,0,2,1:T(2,128)(2,1)} %copy-done) | copy-start | bytes 491524
  95.4 31.7 %copy-start.9 = (pred[8,9]{0,1:T(8,128)(4,1)S(1)}, pred[8,9]{0,1:T(8,128)(4,1)}, u32[]{:S(2)}) copy-start(pred[8,9]{0,1:T(8,128)(4,1)} %constant.261) | copy-start | bytes 220
  95.4 9.1 %collective-permute-start.9 = (f32[2,2,112,128]{3,2,1,0:T(8,128)S(1)}, f32[2,2,112,128]{3,2,1,0:T(8,128)S(1)}, u32[]{:S(2)}, u32[]{:S(2)}) collective-permute-start(f32[2,2,112,128]{3,2,1,0:T(8,128)S(1)} %bitcast_select_fusion.4), channel_id=1, source_target_pairs={{0,3},{1,2},{2,1},{3,0},{4,7},{5,6},{6,5},{7,4},{8,11},{9,10},{10,... | collective-permute-start | bytes 688136 | tf_op jit(solution)/shard_map/ppermute | solution.py:188
  104.6 7.9 %collective-permute-start.10 = (f32[2,112,128]{2,1,0:T(8,128)S(1)}, f32[2,112,128]{2,1,0:T(8,128)S(1)}, u32[]{:S(2)}, u32[]{:S(2)}) collective-permute-start(f32[2,112,128]{2,1,0:T(8,128)S(1)} %select_bitcast_fusion), channel_id=1, source_target_pairs={{0,12},{1,13},{2,14},{3,15},{4,8},{5,9},{6,10},{7,11},{8,4},{9,5},... | collective-permute-start | bytes 344072 | tf_op jit(solution)/shard_map/ppermute | solution.py:188
  107.6 26.6 %copy-start.6 = (bf16[3,3,3,128,128]{4,3,2,1,0:T(8,128)(2,1)S(1)}, bf16[3,3,3,128,128]{4,3,2,1,0:T(8,128)(2,1)}, u32[]{:S(2)}) copy-start(bf16[3,3,3,128,128]{4,3,2,1,0:T(8,128)(2,1)} %param.10) | copy-start | bytes 2654212
  112.6 16.7 %collective-permute-start.11 = (f32[112,128]{1,0:T(8,128)S(1)}, f32[112,128]{1,0:T(8,128)S(1)}, u32[]{:S(2)}, u32[]{:S(2)}) collective-permute-start(f32[112,128]{1,0:T(8,128)S(1)} %dynamic-slice_bitcast_fusion), channel_id=1, source_target_pairs={{0,256},{128,384},{256,0},{384,128},{1,257},{129,385},{257,1},{385... | collective-permute-start | bytes 172040 | tf_op jit(solution)/shard_map/ppermute | solution.py:175
  129.2 7.0 %collective-permute-start.12 = (f32[112,128]{1,0:T(8,128)S(1)}, f32[112,128]{1,0:T(8,128)S(1)}, u32[]{:S(2)}, u32[]{:S(2)}) collective-permute-start(f32[112,128]{1,0:T(8,128)S(1)} %bitcast_add_fusion.1), channel_id=1, source_target_pairs={{0,16},{16,0},{32,48},{48,32},{64,80},{80,64},{96,112},{112,96},{1... | collective-permute-start | bytes 172040 | tf_op jit(solution)/shard_map/ppermute | solution.py:175
  136.3 7.7 %collective-permute-start.13 = (f32[112,128]{1,0:T(8,128)S(1)}, f32[112,128]{1,0:T(8,128)S(1)}, u32[]{:S(2)}, u32[]{:S(2)}) collective-permute-start(f32[112,128]{1,0:T(8,128)S(1)} %add.204), channel_id=1, source_target_pairs={{0,32},{16,48},{32,0},{48,16},{64,96},{80,112},{96,64},{112,80},{1... | collective-permute-start | bytes 172040 | tf_op jit(solution)/shard_map/ppermute | solution.py:175
  144.0 12.7 %collective-permute-start.14 = (f32[112,128]{1,0:T(8,128)S(1)}, f32[112,128]{1,0:T(8,128)S(1)}, u32[]{:S(2)}, u32[]{:S(2)}) collective-permute-start(f32[112,128]{1,0:T(8,128)S(1)} %add.205), channel_id=1, source_target_pairs={{0,64},{16,80},{32,96},{48,112},{64,0},{80,16},{96,32},{112,48},{1... | collective-permute-start | bytes 172040 | tf_op jit(solution)/shard_map/ppermute | solution.py:175

commit v10 on v9

--- a/solution.py
+++ b/solution.py
@@ -231,13 +231,23 @@
         mine = jnp.where(core == 0, parts[0][0], parts[1][0])
         other = jnp.where(core == 0, parts[0][1], parts[1][1])
         blocks = mine + swap_rows(other, bits, low_bits)
-    far = dp_bits[-1]
+    for bit in frame_bits[:-1]:
+        blocks = blocks + swap(blocks, "tm", bit)
+    far, top = dp_bits[-1], frame_bits[-1]
+    frames = lax.axis_size("tm")
     high = (lax.axis_index("dp") // far) % 2
     mine, other, _ = split_bit(blocks, held[0], ("dp", far), high)
-    blocks = mine + swap(other, "dp", far)
-    for bit in frame_bits:
-        blocks = blocks + swap(blocks, "tm", bit)
-    piece = blocks.astype(jnp.bfloat16)
+
+    def send(value, group_flip, frame_flip):
+        pairs = [
+            (group * frames + t, (group ^ group_flip) * frames + (t ^ frame_flip))
+            for group in range(lax.axis_size("dp"))
+            for t in range(frames)
+        ]
+        return lax.ppermute(value, ("dp", "tm"), pairs)
+
+    total = mine + send(mine, 0, top) + send(other, far, 0) + send(other, far, top)
+    piece = total.astype(jnp.bfloat16)
     gathered = lax.all_gather(piece, "height", axis=0, tiled=False)
     owner = [h ^ sum((h >> 1) & bit for bit in low_bits) for h in range(gathered.shape[0])]
     return gathered[np.array(owner)]

time: 182 us -> 185 us (1.016)
  matrix products: 15.7 us -> 17.7 us
    ppermute x5 -> x3, starting transfers between devices: 36.3 us -> 13.7 us  [swap(): lax.ppermute(value, axis, [(i, i ^ bit) for i in range(lax.axis_size(axis...]
    ppermute x0 -> x3, starting transfers between devices: none -> 22.5 us  [send(): return lax.ppermute(value, ('dp', 'tm'), pairs)]
    ppermute x0 -> x3, waiting for transfers between devices: none -> 5.97 us  [send(): return lax.ppermute(value, ('dp', 'tm'), pairs)]
    ppermute x5 -> x3, waiting for transfers between devices: 8.71 us -> 5.33 us  [swap(): lax.ppermute(value, axis, [(i, i ^ bit) for i in range(lax.axis_size(axis...]
    ppermute x4, waiting for transfers between devices: 29.4 us -> 27.4 us  [swap_rows(): return lax.ppermute(value, ('dp', 'height'), pairs)]
    conv_general_dilated x6, matrix products: 6.3 us -> 8.25 us  [conv_layer(): lax.conv_general_dilated(frame_slab, weight[tap_time], (stride, stride),...]
  transfers between devices with their start and end apart: 15 -> 16, of which waited for: 11 -> 11; matrix products, arithmetic and copies ran while one was open for 12% -> 13% of each run, Pallas kernels for 0% -> 0%
where the time goes in v10:
time: 185 us; the launch traced here: 184 us
  starting transfers between devices  67.8 us (37%)
  waiting for transfers between devices  46.4 us (25%)
  blocking collectives  23.4 us (13%)
  matrix products  17.7 us (10%)
  other arithmetic  14.5 us (8%)
  local copies, waits for them, and re-layouts  10.4 us (6%)
  between operations  3.92 us (2%)
    ppermute x4, waiting for transfers between devices, swap_rows(): return lax.ppermute(value, ('dp', 'height'), pairs)  27.4 us
    all_gather x1, blocking collectives, reduce_gradients(): gathered = lax.all_gather(piece, 'height', axis=0, tiled=False)  23.4 us
    ppermute x3, starting transfers between devices, send(): return lax.ppermute(value, ('dp', 'tm'), pairs)  22.5 us
    ppermute x6, starting transfers between devices, shifted(): lax.ppermute(value, axis, [(source, source + steps) for source in range(l...  18.6 us
    ppermute x3, starting transfers between devices, swap(): lax.ppermute(value, axis, [(i, i ^ bit) for i in range(lax.axis_size(axis...  13.7 us
    ppermute x4, starting transfers between devices, swap_rows(): return lax.ppermute(value, ('dp', 'height'), pairs)  13.1 us
    conv_general_dilated x6, matrix products, weight_grad(): lax.conv_general_dilated(frame_slab, masked, (1, 1), ((0, 0), pad_cols),...  8.43 us
    conv_general_dilated x6, matrix products, conv_layer(): lax.conv_general_dilated(frame_slab, weight[tap_time], (stride, stride),...  8.25 us
  transfers between devices with their start and end apart: 16, of which 11 were waited for; matrix products, arithmetic and copies ran while one was open for 13% of the time, Pallas kernels for 0%

profile of v10, /device:TPU:6, one launch (start us, length us, event | category | flops | bytes accessed | tf_op | source)
XLA Modules:
  0.0 184.1 jit_solution(5021880383944154137)
XLA Ops:
  0.6 0.8 fusion.118
  1.4 1.2 copy.350
  2.8 5.2 %collective-permute-start.1 = (bf16[40960]{0:T(1024)(128)(2,1)S(1)}, bf16[40960]{0:T(1024)(128)(2,1)S(1)}, u32[]{:S(2)}, u32[]{:S(2)}) collective-permute-start(bf16[40960]{0:T(1024)(128)(2,1)S(1)} %pad_maximum_fusion.8), channel_id=1, source_target_pairs={{1,0},{2,1},{3,2},{4,3},{5,4},{6,5},{7,6},{8,7},{9,8},{10,9},{11,1... | collective-permute-start | bytes 245768 | tf_op jit(solution)/shard_map/ppermute | solution.py:30
  8.0 1.9 %collective-permute-start = (bf16[2,1,128,128]{3,0,2,1:T(2,128)(2,1)S(1)}, bf16[2,1,128,128]{3,0,2,1:T(2,128)(2,1)S(1)}, u32[]{:S(2)}, u32[]{:S(2)}) collective-permute-start(bf16[2,1,128,128]{3,0,2,1:T(2,128)(2,1)S(1)} %get-tuple-element.37), channel_id=1, source_target_pairs={{0,1},{1,2},{2,3},{3,4},{4,5},{5,6},{6,7},{7,8},{8,9},{9,10},{10,1... | collective-permute-start | bytes 196616 | tf_op jit(solution)/shard_map/ppermute | solution.py:30
  9.9 0.8 reduce-window_clone.1
  10.7 0.7 subtract_bitcast_fusion
  11.7 0.6 fusion.161
  14.3 1.4 broadcast_multiply_fusion.5
  15.7 0.7 slice.206
  16.4 0.6 slice.210
  17.1 0.6 pad_maximum_fusion.5
  17.7 4.0 %collective-permute-start.2 = (bf16[2,6,128,128]{3,0,2,1:T(2,128)(2,1)S(1)}, bf16[2,6,128,128]{3,0,2,1:T(2,128)(2,1)S(1)}, u32[]{:S(2)}, u32[]{:S(2)}) collective-permute-start(bf16[2,6,128,128]{3,0,2,1:T(2,128)(2,1)S(1)} %pad_maximum_fusion.5), channel_id=1, source_target_pairs={{0,16},{16,32},{32,48},{48,64},{64,80},{80,96},{96,112},{1,17},{17... | collective-permute-start | bytes 1179656 | tf_op jit(solution)/shard_map/ppermute | solution.py:30
  21.7 1.3 collective-permute-start.5
  23.0 0.6 fusion.168
  24.0 3.7 %collective-permute-done.5 = bf16[1,3,64,128]{3,2,1,0:T(8,128)(2,1)S(1)} collective-permute-done((bf16[1,3,64,128]{3,2,1,0:T(8,128)(2,1)S(1)}, bf16[1,3,64,128]{3,2,1,0:T(8,128)(2,1)S(1)}, u32[]{:S(2)}, u32[]{:S(2)}) %collective-permute-start.5) | collective-permute-done | bytes 49184 | tf_op jit(solution)/shard_map/ppermute | solution.py:30
  27.7 1.3 multiply_bitcast_fusion.1
  29.1 0.3 fusion.9
  29.8 0.3 convolution_select_fusion.5
  30.2 0.3 fusion.8
  31.1 1.0 pad_maximum_fusion.2
  32.7 0.8 fusion.6
  33.7 0.8 fusion.5
  34.7 1.0 add_divide_fusion
  35.9 2.4 %collective-permute-start.3 = (bf16[2,1,128,128]{3,0,2,1:T(2,128)(2,1)S(1)}, bf16[2,1,128,128]{3,0,2,1:T(2,128)(2,1)S(1)}, u32[]{:S(2)}, u32[]{:S(2)}) collective-permute-start(bf16[2,1,128,128]{3,0,2,1:T(2,128)(2,1)S(1)} %bitcast.307), channel_id=1, source_target_pairs={{0,1},{1,2},{2,3},{3,4},{4,5},{5,6},{6,7},{7,8},{8,9},{9,10},{10,1... | collective-permute-start | bytes 196616 | tf_op jit(solution)/shard_map/ppermute | solution.py:30
  39.1 2.0 %convolution_bitcast_fusion.3 = f32[1,3,3,128,128]{4,3,2,1,0:T(8,128)S(1)} fusion(bf16[2,6,128,128]{3,0,2,1:T(2,128)(2,1)S(1)} %pad_maximum_fusion.5, bf16[2,4,128,128]{3,2,1,0:T(8,128)(2,1)S(1)} %get-tuple-element.36), kind=kOutput, calls=%fused_computation.14 | convolution fusion | flops 300417024 | bytes 1245184 | tf_op jit(solution)/shard_map/conv_general_dilated | solution.py:57
  41.1 2.0 %convolution_bitcast_fusion.4 = f32[1,3,3,128,128]{4,3,2,1,0:T(8,128)S(1)} fusion(bf16[2,6,128,128]{3,0,2,1:T(2,128)(2,1)S(1)} %pad_maximum_fusion.2, bf16[2,4,128,128]{3,2,1,0:T(8,128)(2,1)S(1)} %get-tuple-element.35), kind=kOutput, calls=%fused_computation.15 | convolution fusion | flops 300417024 | bytes 1245184 | tf_op jit(solution)/shard_map/conv_general_dilated | solution.py:57
  43.1 2.0 %convolution_bitcast_fusion.5 = f32[1,3,3,128,128]{4,3,2,1,0:T(8,128)S(1)} fusion(bf16[2,6,128,128]{3,0,2,1:T(2,128)(2,1)S(1)} %collective-permute-done.2, bf16[2,4,128,128]{3,2,1,0:T(8,128)(2,1)S(1)} %get-tuple-element.24), kind=kOutput, calls=%fused_computation.16 | convolution fusion | flops 300417024 | bytes 1245184 | tf_op jit(solution)/shard_map/conv_general_dilated | solution.py:57
  45.7 0.4 pad_maximum_fusion.6
  46.2 3.8 %collective-permute-start.4 = (bf16[2,5,128,128]{3,0,2,1:T(2,128)(2,1)S(1)}, bf16[2,5,128,128]{3,0,2,1:T(2,128)(2,1)S(1)}, u32[]{:S(2)}, u32[]{:S(2)}) collective-permute-start(bf16[2,5,128,128]{3,0,2,1:T(2,128)(2,1)S(1)} %pad_maximum_fusion.6), channel_id=1, source_target_pairs={{0,16},{16,32},{32,48},{48,64},{64,80},{80,96},{96,112},{1,17},{17... | collective-permute-start | bytes 983048 | tf_op jit(solution)/shard_map/ppermute | solution.py:30
  50.0 0.4 slice_maximum_fusion
  50.4 0.8 convolution_bitcast_fusion
  51.3 4.1 %collective-permute-done.4 = bf16[2,5,128,128]{3,0,2,1:T(2,128)(2,1)S(1)} collective-permute-done((bf16[2,5,128,128]{3,0,2,1:T(2,128)(2,1)S(1)}, bf16[2,5,128,128]{3,0,2,1:T(2,128)(2,1)S(1)}, u32[]{:S(2)}, u32[]{:S(2)}) %collective-permute-start.4) | collective-permute-done | bytes 327712 | tf_op jit(solution)/shard_map/ppermute | solution.py:30
  55.4 0.5 fusion.159
  56.1 0.8 convolution_bitcast_fusion.1
  56.9 0.8 convolution_bitcast_fusion.2
  58.4 1.5 fusion.1
  60.0 1.9 %collective-permute-start.6 = (f32[2,2,2,2,2,112,128]{6,5,4,3,2,1,0:T(8,128)S(1)}, f32[2,2,2,2,2,112,128]{6,5,4,3,2,1,0:T(8,128)}, u32[]{:S(2)}, u32[]{:S(2)}) collective-permute-start(f32[2,2,2,2,2,112,128]{6,5,4,3,2,1,0:T(8,128)S(1)} %bitcast.280), channel_id=1, source_target_pairs={{0,128},{128,0},{256,384},{384,256},{1,129},{129,1},{257,385},{385... | collective-permute-start | bytes 5505032 | tf_op jit(solution)/shard_map/ppermute | solution.py:175
  62.0 3.8 %collective-permute-done.6 = f32[2,2,2,2,2,112,128]{6,5,4,3,2,1,0:T(8,128)} collective-permute-done((f32[2,2,2,2,2,112,128]{6,5,4,3,2,1,0:T(8,128)S(1)}, f32[2,2,2,2,2,112,128]{6,5,4,3,2,1,0:T(8,128)}, u32[]{:S(2)}, u32[]{:S(2)}) %collective-permute-start.6) | collective-permute-done | bytes 1835040 | tf_op jit(solution)/shard_map/ppermute | solution.py:175
  65.8 2.3 %bitcast_add_fusion = f32[2,2,2,2,2,112,128]{6,5,4,3,2,1,0:T(8,128)S(1)} fusion(f32[2,2,2,2,2,112,128]{6,5,4,3,2,1,0:T(8,128)} %collective-permute-done.6, f32[2,1,2,2,2,2,112,128]{7,6,5,4,3,1,0,2:T(8,128)} %get-tuple-element.26), kind=kLoop, calls=%fused_computation.7 | loop fusion | flops 458752 | bytes 5505024 | tf_op jit(solution)/shard_map/add | solution.py:217
  68.3 3.2 %collective-permute-start.7 = (f32[2,2,2,2,112,128]{5,4,3,2,1,0:T(8,128)S(1)}, f32[2,2,2,2,112,128]{5,4,3,2,1,0:T(8,128)}, u32[]{:S(2)}, u32[]{:S(2)}) collective-permute-start(f32[2,2,2,2,112,128]{5,4,3,2,1,0:T(8,128)S(1)} %bitcast_select_fusion), channel_id=1, source_target_pairs={{0,1},{1,0},{2,3},{3,2},{4,5},{5,4},{6,7},{7,6},{8,9},{9,8},{10,11... | collective-permute-start | bytes 2752520 | tf_op jit(solution)/shard_map/ppermute | solution.py:188
  71.5 12.2 %collective-permute-done.7 = f32[2,2,2,2,112,128]{5,4,3,2,1,0:T(8,128)} collective-permute-done((f32[2,2,2,2,112,128]{5,4,3,2,1,0:T(8,128)S(1)}, f32[2,2,2,2,112,128]{5,4,3,2,1,0:T(8,128)}, u32[]{:S(2)}, u32[]{:S(2)}) %collective-permute-start.7) | collective-permute-done | bytes 917536 | tf_op jit(solution)/shard_map/ppermute | solution.py:188
  83.7 1.3 fusion.19
  85.1 2.8 %collective-permute-start.8 = (f32[2,2,2,112,128]{4,3,2,1,0:T(8,128)S(1)}, f32[2,2,2,112,128]{4,3,2,1,0:T(8,128)S(1)}, u32[]{:S(2)}, u32[]{:S(2)}) collective-permute-start(f32[2,2,2,112,128]{4,3,2,1,0:T(8,128)S(1)} %bitcast_select_fusion.2), channel_id=1, source_target_pairs={{0,4},{1,5},{2,6},{3,7},{4,0},{5,1},{6,2},{7,3},{8,12},{9,13},{10,... | collective-permute-start | bytes 1376264 | tf_op jit(solution)/shard_map/ppermute | solution.py:188
  87.9 7.6 %collective-permute-done.8 = f32[2,2,2,112,128]{4,3,2,1,0:T(8,128)S(1)} collective-permute-done((f32[2,2,2,112,128]{4,3,2,1,0:T(8,128)S(1)}, f32[2,2,2,112,128]{4,3,2,1,0:T(8,128)S(1)}, u32[]{:S(2)}, u32[]{:S(2)}) %collective-permute-start.8) | collective-permute-done | bytes 458784 | tf_op jit(solution)/shard_map/ppermute | solution.py:188
  95.7 4.3 %collective-permute-start.9 = (f32[2,2,112,128]{3,2,1,0:T(8,128)S(1)}, f32[2,2,112,128]{3,2,1,0:T(8,128)S(1)}, u32[]{:S(2)}, u32[]{:S(2)}) collective-permute-start(f32[2,2,112,128]{3,2,1,0:T(8,128)S(1)} %bitcast_select_fusion.4), channel_id=1, source_target_pairs={{0,3},{1,2},{2,1},{3,0},{4,7},{5,6},{6,5},{7,4},{8,11},{9,10},{10,... | collective-permute-start | bytes 688136 | tf_op jit(solution)/shard_map/ppermute | solution.py:188
  100.3 4.5 %collective-permute-done.9 = f32[2,2,112,128]{3,2,1,0:T(8,128)S(1)} collective-permute-done((f32[2,2,112,128]{3,2,1,0:T(8,128)S(1)}, f32[2,2,112,128]{3,2,1,0:T(8,128)S(1)}, u32[]{:S(2)}, u32[]{:S(2)}) %collective-permute-start.9) | collective-permute-done | bytes 229408 | tf_op jit(solution)/shard_map/ppermute | solution.py:188
  104.9 2.7 %collective-permute-start.10 = (f32[2,112,128]{2,1,0:T(8,128)S(1)}, f32[2,112,128]{2,1,0:T(8,128)S(1)}, u32[]{:S(2)}, u32[]{:S(2)}) collective-permute-start(f32[2,112,128]{2,1,0:T(8,128)S(1)} %select_bitcast_fusion), channel_id=1, source_target_pairs={{0,12},{1,13},{2,14},{3,15},{4,8},{5,9},{6,10},{7,11},{8,4},{9,5},... | collective-permute-start | bytes 344072 | tf_op jit(solution)/shard_map/ppermute | solution.py:188
  107.7 1.9 %fusion.10 = f32[2,8,9,128]{3,1,2,0:T(8,128)S(1)} fusion(bf16[3,3,3,128,128]{4,3,2,1,0:T(8,128)(2,1)} %param.10, bf16[5,1,7,2,128]{4,2,3,0,1:T(8,128)(2,1)S(1)} %slice.219, bf16[5,1,8,18,128]{4,2,3,0,1:T(8,128)(2,1)S(1)} %copy.286, f32[]{:T(128)} %bitcast.60, pred[8,9]{0,1:T(8,128)(4,1)S(1)} %copy-done.8), kind=kOutput, calls=%fused_computation.32 | convolution fusion | flops 43118592 | bytes 571464 | tf_op jit(solution)/shard_map/conv_general_dilated | solution.py:37
  109.8 3.0 %collective-permute-done.10 = f32[2,112,128]{2,1,0:T(8,128)S(1)} collective-permute-done((f32[2,112,128]{2,1,0:T(8,128)S(1)}, f32[2,112,128]{2,1,0:T(8,128)S(1)}, u32[]{:S(2)}, u32[]{:S(2)}) %collective-permute-start.10) | collective-permute-done | bytes 114720 | tf_op jit(solution)/shard_map/ppermute | solution.py:188
  112.8 5.0 %collective-permute-start.11 = (f32[2,112,128]{2,1,0:T(8,128)S(1)}, f32[2,112,128]{2,1,0:T(8,128)S(1)}, u32[]{:S(2)}, u32[]{:S(2)}) collective-permute-start(f32[2,112,128]{2,1,0:T(8,128)S(1)} %fusion.92), channel_id=1, source_target_pairs={{0,16},{16,0},{32,48},{48,32},{64,80},{80,64},{96,112},{112,96},{1... | collective-permute-start | bytes 344072 | tf_op jit(solution)/shard_map/ppermute | solution.py:175
  117.9 1.9 %fusion.11 = f32[2,8,9,128]{3,1,2,0:T(8,128)S(1)} fusion(bf16[3,3,3,128,128]{4,3,2,1,0:T(8,128)(2,1)} %param.10, bf16[5,1,7,2,128]{4,2,3,0,1:T(8,128)(2,1)S(1)} %slice.216, bf16[5,1,8,18,128]{4,2,3,0,1:T(8,128)(2,1)S(1)} %copy.284, f32[]{:T(128)} %bitcast.58, pred[8,9]{0,1:T(8,128)(4,1)S(1)} %copy-done.8), kind=kOutput, calls=%fused_computation.34 | convolution fusion | flops 43118592 | bytes 571464 | tf_op jit(solution)/shard_map/conv_general_dilated | solution.py:37
  119.9 0.7 collective-permute-done.11
  120.6 6.7 %collective-permute-start.12 = (f32[2,112,128]{2,1,0:T(8,128)S(1)}, f32[2,112,128]{2,1,0:T(8,128)S(1)}, u32[]{:S(2)}, u32[]{:S(2)}) collective-permute-start(f32[2,112,128]{2,1,0:T(8,128)S(1)} %add.203), channel_id=1, source_target_pairs={{0,32},{16,48},{32,0},{48,16},{64,96},{80,112},{96,64},{112,80},{1... | collective-permute-start | bytes 344072 | tf_op jit(solution)/shard_map/ppermute | solution.py:175
  127.4 1.9 %fusion.15 = bf16[2,8,9,128]{3,1,2,0:T(8,128)(2,1)S(1)} fusion(f32[2,8,9,128]{3,1,2,0:T(8,128)S(1)} %fusion.10, f32[2,8,9,128]{3,1,2,0:T(8,128)S(1)} %fusion.11, bf16[3,3,3,128,128]{4,3,2,1,0:T(8,128)(2,1)} %param.10, bf16[5,1,7,2,128]{4,2,3,0,1:T(8,128)(2,1)S(1)} %slice.215, bf16[5,1,8,18,128]{4,2,3,0,1:T(8,128)(2,1)S(1)} %copy.282, f32[]{:T(128)} %bitcast.56, ...), kind=kOutput, calls=%fused_computation.39 | convolution fusion | flops 43173888 | bytes 682056 | tf_op jit(solution)/shard_map/conv_general_dilated | solution.py:37
  129.3 0.8 collective-permute-done.12
  130.2 13.3 %collective-permute-start.15 = (f32[112,128]{1,0:T(8,128)S(1)}, f32[112,128]{1,0:T(8,128)S(1)}, u32[]{:S(2)}, u32[]{:S(2)}) collective-permute-start(f32[112,128]{1,0:T(8,128)S(1)} %get-tuple-element.40), channel_id=1, source_target_pairs={{0,320},{16,336},{32,352},{48,368},{64,256},{80,272},{96,288},{112... | collective-permute-start | bytes 172040 | tf_op jit(solution)/shard_map/ppermute | solution.py:247
  143.5 3.4 %collective-permute-start.14 = (f32[112,128]{1,0:T(8,128)S(1)}, f32[112,128]{1,0:T(8,128)S(1)}, u32[]{:S(2)}, u32[]{:S(2)}) collective-permute-start(f32[112,128]{1,0:T(8,128)S(1)} %get-tuple-element.40), channel_id=1, source_target_pairs={{0,256},{16,272},{32,288},{48,304},{64,320},{80,336},{96,352},{112... | collective-permute-start | bytes 172040 | tf_op jit(solution)/shard_map/ppermute | solution.py:247
  146.9 5.8 %collective-permute-start.13 = (f32[112,128]{1,0:T(8,128)S(1)}, f32[112,128]{1,0:T(8,128)S(1)}, u32[]{:S(2)}, u32[]{:S(2)}) collective-permute-start(f32[112,128]{1,0:T(8,128)S(1)} %get-tuple-element.39), channel_id=1, source_target_pairs={{0,64},{16,80},{32,96},{48,112},{64,0},{80,16},{96,32},{112,48},{1... | collective-permute-start | bytes 172040 | tf_op jit(solution)/shard_map/ppermute | solution.py:247
  152.7 0.6 copy.298
  153.3 5.5 %collective-permute-done.14 = f32[112,128]{1,0:T(8,128)S(1)} collective-permute-done((f32[112,128]{1,0:T(8,128)S(1)}, f32[112,128]{1,0:T(8,128)S(1)}, u32[]{:S(2)}, u32[]{:S(2)}) %collective-permute-start.14) | collective-permute-done | bytes 57376 | tf_op jit(solution)/shard_map/ppermute | solution.py:247
  158.8 0.5 collective-permute-done.13
  159.3 23.4 %all-gather = bf16[1792,128]{1,0:T(8,128)(2,1)S(1)} all-gather(bf16[112,128]{1,0:T(8,128)(2,1)S(1)} %add_convert_fusion), channel_id=2, replica_groups=mesh['dp'=4,'tm'=8,'height'=16] {'height'}, dimensions={0}, use_global_device_ids=true | all-gather | bytes 487424 | tf_op jit(solution)/shard_map/all_gather | solution.py:251
  182.7 0.6 gather_fusion
  183.3 0.8 fusion.158
  (121 shorter events, 6.2 us)
Async XLA Ops:
  2.8 14.2 %collective-permute-start.1 = (bf16[40960]{0:T(1024)(128)(2,1)S(1)}, bf16[40960]{0:T(1024)(128)(2,1)S(1)}, u32[]{:S(2)}, u32[]{:S(2)}) collective-permute-start(bf16[40960]{0:T(1024)(128)(2,1)S(1)} %pad_maximum_fusion.8), channel_id=1, source_target_pairs={{1,0},{2,1},{3,2},{4,3},{5,4},{6,5},{7,6},{8,7},{9,8},{10,9},{11,1... | collective-permute-start | bytes 245768 | tf_op jit(solution)/shard_map/ppermute | solution.py:30
  8.0 9.1 %collective-permute-start = (bf16[2,1,128,128]{3,0,2,1:T(2,128)(2,1)S(1)}, bf16[2,1,128,128]{3,0,2,1:T(2,128)(2,1)S(1)}, u32[]{:S(2)}, u32[]{:S(2)}) collective-permute-start(bf16[2,1,128,128]{3,0,2,1:T(2,128)(2,1)S(1)} %get-tuple-element.37), channel_id=1, source_target_pairs={{0,1},{1,2},{2,3},{3,4},{4,5},{5,6},{6,7},{7,8},{8,9},{9,10},{10,1... | collective-permute-start | bytes 196616 | tf_op jit(solution)/shard_map/ppermute | solution.py:30
  17.7 11.4 %copy-start.5 = (bf16[3,3,3,128,128]{4,3,2,1,0:T(8,128)(2,1)S(1)}, bf16[3,3,3,128,128]{4,3,2,1,0:T(8,128)(2,1)}, u32[]{:S(2)}) copy-start(bf16[3,3,3,128,128]{4,3,2,1,0:T(8,128)(2,1)} %param.10) | copy-start | bytes 2654212
  17.7 11.4 %copy-start.7 = (pred[8,18]{0,1:T(8,128)(4,1)S(1)}, pred[8,18]{0,1:T(8,128)(4,1)}, u32[]{:S(2)}) copy-start(pred[8,18]{0,1:T(8,128)(4,1)} %constant.265) | copy-start | bytes 436
  17.7 13.0 %collective-permute-start.2 = (bf16[2,6,128,128]{3,0,2,1:T(2,128)(2,1)S(1)}, bf16[2,6,128,128]{3,0,2,1:T(2,128)(2,1)S(1)}, u32[]{:S(2)}, u32[]{:S(2)}) collective-permute-start(bf16[2,6,128,128]{3,0,2,1:T(2,128)(2,1)S(1)} %pad_maximum_fusion.5), channel_id=1, source_target_pairs={{0,16},{16,32},{32,48},{48,64},{64,80},{80,96},{96,112},{1,17},{17... | collective-permute-start | bytes 1179656 | tf_op jit(solution)/shard_map/ppermute | solution.py:30
  21.7 6.0 %collective-permute-start.5 = (bf16[1,3,64,128]{3,2,1,0:T(8,128)(2,1)S(1)}, bf16[1,3,64,128]{3,2,1,0:T(8,128)(2,1)S(1)}, u32[]{:S(2)}, u32[]{:S(2)}) collective-permute-start(bf16[1,3,64,128]{3,2,1,0:T(8,128)(2,1)S(1)} %pad_maximum_fusion.9), channel_id=1, source_target_pairs={{16,0},{32,16},{48,32},{64,48},{80,64},{96,80},{112,96},{17,1},{33... | collective-permute-start | bytes 147464 | tf_op jit(solution)/shard_map/ppermute | solution.py:30
  31.1 1.6 copy-start.4
  31.1 1.6 copy-start.6
  35.9 9.9 %collective-permute-start.3 = (bf16[2,1,128,128]{3,0,2,1:T(2,128)(2,1)S(1)}, bf16[2,1,128,128]{3,0,2,1:T(2,128)(2,1)S(1)}, u32[]{:S(2)}, u32[]{:S(2)}) collective-permute-start(bf16[2,1,128,128]{3,0,2,1:T(2,128)(2,1)S(1)} %bitcast.307), channel_id=1, source_target_pairs={{0,1},{1,2},{2,3},{3,4},{4,5},{5,6},{6,7},{7,8},{8,9},{9,10},{10,1... | collective-permute-start | bytes 196616 | tf_op jit(solution)/shard_map/ppermute | solution.py:30
  46.2 9.2 %collective-permute-start.4 = (bf16[2,5,128,128]{3,0,2,1:T(2,128)(2,1)S(1)}, bf16[2,5,128,128]{3,0,2,1:T(2,128)(2,1)S(1)}, u32[]{:S(2)}, u32[]{:S(2)}) collective-permute-start(bf16[2,5,128,128]{3,0,2,1:T(2,128)(2,1)S(1)} %pad_maximum_fusion.6), channel_id=1, source_target_pairs={{0,16},{16,32},{32,48},{48,64},{64,80},{80,96},{96,112},{1,17},{17... | collective-permute-start | bytes 983048 | tf_op jit(solution)/shard_map/ppermute | solution.py:30
  50.4 0.8 copy-start
  56.1 0.8 copy-start.2
  60.0 5.8 %collective-permute-start.6 = (f32[2,2,2,2,2,112,128]{6,5,4,3,2,1,0:T(8,128)S(1)}, f32[2,2,2,2,2,112,128]{6,5,4,3,2,1,0:T(8,128)}, u32[]{:S(2)}, u32[]{:S(2)}) collective-permute-start(f32[2,2,2,2,2,112,128]{6,5,4,3,2,1,0:T(8,128)S(1)} %bitcast.280), channel_id=1, source_target_pairs={{0,128},{128,0},{256,384},{384,256},{1,129},{129,1},{257,385},{385... | collective-permute-start | bytes 5505032 | tf_op jit(solution)/shard_map/ppermute | solution.py:175
  68.3 15.4 %collective-permute-start.7 = (f32[2,2,2,2,112,128]{5,4,3,2,1,0:T(8,128)S(1)}, f32[2,2,2,2,112,128]{5,4,3,2,1,0:T(8,128)}, u32[]{:S(2)}, u32[]{:S(2)}) collective-permute-start(f32[2,2,2,2,112,128]{5,4,3,2,1,0:T(8,128)S(1)} %bitcast_select_fusion), channel_id=1, source_target_pairs={{0,1},{1,0},{2,3},{3,2},{4,5},{5,4},{6,7},{7,6},{8,9},{9,8},{10,11... | collective-permute-start | bytes 2752520 | tf_op jit(solution)/shard_map/ppermute | solution.py:188
  85.0 15.1 %copy-start.3 = (s32[16]{0:T(128)S(1)}, s32[16]{0:T(128)}, u32[]{:S(2)}) copy-start(s32[16]{0:T(128)} %constant.271) | copy-start | bytes 196
  85.0 15.1 %copy-start.1 = (bf16[1,5,128,128]{3,0,2,1:T(2,128)(2,1)S(1)}, bf16[1,5,128,128]{3,0,2,1:T(2,128)(2,1)}, u32[]{:S(2)}) copy-start(bf16[1,5,128,128]{3,0,2,1:T(2,128)(2,1)} %copy-done) | copy-start | bytes 491524
  85.1 10.5 %collective-permute-start.8 = (f32[2,2,2,112,128]{4,3,2,1,0:T(8,128)S(1)}, f32[2,2,2,112,128]{4,3,2,1,0:T(8,128)S(1)}, u32[]{:S(2)}, u32[]{:S(2)}) collective-permute-start(f32[2,2,2,112,128]{4,3,2,1,0:T(8,128)S(1)} %bitcast_select_fusion.2), channel_id=1, source_target_pairs={{0,4},{1,5},{2,6},{3,7},{4,0},{5,1},{6,2},{7,3},{8,12},{9,13},{10,... | collective-permute-start | bytes 1376264 | tf_op jit(solution)/shard_map/ppermute | solution.py:188
  95.6 12.0 %copy-start.8 = (pred[8,9]{0,1:T(8,128)(4,1)S(1)}, pred[8,9]{0,1:T(8,128)(4,1)}, u32[]{:S(2)}) copy-start(pred[8,9]{0,1:T(8,128)(4,1)} %constant.261) | copy-start | bytes 220
  95.7 9.1 %collective-permute-start.9 = (f32[2,2,112,128]{3,2,1,0:T(8,128)S(1)}, f32[2,2,112,128]{3,2,1,0:T(8,128)S(1)}, u32[]{:S(2)}, u32[]{:S(2)}) collective-permute-start(f32[2,2,112,128]{3,2,1,0:T(8,128)S(1)} %bitcast_select_fusion.4), channel_id=1, source_target_pairs={{0,3},{1,2},{2,1},{3,0},{4,7},{5,6},{6,5},{7,4},{8,11},{9,10},{10,... | collective-permute-start | bytes 688136 | tf_op jit(solution)/shard_map/ppermute | solution.py:188
  104.9 7.9 %collective-permute-start.10 = (f32[2,112,128]{2,1,0:T(8,128)S(1)}, f32[2,112,128]{2,1,0:T(8,128)S(1)}, u32[]{:S(2)}, u32[]{:S(2)}) collective-permute-start(f32[2,112,128]{2,1,0:T(8,128)S(1)} %select_bitcast_fusion), channel_id=1, source_target_pairs={{0,12},{1,13},{2,14},{3,15},{4,8},{5,9},{6,10},{7,11},{8,4},{9,5},... | collective-permute-start | bytes 344072 | tf_op jit(solution)/shard_map/ppermute | solution.py:188
  112.8 7.8 %collective-permute-start.11 = (f32[2,112,128]{2,1,0:T(8,128)S(1)}, f32[2,112,128]{2,1,0:T(8,128)S(1)}, u32[]{:S(2)}, u32[]{:S(2)}) collective-permute-start(f32[2,112,128]{2,1,0:T(8,128)S(1)} %fusion.92), channel_id=1, source_target_pairs={{0,16},{16,0},{32,48},{48,32},{64,80},{80,64},{96,112},{112,96},{1... | collective-permute-start | bytes 344072 | tf_op jit(solution)/shard_map/ppermute | solution.py:175
  120.6 9.5 %collective-permute-start.12 = (f32[2,112,128]{2,1,0:T(8,128)S(1)}, f32[2,112,128]{2,1,0:T(8,128)S(1)}, u32[]{:S(2)}, u32[]{:S(2)}) collective-permute-start(f32[2,112,128]{2,1,0:T(8,128)S(1)} %add.203), channel_id=1, source_target_pairs={{0,32},{16,48},{32,0},{48,16},{64,96},{80,112},{96,64},{112,80},{1... | collective-permute-start | bytes 344072 | tf_op jit(solution)/shard_map/ppermute | solution.py:175
  130.2 23.2 %collective-permute-start.15 = (f32[112,128]{1,0:T(8,128)S(1)}, f32[112,128]{1,0:T(8,128)S(1)}, u32[]{:S(2)}, u32[]{:S(2)}) collective-permute-start(f32[112,128]{1,0:T(8,128)S(1)} %get-tuple-element.40), channel_id=1, source_target_pairs={{0,320},{16,336},{32,352},{48,368},{64,256},{80,272},{96,288},{112... | collective-permute-start | bytes 172040 | tf_op jit(solution)/shard_map/ppermute | solution.py:247
  143.5 15.3 %collective-permute-start.14 = (f32[112,128]{1,0:T(8,128)S(1)}, f32[112,128]{1,0:T(8,128)S(1)}, u32[]{:S(2)}, u32[]{:S(2)}) collective-permute-start(f32[112,128]{1,0:T(8,128)S(1)} %get-tuple-element.40), channel_id=1, source_target_pairs={{0,256},{16,272},{32,288},{48,304},{64,320},{80,336},{96,352},{112... | collective-permute-start | bytes 172040 | tf_op jit(solution)/shard_map/ppermute | solution.py:247
  146.9 12.4 %collective-permute-start.13 = (f32[112,128]{1,0:T(8,128)S(1)}, f32[112,128]{1,0:T(8,128)S(1)}, u32[]{:S(2)}, u32[]{:S(2)}) collective-permute-start(f32[112,128]{1,0:T(8,128)S(1)} %get-tuple-element.39), channel_id=1, source_target_pairs={{0,64},{16,80},{32,96},{48,112},{64,0},{80,16},{96,32},{112,48},{1... | collective-permute-start | bytes 172040 | tf_op jit(solution)/shard_map/ppermute | solution.py:247

commit v11 on v8

--- a/solution.py
+++ b/solution.py
@@ -137,11 +137,6 @@
     pre_act = wide_pre[:, 1:]
     input_ext = wide_ext[:, 1:]
     hidden_past = shifted(hidden_rows, "tm", 1)
-    hidden_ext = jnp.concatenate([hidden_past, hidden_rows], axis=0)
-    encoded = conv_layer(hidden_ext, conv_down, down_mask, down_frames, 2, (1, 0)).astype(
-        jnp.bfloat16
-    )
-    down_local = weight_grad(hidden_ext, grads, down_mask, 2, (1, 0))
     grads_rows = jnp.concatenate([grads, below], axis=1)
     grads_next = shifted(grads_rows, "tm", -1)
     grads_ext = jnp.concatenate([grads_rows, grads_next], axis=0)
@@ -151,6 +146,12 @@
         jnp.bfloat16
     )
     first_local = weight_grad(input_ext, pre_grad, first_mask, 1, (1, 1))
+    hidden_past, first_local = lax.optimization_barrier((hidden_past, first_local))
+    hidden_ext = jnp.concatenate([hidden_past, hidden_rows], axis=0)
+    encoded = conv_layer(hidden_ext, conv_down, down_mask, down_frames, 2, (1, 0)).astype(
+        jnp.bfloat16
+    )
+    down_local = weight_grad(hidden_ext, grads, down_mask, 2, (1, 0))
     share = conv_first.shape[3] // lax.axis_size("dp")
     quarters = lax.axis_size("dp")
 

time: 182 us -> 182 us (level)
  no operation moved by 1% of the time
where the time goes in v11:
time: 182 us; the launch traced here: 180 us
  starting transfers between devices  63.3 us (35%)
  waiting for transfers between devices  44.9 us (25%)
  blocking collectives  23.3 us (13%)
  matrix products  17.4 us (10%)
  local copies, waits for them, and re-layouts  14.3 us (8%)
  other arithmetic  13.1 us (7%)
  between operations  3.93 us (2%)
    ppermute x5, starting transfers between devices, swap(): lax.ppermute(value, axis, [(i, i ^ bit) for i in range(lax.axis_size(axis...  33.7 us
    ppermute x4, waiting for transfers between devices, swap_rows(): return lax.ppermute(value, ('dp', 'height'), pairs)  30.7 us
    all_gather x1, blocking collectives, reduce_gradients(): gathered = lax.all_gather(piece, 'height', axis=0, tiled=False)  23.3 us
    ppermute x5, starting transfers between devices, shifted(): lax.ppermute(value, axis, [(source, source + steps) for source in range(l...  17.6 us
    ppermute x4, starting transfers between devices, swap_rows(): return lax.ppermute(value, ('dp', 'height'), pairs)  12 us
    conv_general_dilated x6, matrix products, weight_grad(): lax.conv_general_dilated(frame_slab, masked, (1, 1), ((0, 0), pad_cols),...  9.56 us
    ppermute x5, waiting for transfers between devices, swap(): lax.ppermute(value, axis, [(i, i ^ bit) for i in range(lax.axis_size(axis...  9.38 us
    conv_general_dilated x6, matrix products, conv_layer(): lax.conv_general_dilated(frame_slab, weight[tap_time], (stride, stride),...  6.87 us
  transfers between devices with their start and end apart: 14, of which 10 were waited for; matrix products, arithmetic and copies ran while one was open for 14% of the time, Pallas kernels for 0%

profile of v11, /device:TPU:6, one launch (start us, length us, event | category | flops | bytes accessed | tf_op | source)
XLA Modules:
  0.0 180.3 jit_solution(5397155313829638726)
XLA Ops:
  0.6 0.8 fusion.124
  1.4 1.2 copy.338
  2.7 5.2 %collective-permute-start.1 = (bf16[40960]{0:T(1024)(128)(2,1)S(1)}, bf16[40960]{0:T(1024)(128)(2,1)S(1)}, u32[]{:S(2)}, u32[]{:S(2)}) collective-permute-start(bf16[40960]{0:T(1024)(128)(2,1)S(1)} %pad_maximum_fusion.6), channel_id=1, source_target_pairs={{1,0},{2,1},{3,2},{4,3},{5,4},{6,5},{7,6},{8,7},{9,8},{10,9},{11,1... | collective-permute-start | bytes 245768 | tf_op jit(solution)/shard_map/ppermute | solution.py:30
  8.0 1.9 %collective-permute-start = (bf16[2,2,128,128]{3,0,2,1:T(2,128)(2,1)S(1)}, bf16[2,2,128,128]{3,0,2,1:T(2,128)(2,1)S(1)}, u32[]{:S(2)}, u32[]{:S(2)}) collective-permute-start(bf16[2,2,128,128]{3,0,2,1:T(2,128)(2,1)S(1)} %slice.201), channel_id=1, source_target_pairs={{0,1},{1,2},{2,3},{3,4},{4,5},{5,6},{6,7},{7,8},{8,9},{9,10},{10,1... | collective-permute-start | bytes 393224 | tf_op jit(solution)/shard_map/ppermute | solution.py:30
  10.0 0.8 reduce-window_clone.1
  10.8 0.7 subtract_bitcast_fusion
  11.9 1.0 reshape.218
  13.1 1.0 reshape.212
  14.3 0.5 fusion.167
  14.8 0.6 slice.215
  15.4 0.7 slice.219
  18.0 0.6 broadcast_multiply_fusion.5
  18.8 1.3 collective-permute-start.4
  20.1 0.7 fusion.173
  20.8 0.7 pad_maximum_fusion.2
  21.5 0.4 pad.13
  22.0 4.6 %collective-permute-start.2 = (bf16[2,7,128,128]{3,0,2,1:T(2,128)(2,1)S(1)}, bf16[2,7,128,128]{3,0,2,1:T(2,128)(2,1)S(1)}, u32[]{:S(2)}, u32[]{:S(2)}) collective-permute-start(bf16[2,7,128,128]{3,0,2,1:T(2,128)(2,1)S(1)} %pad_maximum_fusion.2), channel_id=1, source_target_pairs={{0,16},{16,32},{32,48},{48,64},{64,80},{80,96},{96,112},{1,17},{17... | collective-permute-start | bytes 1376264 | tf_op jit(solution)/shard_map/ppermute | solution.py:30
  26.6 1.3 multiply_bitcast_fusion.1
  30.0 1.1 fusion.2
  31.1 4.9 %collective-permute-done.2 = bf16[2,7,128,128]{3,0,2,1:T(2,128)(2,1)S(1)} collective-permute-done((bf16[2,7,128,128]{3,0,2,1:T(2,128)(2,1)S(1)}, bf16[2,7,128,128]{3,0,2,1:T(2,128)(2,1)S(1)}, u32[]{:S(2)}, u32[]{:S(2)}) %collective-permute-start.2) | collective-permute-done | bytes 458784 | tf_op jit(solution)/shard_map/ppermute | solution.py:30
  35.9 0.9 maximum_maximum_fusion
  36.9 0.5 slice_bitcast_fusion
  37.4 0.4 pad.11
  37.9 0.4 pad.9
  38.6 1.1 fusion.3
  39.7 2.0 %fusion.50 = (bf16[5,16,17,128]{3,1,2,0:T(8,128)(2,1)S(1)}, f32[5,16,17,128]{3,1,2,0:T(8,128)}) fusion(pred[5]{0:T(512)(128)(4,1)S(1)} %iota_compare_fusion.3, f32[5,16,17,128]{3,1,2,0:T(8,128)S(1)} %fusion.2, f32[5,16,17,128]{3,1,2,0:T(8,128)S(1)} %fusion.3, f32[5,16,17,128]{3,2,1,0:T(8,128)S(1)} %reshape.206, ...), kind=kOutput, calls=%fused_computation.86 | convolution fusion | flops 404455424 | bytes 4263424 | tf_op jit(solution)/shard_map/conv_general_dilated | solution.py:37
  42.0 0.3 copy.337
  42.3 4.6 %collective-permute-start.3 = (bf16[2,5,128,128]{3,0,2,1:T(2,128)(2,1)S(1)}, bf16[2,5,128,128]{3,0,2,1:T(2,128)(2,1)S(1)}, u32[]{:S(2)}, u32[]{:S(2)}) collective-permute-start(bf16[2,5,128,128]{3,0,2,1:T(2,128)(2,1)S(1)} %bitcast.287), channel_id=1, source_target_pairs={{0,16},{16,32},{32,48},{48,64},{64,80},{80,96},{96,112},{1,17},{17... | collective-permute-start | bytes 983048 | tf_op jit(solution)/shard_map/ppermute | solution.py:30
  47.9 0.7 copy-done.5
  48.6 2.1 %convolution_bitcast_fusion.3 = f32[1,3,3,128,128]{4,3,2,1,0:T(8,128)S(1)} fusion(bf16[2,7,128,128]{3,0,2,1:T(2,128)(2,1)S(1)} %copy-done.5, bf16[2,4,128,128]{3,2,1,0:T(8,128)(2,1)S(1)} %get-tuple-element.35), kind=kOutput, calls=%fused_computation.22 | convolution fusion | flops 300417024 | bytes 1310720 | tf_op jit(solution)/shard_map/conv_general_dilated | solution.py:57
  50.7 3.0 %convolution_bitcast_fusion.4 = f32[1,3,3,128,128]{4,3,2,1,0:T(8,128)S(1)} fusion(bf16[2,7,128,128]{3,0,2,1:T(2,128)(2,1)S(1)} %collective-permute-done.2, bf16[2,1,128,128]{3,0,2,1:T(2,128)(2,1)S(1)} %copy.239, bf16[2,4,128,128]{3,0,2,1:T(2,128)(2,1)S(1)} %bitcast.277, bf16[2,2,128,128]{3,0,2,1:T(2,128)(2,1)S(1)} %collective-permute-done, ...), kind=kOutput, calls=%fused_computation.23 | convolution fusion | flops 301989888 | bytes 1769472 | tf_op jit(solution)/shard_map/conv_general_dilated | solution.py:57
  53.7 2.0 %convolution_bitcast_fusion.5 = f32[1,3,3,128,128]{4,3,2,1,0:T(8,128)S(1)} fusion(bf16[2,7,128,128]{3,0,2,1:T(2,128)(2,1)S(1)} %collective-permute-done.2, bf16[2,4,128,128]{3,2,1,0:T(8,128)(2,1)S(1)} %get-tuple-element.24), kind=kOutput, calls=%fused_computation.24 | convolution fusion | flops 300417024 | bytes 1310720 | tf_op jit(solution)/shard_map/conv_general_dilated | solution.py:57
  55.7 0.8 convolution_bitcast_fusion
  56.7 0.5 fusion.166
  57.3 0.9 convolution_bitcast_fusion.1
  58.2 0.8 convolution_bitcast_fusion.2
  59.6 1.5 fusion.1
  61.2 1.9 %collective-permute-start.5 = (f32[2,2,2,2,2,112,128]{6,5,4,3,2,1,0:T(8,128)S(1)}, f32[2,2,2,2,2,112,128]{6,5,4,3,2,1,0:T(8,128)}, u32[]{:S(2)}, u32[]{:S(2)}) collective-permute-start(f32[2,2,2,2,2,112,128]{6,5,4,3,2,1,0:T(8,128)S(1)} %bitcast.284), channel_id=1, source_target_pairs={{0,128},{128,0},{256,384},{384,256},{1,129},{129,1},{257,385},{385... | collective-permute-start | bytes 5505032 | tf_op jit(solution)/shard_map/ppermute | solution.py:178
  63.3 3.8 %collective-permute-done.5 = f32[2,2,2,2,2,112,128]{6,5,4,3,2,1,0:T(8,128)} collective-permute-done((f32[2,2,2,2,2,112,128]{6,5,4,3,2,1,0:T(8,128)S(1)}, f32[2,2,2,2,2,112,128]{6,5,4,3,2,1,0:T(8,128)}, u32[]{:S(2)}, u32[]{:S(2)}) %collective-permute-start.5) | collective-permute-done | bytes 1835040 | tf_op jit(solution)/shard_map/ppermute | solution.py:178
  67.1 2.3 %bitcast_add_fusion = f32[2,2,2,2,2,112,128]{6,5,4,3,2,1,0:T(8,128)S(1)} fusion(f32[2,2,2,2,2,112,128]{6,5,4,3,2,1,0:T(8,128)} %collective-permute-done.5, f32[2,1,2,2,2,2,112,128]{7,6,5,4,3,1,0,2:T(8,128)} %get-tuple-element.26), kind=kLoop, calls=%fused_computation.7 | loop fusion | flops 458752 | bytes 5505024 | tf_op jit(solution)/shard_map/add | solution.py:220
  69.5 1.9 %collective-permute-start.6 = (f32[2,2,2,2,112,128]{5,4,3,2,1,0:T(8,128)S(1)}, f32[2,2,2,2,112,128]{5,4,3,2,1,0:T(8,128)}, u32[]{:S(2)}, u32[]{:S(2)}) collective-permute-start(f32[2,2,2,2,112,128]{5,4,3,2,1,0:T(8,128)S(1)} %bitcast_select_fusion), channel_id=1, source_target_pairs={{0,1},{1,0},{2,3},{3,2},{4,5},{5,4},{6,7},{7,6},{8,9},{9,8},{10,11... | collective-permute-start | bytes 2752520 | tf_op jit(solution)/shard_map/ppermute | solution.py:191
  71.4 13.4 %collective-permute-done.6 = f32[2,2,2,2,112,128]{5,4,3,2,1,0:T(8,128)} collective-permute-done((f32[2,2,2,2,112,128]{5,4,3,2,1,0:T(8,128)S(1)}, f32[2,2,2,2,112,128]{5,4,3,2,1,0:T(8,128)}, u32[]{:S(2)}, u32[]{:S(2)}) %collective-permute-start.6) | collective-permute-done | bytes 917536 | tf_op jit(solution)/shard_map/ppermute | solution.py:191
  84.9 1.3 fusion.19
  86.3 2.4 %collective-permute-start.7 = (f32[2,2,2,112,128]{4,3,2,1,0:T(8,128)S(1)}, f32[2,2,2,112,128]{4,3,2,1,0:T(8,128)S(1)}, u32[]{:S(2)}, u32[]{:S(2)}) collective-permute-start(f32[2,2,2,112,128]{4,3,2,1,0:T(8,128)S(1)} %bitcast_select_fusion.2), channel_id=1, source_target_pairs={{0,4},{1,5},{2,6},{3,7},{4,0},{5,1},{6,2},{7,3},{8,12},{9,13},{10,... | collective-permute-start | bytes 1376264 | tf_op jit(solution)/shard_map/ppermute | solution.py:191
  88.8 7.9 %collective-permute-done.7 = f32[2,2,2,112,128]{4,3,2,1,0:T(8,128)S(1)} collective-permute-done((f32[2,2,2,112,128]{4,3,2,1,0:T(8,128)S(1)}, f32[2,2,2,112,128]{4,3,2,1,0:T(8,128)S(1)}, u32[]{:S(2)}, u32[]{:S(2)}) %collective-permute-start.7) | collective-permute-done | bytes 458784 | tf_op jit(solution)/shard_map/ppermute | solution.py:191
  96.8 4.4 %collective-permute-start.8 = (f32[2,2,112,128]{3,2,1,0:T(8,128)S(1)}, f32[2,2,112,128]{3,2,1,0:T(8,128)S(1)}, u32[]{:S(2)}, u32[]{:S(2)}) collective-permute-start(f32[2,2,112,128]{3,2,1,0:T(8,128)S(1)} %bitcast_select_fusion.4), channel_id=1, source_target_pairs={{0,3},{1,2},{2,1},{3,0},{4,7},{5,6},{6,5},{7,4},{8,11},{9,10},{10,... | collective-permute-start | bytes 688136 | tf_op jit(solution)/shard_map/ppermute | solution.py:191
  101.2 4.8 %collective-permute-done.8 = f32[2,2,112,128]{3,2,1,0:T(8,128)S(1)} collective-permute-done((f32[2,2,112,128]{3,2,1,0:T(8,128)S(1)}, f32[2,2,112,128]{3,2,1,0:T(8,128)S(1)}, u32[]{:S(2)}, u32[]{:S(2)}) %collective-permute-start.8) | collective-permute-done | bytes 229408 | tf_op jit(solution)/shard_map/ppermute | solution.py:191
  106.1 3.2 %collective-permute-start.9 = (f32[2,112,128]{2,1,0:T(8,128)S(1)}, f32[2,112,128]{2,1,0:T(8,128)S(1)}, u32[]{:S(2)}, u32[]{:S(2)}) collective-permute-start(f32[2,112,128]{2,1,0:T(8,128)S(1)} %select_bitcast_fusion), channel_id=1, source_target_pairs={{0,12},{1,13},{2,14},{3,15},{4,8},{5,9},{6,10},{7,11},{8,4},{9,5},... | collective-permute-start | bytes 344072 | tf_op jit(solution)/shard_map/ppermute | solution.py:191
  109.6 4.5 %collective-permute-done.9 = f32[2,112,128]{2,1,0:T(8,128)S(1)} collective-permute-done((f32[2,112,128]{2,1,0:T(8,128)S(1)}, f32[2,112,128]{2,1,0:T(8,128)S(1)}, u32[]{:S(2)}, u32[]{:S(2)}) %collective-permute-start.9) | collective-permute-done | bytes 114720 | tf_op jit(solution)/shard_map/ppermute | solution.py:191
  114.2 15.5 %collective-permute-start.10 = (f32[112,128]{1,0:T(8,128)S(1)}, f32[112,128]{1,0:T(8,128)S(1)}, u32[]{:S(2)}, u32[]{:S(2)}) collective-permute-start(f32[112,128]{1,0:T(8,128)S(1)} %dynamic-slice_bitcast_fusion), channel_id=1, source_target_pairs={{0,256},{128,384},{256,0},{384,128},{1,257},{129,385},{257,1},{385... | collective-permute-start | bytes 172040 | tf_op jit(solution)/shard_map/ppermute | solution.py:178
  129.8 0.9 fusion.10
  130.9 1.4 collective-permute-done.10
  132.3 3.5 %collective-permute-start.11 = (f32[112,128]{1,0:T(8,128)S(1)}, f32[112,128]{1,0:T(8,128)S(1)}, u32[]{:S(2)}, u32[]{:S(2)}) collective-permute-start(f32[112,128]{1,0:T(8,128)S(1)} %bitcast_add_fusion.1), channel_id=1, source_target_pairs={{0,16},{16,0},{32,48},{48,32},{64,80},{80,64},{96,112},{112,96},{1... | collective-permute-start | bytes 172040 | tf_op jit(solution)/shard_map/ppermute | solution.py:178
  135.8 0.9 fusion.11
  136.9 1.4 collective-permute-done.11
  138.3 5.0 %collective-permute-start.12 = (f32[112,128]{1,0:T(8,128)S(1)}, f32[112,128]{1,0:T(8,128)S(1)}, u32[]{:S(2)}, u32[]{:S(2)}) collective-permute-start(f32[112,128]{1,0:T(8,128)S(1)} %add.207), channel_id=1, source_target_pairs={{0,32},{16,48},{32,0},{48,16},{64,96},{80,112},{96,64},{112,80},{1... | collective-permute-start | bytes 172040 | tf_op jit(solution)/shard_map/ppermute | solution.py:178
  143.3 0.9 fusion.15
  144.3 1.2 collective-permute-done.12
  145.5 7.7 %collective-permute-start.13 = (f32[112,128]{1,0:T(8,128)S(1)}, f32[112,128]{1,0:T(8,128)S(1)}, u32[]{:S(2)}, u32[]{:S(2)}) collective-permute-start(f32[112,128]{1,0:T(8,128)S(1)} %add.208), channel_id=1, source_target_pairs={{0,64},{16,80},{32,96},{48,112},{64,0},{80,16},{96,32},{112,48},{1... | collective-permute-start | bytes 172040 | tf_op jit(solution)/shard_map/ppermute | solution.py:178
  153.2 0.6 copy.288
  153.9 1.6 collective-permute-done.13
  155.5 23.3 %all-gather = bf16[1792,128]{1,0:T(8,128)(2,1)S(1)} all-gather(bf16[112,128]{1,0:T(8,128)(2,1)S(1)} %add_convert_fusion), channel_id=2, replica_groups=mesh['dp'=4,'tm'=8,'height'=16] {'height'}, dimensions={0}, use_global_device_ids=true | all-gather | bytes 487424 | tf_op jit(solution)/shard_map/all_gather | solution.py:244
  178.8 0.6 gather_fusion
  179.5 0.8 fusion.165
  (133 shorter events, 6.7 us)
Async XLA Ops:
  2.7 15.9 %collective-permute-start.1 = (bf16[40960]{0:T(1024)(128)(2,1)S(1)}, bf16[40960]{0:T(1024)(128)(2,1)S(1)}, u32[]{:S(2)}, u32[]{:S(2)}) collective-permute-start(bf16[40960]{0:T(1024)(128)(2,1)S(1)} %pad_maximum_fusion.6), channel_id=1, source_target_pairs={{1,0},{2,1},{3,2},{4,3},{5,4},{6,5},{7,6},{8,7},{9,8},{10,9},{11,1... | collective-permute-start | bytes 245768 | tf_op jit(solution)/shard_map/ppermute | solution.py:30
  8.0 12.0 %collective-permute-start = (bf16[2,2,128,128]{3,0,2,1:T(2,128)(2,1)S(1)}, bf16[2,2,128,128]{3,0,2,1:T(2,128)(2,1)S(1)}, u32[]{:S(2)}, u32[]{:S(2)}) collective-permute-start(bf16[2,2,128,128]{3,0,2,1:T(2,128)(2,1)S(1)} %slice.201), channel_id=1, source_target_pairs={{0,1},{1,2},{2,3},{3,4},{4,5},{5,6},{6,7},{7,8},{8,9},{9,10},{10,1... | collective-permute-start | bytes 393224 | tf_op jit(solution)/shard_map/ppermute | solution.py:30
  13.1 4.9 %copy-start.7 = (bf16[1,1,2,64,128]{4,3,2,1,0:T(8,128)(2,1)S(1)}, bf16[1,1,2,64,128]{4,3,2,1,0:T(8,128)(2,1)}, u32[]{:S(2)}) copy-start(bf16[1,1,2,64,128]{4,3,2,1,0:T(8,128)(2,1)} %param.11) | copy-start | bytes 98308
  18.8 7.8 %collective-permute-start.4 = (bf16[1,3,64,128]{3,2,1,0:T(8,128)(2,1)S(1)}, bf16[1,3,64,128]{3,2,1,0:T(8,128)(2,1)S(1)}, u32[]{:S(2)}, u32[]{:S(2)}) collective-permute-start(bf16[1,3,64,128]{3,2,1,0:T(8,128)(2,1)S(1)} %pad_maximum_fusion.7), channel_id=1, source_target_pairs={{16,0},{32,16},{48,32},{64,48},{80,64},{96,80},{112,96},{17,1},{33... | collective-permute-start | bytes 147464 | tf_op jit(solution)/shard_map/ppermute | solution.py:30
  20.8 7.2 %copy-start.11 = (bf16[3,3,3,128,128]{4,3,2,1,0:T(8,128)(2,1)S(1)}, bf16[3,3,3,128,128]{4,3,2,1,0:T(8,128)(2,1)}, u32[]{:S(2)}) copy-start(bf16[3,3,3,128,128]{4,3,2,1,0:T(8,128)(2,1)} %param.10) | copy-start | bytes 2654212
  20.8 7.2 %copy-start.14 = (pred[8,18]{0,1:T(8,128)(4,1)S(1)}, pred[8,18]{0,1:T(8,128)(4,1)}, u32[]{:S(2)}) copy-start(pred[8,18]{0,1:T(8,128)(4,1)} %constant.267) | copy-start | bytes 436
  21.5 6.9 %copy-start.4 = (bf16[2,7,128,128]{3,0,2,1:T(2,128)(2,1)}, bf16[2,7,128,128]{3,0,2,1:T(2,128)(2,1)S(1)}, u32[]{:S(2)}) copy-start(bf16[2,7,128,128]{3,0,2,1:T(2,128)(2,1)S(1)} %pad_maximum_fusion.2) | copy-start | bytes 1376260
  22.0 13.9 %collective-permute-start.2 = (bf16[2,7,128,128]{3,0,2,1:T(2,128)(2,1)S(1)}, bf16[2,7,128,128]{3,0,2,1:T(2,128)(2,1)S(1)}, u32[]{:S(2)}, u32[]{:S(2)}) collective-permute-start(bf16[2,7,128,128]{3,0,2,1:T(2,128)(2,1)S(1)} %pad_maximum_fusion.2), channel_id=1, source_target_pairs={{0,16},{16,32},{32,48},{48,64},{64,80},{80,96},{96,112},{1,17},{17... | collective-permute-start | bytes 1376264 | tf_op jit(solution)/shard_map/ppermute | solution.py:30
  28.5 1.2 copy-start.3
  28.5 1.5 copy-start.10
  28.5 1.4 copy-start.13
  37.4 1.2 copy-start.2
  41.7 5.2 %copy-start.6 = (f32[5,16,17,128]{3,1,2,0:T(8,128)S(1)}, f32[5,16,17,128]{3,1,2,0:T(8,128)}, u32[]{:S(2)}) copy-start(f32[5,16,17,128]{3,1,2,0:T(8,128)} %get-tuple-element.58) | copy-start | bytes 2088964
  42.3 14.3 %collective-permute-start.3 = (bf16[2,5,128,128]{3,0,2,1:T(2,128)(2,1)S(1)}, bf16[2,5,128,128]{3,0,2,1:T(2,128)(2,1)S(1)}, u32[]{:S(2)}, u32[]{:S(2)}) collective-permute-start(bf16[2,5,128,128]{3,0,2,1:T(2,128)(2,1)S(1)} %bitcast.287), channel_id=1, source_target_pairs={{0,16},{16,32},{32,48},{48,64},{64,80},{80,96},{96,112},{1,17},{17... | collective-permute-start | bytes 983048 | tf_op jit(solution)/shard_map/ppermute | solution.py:30
  47.6 1.0 copy-start.5
  57.1 1.1 copy-start
  57.3 0.9 copy-start.8
  61.2 5.8 %collective-permute-start.5 = (f32[2,2,2,2,2,112,128]{6,5,4,3,2,1,0:T(8,128)S(1)}, f32[2,2,2,2,2,112,128]{6,5,4,3,2,1,0:T(8,128)}, u32[]{:S(2)}, u32[]{:S(2)}) collective-permute-start(f32[2,2,2,2,2,112,128]{6,5,4,3,2,1,0:T(8,128)S(1)} %bitcast.284), channel_id=1, source_target_pairs={{0,128},{128,0},{256,384},{384,256},{1,129},{129,1},{257,385},{385... | collective-permute-start | bytes 5505032 | tf_op jit(solution)/shard_map/ppermute | solution.py:178
  69.5 15.4 %collective-permute-start.6 = (f32[2,2,2,2,112,128]{5,4,3,2,1,0:T(8,128)S(1)}, f32[2,2,2,2,112,128]{5,4,3,2,1,0:T(8,128)}, u32[]{:S(2)}, u32[]{:S(2)}) collective-permute-start(f32[2,2,2,2,112,128]{5,4,3,2,1,0:T(8,128)S(1)} %bitcast_select_fusion), channel_id=1, source_target_pairs={{0,1},{1,0},{2,3},{3,2},{4,5},{5,4},{6,7},{7,6},{8,9},{9,8},{10,11... | collective-permute-start | bytes 2752520 | tf_op jit(solution)/shard_map/ppermute | solution.py:191
  86.3 10.4 %collective-permute-start.7 = (f32[2,2,2,112,128]{4,3,2,1,0:T(8,128)S(1)}, f32[2,2,2,112,128]{4,3,2,1,0:T(8,128)S(1)}, u32[]{:S(2)}, u32[]{:S(2)}) collective-permute-start(f32[2,2,2,112,128]{4,3,2,1,0:T(8,128)S(1)} %bitcast_select_fusion.2), channel_id=1, source_target_pairs={{0,4},{1,5},{2,6},{3,7},{4,0},{5,1},{6,2},{7,3},{8,12},{9,13},{10,... | collective-permute-start | bytes 1376264 | tf_op jit(solution)/shard_map/ppermute | solution.py:191
  88.8 20.6 %copy-start.9 = (s32[16]{0:T(128)S(1)}, s32[16]{0:T(128)}, u32[]{:S(2)}) copy-start(s32[16]{0:T(128)} %constant.273) | copy-start | bytes 196
  96.7 33.0 %copy-start.12 = (bf16[3,3,3,128,128]{4,3,2,1,0:T(8,128)(2,1)S(1)}, bf16[3,3,3,128,128]{4,3,2,1,0:T(8,128)(2,1)}, u32[]{:S(2)}) copy-start(bf16[3,3,3,128,128]{4,3,2,1,0:T(8,128)(2,1)} %param.10) | copy-start | bytes 2654212
  96.8 33.0 %copy-start.15 = (pred[8,9]{0,1:T(8,128)(4,1)S(1)}, pred[8,9]{0,1:T(8,128)(4,1)}, u32[]{:S(2)}) copy-start(pred[8,9]{0,1:T(8,128)(4,1)} %constant.263) | copy-start | bytes 220
  96.8 9.3 %collective-permute-start.8 = (f32[2,2,112,128]{3,2,1,0:T(8,128)S(1)}, f32[2,2,112,128]{3,2,1,0:T(8,128)S(1)}, u32[]{:S(2)}, u32[]{:S(2)}) collective-permute-start(f32[2,2,112,128]{3,2,1,0:T(8,128)S(1)} %bitcast_select_fusion.4), channel_id=1, source_target_pairs={{0,3},{1,2},{2,1},{3,0},{4,7},{5,6},{6,5},{7,4},{8,11},{9,10},{10,... | collective-permute-start | bytes 688136 | tf_op jit(solution)/shard_map/ppermute | solution.py:191
  106.1 24.6 %copy-start.1 = (bf16[1,5,128,128]{3,0,2,1:T(2,128)(2,1)S(1)}, bf16[1,5,128,128]{3,0,2,1:T(2,128)(2,1)}, u32[]{:S(2)}) copy-start(bf16[1,5,128,128]{3,0,2,1:T(2,128)(2,1)} %copy-done) | copy-start | bytes 491524
  106.1 8.0 %collective-permute-start.9 = (f32[2,112,128]{2,1,0:T(8,128)S(1)}, f32[2,112,128]{2,1,0:T(8,128)S(1)}, u32[]{:S(2)}, u32[]{:S(2)}) collective-permute-start(f32[2,112,128]{2,1,0:T(8,128)S(1)} %select_bitcast_fusion), channel_id=1, source_target_pairs={{0,12},{1,13},{2,14},{3,15},{4,8},{5,9},{6,10},{7,11},{8,4},{9,5},... | collective-permute-start | bytes 344072 | tf_op jit(solution)/shard_map/ppermute | solution.py:191
  114.2 18.1 %collective-permute-start.10 = (f32[112,128]{1,0:T(8,128)S(1)}, f32[112,128]{1,0:T(8,128)S(1)}, u32[]{:S(2)}, u32[]{:S(2)}) collective-permute-start(f32[112,128]{1,0:T(8,128)S(1)} %dynamic-slice_bitcast_fusion), channel_id=1, source_target_pairs={{0,256},{128,384},{256,0},{384,128},{1,257},{129,385},{257,1},{385... | collective-permute-start | bytes 172040 | tf_op jit(solution)/shard_map/ppermute | solution.py:178
  132.3 6.1 %collective-permute-start.11 = (f32[112,128]{1,0:T(8,128)S(1)}, f32[112,128]{1,0:T(8,128)S(1)}, u32[]{:S(2)}, u32[]{:S(2)}) collective-permute-start(f32[112,128]{1,0:T(8,128)S(1)} %bitcast_add_fusion.1), channel_id=1, source_target_pairs={{0,16},{16,0},{32,48},{48,32},{64,80},{80,64},{96,112},{112,96},{1... | collective-permute-start | bytes 172040 | tf_op jit(solution)/shard_map/ppermute | solution.py:178
  138.3 7.2 %collective-permute-start.12 = (f32[112,128]{1,0:T(8,128)S(1)}, f32[112,128]{1,0:T(8,128)S(1)}, u32[]{:S(2)}, u32[]{:S(2)}) collective-permute-start(f32[112,128]{1,0:T(8,128)S(1)} %add.207), channel_id=1, source_target_pairs={{0,32},{16,48},{32,0},{48,16},{64,96},{80,112},{96,64},{112,80},{1... | collective-permute-start | bytes 172040 | tf_op jit(solution)/shard_map/ppermute | solution.py:178
  145.5 10.0 %collective-permute-start.13 = (f32[112,128]{1,0:T(8,128)S(1)}, f32[112,128]{1,0:T(8,128)S(1)}, u32[]{:S(2)}, u32[]{:S(2)}) collective-permute-start(f32[112,128]{1,0:T(8,128)S(1)} %add.208), channel_id=1, source_target_pairs={{0,64},{16,80},{32,96},{48,112},{64,0},{80,16},{96,32},{112,48},{1... | collective-permute-start | bytes 172040 | tf_op jit(solution)/shard_map/ppermute | solution.py:178
